TPU v7x, 32 devices: a whole 2x2x4 slice. The times are simulated.
32 devices in a mesh: survey: 2 (over x), dom: 16 (over z, y, core).
Axes of the slice: x: 2, y: 2, z: 4, core: 2. Of those that a mesh axis runs over, the one named last changes fastest.
Arguments:
- older_fields: float32 [2, 256, 128, 128], P(None, 'survey', 'dom'), parts along dimension 1, may hold values from -6 to 6
- fields_now: float32 [2, 256, 128, 128], P(None, 'survey', 'dom'), parts along dimension 1, may hold values from -6 to 6
- velocity: float32 [128, 256, 128], P('dom', 'survey'), parts along dimension 1, may hold values from 1.5 to 4.5
- aperture: int32 [32], P('survey'), parts along dimension 0, may hold values from 0 to 15, as said below
- source_pos: int32 [3, 16], P(None, 'survey'), parts along dimension 1, may hold values from 0 to 127, as said below
- wavelet: float32 [20, 16], P(None, 'survey'), parts along dimension 1, may hold values from -16 to 16
- receiver_pos: int32 [3, 16384], P(None, 'survey'), parts along dimension 1, may hold values from 0 to 127, as said below
- traces: float32 [20, 16384], P(None, 'survey'), parts along dimension 1, may hold values from -16 to 16
Outputs:
- older_out: float32 [2, 256, 128, 128], P(None, 'survey', 'dom'), parts along dimension 1
- fields_out: float32 [2, 256, 128, 128], P(None, 'survey', 'dom'), parts along dimension 1
- image_model: float32 [128, 256, 128], P('dom', 'survey'), parts along dimension 1
There are 2 independent parts, one for each index of `survey`. A program takes and returns all parts, laid end to end along the dimension named above; each array names one. Nothing has to cross between parts.
Inputs may be any that keep to these rules, and one draw needn't show every extreme that they name: aperture[j] = min(max(j + s, 0), 15) for one shift s with |s| <= 4. `source_pos`: row 0 holds x below 128, row 1 y below 128, row 2 depth below 4. `receiver_pos`: row 0 holds x below 128, row 1 y below 128, row 2 depth below 4.
All inputs are finite; a program needn't handle non-finite values.
Results may differ from a plain program's by a relative error of at most 0.0003.
Values sent between devices are 32-bit elements; how exact they have to be, the bound alone decides.
No kernel may reach another device: no remote copies, remote signals or barrier semaphores. Data moves between devices by JAX's collectives and lax.ppermute only.
A program may use at most 64 MiB of HBM per device.

v0:
```python
import jax
import jax.numpy as jnp
from jax import lax
from jax.sharding import PartitionSpec as P

courant = 0.09
stencil_weights = (8.0 / 5.0, -1.0 / 5.0, 8.0 / 315.0, -1.0 / 560.0)
center_weight = 3.0 * (-205.0 / 72.0)


def with_halo(cells, sides, width):
    for axis, dim in sides:
        count = lax.axis_size(axis)
        ends = count - 1
        head = lax.slice_in_dim(cells, 0, width, axis=dim)
        tail = lax.slice_in_dim(cells, cells.shape[dim] - width, cells.shape[dim], axis=dim)
        cells = jnp.concatenate(
            [
                lax.ppermute(tail, axis, [(i, (i + 1) % count) for i in range(ends)]),
                cells,
                lax.ppermute(head, axis, [((i + 1) % count, i) for i in range(ends)]),
            ],
            axis=dim,
        )
    return cells


def laplace(extended):
    cells_wide = extended.shape[2] - 8
    depth_y = extended.shape[1]
    depth_z = extended.shape[3]
    middle = extended[:, :, 4 : 4 + cells_wide, :]
    padded = jnp.pad(middle, ((0, 0), (4, 4), (0, 0), (4, 4)))
    summed = center_weight * middle
    for offset in range(1, 5):
        weight = stencil_weights[offset - 1]
        beside_all = (
            extended[:, :, 4 + offset : 4 + offset + cells_wide, :]
            + extended[:, :, 4 - offset : 4 - offset + cells_wide, :]
        )
        beside_all = (
            beside_all
            + padded[:, 4 + offset : 4 + offset + depth_y, :, 4 : 4 + depth_z]
            + padded[:, 4 - offset : 4 - offset + depth_y, :, 4 : 4 + depth_z]
        )
        beside_all = (
            beside_all
            + padded[:, 4 : 4 + depth_y, :, 4 + offset : 4 + offset + depth_z]
            + padded[:, 4 : 4 + depth_y, :, 4 - offset : 4 - offset + depth_z]
        )
        summed = summed + weight * beside_all
    return summed


def point_tables(cell_rows, x_start, cells_wide, depth_y):
    local_x = cell_rows[0] - x_start
    inside = (local_x >= 0) & (local_x < cells_wide)
    rows_y = (cell_rows[1][:, None] == jnp.arange(depth_y, dtype=jnp.int32)[None, :]).astype(
        jnp.float32
    )
    column = local_x * 4 + cell_rows[2]
    places = (column[:, None] == jnp.arange(cells_wide * 4, dtype=jnp.int32)[None, :]) & inside[
        :, None
    ]
    return (rows_y, places.astype(jnp.float32))


def spread_points(tables, amounts, depth_z):
    rows_y, places = tables
    weighted = rows_y * amounts[:, None]
    plane = jnp.einsum("ny,nc->yc", weighted, places, precision=lax.Precision.HIGHEST)
    plane = plane.reshape(rows_y.shape[1], places.shape[1] // 4, 4)
    return jnp.pad(plane, ((0, 0), (0, 0), (0, depth_z - 4)))


def inject(laplacian, source_tables, receiver_tables, pulses, recorded):
    depth_z = laplacian.shape[3]
    added = jnp.stack(
        [
            spread_points(source_tables, pulses, depth_z),
            spread_points(receiver_tables, recorded, depth_z),
        ]
    )
    return laplacian + added


def shards(older_fields, fields_now, velocity, aperture, source_pos, wavelet, receiver_pos, traces):
    slab_count = lax.axis_size("dom")
    depth_y = fields_now.shape[1]
    cells_x = fields_now.shape[2]
    depth_z = fields_now.shape[3]
    block_y = velocity.shape[0]
    steps_total = wavelet.shape[0]
    x_anchor = lax.axis_index("dom") * cells_x
    bricks = velocity.reshape(block_y, slab_count, cells_x, depth_z)
    chosen = jnp.take(bricks, aperture, axis=1)
    arrived = lax.all_to_all(chosen, "dom", split_axis=1, concat_axis=0, tiled=True)
    scaled = courant * arrived.reshape(depth_y, cells_x, depth_z)
    speed_sq = scaled * scaled
    image_zero = jnp.zeros((depth_y, cells_x, depth_z), jnp.float32)
    source_core = point_tables(source_pos, x_anchor, cells_x, depth_y)
    receiver_core = point_tables(receiver_pos, x_anchor, cells_x, depth_y)

    def amounts_at(moment):
        pulses = lax.dynamic_index_in_dim(wavelet, moment, 0, keepdims=False)
        recorded = lax.dynamic_index_in_dim(traces, moment, 0, keepdims=False)
        return (pulses, recorded)

    def advance(moment, state_carry):
        previous, current, image_acc = state_carry
        extended = with_halo(current, (("dom", 2),), 4)
        pulses, recorded = amounts_at(moment)
        laplacian = inject(laplace(extended), source_core, receiver_core, pulses, recorded)
        updated = 2.0 * current - previous + speed_sq[None] * laplacian
        image_acc = image_acc + updated[0] * updated[1]
        return (current, updated, image_acc)

    previous, current, image_acc = lax.fori_loop(
        0, steps_total, advance, (older_fields, fields_now, image_zero)
    )
    image_acc = image_acc * (1.0 / steps_total)
    outgoing = image_acc.reshape(depth_y, 1, cells_x, depth_z)
    one_hot = (aperture[None, :] == jnp.arange(slab_count, dtype=jnp.int32)[:, None]).astype(
        jnp.float32
    )
    received = lax.all_to_all(outgoing, "dom", split_axis=0, concat_axis=1, tiled=True)
    summed = jnp.einsum("mj,yjcz->ymcz", one_hot, received, precision=lax.Precision.HIGHEST)
    image_model = summed.reshape(received.shape[0], slab_count * cells_x, received.shape[3])
    return (previous, current, image_model)


def solution(mesh):
    in_specs = (
        P(None, "survey", "dom", None),
        P(None, "survey", "dom", None),
        P("dom", "survey", None),
        P("survey"),
        P(None, "survey"),
        P(None, "survey"),
        P(None, "survey"),
        P(None, "survey"),
    )
    out_specs = (
        P(None, "survey", "dom", None),
        P(None, "survey", "dom", None),
        P("dom", "survey", None),
    )
    return jax.shard_map(shards, mesh=mesh, in_specs=in_specs, out_specs=out_specs, check_vma=False)
```

profile of v0, /device:TPU:0, one launch (start us, length us, event | category | flops | bytes accessed | tf_op | source)
XLA Modules:
  0.0 510.4 jit_solution(12228661833826001847)
XLA Ops:
  3.6 7.4 %all-to-all-start = ((f32[8,16,8,128]{3,2,0,1:T(8,128)}), f32[8,16,8,128]{3,2,0,1:T(8,128)S(1)}, u32[]{:S(2)}, u32[]{:S(2)}) async-start(f32[8,16,8,128]{3,2,0,1:T(8,128)} %select_bitcast_fusion), calls=%async_computation | async-start | bytes 1048576 | tf_op jit(solution)/shard_map/all_to_all | solution.py:97
  14.5 10.9 %all-to-all-done = f32[8,16,8,128]{3,2,0,1:T(8,128)S(1)} async-done(((f32[8,16,8,128]{3,2,0,1:T(8,128)}), f32[8,16,8,128]{3,2,0,1:T(8,128)S(1)}, u32[]{:S(2)}, u32[]{:S(2)}) %all-to-all-start) | async-done | bytes 524320 | tf_op jit(solution)/shard_map/all_to_all | solution.py:97
  27.5 454.9 %while.20 = (s32[]{:T(128)}, f32[2,128,8,128]{1,3,2,0:T(8,128)S(1)}, f32[2,128,8,128]{1,3,2,0:T(8,128)S(1)}, f32[128,8,128]{0,2,1:T(8,128)}, f32[128,8,128]{0,2,...) while((s32[]{:T(128)}, ...), condition=%wide.region_1.2_spmd.clone, body=%wide.region_0.1_spmd.clone.sunk | while | flops 415501056 | bytes 36413908 | solution.py:118
  46.0 8.1 %collective-permute-start = (f32[2,128,4,128]{1,3,2,0:T(8,128)}, f32[2,128,4,128]{1,3,2,0:T(8,128)}, u32[]{:S(2)}, u32[]{:S(2)}) collective-permute-start(f32[2,128,4,128]{1,3,2,0:T(8,128)} %get-tuple-element.513), channel_id=1, source_target_pairs={{0,1},{1,2},{2,3},{3,4},{4,5},{5,6},{6,7},{7,8},{8,9},{9,10},{10,1... | collective-permute-start | bytes 1572872 | tf_op jit(solution)/shard_map/while/body/eval_jaxpr/ppermute | solution.py:19
  68.7 10.0 %collective-permute-start = (f32[2,128,4,128]{1,3,2,0:T(8,128)}, f32[2,128,4,128]{1,3,2,0:T(8,128)}, u32[]{:S(2)}, u32[]{:S(2)}) collective-permute-start(f32[2,128,4,128]{1,3,2,0:T(8,128)} %get-tuple-element.513), channel_id=1, source_target_pairs={{0,1},{1,2},{2,3},{3,4},{4,5},{5,6},{6,7},{7,8},{8,9},{9,10},{10,1... | collective-permute-start | bytes 1572872 | tf_op jit(solution)/shard_map/while/body/eval_jaxpr/ppermute | solution.py:19
  93.3 10.0 %collective-permute-start = (f32[2,128,4,128]{1,3,2,0:T(8,128)}, f32[2,128,4,128]{1,3,2,0:T(8,128)}, u32[]{:S(2)}, u32[]{:S(2)}) collective-permute-start(f32[2,128,4,128]{1,3,2,0:T(8,128)} %get-tuple-element.513), channel_id=1, source_target_pairs={{0,1},{1,2},{2,3},{3,4},{4,5},{5,6},{6,7},{7,8},{8,9},{9,10},{10,1... | collective-permute-start | bytes 1572872 | tf_op jit(solution)/shard_map/while/body/eval_jaxpr/ppermute | solution.py:19
  105.6 3.7 fusion.79
  118.0 10.0 %collective-permute-start = (f32[2,128,4,128]{1,3,2,0:T(8,128)}, f32[2,128,4,128]{1,3,2,0:T(8,128)}, u32[]{:S(2)}, u32[]{:S(2)}) collective-permute-start(f32[2,128,4,128]{1,3,2,0:T(8,128)} %get-tuple-element.513), channel_id=1, source_target_pairs={{0,1},{1,2},{2,3},{3,4},{4,5},{5,6},{6,7},{7,8},{8,9},{9,10},{10,1... | collective-permute-start | bytes 1572872 | tf_op jit(solution)/shard_map/while/body/eval_jaxpr/ppermute | solution.py:19
  130.2 3.7 fusion.79
  142.6 8.7 %collective-permute-start = (f32[2,128,4,128]{1,3,2,0:T(8,128)}, f32[2,128,4,128]{1,3,2,0:T(8,128)}, u32[]{:S(2)}, u32[]{:S(2)}) collective-permute-start(f32[2,128,4,128]{1,3,2,0:T(8,128)} %get-tuple-element.513), channel_id=1, source_target_pairs={{0,1},{1,2},{2,3},{3,4},{4,5},{5,6},{6,7},{7,8},{8,9},{9,10},{10,1... | collective-permute-start | bytes 1572872 | tf_op jit(solution)/shard_map/while/body/eval_jaxpr/ppermute | solution.py:19
  153.5 3.7 fusion.79
  165.9 8.7 %collective-permute-start = (f32[2,128,4,128]{1,3,2,0:T(8,128)}, f32[2,128,4,128]{1,3,2,0:T(8,128)}, u32[]{:S(2)}, u32[]{:S(2)}) collective-permute-start(f32[2,128,4,128]{1,3,2,0:T(8,128)} %get-tuple-element.513), channel_id=1, source_target_pairs={{0,1},{1,2},{2,3},{3,4},{4,5},{5,6},{6,7},{7,8},{8,9},{9,10},{10,1... | collective-permute-start | bytes 1572872 | tf_op jit(solution)/shard_map/while/body/eval_jaxpr/ppermute | solution.py:19
  189.2 7.4 %collective-permute-start = (f32[2,128,4,128]{1,3,2,0:T(8,128)}, f32[2,128,4,128]{1,3,2,0:T(8,128)}, u32[]{:S(2)}, u32[]{:S(2)}) collective-permute-start(f32[2,128,4,128]{1,3,2,0:T(8,128)} %get-tuple-element.513), channel_id=1, source_target_pairs={{0,1},{1,2},{2,3},{3,4},{4,5},{5,6},{6,7},{7,8},{8,9},{9,10},{10,1... | collective-permute-start | bytes 1572872 | tf_op jit(solution)/shard_map/while/body/eval_jaxpr/ppermute | solution.py:19
  211.3 8.7 %collective-permute-start = (f32[2,128,4,128]{1,3,2,0:T(8,128)}, f32[2,128,4,128]{1,3,2,0:T(8,128)}, u32[]{:S(2)}, u32[]{:S(2)}) collective-permute-start(f32[2,128,4,128]{1,3,2,0:T(8,128)} %get-tuple-element.513), channel_id=1, source_target_pairs={{0,1},{1,2},{2,3},{3,4},{4,5},{5,6},{6,7},{7,8},{8,9},{9,10},{10,1... | collective-permute-start | bytes 1572872 | tf_op jit(solution)/shard_map/while/body/eval_jaxpr/ppermute | solution.py:19
  222.2 3.7 fusion.79
  234.6 7.4 %collective-permute-start = (f32[2,128,4,128]{1,3,2,0:T(8,128)}, f32[2,128,4,128]{1,3,2,0:T(8,128)}, u32[]{:S(2)}, u32[]{:S(2)}) collective-permute-start(f32[2,128,4,128]{1,3,2,0:T(8,128)} %get-tuple-element.513), channel_id=1, source_target_pairs={{0,1},{1,2},{2,3},{3,4},{4,5},{5,6},{6,7},{7,8},{8,9},{9,10},{10,1... | collective-permute-start | bytes 1572872 | tf_op jit(solution)/shard_map/while/body/eval_jaxpr/ppermute | solution.py:19
  244.3 3.7 fusion.79
  256.6 8.7 %collective-permute-start = (f32[2,128,4,128]{1,3,2,0:T(8,128)}, f32[2,128,4,128]{1,3,2,0:T(8,128)}, u32[]{:S(2)}, u32[]{:S(2)}) collective-permute-start(f32[2,128,4,128]{1,3,2,0:T(8,128)} %get-tuple-element.513), channel_id=1, source_target_pairs={{0,1},{1,2},{2,3},{3,4},{4,5},{5,6},{6,7},{7,8},{8,9},{9,10},{10,1... | collective-permute-start | bytes 1572872 | tf_op jit(solution)/shard_map/while/body/eval_jaxpr/ppermute | solution.py:19
  280.0 7.4 %collective-permute-start = (f32[2,128,4,128]{1,3,2,0:T(8,128)}, f32[2,128,4,128]{1,3,2,0:T(8,128)}, u32[]{:S(2)}, u32[]{:S(2)}) collective-permute-start(f32[2,128,4,128]{1,3,2,0:T(8,128)} %get-tuple-element.513), channel_id=1, source_target_pairs={{0,1},{1,2},{2,3},{3,4},{4,5},{5,6},{6,7},{7,8},{8,9},{9,10},{10,1... | collective-permute-start | bytes 1572872 | tf_op jit(solution)/shard_map/while/body/eval_jaxpr/ppermute | solution.py:19
  302.0 8.7 %collective-permute-start = (f32[2,128,4,128]{1,3,2,0:T(8,128)}, f32[2,128,4,128]{1,3,2,0:T(8,128)}, u32[]{:S(2)}, u32[]{:S(2)}) collective-permute-start(f32[2,128,4,128]{1,3,2,0:T(8,128)} %get-tuple-element.513), channel_id=1, source_target_pairs={{0,1},{1,2},{2,3},{3,4},{4,5},{5,6},{6,7},{7,8},{8,9},{9,10},{10,1... | collective-permute-start | bytes 1572872 | tf_op jit(solution)/shard_map/while/body/eval_jaxpr/ppermute | solution.py:19
  312.9 3.7 fusion.79
  325.3 7.4 %collective-permute-start = (f32[2,128,4,128]{1,3,2,0:T(8,128)}, f32[2,128,4,128]{1,3,2,0:T(8,128)}, u32[]{:S(2)}, u32[]{:S(2)}) collective-permute-start(f32[2,128,4,128]{1,3,2,0:T(8,128)} %get-tuple-element.513), channel_id=1, source_target_pairs={{0,1},{1,2},{2,3},{3,4},{4,5},{5,6},{6,7},{7,8},{8,9},{9,10},{10,1... | collective-permute-start | bytes 1572872 | tf_op jit(solution)/shard_map/while/body/eval_jaxpr/ppermute | solution.py:19
  335.0 3.7 fusion.79
  347.4 8.7 %collective-permute-start = (f32[2,128,4,128]{1,3,2,0:T(8,128)}, f32[2,128,4,128]{1,3,2,0:T(8,128)}, u32[]{:S(2)}, u32[]{:S(2)}) collective-permute-start(f32[2,128,4,128]{1,3,2,0:T(8,128)} %get-tuple-element.513), channel_id=1, source_target_pairs={{0,1},{1,2},{2,3},{3,4},{4,5},{5,6},{6,7},{7,8},{8,9},{9,10},{10,1... | collective-permute-start | bytes 1572872 | tf_op jit(solution)/shard_map/while/body/eval_jaxpr/ppermute | solution.py:19
  370.7 7.4 %collective-permute-start = (f32[2,128,4,128]{1,3,2,0:T(8,128)}, f32[2,128,4,128]{1,3,2,0:T(8,128)}, u32[]{:S(2)}, u32[]{:S(2)}) collective-permute-start(f32[2,128,4,128]{1,3,2,0:T(8,128)} %get-tuple-element.513), channel_id=1, source_target_pairs={{0,1},{1,2},{2,3},{3,4},{4,5},{5,6},{6,7},{7,8},{8,9},{9,10},{10,1... | collective-permute-start | bytes 1572872 | tf_op jit(solution)/shard_map/while/body/eval_jaxpr/ppermute | solution.py:19
  392.7 8.7 %collective-permute-start = (f32[2,128,4,128]{1,3,2,0:T(8,128)}, f32[2,128,4,128]{1,3,2,0:T(8,128)}, u32[]{:S(2)}, u32[]{:S(2)}) collective-permute-start(f32[2,128,4,128]{1,3,2,0:T(8,128)} %get-tuple-element.513), channel_id=1, source_target_pairs={{0,1},{1,2},{2,3},{3,4},{4,5},{5,6},{6,7},{7,8},{8,9},{9,10},{10,1... | collective-permute-start | bytes 1572872 | tf_op jit(solution)/shard_map/while/body/eval_jaxpr/ppermute | solution.py:19
  403.7 3.7 fusion.79
  416.0 7.4 %collective-permute-start = (f32[2,128,4,128]{1,3,2,0:T(8,128)}, f32[2,128,4,128]{1,3,2,0:T(8,128)}, u32[]{:S(2)}, u32[]{:S(2)}) collective-permute-start(f32[2,128,4,128]{1,3,2,0:T(8,128)} %get-tuple-element.513), channel_id=1, source_target_pairs={{0,1},{1,2},{2,3},{3,4},{4,5},{5,6},{6,7},{7,8},{8,9},{9,10},{10,1... | collective-permute-start | bytes 1572872 | tf_op jit(solution)/shard_map/while/body/eval_jaxpr/ppermute | solution.py:19
  438.1 8.7 %collective-permute-start = (f32[2,128,4,128]{1,3,2,0:T(8,128)}, f32[2,128,4,128]{1,3,2,0:T(8,128)}, u32[]{:S(2)}, u32[]{:S(2)}) collective-permute-start(f32[2,128,4,128]{1,3,2,0:T(8,128)} %get-tuple-element.513), channel_id=1, source_target_pairs={{0,1},{1,2},{2,3},{3,4},{4,5},{5,6},{6,7},{7,8},{8,9},{9,10},{10,1... | collective-permute-start | bytes 1572872 | tf_op jit(solution)/shard_map/while/body/eval_jaxpr/ppermute | solution.py:19
  461.4 7.4 %collective-permute-start = (f32[2,128,4,128]{1,3,2,0:T(8,128)}, f32[2,128,4,128]{1,3,2,0:T(8,128)}, u32[]{:S(2)}, u32[]{:S(2)}) collective-permute-start(f32[2,128,4,128]{1,3,2,0:T(8,128)} %get-tuple-element.513), channel_id=1, source_target_pairs={{0,1},{1,2},{2,3},{3,4},{4,5},{5,6},{6,7},{7,8},{8,9},{9,10},{10,1... | collective-permute-start | bytes 1572872 | tf_op jit(solution)/shard_map/while/body/eval_jaxpr/ppermute | solution.py:19
  484.5 9.7 %all-to-all-start.1 = ((f32[128,1,8,128]{3,2,1,0:T(8,128)}), f32[128,1,8,128]{3,2,1,0:T(8,128)S(1)}, u32[]{:S(2)}, u32[]{:S(2)}) async-start(f32[128,1,8,128]{3,2,1,0:T(8,128)} %multiply_bitcast_fusion), calls=%async_computation.1 | async-start | bytes 1048576 | tf_op jit(solution)/shard_map/all_to_all | solution.py:126
  496.9 11.9 %all-to-all-done.1 = f32[128,1,8,128]{3,2,1,0:T(8,128)S(1)} async-done(((f32[128,1,8,128]{3,2,1,0:T(8,128)}), f32[128,1,8,128]{3,2,1,0:T(8,128)S(1)}, u32[]{:S(2)}, u32[]{:S(2)}) %all-to-all-start.1) | async-done | bytes 524320 | tf_op jit(solution)/shard_map/all_to_all | solution.py:126
  (424 shorter events, 278.3 us)
Async XLA Ops:
  3.6 21.9 %all-to-all-start = ((f32[8,16,8,128]{3,2,0,1:T(8,128)}), f32[8,16,8,128]{3,2,0,1:T(8,128)S(1)}, u32[]{:S(2)}, u32[]{:S(2)}) async-start(f32[8,16,8,128]{3,2,0,1:T(8,128)} %select_bitcast_fusion), calls=%async_computation | async-start | bytes 1048576 | tf_op jit(solution)/shard_map/all_to_all | solution.py:97
  28.6 9.1 %collective-permute-start = (f32[2,128,4,128]{1,3,2,0:T(8,128)}, f32[2,128,4,128]{1,3,2,0:T(8,128)}, u32[]{:S(2)}, u32[]{:S(2)}) collective-permute-start(f32[2,128,4,128]{1,3,2,0:T(8,128)} %get-tuple-element.513), channel_id=1, source_target_pairs={{0,1},{1,2},{2,3},{3,4},{4,5},{5,6},{6,7},{7,8},{8,9},{9,10},{10,1... | collective-permute-start | bytes 1572872 | tf_op jit(solution)/shard_map/while/body/eval_jaxpr/ppermute | solution.py:19
  31.3 7.8 %collective-permute-start.1 = (f32[2,128,4,128]{1,3,2,0:T(8,128)}, f32[2,128,4,128]{1,3,2,0:T(8,128)}, u32[]{:S(2)}, u32[]{:S(2)}) collective-permute-start(f32[2,128,4,128]{1,3,2,0:T(8,128)} %get-tuple-element.516), channel_id=1, source_target_pairs={{1,0},{2,1},{3,2},{4,3},{5,4},{6,5},{7,6},{8,7},{9,8},{10,9},{11,1... | collective-permute-start | bytes 1572872 | tf_op jit(solution)/shard_map/while/body/eval_jaxpr/ppermute | solution.py:21
  46.0 14.5 %collective-permute-start = (f32[2,128,4,128]{1,3,2,0:T(8,128)}, f32[2,128,4,128]{1,3,2,0:T(8,128)}, u32[]{:S(2)}, u32[]{:S(2)}) collective-permute-start(f32[2,128,4,128]{1,3,2,0:T(8,128)} %get-tuple-element.513), channel_id=1, source_target_pairs={{0,1},{1,2},{2,3},{3,4},{4,5},{5,6},{6,7},{7,8},{8,9},{9,10},{10,1... | collective-permute-start | bytes 1572872 | tf_op jit(solution)/shard_map/while/body/eval_jaxpr/ppermute | solution.py:19
  54.0 7.8 %collective-permute-start.1 = (f32[2,128,4,128]{1,3,2,0:T(8,128)}, f32[2,128,4,128]{1,3,2,0:T(8,128)}, u32[]{:S(2)}, u32[]{:S(2)}) collective-permute-start(f32[2,128,4,128]{1,3,2,0:T(8,128)} %get-tuple-element.516), channel_id=1, source_target_pairs={{1,0},{2,1},{3,2},{4,3},{5,4},{6,5},{7,6},{8,7},{9,8},{10,9},{11,1... | collective-permute-start | bytes 1572872 | tf_op jit(solution)/shard_map/while/body/eval_jaxpr/ppermute | solution.py:21
  68.7 16.4 %collective-permute-start = (f32[2,128,4,128]{1,3,2,0:T(8,128)}, f32[2,128,4,128]{1,3,2,0:T(8,128)}, u32[]{:S(2)}, u32[]{:S(2)}) collective-permute-start(f32[2,128,4,128]{1,3,2,0:T(8,128)} %get-tuple-element.513), channel_id=1, source_target_pairs={{0,1},{1,2},{2,3},{3,4},{4,5},{5,6},{6,7},{7,8},{8,9},{9,10},{10,1... | collective-permute-start | bytes 1572872 | tf_op jit(solution)/shard_map/while/body/eval_jaxpr/ppermute | solution.py:19
  78.7 7.8 %collective-permute-start.1 = (f32[2,128,4,128]{1,3,2,0:T(8,128)}, f32[2,128,4,128]{1,3,2,0:T(8,128)}, u32[]{:S(2)}, u32[]{:S(2)}) collective-permute-start(f32[2,128,4,128]{1,3,2,0:T(8,128)} %get-tuple-element.516), channel_id=1, source_target_pairs={{1,0},{2,1},{3,2},{4,3},{5,4},{6,5},{7,6},{8,7},{9,8},{10,9},{11,1... | collective-permute-start | bytes 1572872 | tf_op jit(solution)/shard_map/while/body/eval_jaxpr/ppermute | solution.py:21
  93.3 16.4 %collective-permute-start = (f32[2,128,4,128]{1,3,2,0:T(8,128)}, f32[2,128,4,128]{1,3,2,0:T(8,128)}, u32[]{:S(2)}, u32[]{:S(2)}) collective-permute-start(f32[2,128,4,128]{1,3,2,0:T(8,128)} %get-tuple-element.513), channel_id=1, source_target_pairs={{0,1},{1,2},{2,3},{3,4},{4,5},{5,6},{6,7},{7,8},{8,9},{9,10},{10,1... | collective-permute-start | bytes 1572872 | tf_op jit(solution)/shard_map/while/body/eval_jaxpr/ppermute | solution.py:19
  103.3 7.8 %collective-permute-start.1 = (f32[2,128,4,128]{1,3,2,0:T(8,128)}, f32[2,128,4,128]{1,3,2,0:T(8,128)}, u32[]{:S(2)}, u32[]{:S(2)}) collective-permute-start(f32[2,128,4,128]{1,3,2,0:T(8,128)} %get-tuple-element.516), channel_id=1, source_target_pairs={{1,0},{2,1},{3,2},{4,3},{5,4},{6,5},{7,6},{8,7},{9,8},{10,9},{11,1... | collective-permute-start | bytes 1572872 | tf_op jit(solution)/shard_map/while/body/eval_jaxpr/ppermute | solution.py:21
  118.0 16.4 %collective-permute-start = (f32[2,128,4,128]{1,3,2,0:T(8,128)}, f32[2,128,4,128]{1,3,2,0:T(8,128)}, u32[]{:S(2)}, u32[]{:S(2)}) collective-permute-start(f32[2,128,4,128]{1,3,2,0:T(8,128)} %get-tuple-element.513), channel_id=1, source_target_pairs={{0,1},{1,2},{2,3},{3,4},{4,5},{5,6},{6,7},{7,8},{8,9},{9,10},{10,1... | collective-permute-start | bytes 1572872 | tf_op jit(solution)/shard_map/while/body/eval_jaxpr/ppermute | solution.py:19
  128.0 7.8 %collective-permute-start.1 = (f32[2,128,4,128]{1,3,2,0:T(8,128)}, f32[2,128,4,128]{1,3,2,0:T(8,128)}, u32[]{:S(2)}, u32[]{:S(2)}) collective-permute-start(f32[2,128,4,128]{1,3,2,0:T(8,128)} %get-tuple-element.516), channel_id=1, source_target_pairs={{1,0},{2,1},{3,2},{4,3},{5,4},{6,5},{7,6},{8,7},{9,8},{10,9},{11,1... | collective-permute-start | bytes 1572872 | tf_op jit(solution)/shard_map/while/body/eval_jaxpr/ppermute | solution.py:21
  142.6 15.1 %collective-permute-start = (f32[2,128,4,128]{1,3,2,0:T(8,128)}, f32[2,128,4,128]{1,3,2,0:T(8,128)}, u32[]{:S(2)}, u32[]{:S(2)}) collective-permute-start(f32[2,128,4,128]{1,3,2,0:T(8,128)} %get-tuple-element.513), channel_id=1, source_target_pairs={{0,1},{1,2},{2,3},{3,4},{4,5},{5,6},{6,7},{7,8},{8,9},{9,10},{10,1... | collective-permute-start | bytes 1572872 | tf_op jit(solution)/shard_map/while/body/eval_jaxpr/ppermute | solution.py:19
  151.3 7.8 %collective-permute-start.1 = (f32[2,128,4,128]{1,3,2,0:T(8,128)}, f32[2,128,4,128]{1,3,2,0:T(8,128)}, u32[]{:S(2)}, u32[]{:S(2)}) collective-permute-start(f32[2,128,4,128]{1,3,2,0:T(8,128)} %get-tuple-element.516), channel_id=1, source_target_pairs={{1,0},{2,1},{3,2},{4,3},{5,4},{6,5},{7,6},{8,7},{9,8},{10,9},{11,1... | collective-permute-start | bytes 1572872 | tf_op jit(solution)/shard_map/while/body/eval_jaxpr/ppermute | solution.py:21
  165.9 15.1 %collective-permute-start = (f32[2,128,4,128]{1,3,2,0:T(8,128)}, f32[2,128,4,128]{1,3,2,0:T(8,128)}, u32[]{:S(2)}, u32[]{:S(2)}) collective-permute-start(f32[2,128,4,128]{1,3,2,0:T(8,128)} %get-tuple-element.513), channel_id=1, source_target_pairs={{0,1},{1,2},{2,3},{3,4},{4,5},{5,6},{6,7},{7,8},{8,9},{9,10},{10,1... | collective-permute-start | bytes 1572872 | tf_op jit(solution)/shard_map/while/body/eval_jaxpr/ppermute | solution.py:19
  174.6 7.8 %collective-permute-start.1 = (f32[2,128,4,128]{1,3,2,0:T(8,128)}, f32[2,128,4,128]{1,3,2,0:T(8,128)}, u32[]{:S(2)}, u32[]{:S(2)}) collective-permute-start(f32[2,128,4,128]{1,3,2,0:T(8,128)} %get-tuple-element.516), channel_id=1, source_target_pairs={{1,0},{2,1},{3,2},{4,3},{5,4},{6,5},{7,6},{8,7},{9,8},{10,9},{11,1... | collective-permute-start | bytes 1572872 | tf_op jit(solution)/shard_map/while/body/eval_jaxpr/ppermute | solution.py:21
  189.2 13.8 %collective-permute-start = (f32[2,128,4,128]{1,3,2,0:T(8,128)}, f32[2,128,4,128]{1,3,2,0:T(8,128)}, u32[]{:S(2)}, u32[]{:S(2)}) collective-permute-start(f32[2,128,4,128]{1,3,2,0:T(8,128)} %get-tuple-element.513), channel_id=1, source_target_pairs={{0,1},{1,2},{2,3},{3,4},{4,5},{5,6},{6,7},{7,8},{8,9},{9,10},{10,1... | collective-permute-start | bytes 1572872 | tf_op jit(solution)/shard_map/while/body/eval_jaxpr/ppermute | solution.py:19
  196.6 7.8 %collective-permute-start.1 = (f32[2,128,4,128]{1,3,2,0:T(8,128)}, f32[2,128,4,128]{1,3,2,0:T(8,128)}, u32[]{:S(2)}, u32[]{:S(2)}) collective-permute-start(f32[2,128,4,128]{1,3,2,0:T(8,128)} %get-tuple-element.516), channel_id=1, source_target_pairs={{1,0},{2,1},{3,2},{4,3},{5,4},{6,5},{7,6},{8,7},{9,8},{10,9},{11,1... | collective-permute-start | bytes 1572872 | tf_op jit(solution)/shard_map/while/body/eval_jaxpr/ppermute | solution.py:21
  211.3 15.1 %collective-permute-start = (f32[2,128,4,128]{1,3,2,0:T(8,128)}, f32[2,128,4,128]{1,3,2,0:T(8,128)}, u32[]{:S(2)}, u32[]{:S(2)}) collective-permute-start(f32[2,128,4,128]{1,3,2,0:T(8,128)} %get-tuple-element.513), channel_id=1, source_target_pairs={{0,1},{1,2},{2,3},{3,4},{4,5},{5,6},{6,7},{7,8},{8,9},{9,10},{10,1... | collective-permute-start | bytes 1572872 | tf_op jit(solution)/shard_map/while/body/eval_jaxpr/ppermute | solution.py:19
  219.9 7.8 %collective-permute-start.1 = (f32[2,128,4,128]{1,3,2,0:T(8,128)}, f32[2,128,4,128]{1,3,2,0:T(8,128)}, u32[]{:S(2)}, u32[]{:S(2)}) collective-permute-start(f32[2,128,4,128]{1,3,2,0:T(8,128)} %get-tuple-element.516), channel_id=1, source_target_pairs={{1,0},{2,1},{3,2},{4,3},{5,4},{6,5},{7,6},{8,7},{9,8},{10,9},{11,1... | collective-permute-start | bytes 1572872 | tf_op jit(solution)/shard_map/while/body/eval_jaxpr/ppermute | solution.py:21
  234.6 13.8 %collective-permute-start = (f32[2,128,4,128]{1,3,2,0:T(8,128)}, f32[2,128,4,128]{1,3,2,0:T(8,128)}, u32[]{:S(2)}, u32[]{:S(2)}) collective-permute-start(f32[2,128,4,128]{1,3,2,0:T(8,128)} %get-tuple-element.513), channel_id=1, source_target_pairs={{0,1},{1,2},{2,3},{3,4},{4,5},{5,6},{6,7},{7,8},{8,9},{9,10},{10,1... | collective-permute-start | bytes 1572872 | tf_op jit(solution)/shard_map/while/body/eval_jaxpr/ppermute | solution.py:19
  242.0 7.8 %collective-permute-start.1 = (f32[2,128,4,128]{1,3,2,0:T(8,128)}, f32[2,128,4,128]{1,3,2,0:T(8,128)}, u32[]{:S(2)}, u32[]{:S(2)}) collective-permute-start(f32[2,128,4,128]{1,3,2,0:T(8,128)} %get-tuple-element.516), channel_id=1, source_target_pairs={{1,0},{2,1},{3,2},{4,3},{5,4},{6,5},{7,6},{8,7},{9,8},{10,9},{11,1... | collective-permute-start | bytes 1572872 | tf_op jit(solution)/shard_map/while/body/eval_jaxpr/ppermute | solution.py:21
  256.6 15.1 %collective-permute-start = (f32[2,128,4,128]{1,3,2,0:T(8,128)}, f32[2,128,4,128]{1,3,2,0:T(8,128)}, u32[]{:S(2)}, u32[]{:S(2)}) collective-permute-start(f32[2,128,4,128]{1,3,2,0:T(8,128)} %get-tuple-element.513), channel_id=1, source_target_pairs={{0,1},{1,2},{2,3},{3,4},{4,5},{5,6},{6,7},{7,8},{8,9},{9,10},{10,1... | collective-permute-start | bytes 1572872 | tf_op jit(solution)/shard_map/while/body/eval_jaxpr/ppermute | solution.py:19
  280.0 13.8 %collective-permute-start = (f32[2,128,4,128]{1,3,2,0:T(8,128)}, f32[2,128,4,128]{1,3,2,0:T(8,128)}, u32[]{:S(2)}, u32[]{:S(2)}) collective-permute-start(f32[2,128,4,128]{1,3,2,0:T(8,128)} %get-tuple-element.513), channel_id=1, source_target_pairs={{0,1},{1,2},{2,3},{3,4},{4,5},{5,6},{6,7},{7,8},{8,9},{9,10},{10,1... | collective-permute-start | bytes 1572872 | tf_op jit(solution)/shard_map/while/body/eval_jaxpr/ppermute | solution.py:19
  302.0 15.1 %collective-permute-start = (f32[2,128,4,128]{1,3,2,0:T(8,128)}, f32[2,128,4,128]{1,3,2,0:T(8,128)}, u32[]{:S(2)}, u32[]{:S(2)}) collective-permute-start(f32[2,128,4,128]{1,3,2,0:T(8,128)} %get-tuple-element.513), channel_id=1, source_target_pairs={{0,1},{1,2},{2,3},{3,4},{4,5},{5,6},{6,7},{7,8},{8,9},{9,10},{10,1... | collective-permute-start | bytes 1572872 | tf_op jit(solution)/shard_map/while/body/eval_jaxpr/ppermute | solution.py:19
  325.3 13.8 %collective-permute-start = (f32[2,128,4,128]{1,3,2,0:T(8,128)}, f32[2,128,4,128]{1,3,2,0:T(8,128)}, u32[]{:S(2)}, u32[]{:S(2)}) collective-permute-start(f32[2,128,4,128]{1,3,2,0:T(8,128)} %get-tuple-element.513), channel_id=1, source_target_pairs={{0,1},{1,2},{2,3},{3,4},{4,5},{5,6},{6,7},{7,8},{8,9},{9,10},{10,1... | collective-permute-start | bytes 1572872 | tf_op jit(solution)/shard_map/while/body/eval_jaxpr/ppermute | solution.py:19
  347.4 15.1 %collective-permute-start = (f32[2,128,4,128]{1,3,2,0:T(8,128)}, f32[2,128,4,128]{1,3,2,0:T(8,128)}, u32[]{:S(2)}, u32[]{:S(2)}) collective-permute-start(f32[2,128,4,128]{1,3,2,0:T(8,128)} %get-tuple-element.513), channel_id=1, source_target_pairs={{0,1},{1,2},{2,3},{3,4},{4,5},{5,6},{6,7},{7,8},{8,9},{9,10},{10,1... | collective-permute-start | bytes 1572872 | tf_op jit(solution)/shard_map/while/body/eval_jaxpr/ppermute | solution.py:19
  370.7 13.8 %collective-permute-start = (f32[2,128,4,128]{1,3,2,0:T(8,128)}, f32[2,128,4,128]{1,3,2,0:T(8,128)}, u32[]{:S(2)}, u32[]{:S(2)}) collective-permute-start(f32[2,128,4,128]{1,3,2,0:T(8,128)} %get-tuple-element.513), channel_id=1, source_target_pairs={{0,1},{1,2},{2,3},{3,4},{4,5},{5,6},{6,7},{7,8},{8,9},{9,10},{10,1... | collective-permute-start | bytes 1572872 | tf_op jit(solution)/shard_map/while/body/eval_jaxpr/ppermute | solution.py:19
  392.7 15.1 %collective-permute-start = (f32[2,128,4,128]{1,3,2,0:T(8,128)}, f32[2,128,4,128]{1,3,2,0:T(8,128)}, u32[]{:S(2)}, u32[]{:S(2)}) collective-permute-start(f32[2,128,4,128]{1,3,2,0:T(8,128)} %get-tuple-element.513), channel_id=1, source_target_pairs={{0,1},{1,2},{2,3},{3,4},{4,5},{5,6},{6,7},{7,8},{8,9},{9,10},{10,1... | collective-permute-start | bytes 1572872 | tf_op jit(solution)/shard_map/while/body/eval_jaxpr/ppermute | solution.py:19
  416.0 13.8 %collective-permute-start = (f32[2,128,4,128]{1,3,2,0:T(8,128)}, f32[2,128,4,128]{1,3,2,0:T(8,128)}, u32[]{:S(2)}, u32[]{:S(2)}) collective-permute-start(f32[2,128,4,128]{1,3,2,0:T(8,128)} %get-tuple-element.513), channel_id=1, source_target_pairs={{0,1},{1,2},{2,3},{3,4},{4,5},{5,6},{6,7},{7,8},{8,9},{9,10},{10,1... | collective-permute-start | bytes 1572872 | tf_op jit(solution)/shard_map/while/body/eval_jaxpr/ppermute | solution.py:19
  438.1 15.1 %collective-permute-start = (f32[2,128,4,128]{1,3,2,0:T(8,128)}, f32[2,128,4,128]{1,3,2,0:T(8,128)}, u32[]{:S(2)}, u32[]{:S(2)}) collective-permute-start(f32[2,128,4,128]{1,3,2,0:T(8,128)} %get-tuple-element.513), channel_id=1, source_target_pairs={{0,1},{1,2},{2,3},{3,4},{4,5},{5,6},{6,7},{7,8},{8,9},{9,10},{10,1... | collective-permute-start | bytes 1572872 | tf_op jit(solution)/shard_map/while/body/eval_jaxpr/ppermute | solution.py:19
  461.4 13.8 %collective-permute-start = (f32[2,128,4,128]{1,3,2,0:T(8,128)}, f32[2,128,4,128]{1,3,2,0:T(8,128)}, u32[]{:S(2)}, u32[]{:S(2)}) collective-permute-start(f32[2,128,4,128]{1,3,2,0:T(8,128)} %get-tuple-element.513), channel_id=1, source_target_pairs={{0,1},{1,2},{2,3},{3,4},{4,5},{5,6},{6,7},{7,8},{8,9},{9,10},{10,1... | collective-permute-start | bytes 1572872 | tf_op jit(solution)/shard_map/while/body/eval_jaxpr/ppermute | solution.py:19
  484.5 24.2 %all-to-all-start.1 = ((f32[128,1,8,128]{3,2,1,0:T(8,128)}), f32[128,1,8,128]{3,2,1,0:T(8,128)S(1)}, u32[]{:S(2)}, u32[]{:S(2)}) async-start(f32[128,1,8,128]{3,2,1,0:T(8,128)} %multiply_bitcast_fusion), calls=%async_computation.1 | async-start | bytes 1048576 | tf_op jit(solution)/shard_map/all_to_all | solution.py:126
  (55 other events, 141.5 us)
where the time goes:
time: 515 us; the launch traced here: 510 us
  starting transfers between devices  205 us (40%)
  local copies, waits for them, and re-layouts  140 us (27%)
  matrix products  80.5 us (16%)
  other arithmetic  59.3 us (12%)
  waiting for transfers between devices  22.9 us (4%)
    ppermute x20, starting transfers between devices, with_halo(): lax.ppermute(tail, axis, [(i, (i + 1) % count) for i in range(ends)])  162 us
    dot_general x40, matrix products, spread_points(): jnp.einsum('ny,nc->yc', weighted, places, precision=lax.Precision.HIGHEST)  79.8 us
    while x160, local copies, waits for them, and re-layouts  65.3 us
    add x20, other arithmetic, advance(): updated = 2.0 * current - previous + speed_sq[None] * laplacian  48.6 us
    ppermute x20, starting transfers between devices, with_halo(): lax.ppermute(head, axis, [((i + 1) % count, i) for i in range(ends)])  25.6 us
    concatenate x20, local copies, waits for them, and re-layouts, with_halo(): jnp.concatenate([lax.ppermute(tail, axis, [(i, (i + 1) % count) for i in...  21.6 us
    slice x20, local copies, waits for them, and re-layouts, with_halo(): head = lax.slice_in_dim(cells, 0, width, axis=dim)  21.3 us
    dynamic_slice x20, local copies, waits for them, and re-layouts, amounts_at(): recorded = lax.dynamic_index_in_dim(traces, moment, 0, keepdims=False)  19.6 us
  transfers between devices with their start and end apart: 42, of which 2 were waited for; matrix products, arithmetic and copies ran while one was open for 26% of the time, Pallas kernels for 0%

commit v1 on v0

v1 whole, which is shorter than its diff:
```python
import functools

import jax
import jax.numpy as jnp
from jax import lax
from jax.experimental import pallas as pl
from jax.experimental.pallas import tpu as pltpu
from jax.sharding import PartitionSpec as P

courant = 0.09
stencil_weights = (8.0 / 5.0, -1.0 / 5.0, 8.0 / 315.0, -1.0 / 560.0)
center_weight = 3.0 * (-205.0 / 72.0)
HALO = 4
XOFF = 8


def with_halo(cells, axis, dim, width):
    count = lax.axis_size(axis)
    ends = count - 1
    head = lax.slice_in_dim(cells, 0, width, axis=dim)
    tail = lax.slice_in_dim(cells, cells.shape[dim] - width, cells.shape[dim], axis=dim)
    low = lax.ppermute(tail, axis, [(i, (i + 1) % count) for i in range(ends)])
    high = lax.ppermute(head, axis, [((i + 1) % count, i) for i in range(ends)])
    return low, high


def step_kernel(
    cur_ref, prev_ref, s_ref, img_ref, xlo_ref, xhi_ref, inj_ref, out_ref, imgo_ref, ext_ref
):
    comps, block_y, block_x, depth_z = cur_ref.shape
    zeros_y = jnp.zeros((comps, HALO, block_x, depth_z), jnp.float32)
    ext_ref[:, 0:HALO, XOFF : XOFF + block_x, :] = zeros_y
    ext_ref[:, HALO + block_y : 2 * HALO + block_y, XOFF : XOFF + block_x, :] = zeros_y
    ext_ref[:, HALO : HALO + block_y, XOFF - HALO : XOFF, :] = xlo_ref[...]
    ext_ref[:, HALO : HALO + block_y, XOFF : XOFF + block_x, :] = cur_ref[...]
    ext_ref[:, HALO : HALO + block_y, XOFF + block_x : XOFF + block_x + HALO, :] = xhi_ref[...]
    lane = lax.broadcasted_iota(jnp.int32, (block_x, depth_z), 1)

    def row(y, carry):
        done = []
        for c in range(comps):
            ctr = cur_ref[c, y]
            acc = center_weight * ctr
            for m in range(1, HALO + 1):
                b = ext_ref[c, HALO + y, XOFF + m : XOFF + m + block_x, :] + ext_ref[
                    c, HALO + y, XOFF - m : XOFF - m + block_x, :
                ]
                b = (
                    b
                    + ext_ref[c, HALO + y + m, XOFF : XOFF + block_x, :]
                    + ext_ref[c, HALO + y - m, XOFF : XOFF + block_x, :]
                )
                up = jnp.where(lane < depth_z - m, pltpu.roll(ctr, depth_z - m, 1), 0.0)
                down = jnp.where(lane >= m, pltpu.roll(ctr, m, 1), 0.0)
                b = b + up + down
                acc = acc + stencil_weights[m - 1] * b
            lap = acc + inj_ref[c, y]
            upd = 2.0 * ctr - prev_ref[c, y] + s_ref[y] * lap
            out_ref[c, y] = upd
            done.append(upd)
        imgo_ref[y] = img_ref[y] + done[0] * done[1]
        return carry

    lax.fori_loop(0, block_y, row, 0)


def step_call(cur, prev, s, img, xlo, xhi, inj):
    comps, block_y, block_x, depth_z = cur.shape
    vmem = pl.BlockSpec(memory_space=pltpu.VMEM)
    return pl.pallas_call(
        step_kernel,
        out_shape=(
            jax.ShapeDtypeStruct(cur.shape, jnp.float32),
            jax.ShapeDtypeStruct(img.shape, jnp.float32),
        ),
        in_specs=[vmem] * 7,
        out_specs=(vmem, vmem),
        scratch_shapes=[
            pltpu.VMEM((comps, block_y + 2 * HALO, block_x + 2 * XOFF, depth_z), jnp.float32)
        ],
        compiler_params=pltpu.CompilerParams(vmem_limit_bytes=48 * 1024 * 1024),
        cost_estimate=pl.CostEstimate(
            flops=60 * cur.size, bytes_accessed=4 * 6 * cur.size, transcendentals=0
        ),
    )(cur, prev, s, img, xlo, xhi, inj)


def point_tables(cell_rows, x_start, cells_wide, depth_y):
    local_x = cell_rows[0] - x_start
    inside = (local_x >= 0) & (local_x < cells_wide)
    rows_y = (cell_rows[1][:, None] == jnp.arange(depth_y, dtype=jnp.int32)[None, :]).astype(
        jnp.float32
    )
    column = local_x * 4 + cell_rows[2]
    places = (column[:, None] == jnp.arange(cells_wide * 4, dtype=jnp.int32)[None, :]) & inside[
        :, None
    ]
    return (rows_y, places.astype(jnp.float32))


def spread_points(tables, amounts, depth_z):
    rows_y, places = tables
    weighted = rows_y * amounts[:, None]
    plane = jnp.einsum("ny,nc->yc", weighted, places, precision=lax.Precision.HIGHEST)
    plane = plane.reshape(rows_y.shape[1], places.shape[1] // 4, 4)
    return jnp.pad(plane, ((0, 0), (0, 0), (0, depth_z - 4)))


def shards(older_fields, fields_now, velocity, aperture, source_pos, wavelet, receiver_pos, traces):
    slab_count = lax.axis_size("dom")
    depth_y = fields_now.shape[1]
    cells_x = fields_now.shape[2]
    depth_z = fields_now.shape[3]
    block_y = velocity.shape[0]
    steps_total = wavelet.shape[0]
    x_anchor = lax.axis_index("dom") * cells_x
    bricks = velocity.reshape(block_y, slab_count, cells_x, depth_z)
    chosen = jnp.take(bricks, aperture, axis=1)
    arrived = lax.all_to_all(chosen, "dom", split_axis=1, concat_axis=0, tiled=True)
    scaled = courant * arrived.reshape(depth_y, cells_x, depth_z)
    speed_sq = scaled * scaled
    image_zero = jnp.zeros((depth_y, cells_x, depth_z), jnp.float32)
    source_core = point_tables(source_pos, x_anchor, cells_x, depth_y)
    receiver_core = point_tables(receiver_pos, x_anchor, cells_x, depth_y)

    def advance(moment, state_carry):
        previous, current, image_acc = state_carry
        low, high = with_halo(current, "dom", 2, HALO)
        pulses = lax.dynamic_index_in_dim(wavelet, moment, 0, keepdims=False)
        recorded = lax.dynamic_index_in_dim(traces, moment, 0, keepdims=False)
        added = jnp.stack(
            [
                spread_points(source_core, pulses, depth_z),
                spread_points(receiver_core, recorded, depth_z),
            ]
        )
        updated, image_acc = step_call(current, previous, speed_sq, image_acc, low, high, added)
        return (current, updated, image_acc)

    previous, current, image_acc = lax.fori_loop(
        0, steps_total, advance, (older_fields, fields_now, image_zero)
    )
    image_acc = image_acc * (1.0 / steps_total)
    outgoing = image_acc.reshape(depth_y, 1, cells_x, depth_z)
    one_hot = (aperture[None, :] == jnp.arange(slab_count, dtype=jnp.int32)[:, None]).astype(
        jnp.float32
    )
    received = lax.all_to_all(outgoing, "dom", split_axis=0, concat_axis=1, tiled=True)
    summed = jnp.einsum("mj,yjcz->ymcz", one_hot, received, precision=lax.Precision.HIGHEST)
    image_model = summed.reshape(received.shape[0], slab_count * cells_x, received.shape[3])
    return (previous, current, image_model)


def solution(mesh):
    in_specs = (
        P(None, "survey", "dom", None),
        P(None, "survey", "dom", None),
        P("dom", "survey", None),
        P("survey"),
        P(None, "survey"),
        P(None, "survey"),
        P(None, "survey"),
        P(None, "survey"),
    )
    out_specs = (
        P(None, "survey", "dom", None),
        P(None, "survey", "dom", None),
        P("dom", "survey", None),
    )
    return jax.shard_map(shards, mesh=mesh, in_specs=in_specs, out_specs=out_specs, check_vma=False)
```

time: 515 us -> 683 us (1.33)
  Pallas kernels: 0 us -> 259 us
  starting transfers between devices: 205 us -> 149 us
  other arithmetic: 59.3 us -> 4.84 us
  blocking collectives: 0 us -> 23.7 us
  waiting for transfers between devices: 22.9 us -> 14.2 us
    pallas_call x0 -> x20, Pallas kernels: none -> 259 us  [step_call(): pl.pallas_call(step_kernel, out_shape=(jax.ShapeDtypeStruct(cur.shape, jn...]
    add x40 -> x0, other arithmetic: 55.1 us -> none  [the longest x20 48.6 us: advance(): updated = 2.0 * current - previous + speed_sq[None] * laplacian]
    ppermute x40, starting transfers between devices: 188 us -> 141 us  [the longest x20 115 us: with_halo(): low = lax.ppermute(tail, axis, [(i, (i + 1) % count) for i in range(ends)])]
    reshape x0 -> x40, local copies, waits for them, and re-layouts: none -> 26.2 us  [spread_points(): plane = plane.reshape(rows_y.shape[1], places.shape[1] // 4, 4)]
    all_to_all x0 -> x1, blocking collectives: none -> 23.7 us  [shards(): lax.all_to_all(outgoing, 'dom', split_axis=0, concat_axis=1, tiled=True)]
    concatenate x20 -> x0, local copies, waits for them, and re-layouts: 21.6 us -> none  [with_halo(): jnp.concatenate([lax.ppermute(tail, axis, [(i, (i + 1) % count) for i in...]
    all_to_all x1 -> x0, waiting for transfers between devices: 11.9 us -> none  [shards(): lax.all_to_all(outgoing, 'dom', split_axis=0, concat_axis=1, tiled=True)]
    all_to_all x1 -> x0, starting transfers between devices: 9.72 us -> none  [shards(): lax.all_to_all(outgoing, 'dom', split_axis=0, concat_axis=1, tiled=True)]
  transfers between devices with their start and end apart: 42 -> 41, of which waited for: 2 -> 1; matrix products, arithmetic and copies ran while one was open for 26% -> 22% of each run, Pallas kernels for 0% -> 0%
where the time goes in v1:
time: 683 us; the launch traced here: 680 us
  Pallas kernels  259 us (38%)
  starting transfers between devices  149 us (22%)
  local copies, waits for them, and re-layouts  145 us (21%)
  matrix products  80.5 us (12%)
  blocking collectives  23.7 us (3%)
  waiting for transfers between devices  14.2 us (2%)
    pallas_call x20, Pallas kernels, step_call(): pl.pallas_call(step_kernel, out_shape=(jax.ShapeDtypeStruct(cur.shape, jn...  259 us
    ppermute x20, starting transfers between devices, with_halo(): low = lax.ppermute(tail, axis, [(i, (i + 1) % count) for i in range(ends)])  115 us
    dot_general x40, matrix products, spread_points(): jnp.einsum('ny,nc->yc', weighted, places, precision=lax.Precision.HIGHEST)  79.8 us
    while x180, local copies, waits for them, and re-layouts  69.6 us
    reshape x40, local copies, waits for them, and re-layouts, spread_points(): plane = plane.reshape(rows_y.shape[1], places.shape[1] // 4, 4)  26.2 us
    ppermute x20, starting transfers between devices, with_halo(): high = lax.ppermute(head, axis, [((i + 1) % count, i) for i in range(ends)])  25.8 us
    all_to_all x1, blocking collectives, shards(): lax.all_to_all(outgoing, 'dom', split_axis=0, concat_axis=1, tiled=True)  23.7 us
    slice x20, local copies, waits for them, and re-layouts, with_halo(): head = lax.slice_in_dim(cells, 0, width, axis=dim)  22.9 us
  transfers between devices with their start and end apart: 41, of which 1 were waited for; matrix products, arithmetic and copies ran while one was open for 22% of the time, Pallas kernels for 0%

profile of v1, /device:TPU:0, one launch (start us, length us, event | category | flops | bytes accessed | tf_op | source)
XLA Modules:
  0.0 679.6 jit_solution(8111026803886938925)
XLA Ops:
  5.2 7.4 %all-to-all-start = ((f32[8,16,8,128]{3,2,0,1:T(8,128)}), f32[8,16,8,128]{3,2,0,1:T(8,128)S(1)}, u32[]{:S(2)}, u32[]{:S(2)}) async-start(f32[8,16,8,128]{3,2,0,1:T(8,128)} %select_bitcast_fusion), calls=%async_computation | async-start | bytes 1048576 | tf_op jit(solution)/shard_map/all_to_all | solution.py:119
  13.0 14.1 %all-to-all-done = f32[8,16,8,128]{3,2,0,1:T(8,128)S(1)} async-done(((f32[8,16,8,128]{3,2,0,1:T(8,128)}), f32[8,16,8,128]{3,2,0,1:T(8,128)S(1)}, u32[]{:S(2)}, u32[]{:S(2)}) %all-to-all-start) | async-done | bytes 524320 | tf_op jit(solution)/shard_map/all_to_all | solution.py:119
  28.7 624.0 %while.20 = (s32[]{:T(128)}, f32[2,128,8,128]{3,2,1,0:T(8,128)}, f32[2,128,8,128]{3,2,1,0:T(8,128)S(1)}, f32[128,8,128]{2,1,0:T(8,128)}, f32[20,8]{1,0:T(8,128)S...) while((s32[]{:T(128)}, f32[2,128,8,128]{3,2,1,0:T(8,128)}, ...), condition=%wide.region_1.2_spmd.clone, body=%wide.region_0.1_spmd.clone.sunk | while | flops 421923584 | bytes 27632088 | solution.py:140
  42.1 13.0 %eval_jaxpr.8 = (f32[2,128,8,128]{3,2,1,0:T(8,128)S(1)}, f32[128,8,128]{2,1,0:T(8,128)}) custom-call(f32[2,128,8,128]{3,2,1,0:T(8,128)S(1)} %get-tuple-element.506.cur_ref, f32[2,128,8,128]{3,2,1,0:T(8,128)S(1)} %copy-done.4, f32[128,8,128]{2,1,0:T(8,128)S(1)} %copy-done.5, f32[128,8,128]{2,1,0:T(8,128)S(1)} %copy.59.img_ref, ...), custom_call_target="tpu_custom_call" | custom-call | flops 15728640 | bytes 6291456 | tf_op jit(solution)/shard_map/while/body/eval_jaxpr/pallas_call | solution.py:70
  71.7 13.0 %eval_jaxpr.8 = (f32[2,128,8,128]{3,2,1,0:T(8,128)S(1)}, f32[128,8,128]{2,1,0:T(8,128)}) custom-call(f32[2,128,8,128]{3,2,1,0:T(8,128)S(1)} %get-tuple-element.506.cur_ref, f32[2,128,8,128]{3,2,1,0:T(8,128)S(1)} %copy-done.4, f32[128,8,128]{2,1,0:T(8,128)S(1)} %copy-done.5, f32[128,8,128]{2,1,0:T(8,128)S(1)} %copy.59.img_ref, ...), custom_call_target="tpu_custom_call" | custom-call | flops 15728640 | bytes 6291456 | tf_op jit(solution)/shard_map/while/body/eval_jaxpr/pallas_call | solution.py:70
  103.2 13.0 %eval_jaxpr.8 = (f32[2,128,8,128]{3,2,1,0:T(8,128)S(1)}, f32[128,8,128]{2,1,0:T(8,128)}) custom-call(f32[2,128,8,128]{3,2,1,0:T(8,128)S(1)} %get-tuple-element.506.cur_ref, f32[2,128,8,128]{3,2,1,0:T(8,128)S(1)} %copy-done.4, f32[128,8,128]{2,1,0:T(8,128)S(1)} %copy-done.5, f32[128,8,128]{2,1,0:T(8,128)S(1)} %copy.59.img_ref, ...), custom_call_target="tpu_custom_call" | custom-call | flops 15728640 | bytes 6291456 | tf_op jit(solution)/shard_map/while/body/eval_jaxpr/pallas_call | solution.py:70
  118.4 6.1 collective-permute-start
  134.7 13.0 %eval_jaxpr.8 = (f32[2,128,8,128]{3,2,1,0:T(8,128)S(1)}, f32[128,8,128]{2,1,0:T(8,128)}) custom-call(f32[2,128,8,128]{3,2,1,0:T(8,128)S(1)} %get-tuple-element.506.cur_ref, f32[2,128,8,128]{3,2,1,0:T(8,128)S(1)} %copy-done.4, f32[128,8,128]{2,1,0:T(8,128)S(1)} %copy-done.5, f32[128,8,128]{2,1,0:T(8,128)S(1)} %copy.59.img_ref, ...), custom_call_target="tpu_custom_call" | custom-call | flops 15728640 | bytes 6291456 | tf_op jit(solution)/shard_map/while/body/eval_jaxpr/pallas_call | solution.py:70
  149.9 6.1 collective-permute-start
  166.2 13.0 %eval_jaxpr.8 = (f32[2,128,8,128]{3,2,1,0:T(8,128)S(1)}, f32[128,8,128]{2,1,0:T(8,128)}) custom-call(f32[2,128,8,128]{3,2,1,0:T(8,128)S(1)} %get-tuple-element.506.cur_ref, f32[2,128,8,128]{3,2,1,0:T(8,128)S(1)} %copy-done.4, f32[128,8,128]{2,1,0:T(8,128)S(1)} %copy-done.5, f32[128,8,128]{2,1,0:T(8,128)S(1)} %copy.59.img_ref, ...), custom_call_target="tpu_custom_call" | custom-call | flops 15728640 | bytes 6291456 | tf_op jit(solution)/shard_map/while/body/eval_jaxpr/pallas_call | solution.py:70
  181.4 6.1 collective-permute-start
  197.7 13.0 %eval_jaxpr.8 = (f32[2,128,8,128]{3,2,1,0:T(8,128)S(1)}, f32[128,8,128]{2,1,0:T(8,128)}) custom-call(f32[2,128,8,128]{3,2,1,0:T(8,128)S(1)} %get-tuple-element.506.cur_ref, f32[2,128,8,128]{3,2,1,0:T(8,128)S(1)} %copy-done.4, f32[128,8,128]{2,1,0:T(8,128)S(1)} %copy-done.5, f32[128,8,128]{2,1,0:T(8,128)S(1)} %copy.59.img_ref, ...), custom_call_target="tpu_custom_call" | custom-call | flops 15728640 | bytes 6291456 | tf_op jit(solution)/shard_map/while/body/eval_jaxpr/pallas_call | solution.py:70
  229.2 13.0 %eval_jaxpr.8 = (f32[2,128,8,128]{3,2,1,0:T(8,128)S(1)}, f32[128,8,128]{2,1,0:T(8,128)}) custom-call(f32[2,128,8,128]{3,2,1,0:T(8,128)S(1)} %get-tuple-element.506.cur_ref, f32[2,128,8,128]{3,2,1,0:T(8,128)S(1)} %copy-done.4, f32[128,8,128]{2,1,0:T(8,128)S(1)} %copy-done.5, f32[128,8,128]{2,1,0:T(8,128)S(1)} %copy.59.img_ref, ...), custom_call_target="tpu_custom_call" | custom-call | flops 15728640 | bytes 6291456 | tf_op jit(solution)/shard_map/while/body/eval_jaxpr/pallas_call | solution.py:70
  244.4 6.1 collective-permute-start
  260.7 13.0 %eval_jaxpr.8 = (f32[2,128,8,128]{3,2,1,0:T(8,128)S(1)}, f32[128,8,128]{2,1,0:T(8,128)}) custom-call(f32[2,128,8,128]{3,2,1,0:T(8,128)S(1)} %get-tuple-element.506.cur_ref, f32[2,128,8,128]{3,2,1,0:T(8,128)S(1)} %copy-done.4, f32[128,8,128]{2,1,0:T(8,128)S(1)} %copy-done.5, f32[128,8,128]{2,1,0:T(8,128)S(1)} %copy.59.img_ref, ...), custom_call_target="tpu_custom_call" | custom-call | flops 15728640 | bytes 6291456 | tf_op jit(solution)/shard_map/while/body/eval_jaxpr/pallas_call | solution.py:70
  292.2 13.0 %eval_jaxpr.8 = (f32[2,128,8,128]{3,2,1,0:T(8,128)S(1)}, f32[128,8,128]{2,1,0:T(8,128)}) custom-call(f32[2,128,8,128]{3,2,1,0:T(8,128)S(1)} %get-tuple-element.506.cur_ref, f32[2,128,8,128]{3,2,1,0:T(8,128)S(1)} %copy-done.4, f32[128,8,128]{2,1,0:T(8,128)S(1)} %copy-done.5, f32[128,8,128]{2,1,0:T(8,128)S(1)} %copy.59.img_ref, ...), custom_call_target="tpu_custom_call" | custom-call | flops 15728640 | bytes 6291456 | tf_op jit(solution)/shard_map/while/body/eval_jaxpr/pallas_call | solution.py:70
  323.7 13.0 %eval_jaxpr.8 = (f32[2,128,8,128]{3,2,1,0:T(8,128)S(1)}, f32[128,8,128]{2,1,0:T(8,128)}) custom-call(f32[2,128,8,128]{3,2,1,0:T(8,128)S(1)} %get-tuple-element.506.cur_ref, f32[2,128,8,128]{3,2,1,0:T(8,128)S(1)} %copy-done.4, f32[128,8,128]{2,1,0:T(8,128)S(1)} %copy-done.5, f32[128,8,128]{2,1,0:T(8,128)S(1)} %copy.59.img_ref, ...), custom_call_target="tpu_custom_call" | custom-call | flops 15728640 | bytes 6291456 | tf_op jit(solution)/shard_map/while/body/eval_jaxpr/pallas_call | solution.py:70
  338.9 6.1 collective-permute-start
  355.2 13.0 %eval_jaxpr.8 = (f32[2,128,8,128]{3,2,1,0:T(8,128)S(1)}, f32[128,8,128]{2,1,0:T(8,128)}) custom-call(f32[2,128,8,128]{3,2,1,0:T(8,128)S(1)} %get-tuple-element.506.cur_ref, f32[2,128,8,128]{3,2,1,0:T(8,128)S(1)} %copy-done.4, f32[128,8,128]{2,1,0:T(8,128)S(1)} %copy-done.5, f32[128,8,128]{2,1,0:T(8,128)S(1)} %copy.59.img_ref, ...), custom_call_target="tpu_custom_call" | custom-call | flops 15728640 | bytes 6291456 | tf_op jit(solution)/shard_map/while/body/eval_jaxpr/pallas_call | solution.py:70
  386.7 13.0 %eval_jaxpr.8 = (f32[2,128,8,128]{3,2,1,0:T(8,128)S(1)}, f32[128,8,128]{2,1,0:T(8,128)}) custom-call(f32[2,128,8,128]{3,2,1,0:T(8,128)S(1)} %get-tuple-element.506.cur_ref, f32[2,128,8,128]{3,2,1,0:T(8,128)S(1)} %copy-done.4, f32[128,8,128]{2,1,0:T(8,128)S(1)} %copy-done.5, f32[128,8,128]{2,1,0:T(8,128)S(1)} %copy.59.img_ref, ...), custom_call_target="tpu_custom_call" | custom-call | flops 15728640 | bytes 6291456 | tf_op jit(solution)/shard_map/while/body/eval_jaxpr/pallas_call | solution.py:70
  418.2 13.0 %eval_jaxpr.8 = (f32[2,128,8,128]{3,2,1,0:T(8,128)S(1)}, f32[128,8,128]{2,1,0:T(8,128)}) custom-call(f32[2,128,8,128]{3,2,1,0:T(8,128)S(1)} %get-tuple-element.506.cur_ref, f32[2,128,8,128]{3,2,1,0:T(8,128)S(1)} %copy-done.4, f32[128,8,128]{2,1,0:T(8,128)S(1)} %copy-done.5, f32[128,8,128]{2,1,0:T(8,128)S(1)} %copy.59.img_ref, ...), custom_call_target="tpu_custom_call" | custom-call | flops 15728640 | bytes 6291456 | tf_op jit(solution)/shard_map/while/body/eval_jaxpr/pallas_call | solution.py:70
  433.4 6.1 collective-permute-start
  449.7 13.0 %eval_jaxpr.8 = (f32[2,128,8,128]{3,2,1,0:T(8,128)S(1)}, f32[128,8,128]{2,1,0:T(8,128)}) custom-call(f32[2,128,8,128]{3,2,1,0:T(8,128)S(1)} %get-tuple-element.506.cur_ref, f32[2,128,8,128]{3,2,1,0:T(8,128)S(1)} %copy-done.4, f32[128,8,128]{2,1,0:T(8,128)S(1)} %copy-done.5, f32[128,8,128]{2,1,0:T(8,128)S(1)} %copy.59.img_ref, ...), custom_call_target="tpu_custom_call" | custom-call | flops 15728640 | bytes 6291456 | tf_op jit(solution)/shard_map/while/body/eval_jaxpr/pallas_call | solution.py:70
  481.2 13.0 %eval_jaxpr.8 = (f32[2,128,8,128]{3,2,1,0:T(8,128)S(1)}, f32[128,8,128]{2,1,0:T(8,128)}) custom-call(f32[2,128,8,128]{3,2,1,0:T(8,128)S(1)} %get-tuple-element.506.cur_ref, f32[2,128,8,128]{3,2,1,0:T(8,128)S(1)} %copy-done.4, f32[128,8,128]{2,1,0:T(8,128)S(1)} %copy-done.5, f32[128,8,128]{2,1,0:T(8,128)S(1)} %copy.59.img_ref, ...), custom_call_target="tpu_custom_call" | custom-call | flops 15728640 | bytes 6291456 | tf_op jit(solution)/shard_map/while/body/eval_jaxpr/pallas_call | solution.py:70
  496.4 6.1 collective-permute-start
  512.7 13.0 %eval_jaxpr.8 = (f32[2,128,8,128]{3,2,1,0:T(8,128)S(1)}, f32[128,8,128]{2,1,0:T(8,128)}) custom-call(f32[2,128,8,128]{3,2,1,0:T(8,128)S(1)} %get-tuple-element.506.cur_ref, f32[2,128,8,128]{3,2,1,0:T(8,128)S(1)} %copy-done.4, f32[128,8,128]{2,1,0:T(8,128)S(1)} %copy-done.5, f32[128,8,128]{2,1,0:T(8,128)S(1)} %copy.59.img_ref, ...), custom_call_target="tpu_custom_call" | custom-call | flops 15728640 | bytes 6291456 | tf_op jit(solution)/shard_map/while/body/eval_jaxpr/pallas_call | solution.py:70
  544.2 13.0 %eval_jaxpr.8 = (f32[2,128,8,128]{3,2,1,0:T(8,128)S(1)}, f32[128,8,128]{2,1,0:T(8,128)}) custom-call(f32[2,128,8,128]{3,2,1,0:T(8,128)S(1)} %get-tuple-element.506.cur_ref, f32[2,128,8,128]{3,2,1,0:T(8,128)S(1)} %copy-done.4, f32[128,8,128]{2,1,0:T(8,128)S(1)} %copy-done.5, f32[128,8,128]{2,1,0:T(8,128)S(1)} %copy.59.img_ref, ...), custom_call_target="tpu_custom_call" | custom-call | flops 15728640 | bytes 6291456 | tf_op jit(solution)/shard_map/while/body/eval_jaxpr/pallas_call | solution.py:70
  575.7 13.0 %eval_jaxpr.8 = (f32[2,128,8,128]{3,2,1,0:T(8,128)S(1)}, f32[128,8,128]{2,1,0:T(8,128)}) custom-call(f32[2,128,8,128]{3,2,1,0:T(8,128)S(1)} %get-tuple-element.506.cur_ref, f32[2,128,8,128]{3,2,1,0:T(8,128)S(1)} %copy-done.4, f32[128,8,128]{2,1,0:T(8,128)S(1)} %copy-done.5, f32[128,8,128]{2,1,0:T(8,128)S(1)} %copy.59.img_ref, ...), custom_call_target="tpu_custom_call" | custom-call | flops 15728640 | bytes 6291456 | tf_op jit(solution)/shard_map/while/body/eval_jaxpr/pallas_call | solution.py:70
  590.9 6.1 collective-permute-start
  607.2 13.0 %eval_jaxpr.8 = (f32[2,128,8,128]{3,2,1,0:T(8,128)S(1)}, f32[128,8,128]{2,1,0:T(8,128)}) custom-call(f32[2,128,8,128]{3,2,1,0:T(8,128)S(1)} %get-tuple-element.506.cur_ref, f32[2,128,8,128]{3,2,1,0:T(8,128)S(1)} %copy-done.4, f32[128,8,128]{2,1,0:T(8,128)S(1)} %copy-done.5, f32[128,8,128]{2,1,0:T(8,128)S(1)} %copy.59.img_ref, ...), custom_call_target="tpu_custom_call" | custom-call | flops 15728640 | bytes 6291456 | tf_op jit(solution)/shard_map/while/body/eval_jaxpr/pallas_call | solution.py:70
  638.7 13.0 %eval_jaxpr.8 = (f32[2,128,8,128]{3,2,1,0:T(8,128)S(1)}, f32[128,8,128]{2,1,0:T(8,128)}) custom-call(f32[2,128,8,128]{3,2,1,0:T(8,128)S(1)} %get-tuple-element.506.cur_ref, f32[2,128,8,128]{3,2,1,0:T(8,128)S(1)} %copy-done.4, f32[128,8,128]{2,1,0:T(8,128)S(1)} %copy-done.5, f32[128,8,128]{2,1,0:T(8,128)S(1)} %copy.59.img_ref, ...), custom_call_target="tpu_custom_call" | custom-call | flops 15728640 | bytes 6291456 | tf_op jit(solution)/shard_map/while/body/eval_jaxpr/pallas_call | solution.py:70
  654.2 23.7 %all_to_all.27 = f32[128,1,8,128]{3,2,1,0:T(8,128)S(1)} all-to-all(f32[128,1,8,128]{3,2,1,0:T(8,128)S(1)} %multiply_bitcast_fusion), channel_id=1, replica_groups=mesh['survey'=2,'dom'=16] {'dom'}, dimensions={0} | all-to-all | bytes 1048576 | tf_op jit(solution)/shard_map/all_to_all | solution.py:148
  (462 shorter events, 323.6 us)
Async XLA Ops:
  5.2 21.9 %all-to-all-start = ((f32[8,16,8,128]{3,2,0,1:T(8,128)}), f32[8,16,8,128]{3,2,0,1:T(8,128)S(1)}, u32[]{:S(2)}, u32[]{:S(2)}) async-start(f32[8,16,8,128]{3,2,0,1:T(8,128)} %select_bitcast_fusion), calls=%async_computation | async-start | bytes 1048576 | tf_op jit(solution)/shard_map/all_to_all | solution.py:119
  29.9 10.9 %collective-permute-start = (f32[2,128,4,128]{3,2,1,0:T(4,128)}, f32[2,128,4,128]{3,2,1,0:T(4,128)S(1)}, u32[]{:S(2)}, u32[]{:S(2)}) collective-permute-start(f32[2,128,4,128]{3,2,1,0:T(4,128)} %get-tuple-element.484), channel_id=1, source_target_pairs={{0,1},{1,2},{2,3},{3,4},{4,5},{5,6},{6,7},{7,8},{8,9},{9,10},{10,1... | collective-permute-start | bytes 1572872 | tf_op jit(solution)/shard_map/while/body/eval_jaxpr/ppermute | solution.py:22
  31.8 9.0 %collective-permute-start.1 = (f32[2,128,4,128]{3,2,1,0:T(4,128)}, f32[2,128,4,128]{3,2,1,0:T(4,128)S(1)}, u32[]{:S(2)}, u32[]{:S(2)}) collective-permute-start(f32[2,128,4,128]{3,2,1,0:T(4,128)} %get-tuple-element.485), channel_id=1, source_target_pairs={{1,0},{2,1},{3,2},{4,3},{5,4},{6,5},{7,6},{8,7},{9,8},{10,9},{11,1... | collective-permute-start | bytes 1572872 | tf_op jit(solution)/shard_map/while/body/eval_jaxpr/ppermute | solution.py:23
  57.3 13.2 %collective-permute-start = (f32[2,128,4,128]{3,2,1,0:T(4,128)}, f32[2,128,4,128]{3,2,1,0:T(4,128)S(1)}, u32[]{:S(2)}, u32[]{:S(2)}) collective-permute-start(f32[2,128,4,128]{3,2,1,0:T(4,128)} %get-tuple-element.484), channel_id=1, source_target_pairs={{0,1},{1,2},{2,3},{3,4},{4,5},{5,6},{6,7},{7,8},{8,9},{9,10},{10,1... | collective-permute-start | bytes 1572872 | tf_op jit(solution)/shard_map/while/body/eval_jaxpr/ppermute | solution.py:22
  61.5 9.0 %collective-permute-start.1 = (f32[2,128,4,128]{3,2,1,0:T(4,128)}, f32[2,128,4,128]{3,2,1,0:T(4,128)S(1)}, u32[]{:S(2)}, u32[]{:S(2)}) collective-permute-start(f32[2,128,4,128]{3,2,1,0:T(4,128)} %get-tuple-element.485), channel_id=1, source_target_pairs={{1,0},{2,1},{3,2},{4,3},{5,4},{6,5},{7,6},{8,7},{9,8},{10,9},{11,1... | collective-permute-start | bytes 1572872 | tf_op jit(solution)/shard_map/while/body/eval_jaxpr/ppermute | solution.py:23
  86.9 15.0 %collective-permute-start = (f32[2,128,4,128]{3,2,1,0:T(4,128)}, f32[2,128,4,128]{3,2,1,0:T(4,128)S(1)}, u32[]{:S(2)}, u32[]{:S(2)}) collective-permute-start(f32[2,128,4,128]{3,2,1,0:T(4,128)} %get-tuple-element.484), channel_id=1, source_target_pairs={{0,1},{1,2},{2,3},{3,4},{4,5},{5,6},{6,7},{7,8},{8,9},{9,10},{10,1... | collective-permute-start | bytes 1572872 | tf_op jit(solution)/shard_map/while/body/eval_jaxpr/ppermute | solution.py:22
  93.0 9.0 %collective-permute-start.1 = (f32[2,128,4,128]{3,2,1,0:T(4,128)}, f32[2,128,4,128]{3,2,1,0:T(4,128)S(1)}, u32[]{:S(2)}, u32[]{:S(2)}) collective-permute-start(f32[2,128,4,128]{3,2,1,0:T(4,128)} %get-tuple-element.485), channel_id=1, source_target_pairs={{1,0},{2,1},{3,2},{4,3},{5,4},{6,5},{7,6},{8,7},{9,8},{10,9},{11,1... | collective-permute-start | bytes 1572872 | tf_op jit(solution)/shard_map/while/body/eval_jaxpr/ppermute | solution.py:23
  118.4 15.1 %collective-permute-start = (f32[2,128,4,128]{3,2,1,0:T(4,128)}, f32[2,128,4,128]{3,2,1,0:T(4,128)S(1)}, u32[]{:S(2)}, u32[]{:S(2)}) collective-permute-start(f32[2,128,4,128]{3,2,1,0:T(4,128)} %get-tuple-element.484), channel_id=1, source_target_pairs={{0,1},{1,2},{2,3},{3,4},{4,5},{5,6},{6,7},{7,8},{8,9},{9,10},{10,1... | collective-permute-start | bytes 1572872 | tf_op jit(solution)/shard_map/while/body/eval_jaxpr/ppermute | solution.py:22
  124.5 9.0 %collective-permute-start.1 = (f32[2,128,4,128]{3,2,1,0:T(4,128)}, f32[2,128,4,128]{3,2,1,0:T(4,128)S(1)}, u32[]{:S(2)}, u32[]{:S(2)}) collective-permute-start(f32[2,128,4,128]{3,2,1,0:T(4,128)} %get-tuple-element.485), channel_id=1, source_target_pairs={{1,0},{2,1},{3,2},{4,3},{5,4},{6,5},{7,6},{8,7},{9,8},{10,9},{11,1... | collective-permute-start | bytes 1572872 | tf_op jit(solution)/shard_map/while/body/eval_jaxpr/ppermute | solution.py:23
  149.9 15.1 %collective-permute-start = (f32[2,128,4,128]{3,2,1,0:T(4,128)}, f32[2,128,4,128]{3,2,1,0:T(4,128)S(1)}, u32[]{:S(2)}, u32[]{:S(2)}) collective-permute-start(f32[2,128,4,128]{3,2,1,0:T(4,128)} %get-tuple-element.484), channel_id=1, source_target_pairs={{0,1},{1,2},{2,3},{3,4},{4,5},{5,6},{6,7},{7,8},{8,9},{9,10},{10,1... | collective-permute-start | bytes 1572872 | tf_op jit(solution)/shard_map/while/body/eval_jaxpr/ppermute | solution.py:22
  156.0 9.0 %collective-permute-start.1 = (f32[2,128,4,128]{3,2,1,0:T(4,128)}, f32[2,128,4,128]{3,2,1,0:T(4,128)S(1)}, u32[]{:S(2)}, u32[]{:S(2)}) collective-permute-start(f32[2,128,4,128]{3,2,1,0:T(4,128)} %get-tuple-element.485), channel_id=1, source_target_pairs={{1,0},{2,1},{3,2},{4,3},{5,4},{6,5},{7,6},{8,7},{9,8},{10,9},{11,1... | collective-permute-start | bytes 1572872 | tf_op jit(solution)/shard_map/while/body/eval_jaxpr/ppermute | solution.py:23
  181.4 15.1 %collective-permute-start = (f32[2,128,4,128]{3,2,1,0:T(4,128)}, f32[2,128,4,128]{3,2,1,0:T(4,128)S(1)}, u32[]{:S(2)}, u32[]{:S(2)}) collective-permute-start(f32[2,128,4,128]{3,2,1,0:T(4,128)} %get-tuple-element.484), channel_id=1, source_target_pairs={{0,1},{1,2},{2,3},{3,4},{4,5},{5,6},{6,7},{7,8},{8,9},{9,10},{10,1... | collective-permute-start | bytes 1572872 | tf_op jit(solution)/shard_map/while/body/eval_jaxpr/ppermute | solution.py:22
  187.5 9.0 %collective-permute-start.1 = (f32[2,128,4,128]{3,2,1,0:T(4,128)}, f32[2,128,4,128]{3,2,1,0:T(4,128)S(1)}, u32[]{:S(2)}, u32[]{:S(2)}) collective-permute-start(f32[2,128,4,128]{3,2,1,0:T(4,128)} %get-tuple-element.485), channel_id=1, source_target_pairs={{1,0},{2,1},{3,2},{4,3},{5,4},{6,5},{7,6},{8,7},{9,8},{10,9},{11,1... | collective-permute-start | bytes 1572872 | tf_op jit(solution)/shard_map/while/body/eval_jaxpr/ppermute | solution.py:23
  212.9 15.1 %collective-permute-start = (f32[2,128,4,128]{3,2,1,0:T(4,128)}, f32[2,128,4,128]{3,2,1,0:T(4,128)S(1)}, u32[]{:S(2)}, u32[]{:S(2)}) collective-permute-start(f32[2,128,4,128]{3,2,1,0:T(4,128)} %get-tuple-element.484), channel_id=1, source_target_pairs={{0,1},{1,2},{2,3},{3,4},{4,5},{5,6},{6,7},{7,8},{8,9},{9,10},{10,1... | collective-permute-start | bytes 1572872 | tf_op jit(solution)/shard_map/while/body/eval_jaxpr/ppermute | solution.py:22
  219.0 9.0 %collective-permute-start.1 = (f32[2,128,4,128]{3,2,1,0:T(4,128)}, f32[2,128,4,128]{3,2,1,0:T(4,128)S(1)}, u32[]{:S(2)}, u32[]{:S(2)}) collective-permute-start(f32[2,128,4,128]{3,2,1,0:T(4,128)} %get-tuple-element.485), channel_id=1, source_target_pairs={{1,0},{2,1},{3,2},{4,3},{5,4},{6,5},{7,6},{8,7},{9,8},{10,9},{11,1... | collective-permute-start | bytes 1572872 | tf_op jit(solution)/shard_map/while/body/eval_jaxpr/ppermute | solution.py:23
  244.4 15.1 %collective-permute-start = (f32[2,128,4,128]{3,2,1,0:T(4,128)}, f32[2,128,4,128]{3,2,1,0:T(4,128)S(1)}, u32[]{:S(2)}, u32[]{:S(2)}) collective-permute-start(f32[2,128,4,128]{3,2,1,0:T(4,128)} %get-tuple-element.484), channel_id=1, source_target_pairs={{0,1},{1,2},{2,3},{3,4},{4,5},{5,6},{6,7},{7,8},{8,9},{9,10},{10,1... | collective-permute-start | bytes 1572872 | tf_op jit(solution)/shard_map/while/body/eval_jaxpr/ppermute | solution.py:22
  250.5 9.0 %collective-permute-start.1 = (f32[2,128,4,128]{3,2,1,0:T(4,128)}, f32[2,128,4,128]{3,2,1,0:T(4,128)S(1)}, u32[]{:S(2)}, u32[]{:S(2)}) collective-permute-start(f32[2,128,4,128]{3,2,1,0:T(4,128)} %get-tuple-element.485), channel_id=1, source_target_pairs={{1,0},{2,1},{3,2},{4,3},{5,4},{6,5},{7,6},{8,7},{9,8},{10,9},{11,1... | collective-permute-start | bytes 1572872 | tf_op jit(solution)/shard_map/while/body/eval_jaxpr/ppermute | solution.py:23
  275.9 15.1 %collective-permute-start = (f32[2,128,4,128]{3,2,1,0:T(4,128)}, f32[2,128,4,128]{3,2,1,0:T(4,128)S(1)}, u32[]{:S(2)}, u32[]{:S(2)}) collective-permute-start(f32[2,128,4,128]{3,2,1,0:T(4,128)} %get-tuple-element.484), channel_id=1, source_target_pairs={{0,1},{1,2},{2,3},{3,4},{4,5},{5,6},{6,7},{7,8},{8,9},{9,10},{10,1... | collective-permute-start | bytes 1572872 | tf_op jit(solution)/shard_map/while/body/eval_jaxpr/ppermute | solution.py:22
  282.0 9.0 %collective-permute-start.1 = (f32[2,128,4,128]{3,2,1,0:T(4,128)}, f32[2,128,4,128]{3,2,1,0:T(4,128)S(1)}, u32[]{:S(2)}, u32[]{:S(2)}) collective-permute-start(f32[2,128,4,128]{3,2,1,0:T(4,128)} %get-tuple-element.485), channel_id=1, source_target_pairs={{1,0},{2,1},{3,2},{4,3},{5,4},{6,5},{7,6},{8,7},{9,8},{10,9},{11,1... | collective-permute-start | bytes 1572872 | tf_op jit(solution)/shard_map/while/body/eval_jaxpr/ppermute | solution.py:23
  307.4 15.1 %collective-permute-start = (f32[2,128,4,128]{3,2,1,0:T(4,128)}, f32[2,128,4,128]{3,2,1,0:T(4,128)S(1)}, u32[]{:S(2)}, u32[]{:S(2)}) collective-permute-start(f32[2,128,4,128]{3,2,1,0:T(4,128)} %get-tuple-element.484), channel_id=1, source_target_pairs={{0,1},{1,2},{2,3},{3,4},{4,5},{5,6},{6,7},{7,8},{8,9},{9,10},{10,1... | collective-permute-start | bytes 1572872 | tf_op jit(solution)/shard_map/while/body/eval_jaxpr/ppermute | solution.py:22
  313.5 9.0 %collective-permute-start.1 = (f32[2,128,4,128]{3,2,1,0:T(4,128)}, f32[2,128,4,128]{3,2,1,0:T(4,128)S(1)}, u32[]{:S(2)}, u32[]{:S(2)}) collective-permute-start(f32[2,128,4,128]{3,2,1,0:T(4,128)} %get-tuple-element.485), channel_id=1, source_target_pairs={{1,0},{2,1},{3,2},{4,3},{5,4},{6,5},{7,6},{8,7},{9,8},{10,9},{11,1... | collective-permute-start | bytes 1572872 | tf_op jit(solution)/shard_map/while/body/eval_jaxpr/ppermute | solution.py:23
  338.9 15.1 %collective-permute-start = (f32[2,128,4,128]{3,2,1,0:T(4,128)}, f32[2,128,4,128]{3,2,1,0:T(4,128)S(1)}, u32[]{:S(2)}, u32[]{:S(2)}) collective-permute-start(f32[2,128,4,128]{3,2,1,0:T(4,128)} %get-tuple-element.484), channel_id=1, source_target_pairs={{0,1},{1,2},{2,3},{3,4},{4,5},{5,6},{6,7},{7,8},{8,9},{9,10},{10,1... | collective-permute-start | bytes 1572872 | tf_op jit(solution)/shard_map/while/body/eval_jaxpr/ppermute | solution.py:22
  345.0 9.0 %collective-permute-start.1 = (f32[2,128,4,128]{3,2,1,0:T(4,128)}, f32[2,128,4,128]{3,2,1,0:T(4,128)S(1)}, u32[]{:S(2)}, u32[]{:S(2)}) collective-permute-start(f32[2,128,4,128]{3,2,1,0:T(4,128)} %get-tuple-element.485), channel_id=1, source_target_pairs={{1,0},{2,1},{3,2},{4,3},{5,4},{6,5},{7,6},{8,7},{9,8},{10,9},{11,1... | collective-permute-start | bytes 1572872 | tf_op jit(solution)/shard_map/while/body/eval_jaxpr/ppermute | solution.py:23
  370.4 15.1 %collective-permute-start = (f32[2,128,4,128]{3,2,1,0:T(4,128)}, f32[2,128,4,128]{3,2,1,0:T(4,128)S(1)}, u32[]{:S(2)}, u32[]{:S(2)}) collective-permute-start(f32[2,128,4,128]{3,2,1,0:T(4,128)} %get-tuple-element.484), channel_id=1, source_target_pairs={{0,1},{1,2},{2,3},{3,4},{4,5},{5,6},{6,7},{7,8},{8,9},{9,10},{10,1... | collective-permute-start | bytes 1572872 | tf_op jit(solution)/shard_map/while/body/eval_jaxpr/ppermute | solution.py:22
  401.9 15.1 %collective-permute-start = (f32[2,128,4,128]{3,2,1,0:T(4,128)}, f32[2,128,4,128]{3,2,1,0:T(4,128)S(1)}, u32[]{:S(2)}, u32[]{:S(2)}) collective-permute-start(f32[2,128,4,128]{3,2,1,0:T(4,128)} %get-tuple-element.484), channel_id=1, source_target_pairs={{0,1},{1,2},{2,3},{3,4},{4,5},{5,6},{6,7},{7,8},{8,9},{9,10},{10,1... | collective-permute-start | bytes 1572872 | tf_op jit(solution)/shard_map/while/body/eval_jaxpr/ppermute | solution.py:22
  433.4 15.1 %collective-permute-start = (f32[2,128,4,128]{3,2,1,0:T(4,128)}, f32[2,128,4,128]{3,2,1,0:T(4,128)S(1)}, u32[]{:S(2)}, u32[]{:S(2)}) collective-permute-start(f32[2,128,4,128]{3,2,1,0:T(4,128)} %get-tuple-element.484), channel_id=1, source_target_pairs={{0,1},{1,2},{2,3},{3,4},{4,5},{5,6},{6,7},{7,8},{8,9},{9,10},{10,1... | collective-permute-start | bytes 1572872 | tf_op jit(solution)/shard_map/while/body/eval_jaxpr/ppermute | solution.py:22
  464.9 15.1 %collective-permute-start = (f32[2,128,4,128]{3,2,1,0:T(4,128)}, f32[2,128,4,128]{3,2,1,0:T(4,128)S(1)}, u32[]{:S(2)}, u32[]{:S(2)}) collective-permute-start(f32[2,128,4,128]{3,2,1,0:T(4,128)} %get-tuple-element.484), channel_id=1, source_target_pairs={{0,1},{1,2},{2,3},{3,4},{4,5},{5,6},{6,7},{7,8},{8,9},{9,10},{10,1... | collective-permute-start | bytes 1572872 | tf_op jit(solution)/shard_map/while/body/eval_jaxpr/ppermute | solution.py:22
  496.4 15.1 %collective-permute-start = (f32[2,128,4,128]{3,2,1,0:T(4,128)}, f32[2,128,4,128]{3,2,1,0:T(4,128)S(1)}, u32[]{:S(2)}, u32[]{:S(2)}) collective-permute-start(f32[2,128,4,128]{3,2,1,0:T(4,128)} %get-tuple-element.484), channel_id=1, source_target_pairs={{0,1},{1,2},{2,3},{3,4},{4,5},{5,6},{6,7},{7,8},{8,9},{9,10},{10,1... | collective-permute-start | bytes 1572872 | tf_op jit(solution)/shard_map/while/body/eval_jaxpr/ppermute | solution.py:22
  527.9 15.1 %collective-permute-start = (f32[2,128,4,128]{3,2,1,0:T(4,128)}, f32[2,128,4,128]{3,2,1,0:T(4,128)S(1)}, u32[]{:S(2)}, u32[]{:S(2)}) collective-permute-start(f32[2,128,4,128]{3,2,1,0:T(4,128)} %get-tuple-element.484), channel_id=1, source_target_pairs={{0,1},{1,2},{2,3},{3,4},{4,5},{5,6},{6,7},{7,8},{8,9},{9,10},{10,1... | collective-permute-start | bytes 1572872 | tf_op jit(solution)/shard_map/while/body/eval_jaxpr/ppermute | solution.py:22
  559.4 15.1 %collective-permute-start = (f32[2,128,4,128]{3,2,1,0:T(4,128)}, f32[2,128,4,128]{3,2,1,0:T(4,128)S(1)}, u32[]{:S(2)}, u32[]{:S(2)}) collective-permute-start(f32[2,128,4,128]{3,2,1,0:T(4,128)} %get-tuple-element.484), channel_id=1, source_target_pairs={{0,1},{1,2},{2,3},{3,4},{4,5},{5,6},{6,7},{7,8},{8,9},{9,10},{10,1... | collective-permute-start | bytes 1572872 | tf_op jit(solution)/shard_map/while/body/eval_jaxpr/ppermute | solution.py:22
  590.9 15.1 %collective-permute-start = (f32[2,128,4,128]{3,2,1,0:T(4,128)}, f32[2,128,4,128]{3,2,1,0:T(4,128)S(1)}, u32[]{:S(2)}, u32[]{:S(2)}) collective-permute-start(f32[2,128,4,128]{3,2,1,0:T(4,128)} %get-tuple-element.484), channel_id=1, source_target_pairs={{0,1},{1,2},{2,3},{3,4},{4,5},{5,6},{6,7},{7,8},{8,9},{9,10},{10,1... | collective-permute-start | bytes 1572872 | tf_op jit(solution)/shard_map/while/body/eval_jaxpr/ppermute | solution.py:22
  622.4 15.1 %collective-permute-start = (f32[2,128,4,128]{3,2,1,0:T(4,128)}, f32[2,128,4,128]{3,2,1,0:T(4,128)S(1)}, u32[]{:S(2)}, u32[]{:S(2)}) collective-permute-start(f32[2,128,4,128]{3,2,1,0:T(4,128)} %get-tuple-element.484), channel_id=1, source_target_pairs={{0,1},{1,2},{2,3},{3,4},{4,5},{5,6},{6,7},{7,8},{8,9},{9,10},{10,1... | collective-permute-start | bytes 1572872 | tf_op jit(solution)/shard_map/while/body/eval_jaxpr/ppermute | solution.py:22
  (76 other events, 227.0 us)

commit v2 on v1

--- a/solution.py
+++ b/solution.py
@@ -1,5 +1,3 @@
-import functools
-
 import jax
 import jax.numpy as jnp
 from jax import lax
@@ -25,31 +23,30 @@
 
 
 def step_kernel(
-    cur_ref, prev_ref, s_ref, img_ref, xlo_ref, xhi_ref, inj_ref, out_ref, imgo_ref, ext_ref
+    cur_ref, prev_ref, s_ref, img_ref, xlo_ref, xhi_ref, inj_ref, out_ref, imgo_ref, ey_ref, hx_ref
 ):
     comps, block_y, block_x, depth_z = cur_ref.shape
     zeros_y = jnp.zeros((comps, HALO, block_x, depth_z), jnp.float32)
-    ext_ref[:, 0:HALO, XOFF : XOFF + block_x, :] = zeros_y
-    ext_ref[:, HALO + block_y : 2 * HALO + block_y, XOFF : XOFF + block_x, :] = zeros_y
-    ext_ref[:, HALO : HALO + block_y, XOFF - HALO : XOFF, :] = xlo_ref[...]
-    ext_ref[:, HALO : HALO + block_y, XOFF : XOFF + block_x, :] = cur_ref[...]
-    ext_ref[:, HALO : HALO + block_y, XOFF + block_x : XOFF + block_x + HALO, :] = xhi_ref[...]
+    ey_ref[:, 0:HALO] = zeros_y
+    ey_ref[:, HALO + block_y : 2 * HALO + block_y] = zeros_y
+    ey_ref[:, HALO : HALO + block_y] = cur_ref[...]
+    hx_ref[0, :, :, block_x - HALO : block_x, :] = xlo_ref[...]
+    hx_ref[1, :, :, 0:HALO, :] = xhi_ref[...]
     lane = lax.broadcasted_iota(jnp.int32, (block_x, depth_z), 1)
+    sub = lax.broadcasted_iota(jnp.int32, (block_x, depth_z), 0)
 
     def row(y, carry):
         done = []
         for c in range(comps):
-            ctr = cur_ref[c, y]
+            ctr = ey_ref[c, HALO + y]
+            left = hx_ref[0, c, y]
+            right = hx_ref[1, c, y]
             acc = center_weight * ctr
             for m in range(1, HALO + 1):
-                b = ext_ref[c, HALO + y, XOFF + m : XOFF + m + block_x, :] + ext_ref[
-                    c, HALO + y, XOFF - m : XOFF - m + block_x, :
-                ]
-                b = (
-                    b
-                    + ext_ref[c, HALO + y + m, XOFF : XOFF + block_x, :]
-                    + ext_ref[c, HALO + y - m, XOFF : XOFF + block_x, :]
-                )
+                ahead = pltpu.roll(jnp.where(sub >= m, ctr, right), block_x - m, 0)
+                behind = pltpu.roll(jnp.where(sub < block_x - m, ctr, left), m, 0)
+                b = ahead + behind
+                b = b + ey_ref[c, HALO + y + m] + ey_ref[c, HALO + y - m]
                 up = jnp.where(lane < depth_z - m, pltpu.roll(ctr, depth_z - m, 1), 0.0)
                 down = jnp.where(lane >= m, pltpu.roll(ctr, m, 1), 0.0)
                 b = b + up + down
@@ -61,7 +58,7 @@
         imgo_ref[y] = img_ref[y] + done[0] * done[1]
         return carry
 
-    lax.fori_loop(0, block_y, row, 0)
+    lax.fori_loop(0, block_y, row, 0, unroll=2)
 
 
 def step_call(cur, prev, s, img, xlo, xhi, inj):
@@ -76,8 +73,10 @@
         in_specs=[vmem] * 7,
         out_specs=(vmem, vmem),
         scratch_shapes=[
-            pltpu.VMEM((comps, block_y + 2 * HALO, block_x + 2 * XOFF, depth_z), jnp.float32)
+            pltpu.VMEM((comps, block_y + 2 * HALO, block_x, depth_z), jnp.float32),
+            pltpu.VMEM((2, comps, block_y, block_x, depth_z), jnp.float32),
         ],
+        input_output_aliases={1: 0, 3: 1},
         compiler_params=pltpu.CompilerParams(vmem_limit_bytes=48 * 1024 * 1024),
         cost_estimate=pl.CostEstimate(
             flops=60 * cur.size, bytes_accessed=4 * 6 * cur.size, transcendentals=0
@@ -123,8 +122,7 @@
     source_core = point_tables(source_pos, x_anchor, cells_x, depth_y)
     receiver_core = point_tables(receiver_pos, x_anchor, cells_x, depth_y)
 
-    def advance(moment, state_carry):
-        previous, current, image_acc = state_carry
+    def advance(moment, previous, current, image_acc):
         low, high = with_halo(current, "dom", 2, HALO)
         pulses = lax.dynamic_index_in_dim(wavelet, moment, 0, keepdims=False)
         recorded = lax.dynamic_index_in_dim(traces, moment, 0, keepdims=False)
@@ -134,12 +132,20 @@
                 spread_points(receiver_core, recorded, depth_z),
             ]
         )
-        updated, image_acc = step_call(current, previous, speed_sq, image_acc, low, high, added)
-        return (current, updated, image_acc)
+        return step_call(current, previous, speed_sq, image_acc, low, high, added)
+
+    def pair(index, state_carry):
+        previous, current, image_acc = state_carry
+        first, image_acc = advance(2 * index, previous, current, image_acc)
+        second, image_acc = advance(2 * index + 1, current, first, image_acc)
+        return (first, second, image_acc)
 
     previous, current, image_acc = lax.fori_loop(
-        0, steps_total, advance, (older_fields, fields_now, image_zero)
+        0, steps_total // 2, pair, (older_fields, fields_now, image_zero)
     )
+    if steps_total % 2:
+        last, image_acc = advance(steps_total - 1, previous, current, image_acc)
+        previous, current = current, last
     image_acc = image_acc * (1.0 / steps_total)
     outgoing = image_acc.reshape(depth_y, 1, cells_x, depth_z)
     one_hot = (aperture[None, :] == jnp.arange(slab_count, dtype=jnp.int32)[:, None]).astype(

time: 683 us -> 594 us (0.87)
  Pallas kernels: 259 us -> 181 us
    pallas_call x20, Pallas kernels: 259 us -> 181 us  [step_call(): pl.pallas_call(step_kernel, out_shape=(jax.ShapeDtypeStruct(cur.shape, jn...]
    while x180 -> x40, local copies, waits for them, and re-layouts: 69.6 us -> 18.8 us
    another operation x20, local copies, waits for them, and re-layouts: 1.42 us -> 25.4 us  [advance(): jnp.stack([spread_points(source_core, pulses, depth_z), spread_points(rec...]
    slice x20, local copies, waits for them, and re-layouts: 22.9 us -> 38.4 us  [with_halo(): head = lax.slice_in_dim(cells, 0, width, axis=dim)]
    reshape x40, local copies, waits for them, and re-layouts: 26.2 us -> 41.4 us  [spread_points(): plane = plane.reshape(rows_y.shape[1], places.shape[1] // 4, 4)]
    dynamic_slice x20 -> x10, local copies, waits for them, and re-layouts: 19.6 us -> 10.8 us  [advance(): recorded = lax.dynamic_index_in_dim(traces, moment, 0, keepdims=False)]
  transfers between devices with their start and end apart: 41 -> 41, of which waited for: 1 -> 1; matrix products, arithmetic and copies ran while one was open for 22% -> 27% of each run, Pallas kernels for 0% -> 0%
where the time goes in v2:
time: 594 us; the launch traced here: 590 us
  Pallas kernels  181 us (30%)
  starting transfers between devices  148 us (25%)
  local copies, waits for them, and re-layouts  139 us (23%)
  matrix products  80.5 us (14%)
  blocking collectives  22.6 us (4%)
  waiting for transfers between devices  14.2 us (2%)
    pallas_call x20, Pallas kernels, step_call(): pl.pallas_call(step_kernel, out_shape=(jax.ShapeDtypeStruct(cur.shape, jn...  181 us
    ppermute x20, starting transfers between devices, with_halo(): low = lax.ppermute(tail, axis, [(i, (i + 1) % count) for i in range(ends)])  115 us
    dot_general x40, matrix products, spread_points(): jnp.einsum('ny,nc->yc', weighted, places, precision=lax.Precision.HIGHEST)  79.8 us
    reshape x40, local copies, waits for them, and re-layouts, spread_points(): plane = plane.reshape(rows_y.shape[1], places.shape[1] // 4, 4)  41.4 us
    slice x20, local copies, waits for them, and re-layouts, with_halo(): head = lax.slice_in_dim(cells, 0, width, axis=dim)  38.4 us
    ppermute x20, starting transfers between devices, with_halo(): high = lax.ppermute(head, axis, [((i + 1) % count, i) for i in range(ends)])  25.8 us
    another operation x20, local copies, waits for them, and re-layouts, advance(): jnp.stack([spread_points(source_core, pulses, depth_z), spread_points(rec...  25.4 us
    all_to_all x1, blocking collectives, shards(): lax.all_to_all(outgoing, 'dom', split_axis=0, concat_axis=1, tiled=True)  22.6 us
  transfers between devices with their start and end apart: 41, of which 1 were waited for; matrix products, arithmetic and copies ran while one was open for 27% of the time, Pallas kernels for 0%

profile of v2, /device:TPU:0, one launch (start us, length us, event | category | flops | bytes accessed | tf_op | source)
XLA Modules:
  0.0 590.4 jit_solution(12958702237773068590)
XLA Ops:
  4.5 7.4 %all-to-all-start = ((f32[8,16,8,128]{3,2,0,1:T(8,128)}), f32[8,16,8,128]{3,2,0,1:T(8,128)S(1)}, u32[]{:S(2)}, u32[]{:S(2)}) async-start(f32[8,16,8,128]{3,2,0,1:T(8,128)} %select_bitcast_fusion), calls=%async_computation | async-start | bytes 1048576 | tf_op jit(solution)/shard_map/all_to_all | solution.py:118
  12.2 14.1 %all-to-all-done = f32[8,16,8,128]{3,2,0,1:T(8,128)S(1)} async-done(((f32[8,16,8,128]{3,2,0,1:T(8,128)}), f32[8,16,8,128]{3,2,0,1:T(8,128)S(1)}, u32[]{:S(2)}, u32[]{:S(2)}) %all-to-all-start) | async-done | bytes 524320 | tf_op jit(solution)/shard_map/all_to_all | solution.py:118
  27.3 538.9 %while.20 = (s32[]{:T(128)}, f32[2,128,8,128]{3,2,1,0:T(8,128)S(1)}, f32[2,128,8,128]{3,2,1,0:T(8,128)}, f32[128,8,128]{2,1,0:T(8,128)S(1)}, f32[20,8]{1,0:T(8,1...) while((s32[]{:T(128)}, ...), condition=%wide.region_1.2_spmd.clone, body=%wide.region_0.1_spmd.clone.sunk | while | flops 843847168 | bytes 36258616 | solution.py:143
  42.7 8.6 %eval_jaxpr.16 = (f32[2,128,8,128]{3,2,1,0:T(8,128)S(1)}, f32[128,8,128]{2,1,0:T(8,128)S(1)}) custom-call(f32[2,128,8,128]{3,2,1,0:T(8,128)} %get-tuple-element.547.cur_ref.prev_ref, f32[2,128,8,128]{3,2,1,0:T(8,128)S(1)} %get-tuple-element.546.prev_ref, f32[128,8,128]{2,1,0:T(8,128)S(1)} %copy-done.3, ...), custom_call_target="tpu_custom_call", output_to_operand_aliasing={{0}: (1, {}), {1}: (3, {})} | custom-call | flops 15728640 | bytes 6291456 | tf_op jit(solution)/shard_map/while/body/eval_jaxpr/pallas_call | solution.py:67
  65.8 9.5 %eval_jaxpr.17 = (f32[2,128,8,128]{3,2,1,0:T(8,128)}, f32[128,8,128]{2,1,0:T(8,128)S(1)}) custom-call(f32[2,128,8,128]{3,2,1,0:T(8,128)S(1)} %get-tuple-element.564.cur_ref, f32[2,128,8,128]{3,2,1,0:T(8,128)} %get-tuple-element.547.cur_ref.prev_ref, f32[128,8,128]{2,1,0:T(8,128)S(1)} %copy-done.4, ...), custom_call_target="tpu_custom_call", output_to_operand_aliasing={{0}: (1, {}), {1}: (3, {})} | custom-call | flops 15728640 | bytes 6291456 | tf_op jit(solution)/shard_map/while/body/eval_jaxpr/pallas_call | solution.py:67
  78.0 6.6 %collective-permute-start = (f32[2,128,4,128]{3,2,1,0:T(4,128)}, f32[2,128,4,128]{3,2,1,0:T(4,128)S(1)}, u32[]{:S(2)}, u32[]{:S(2)}) collective-permute-start(f32[2,128,4,128]{3,2,1,0:T(4,128)} %get-tuple-element.511), channel_id=1, source_target_pairs={{0,1},{1,2},{2,3},{3,4},{4,5},{5,6},{6,7},{7,8},{8,9},{9,10},{10,1... | collective-permute-start | bytes 1572872 | tf_op jit(solution)/shard_map/while/body/eval_jaxpr/ppermute | solution.py:20
  95.4 8.6 %eval_jaxpr.16 = (f32[2,128,8,128]{3,2,1,0:T(8,128)S(1)}, f32[128,8,128]{2,1,0:T(8,128)S(1)}) custom-call(f32[2,128,8,128]{3,2,1,0:T(8,128)} %get-tuple-element.547.cur_ref.prev_ref, f32[2,128,8,128]{3,2,1,0:T(8,128)S(1)} %get-tuple-element.546.prev_ref, f32[128,8,128]{2,1,0:T(8,128)S(1)} %copy-done.3, ...), custom_call_target="tpu_custom_call", output_to_operand_aliasing={{0}: (1, {}), {1}: (3, {})} | custom-call | flops 15728640 | bytes 6291456 | tf_op jit(solution)/shard_map/while/body/eval_jaxpr/pallas_call | solution.py:67
  120.3 9.5 %eval_jaxpr.17 = (f32[2,128,8,128]{3,2,1,0:T(8,128)}, f32[128,8,128]{2,1,0:T(8,128)S(1)}) custom-call(f32[2,128,8,128]{3,2,1,0:T(8,128)S(1)} %get-tuple-element.564.cur_ref, f32[2,128,8,128]{3,2,1,0:T(8,128)} %get-tuple-element.547.cur_ref.prev_ref, f32[128,8,128]{2,1,0:T(8,128)S(1)} %copy-done.4, ...), custom_call_target="tpu_custom_call", output_to_operand_aliasing={{0}: (1, {}), {1}: (3, {})} | custom-call | flops 15728640 | bytes 6291456 | tf_op jit(solution)/shard_map/while/body/eval_jaxpr/pallas_call | solution.py:67
  132.5 6.6 %collective-permute-start = (f32[2,128,4,128]{3,2,1,0:T(4,128)}, f32[2,128,4,128]{3,2,1,0:T(4,128)S(1)}, u32[]{:S(2)}, u32[]{:S(2)}) collective-permute-start(f32[2,128,4,128]{3,2,1,0:T(4,128)} %get-tuple-element.511), channel_id=1, source_target_pairs={{0,1},{1,2},{2,3},{3,4},{4,5},{5,6},{6,7},{7,8},{8,9},{9,10},{10,1... | collective-permute-start | bytes 1572872 | tf_op jit(solution)/shard_map/while/body/eval_jaxpr/ppermute | solution.py:20
  149.9 8.6 %eval_jaxpr.16 = (f32[2,128,8,128]{3,2,1,0:T(8,128)S(1)}, f32[128,8,128]{2,1,0:T(8,128)S(1)}) custom-call(f32[2,128,8,128]{3,2,1,0:T(8,128)} %get-tuple-element.547.cur_ref.prev_ref, f32[2,128,8,128]{3,2,1,0:T(8,128)S(1)} %get-tuple-element.546.prev_ref, f32[128,8,128]{2,1,0:T(8,128)S(1)} %copy-done.3, ...), custom_call_target="tpu_custom_call", output_to_operand_aliasing={{0}: (1, {}), {1}: (3, {})} | custom-call | flops 15728640 | bytes 6291456 | tf_op jit(solution)/shard_map/while/body/eval_jaxpr/pallas_call | solution.py:67
  174.9 9.5 %eval_jaxpr.17 = (f32[2,128,8,128]{3,2,1,0:T(8,128)}, f32[128,8,128]{2,1,0:T(8,128)S(1)}) custom-call(f32[2,128,8,128]{3,2,1,0:T(8,128)S(1)} %get-tuple-element.564.cur_ref, f32[2,128,8,128]{3,2,1,0:T(8,128)} %get-tuple-element.547.cur_ref.prev_ref, f32[128,8,128]{2,1,0:T(8,128)S(1)} %copy-done.4, ...), custom_call_target="tpu_custom_call", output_to_operand_aliasing={{0}: (1, {}), {1}: (3, {})} | custom-call | flops 15728640 | bytes 6291456 | tf_op jit(solution)/shard_map/while/body/eval_jaxpr/pallas_call | solution.py:67
  187.1 6.6 %collective-permute-start = (f32[2,128,4,128]{3,2,1,0:T(4,128)}, f32[2,128,4,128]{3,2,1,0:T(4,128)S(1)}, u32[]{:S(2)}, u32[]{:S(2)}) collective-permute-start(f32[2,128,4,128]{3,2,1,0:T(4,128)} %get-tuple-element.511), channel_id=1, source_target_pairs={{0,1},{1,2},{2,3},{3,4},{4,5},{5,6},{6,7},{7,8},{8,9},{9,10},{10,1... | collective-permute-start | bytes 1572872 | tf_op jit(solution)/shard_map/while/body/eval_jaxpr/ppermute | solution.py:20
  204.5 8.6 %eval_jaxpr.16 = (f32[2,128,8,128]{3,2,1,0:T(8,128)S(1)}, f32[128,8,128]{2,1,0:T(8,128)S(1)}) custom-call(f32[2,128,8,128]{3,2,1,0:T(8,128)} %get-tuple-element.547.cur_ref.prev_ref, f32[2,128,8,128]{3,2,1,0:T(8,128)S(1)} %get-tuple-element.546.prev_ref, f32[128,8,128]{2,1,0:T(8,128)S(1)} %copy-done.3, ...), custom_call_target="tpu_custom_call", output_to_operand_aliasing={{0}: (1, {}), {1}: (3, {})} | custom-call | flops 15728640 | bytes 6291456 | tf_op jit(solution)/shard_map/while/body/eval_jaxpr/pallas_call | solution.py:67
  229.4 9.5 %eval_jaxpr.17 = (f32[2,128,8,128]{3,2,1,0:T(8,128)}, f32[128,8,128]{2,1,0:T(8,128)S(1)}) custom-call(f32[2,128,8,128]{3,2,1,0:T(8,128)S(1)} %get-tuple-element.564.cur_ref, f32[2,128,8,128]{3,2,1,0:T(8,128)} %get-tuple-element.547.cur_ref.prev_ref, f32[128,8,128]{2,1,0:T(8,128)S(1)} %copy-done.4, ...), custom_call_target="tpu_custom_call", output_to_operand_aliasing={{0}: (1, {}), {1}: (3, {})} | custom-call | flops 15728640 | bytes 6291456 | tf_op jit(solution)/shard_map/while/body/eval_jaxpr/pallas_call | solution.py:67
  241.6 6.6 %collective-permute-start = (f32[2,128,4,128]{3,2,1,0:T(4,128)}, f32[2,128,4,128]{3,2,1,0:T(4,128)S(1)}, u32[]{:S(2)}, u32[]{:S(2)}) collective-permute-start(f32[2,128,4,128]{3,2,1,0:T(4,128)} %get-tuple-element.511), channel_id=1, source_target_pairs={{0,1},{1,2},{2,3},{3,4},{4,5},{5,6},{6,7},{7,8},{8,9},{9,10},{10,1... | collective-permute-start | bytes 1572872 | tf_op jit(solution)/shard_map/while/body/eval_jaxpr/ppermute | solution.py:20
  259.0 8.6 %eval_jaxpr.16 = (f32[2,128,8,128]{3,2,1,0:T(8,128)S(1)}, f32[128,8,128]{2,1,0:T(8,128)S(1)}) custom-call(f32[2,128,8,128]{3,2,1,0:T(8,128)} %get-tuple-element.547.cur_ref.prev_ref, f32[2,128,8,128]{3,2,1,0:T(8,128)S(1)} %get-tuple-element.546.prev_ref, f32[128,8,128]{2,1,0:T(8,128)S(1)} %copy-done.3, ...), custom_call_target="tpu_custom_call", output_to_operand_aliasing={{0}: (1, {}), {1}: (3, {})} | custom-call | flops 15728640 | bytes 6291456 | tf_op jit(solution)/shard_map/while/body/eval_jaxpr/pallas_call | solution.py:67
  284.0 9.5 %eval_jaxpr.17 = (f32[2,128,8,128]{3,2,1,0:T(8,128)}, f32[128,8,128]{2,1,0:T(8,128)S(1)}) custom-call(f32[2,128,8,128]{3,2,1,0:T(8,128)S(1)} %get-tuple-element.564.cur_ref, f32[2,128,8,128]{3,2,1,0:T(8,128)} %get-tuple-element.547.cur_ref.prev_ref, f32[128,8,128]{2,1,0:T(8,128)S(1)} %copy-done.4, ...), custom_call_target="tpu_custom_call", output_to_operand_aliasing={{0}: (1, {}), {1}: (3, {})} | custom-call | flops 15728640 | bytes 6291456 | tf_op jit(solution)/shard_map/while/body/eval_jaxpr/pallas_call | solution.py:67
  296.2 6.6 %collective-permute-start = (f32[2,128,4,128]{3,2,1,0:T(4,128)}, f32[2,128,4,128]{3,2,1,0:T(4,128)S(1)}, u32[]{:S(2)}, u32[]{:S(2)}) collective-permute-start(f32[2,128,4,128]{3,2,1,0:T(4,128)} %get-tuple-element.511), channel_id=1, source_target_pairs={{0,1},{1,2},{2,3},{3,4},{4,5},{5,6},{6,7},{7,8},{8,9},{9,10},{10,1... | collective-permute-start | bytes 1572872 | tf_op jit(solution)/shard_map/while/body/eval_jaxpr/ppermute | solution.py:20
  313.6 8.6 %eval_jaxpr.16 = (f32[2,128,8,128]{3,2,1,0:T(8,128)S(1)}, f32[128,8,128]{2,1,0:T(8,128)S(1)}) custom-call(f32[2,128,8,128]{3,2,1,0:T(8,128)} %get-tuple-element.547.cur_ref.prev_ref, f32[2,128,8,128]{3,2,1,0:T(8,128)S(1)} %get-tuple-element.546.prev_ref, f32[128,8,128]{2,1,0:T(8,128)S(1)} %copy-done.3, ...), custom_call_target="tpu_custom_call", output_to_operand_aliasing={{0}: (1, {}), {1}: (3, {})} | custom-call | flops 15728640 | bytes 6291456 | tf_op jit(solution)/shard_map/while/body/eval_jaxpr/pallas_call | solution.py:67
  338.5 9.5 %eval_jaxpr.17 = (f32[2,128,8,128]{3,2,1,0:T(8,128)}, f32[128,8,128]{2,1,0:T(8,128)S(1)}) custom-call(f32[2,128,8,128]{3,2,1,0:T(8,128)S(1)} %get-tuple-element.564.cur_ref, f32[2,128,8,128]{3,2,1,0:T(8,128)} %get-tuple-element.547.cur_ref.prev_ref, f32[128,8,128]{2,1,0:T(8,128)S(1)} %copy-done.4, ...), custom_call_target="tpu_custom_call", output_to_operand_aliasing={{0}: (1, {}), {1}: (3, {})} | custom-call | flops 15728640 | bytes 6291456 | tf_op jit(solution)/shard_map/while/body/eval_jaxpr/pallas_call | solution.py:67
  350.7 6.6 %collective-permute-start = (f32[2,128,4,128]{3,2,1,0:T(4,128)}, f32[2,128,4,128]{3,2,1,0:T(4,128)S(1)}, u32[]{:S(2)}, u32[]{:S(2)}) collective-permute-start(f32[2,128,4,128]{3,2,1,0:T(4,128)} %get-tuple-element.511), channel_id=1, source_target_pairs={{0,1},{1,2},{2,3},{3,4},{4,5},{5,6},{6,7},{7,8},{8,9},{9,10},{10,1... | collective-permute-start | bytes 1572872 | tf_op jit(solution)/shard_map/while/body/eval_jaxpr/ppermute | solution.py:20
  368.1 8.6 %eval_jaxpr.16 = (f32[2,128,8,128]{3,2,1,0:T(8,128)S(1)}, f32[128,8,128]{2,1,0:T(8,128)S(1)}) custom-call(f32[2,128,8,128]{3,2,1,0:T(8,128)} %get-tuple-element.547.cur_ref.prev_ref, f32[2,128,8,128]{3,2,1,0:T(8,128)S(1)} %get-tuple-element.546.prev_ref, f32[128,8,128]{2,1,0:T(8,128)S(1)} %copy-done.3, ...), custom_call_target="tpu_custom_call", output_to_operand_aliasing={{0}: (1, {}), {1}: (3, {})} | custom-call | flops 15728640 | bytes 6291456 | tf_op jit(solution)/shard_map/while/body/eval_jaxpr/pallas_call | solution.py:67
  393.1 9.5 %eval_jaxpr.17 = (f32[2,128,8,128]{3,2,1,0:T(8,128)}, f32[128,8,128]{2,1,0:T(8,128)S(1)}) custom-call(f32[2,128,8,128]{3,2,1,0:T(8,128)S(1)} %get-tuple-element.564.cur_ref, f32[2,128,8,128]{3,2,1,0:T(8,128)} %get-tuple-element.547.cur_ref.prev_ref, f32[128,8,128]{2,1,0:T(8,128)S(1)} %copy-done.4, ...), custom_call_target="tpu_custom_call", output_to_operand_aliasing={{0}: (1, {}), {1}: (3, {})} | custom-call | flops 15728640 | bytes 6291456 | tf_op jit(solution)/shard_map/while/body/eval_jaxpr/pallas_call | solution.py:67
  422.7 8.6 %eval_jaxpr.16 = (f32[2,128,8,128]{3,2,1,0:T(8,128)S(1)}, f32[128,8,128]{2,1,0:T(8,128)S(1)}) custom-call(f32[2,128,8,128]{3,2,1,0:T(8,128)} %get-tuple-element.547.cur_ref.prev_ref, f32[2,128,8,128]{3,2,1,0:T(8,128)S(1)} %get-tuple-element.546.prev_ref, f32[128,8,128]{2,1,0:T(8,128)S(1)} %copy-done.3, ...), custom_call_target="tpu_custom_call", output_to_operand_aliasing={{0}: (1, {}), {1}: (3, {})} | custom-call | flops 15728640 | bytes 6291456 | tf_op jit(solution)/shard_map/while/body/eval_jaxpr/pallas_call | solution.py:67
  447.6 9.5 %eval_jaxpr.17 = (f32[2,128,8,128]{3,2,1,0:T(8,128)}, f32[128,8,128]{2,1,0:T(8,128)S(1)}) custom-call(f32[2,128,8,128]{3,2,1,0:T(8,128)S(1)} %get-tuple-element.564.cur_ref, f32[2,128,8,128]{3,2,1,0:T(8,128)} %get-tuple-element.547.cur_ref.prev_ref, f32[128,8,128]{2,1,0:T(8,128)S(1)} %copy-done.4, ...), custom_call_target="tpu_custom_call", output_to_operand_aliasing={{0}: (1, {}), {1}: (3, {})} | custom-call | flops 15728640 | bytes 6291456 | tf_op jit(solution)/shard_map/while/body/eval_jaxpr/pallas_call | solution.py:67
  459.8 6.6 %collective-permute-start = (f32[2,128,4,128]{3,2,1,0:T(4,128)}, f32[2,128,4,128]{3,2,1,0:T(4,128)S(1)}, u32[]{:S(2)}, u32[]{:S(2)}) collective-permute-start(f32[2,128,4,128]{3,2,1,0:T(4,128)} %get-tuple-element.511), channel_id=1, source_target_pairs={{0,1},{1,2},{2,3},{3,4},{4,5},{5,6},{6,7},{7,8},{8,9},{9,10},{10,1... | collective-permute-start | bytes 1572872 | tf_op jit(solution)/shard_map/while/body/eval_jaxpr/ppermute | solution.py:20
  477.2 8.6 %eval_jaxpr.16 = (f32[2,128,8,128]{3,2,1,0:T(8,128)S(1)}, f32[128,8,128]{2,1,0:T(8,128)S(1)}) custom-call(f32[2,128,8,128]{3,2,1,0:T(8,128)} %get-tuple-element.547.cur_ref.prev_ref, f32[2,128,8,128]{3,2,1,0:T(8,128)S(1)} %get-tuple-element.546.prev_ref, f32[128,8,128]{2,1,0:T(8,128)S(1)} %copy-done.3, ...), custom_call_target="tpu_custom_call", output_to_operand_aliasing={{0}: (1, {}), {1}: (3, {})} | custom-call | flops 15728640 | bytes 6291456 | tf_op jit(solution)/shard_map/while/body/eval_jaxpr/pallas_call | solution.py:67
  502.2 9.5 %eval_jaxpr.17 = (f32[2,128,8,128]{3,2,1,0:T(8,128)}, f32[128,8,128]{2,1,0:T(8,128)S(1)}) custom-call(f32[2,128,8,128]{3,2,1,0:T(8,128)S(1)} %get-tuple-element.564.cur_ref, f32[2,128,8,128]{3,2,1,0:T(8,128)} %get-tuple-element.547.cur_ref.prev_ref, f32[128,8,128]{2,1,0:T(8,128)S(1)} %copy-done.4, ...), custom_call_target="tpu_custom_call", output_to_operand_aliasing={{0}: (1, {}), {1}: (3, {})} | custom-call | flops 15728640 | bytes 6291456 | tf_op jit(solution)/shard_map/while/body/eval_jaxpr/pallas_call | solution.py:67
  514.4 6.6 %collective-permute-start = (f32[2,128,4,128]{3,2,1,0:T(4,128)}, f32[2,128,4,128]{3,2,1,0:T(4,128)S(1)}, u32[]{:S(2)}, u32[]{:S(2)}) collective-permute-start(f32[2,128,4,128]{3,2,1,0:T(4,128)} %get-tuple-element.511), channel_id=1, source_target_pairs={{0,1},{1,2},{2,3},{3,4},{4,5},{5,6},{6,7},{7,8},{8,9},{9,10},{10,1... | collective-permute-start | bytes 1572872 | tf_op jit(solution)/shard_map/while/body/eval_jaxpr/ppermute | solution.py:20
  531.8 8.6 %eval_jaxpr.16 = (f32[2,128,8,128]{3,2,1,0:T(8,128)S(1)}, f32[128,8,128]{2,1,0:T(8,128)S(1)}) custom-call(f32[2,128,8,128]{3,2,1,0:T(8,128)} %get-tuple-element.547.cur_ref.prev_ref, f32[2,128,8,128]{3,2,1,0:T(8,128)S(1)} %get-tuple-element.546.prev_ref, f32[128,8,128]{2,1,0:T(8,128)S(1)} %copy-done.3, ...), custom_call_target="tpu_custom_call", output_to_operand_aliasing={{0}: (1, {}), {1}: (3, {})} | custom-call | flops 15728640 | bytes 6291456 | tf_op jit(solution)/shard_map/while/body/eval_jaxpr/pallas_call | solution.py:67
  556.6 9.5 %eval_jaxpr.17 = (f32[2,128,8,128]{3,2,1,0:T(8,128)}, f32[128,8,128]{2,1,0:T(8,128)S(1)}) custom-call(f32[2,128,8,128]{3,2,1,0:T(8,128)S(1)} %get-tuple-element.564.cur_ref, f32[2,128,8,128]{3,2,1,0:T(8,128)} %get-tuple-element.547.cur_ref.prev_ref, f32[128,8,128]{2,1,0:T(8,128)S(1)} %copy-done.4, ...), custom_call_target="tpu_custom_call", output_to_operand_aliasing={{0}: (1, {}), {1}: (3, {})} | custom-call | flops 15728640 | bytes 6291456 | tf_op jit(solution)/shard_map/while/body/eval_jaxpr/pallas_call | solution.py:67
  566.2 22.6 %all_to_all.27 = f32[128,1,8,128]{3,2,1,0:T(8,128)S(1)} all-to-all(f32[128,1,8,128]{3,2,1,0:T(8,128)S(1)} %multiply_bitcast_fusion), channel_id=1, replica_groups=mesh['survey'=2,'dom'=16] {'dom'}, dimensions={0} | all-to-all | bytes 1048576 | tf_op jit(solution)/shard_map/all_to_all | solution.py:154
  (304 shorter events, 310.5 us)
Async XLA Ops:
  4.5 21.9 %all-to-all-start = ((f32[8,16,8,128]{3,2,0,1:T(8,128)}), f32[8,16,8,128]{3,2,0,1:T(8,128)S(1)}, u32[]{:S(2)}, u32[]{:S(2)}) async-start(f32[8,16,8,128]{3,2,0,1:T(8,128)} %select_bitcast_fusion), calls=%async_computation | async-start | bytes 1048576 | tf_op jit(solution)/shard_map/all_to_all | solution.py:118
  30.0 11.8 %collective-permute-start = (f32[2,128,4,128]{3,2,1,0:T(4,128)}, f32[2,128,4,128]{3,2,1,0:T(4,128)S(1)}, u32[]{:S(2)}, u32[]{:S(2)}) collective-permute-start(f32[2,128,4,128]{3,2,1,0:T(4,128)} %get-tuple-element.511), channel_id=1, source_target_pairs={{0,1},{1,2},{2,3},{3,4},{4,5},{5,6},{6,7},{7,8},{8,9},{9,10},{10,1... | collective-permute-start | bytes 1572872 | tf_op jit(solution)/shard_map/while/body/eval_jaxpr/ppermute | solution.py:20
  31.9 9.9 %collective-permute-start.1 = (f32[2,128,4,128]{3,2,1,0:T(4,128)}, f32[2,128,4,128]{3,2,1,0:T(4,128)S(1)}, u32[]{:S(2)}, u32[]{:S(2)}) collective-permute-start(f32[2,128,4,128]{3,2,1,0:T(4,128)} %get-tuple-element.512), channel_id=1, source_target_pairs={{1,0},{2,1},{3,2},{4,3},{5,4},{6,5},{7,6},{8,7},{9,8},{10,9},{11,1... | collective-permute-start | bytes 1572872 | tf_op jit(solution)/shard_map/while/body/eval_jaxpr/ppermute | solution.py:21
  52.4 12.4 %collective-permute-start.2 = (f32[2,128,4,128]{3,2,1,0:T(4,128)}, f32[2,128,4,128]{3,2,1,0:T(4,128)S(1)}, u32[]{:S(2)}, u32[]{:S(2)}) collective-permute-start(f32[2,128,4,128]{3,2,1,0:T(4,128)} %get-tuple-element.519), channel_id=1, source_target_pairs={{0,1},{1,2},{2,3},{3,4},{4,5},{5,6},{6,7},{7,8},{8,9},{9,10},{10,1... | collective-permute-start | bytes 1572872 | tf_op jit(solution)/shard_map/while/body/eval_jaxpr/ppermute | solution.py:20
  56.1 8.8 %collective-permute-start.3 = (f32[2,128,4,128]{3,2,1,0:T(4,128)}, f32[2,128,4,128]{3,2,1,0:T(4,128)S(1)}, u32[]{:S(2)}, u32[]{:S(2)}) collective-permute-start(f32[2,128,4,128]{3,2,1,0:T(4,128)} %get-tuple-element.520), channel_id=1, source_target_pairs={{1,0},{2,1},{3,2},{4,3},{5,4},{6,5},{7,6},{8,7},{9,8},{10,9},{11,1... | collective-permute-start | bytes 1572872 | tf_op jit(solution)/shard_map/while/body/eval_jaxpr/ppermute | solution.py:21
  78.0 16.5 %collective-permute-start = (f32[2,128,4,128]{3,2,1,0:T(4,128)}, f32[2,128,4,128]{3,2,1,0:T(4,128)S(1)}, u32[]{:S(2)}, u32[]{:S(2)}) collective-permute-start(f32[2,128,4,128]{3,2,1,0:T(4,128)} %get-tuple-element.511), channel_id=1, source_target_pairs={{0,1},{1,2},{2,3},{3,4},{4,5},{5,6},{6,7},{7,8},{8,9},{9,10},{10,1... | collective-permute-start | bytes 1572872 | tf_op jit(solution)/shard_map/while/body/eval_jaxpr/ppermute | solution.py:20
  84.6 9.9 %collective-permute-start.1 = (f32[2,128,4,128]{3,2,1,0:T(4,128)}, f32[2,128,4,128]{3,2,1,0:T(4,128)S(1)}, u32[]{:S(2)}, u32[]{:S(2)}) collective-permute-start(f32[2,128,4,128]{3,2,1,0:T(4,128)} %get-tuple-element.512), channel_id=1, source_target_pairs={{1,0},{2,1},{3,2},{4,3},{5,4},{6,5},{7,6},{8,7},{9,8},{10,9},{11,1... | collective-permute-start | bytes 1572872 | tf_op jit(solution)/shard_map/while/body/eval_jaxpr/ppermute | solution.py:21
  105.1 14.2 %collective-permute-start.2 = (f32[2,128,4,128]{3,2,1,0:T(4,128)}, f32[2,128,4,128]{3,2,1,0:T(4,128)S(1)}, u32[]{:S(2)}, u32[]{:S(2)}) collective-permute-start(f32[2,128,4,128]{3,2,1,0:T(4,128)} %get-tuple-element.519), channel_id=1, source_target_pairs={{0,1},{1,2},{2,3},{3,4},{4,5},{5,6},{6,7},{7,8},{8,9},{9,10},{10,1... | collective-permute-start | bytes 1572872 | tf_op jit(solution)/shard_map/while/body/eval_jaxpr/ppermute | solution.py:20
  132.5 16.5 %collective-permute-start = (f32[2,128,4,128]{3,2,1,0:T(4,128)}, f32[2,128,4,128]{3,2,1,0:T(4,128)S(1)}, u32[]{:S(2)}, u32[]{:S(2)}) collective-permute-start(f32[2,128,4,128]{3,2,1,0:T(4,128)} %get-tuple-element.511), channel_id=1, source_target_pairs={{0,1},{1,2},{2,3},{3,4},{4,5},{5,6},{6,7},{7,8},{8,9},{9,10},{10,1... | collective-permute-start | bytes 1572872 | tf_op jit(solution)/shard_map/while/body/eval_jaxpr/ppermute | solution.py:20
  139.1 9.9 %collective-permute-start.1 = (f32[2,128,4,128]{3,2,1,0:T(4,128)}, f32[2,128,4,128]{3,2,1,0:T(4,128)S(1)}, u32[]{:S(2)}, u32[]{:S(2)}) collective-permute-start(f32[2,128,4,128]{3,2,1,0:T(4,128)} %get-tuple-element.512), channel_id=1, source_target_pairs={{1,0},{2,1},{3,2},{4,3},{5,4},{6,5},{7,6},{8,7},{9,8},{10,9},{11,1... | collective-permute-start | bytes 1572872 | tf_op jit(solution)/shard_map/while/body/eval_jaxpr/ppermute | solution.py:21
  159.7 14.3 %collective-permute-start.2 = (f32[2,128,4,128]{3,2,1,0:T(4,128)}, f32[2,128,4,128]{3,2,1,0:T(4,128)S(1)}, u32[]{:S(2)}, u32[]{:S(2)}) collective-permute-start(f32[2,128,4,128]{3,2,1,0:T(4,128)} %get-tuple-element.519), channel_id=1, source_target_pairs={{0,1},{1,2},{2,3},{3,4},{4,5},{5,6},{6,7},{7,8},{8,9},{9,10},{10,1... | collective-permute-start | bytes 1572872 | tf_op jit(solution)/shard_map/while/body/eval_jaxpr/ppermute | solution.py:20
  187.1 16.5 %collective-permute-start = (f32[2,128,4,128]{3,2,1,0:T(4,128)}, f32[2,128,4,128]{3,2,1,0:T(4,128)S(1)}, u32[]{:S(2)}, u32[]{:S(2)}) collective-permute-start(f32[2,128,4,128]{3,2,1,0:T(4,128)} %get-tuple-element.511), channel_id=1, source_target_pairs={{0,1},{1,2},{2,3},{3,4},{4,5},{5,6},{6,7},{7,8},{8,9},{9,10},{10,1... | collective-permute-start | bytes 1572872 | tf_op jit(solution)/shard_map/while/body/eval_jaxpr/ppermute | solution.py:20
  193.7 9.9 %collective-permute-start.1 = (f32[2,128,4,128]{3,2,1,0:T(4,128)}, f32[2,128,4,128]{3,2,1,0:T(4,128)S(1)}, u32[]{:S(2)}, u32[]{:S(2)}) collective-permute-start(f32[2,128,4,128]{3,2,1,0:T(4,128)} %get-tuple-element.512), channel_id=1, source_target_pairs={{1,0},{2,1},{3,2},{4,3},{5,4},{6,5},{7,6},{8,7},{9,8},{10,9},{11,1... | collective-permute-start | bytes 1572872 | tf_op jit(solution)/shard_map/while/body/eval_jaxpr/ppermute | solution.py:21
  214.2 14.3 %collective-permute-start.2 = (f32[2,128,4,128]{3,2,1,0:T(4,128)}, f32[2,128,4,128]{3,2,1,0:T(4,128)S(1)}, u32[]{:S(2)}, u32[]{:S(2)}) collective-permute-start(f32[2,128,4,128]{3,2,1,0:T(4,128)} %get-tuple-element.519), channel_id=1, source_target_pairs={{0,1},{1,2},{2,3},{3,4},{4,5},{5,6},{6,7},{7,8},{8,9},{9,10},{10,1... | collective-permute-start | bytes 1572872 | tf_op jit(solution)/shard_map/while/body/eval_jaxpr/ppermute | solution.py:20
  241.6 16.5 %collective-permute-start = (f32[2,128,4,128]{3,2,1,0:T(4,128)}, f32[2,128,4,128]{3,2,1,0:T(4,128)S(1)}, u32[]{:S(2)}, u32[]{:S(2)}) collective-permute-start(f32[2,128,4,128]{3,2,1,0:T(4,128)} %get-tuple-element.511), channel_id=1, source_target_pairs={{0,1},{1,2},{2,3},{3,4},{4,5},{5,6},{6,7},{7,8},{8,9},{9,10},{10,1... | collective-permute-start | bytes 1572872 | tf_op jit(solution)/shard_map/while/body/eval_jaxpr/ppermute | solution.py:20
  248.2 9.9 %collective-permute-start.1 = (f32[2,128,4,128]{3,2,1,0:T(4,128)}, f32[2,128,4,128]{3,2,1,0:T(4,128)S(1)}, u32[]{:S(2)}, u32[]{:S(2)}) collective-permute-start(f32[2,128,4,128]{3,2,1,0:T(4,128)} %get-tuple-element.512), channel_id=1, source_target_pairs={{1,0},{2,1},{3,2},{4,3},{5,4},{6,5},{7,6},{8,7},{9,8},{10,9},{11,1... | collective-permute-start | bytes 1572872 | tf_op jit(solution)/shard_map/while/body/eval_jaxpr/ppermute | solution.py:21
  268.8 14.3 %collective-permute-start.2 = (f32[2,128,4,128]{3,2,1,0:T(4,128)}, f32[2,128,4,128]{3,2,1,0:T(4,128)S(1)}, u32[]{:S(2)}, u32[]{:S(2)}) collective-permute-start(f32[2,128,4,128]{3,2,1,0:T(4,128)} %get-tuple-element.519), channel_id=1, source_target_pairs={{0,1},{1,2},{2,3},{3,4},{4,5},{5,6},{6,7},{7,8},{8,9},{9,10},{10,1... | collective-permute-start | bytes 1572872 | tf_op jit(solution)/shard_map/while/body/eval_jaxpr/ppermute | solution.py:20
  296.2 16.5 %collective-permute-start = (f32[2,128,4,128]{3,2,1,0:T(4,128)}, f32[2,128,4,128]{3,2,1,0:T(4,128)S(1)}, u32[]{:S(2)}, u32[]{:S(2)}) collective-permute-start(f32[2,128,4,128]{3,2,1,0:T(4,128)} %get-tuple-element.511), channel_id=1, source_target_pairs={{0,1},{1,2},{2,3},{3,4},{4,5},{5,6},{6,7},{7,8},{8,9},{9,10},{10,1... | collective-permute-start | bytes 1572872 | tf_op jit(solution)/shard_map/while/body/eval_jaxpr/ppermute | solution.py:20
  302.8 9.9 %collective-permute-start.1 = (f32[2,128,4,128]{3,2,1,0:T(4,128)}, f32[2,128,4,128]{3,2,1,0:T(4,128)S(1)}, u32[]{:S(2)}, u32[]{:S(2)}) collective-permute-start(f32[2,128,4,128]{3,2,1,0:T(4,128)} %get-tuple-element.512), channel_id=1, source_target_pairs={{1,0},{2,1},{3,2},{4,3},{5,4},{6,5},{7,6},{8,7},{9,8},{10,9},{11,1... | collective-permute-start | bytes 1572872 | tf_op jit(solution)/shard_map/while/body/eval_jaxpr/ppermute | solution.py:21
  323.3 14.3 %collective-permute-start.2 = (f32[2,128,4,128]{3,2,1,0:T(4,128)}, f32[2,128,4,128]{3,2,1,0:T(4,128)S(1)}, u32[]{:S(2)}, u32[]{:S(2)}) collective-permute-start(f32[2,128,4,128]{3,2,1,0:T(4,128)} %get-tuple-element.519), channel_id=1, source_target_pairs={{0,1},{1,2},{2,3},{3,4},{4,5},{5,6},{6,7},{7,8},{8,9},{9,10},{10,1... | collective-permute-start | bytes 1572872 | tf_op jit(solution)/shard_map/while/body/eval_jaxpr/ppermute | solution.py:20
  350.7 16.5 %collective-permute-start = (f32[2,128,4,128]{3,2,1,0:T(4,128)}, f32[2,128,4,128]{3,2,1,0:T(4,128)S(1)}, u32[]{:S(2)}, u32[]{:S(2)}) collective-permute-start(f32[2,128,4,128]{3,2,1,0:T(4,128)} %get-tuple-element.511), channel_id=1, source_target_pairs={{0,1},{1,2},{2,3},{3,4},{4,5},{5,6},{6,7},{7,8},{8,9},{9,10},{10,1... | collective-permute-start | bytes 1572872 | tf_op jit(solution)/shard_map/while/body/eval_jaxpr/ppermute | solution.py:20
  357.3 9.9 %collective-permute-start.1 = (f32[2,128,4,128]{3,2,1,0:T(4,128)}, f32[2,128,4,128]{3,2,1,0:T(4,128)S(1)}, u32[]{:S(2)}, u32[]{:S(2)}) collective-permute-start(f32[2,128,4,128]{3,2,1,0:T(4,128)} %get-tuple-element.512), channel_id=1, source_target_pairs={{1,0},{2,1},{3,2},{4,3},{5,4},{6,5},{7,6},{8,7},{9,8},{10,9},{11,1... | collective-permute-start | bytes 1572872 | tf_op jit(solution)/shard_map/while/body/eval_jaxpr/ppermute | solution.py:21
  377.9 14.3 %collective-permute-start.2 = (f32[2,128,4,128]{3,2,1,0:T(4,128)}, f32[2,128,4,128]{3,2,1,0:T(4,128)S(1)}, u32[]{:S(2)}, u32[]{:S(2)}) collective-permute-start(f32[2,128,4,128]{3,2,1,0:T(4,128)} %get-tuple-element.519), channel_id=1, source_target_pairs={{0,1},{1,2},{2,3},{3,4},{4,5},{5,6},{6,7},{7,8},{8,9},{9,10},{10,1... | collective-permute-start | bytes 1572872 | tf_op jit(solution)/shard_map/while/body/eval_jaxpr/ppermute | solution.py:20
  405.3 16.5 %collective-permute-start = (f32[2,128,4,128]{3,2,1,0:T(4,128)}, f32[2,128,4,128]{3,2,1,0:T(4,128)S(1)}, u32[]{:S(2)}, u32[]{:S(2)}) collective-permute-start(f32[2,128,4,128]{3,2,1,0:T(4,128)} %get-tuple-element.511), channel_id=1, source_target_pairs={{0,1},{1,2},{2,3},{3,4},{4,5},{5,6},{6,7},{7,8},{8,9},{9,10},{10,1... | collective-permute-start | bytes 1572872 | tf_op jit(solution)/shard_map/while/body/eval_jaxpr/ppermute | solution.py:20
  411.9 9.9 %collective-permute-start.1 = (f32[2,128,4,128]{3,2,1,0:T(4,128)}, f32[2,128,4,128]{3,2,1,0:T(4,128)S(1)}, u32[]{:S(2)}, u32[]{:S(2)}) collective-permute-start(f32[2,128,4,128]{3,2,1,0:T(4,128)} %get-tuple-element.512), channel_id=1, source_target_pairs={{1,0},{2,1},{3,2},{4,3},{5,4},{6,5},{7,6},{8,7},{9,8},{10,9},{11,1... | collective-permute-start | bytes 1572872 | tf_op jit(solution)/shard_map/while/body/eval_jaxpr/ppermute | solution.py:21
  432.4 14.3 %collective-permute-start.2 = (f32[2,128,4,128]{3,2,1,0:T(4,128)}, f32[2,128,4,128]{3,2,1,0:T(4,128)S(1)}, u32[]{:S(2)}, u32[]{:S(2)}) collective-permute-start(f32[2,128,4,128]{3,2,1,0:T(4,128)} %get-tuple-element.519), channel_id=1, source_target_pairs={{0,1},{1,2},{2,3},{3,4},{4,5},{5,6},{6,7},{7,8},{8,9},{9,10},{10,1... | collective-permute-start | bytes 1572872 | tf_op jit(solution)/shard_map/while/body/eval_jaxpr/ppermute | solution.py:20
  459.8 16.5 %collective-permute-start = (f32[2,128,4,128]{3,2,1,0:T(4,128)}, f32[2,128,4,128]{3,2,1,0:T(4,128)S(1)}, u32[]{:S(2)}, u32[]{:S(2)}) collective-permute-start(f32[2,128,4,128]{3,2,1,0:T(4,128)} %get-tuple-element.511), channel_id=1, source_target_pairs={{0,1},{1,2},{2,3},{3,4},{4,5},{5,6},{6,7},{7,8},{8,9},{9,10},{10,1... | collective-permute-start | bytes 1572872 | tf_op jit(solution)/shard_map/while/body/eval_jaxpr/ppermute | solution.py:20
  466.4 9.9 %collective-permute-start.1 = (f32[2,128,4,128]{3,2,1,0:T(4,128)}, f32[2,128,4,128]{3,2,1,0:T(4,128)S(1)}, u32[]{:S(2)}, u32[]{:S(2)}) collective-permute-start(f32[2,128,4,128]{3,2,1,0:T(4,128)} %get-tuple-element.512), channel_id=1, source_target_pairs={{1,0},{2,1},{3,2},{4,3},{5,4},{6,5},{7,6},{8,7},{9,8},{10,9},{11,1... | collective-permute-start | bytes 1572872 | tf_op jit(solution)/shard_map/while/body/eval_jaxpr/ppermute | solution.py:21
  487.0 14.3 %collective-permute-start.2 = (f32[2,128,4,128]{3,2,1,0:T(4,128)}, f32[2,128,4,128]{3,2,1,0:T(4,128)S(1)}, u32[]{:S(2)}, u32[]{:S(2)}) collective-permute-start(f32[2,128,4,128]{3,2,1,0:T(4,128)} %get-tuple-element.519), channel_id=1, source_target_pairs={{0,1},{1,2},{2,3},{3,4},{4,5},{5,6},{6,7},{7,8},{8,9},{9,10},{10,1... | collective-permute-start | bytes 1572872 | tf_op jit(solution)/shard_map/while/body/eval_jaxpr/ppermute | solution.py:20
  514.4 16.5 %collective-permute-start = (f32[2,128,4,128]{3,2,1,0:T(4,128)}, f32[2,128,4,128]{3,2,1,0:T(4,128)S(1)}, u32[]{:S(2)}, u32[]{:S(2)}) collective-permute-start(f32[2,128,4,128]{3,2,1,0:T(4,128)} %get-tuple-element.511), channel_id=1, source_target_pairs={{0,1},{1,2},{2,3},{3,4},{4,5},{5,6},{6,7},{7,8},{8,9},{9,10},{10,1... | collective-permute-start | bytes 1572872 | tf_op jit(solution)/shard_map/while/body/eval_jaxpr/ppermute | solution.py:20
  521.0 9.9 %collective-permute-start.1 = (f32[2,128,4,128]{3,2,1,0:T(4,128)}, f32[2,128,4,128]{3,2,1,0:T(4,128)S(1)}, u32[]{:S(2)}, u32[]{:S(2)}) collective-permute-start(f32[2,128,4,128]{3,2,1,0:T(4,128)} %get-tuple-element.512), channel_id=1, source_target_pairs={{1,0},{2,1},{3,2},{4,3},{5,4},{6,5},{7,6},{8,7},{9,8},{10,9},{11,1... | collective-permute-start | bytes 1572872 | tf_op jit(solution)/shard_map/while/body/eval_jaxpr/ppermute | solution.py:21
  541.5 14.2 %collective-permute-start.2 = (f32[2,128,4,128]{3,2,1,0:T(4,128)}, f32[2,128,4,128]{3,2,1,0:T(4,128)S(1)}, u32[]{:S(2)}, u32[]{:S(2)}) collective-permute-start(f32[2,128,4,128]{3,2,1,0:T(4,128)} %get-tuple-element.519), channel_id=1, source_target_pairs={{0,1},{1,2},{2,3},{3,4},{4,5},{5,6},{6,7},{7,8},{8,9},{9,10},{10,1... | collective-permute-start | bytes 1572872 | tf_op jit(solution)/shard_map/while/body/eval_jaxpr/ppermute | solution.py:20
  (37 other events, 167.6 us)

commit v3 on v2

--- a/solution.py
+++ b/solution.py
@@ -23,7 +23,7 @@
 
 
 def step_kernel(
-    cur_ref, prev_ref, s_ref, img_ref, xlo_ref, xhi_ref, inj_ref, out_ref, imgo_ref, ey_ref, hx_ref
+    moment_ref, cur_ref, prev_ref, s_ref, img_ref, xlo_ref, xhi_ref, inj_ref, out_ref, imgo_ref, ey_ref, hx_ref
 ):
     comps, block_y, block_x, depth_z = cur_ref.shape
     zeros_y = jnp.zeros((comps, HALO, block_x, depth_z), jnp.float32)
@@ -61,27 +61,46 @@
     lax.fori_loop(0, block_y, row, 0, unroll=2)
 
 
-def step_call(cur, prev, s, img, xlo, xhi, inj):
+def step_call(moment, cur, prev, s, img, xlo, xhi, planes):
     comps, block_y, block_x, depth_z = cur.shape
-    vmem = pl.BlockSpec(memory_space=pltpu.VMEM)
+
+    def whole(shape):
+        return pl.BlockSpec(shape, lambda i, k: (0,) * len(shape))
+
+    plane_spec = pl.BlockSpec(
+        (None, comps, block_y, block_x, depth_z), lambda i, k: (k[0], 0, 0, 0, 0)
+    )
+    grid_spec = pltpu.PrefetchScalarGridSpec(
+        num_scalar_prefetch=1,
+        grid=(1,),
+        in_specs=[
+            whole(cur.shape),
+            whole(prev.shape),
+            whole(s.shape),
+            whole(img.shape),
+            whole(xlo.shape),
+            whole(xhi.shape),
+            plane_spec,
+        ],
+        out_specs=(whole(cur.shape), whole(img.shape)),
+        scratch_shapes=[
+            pltpu.VMEM((comps, block_y + 2 * HALO, block_x, depth_z), jnp.float32),
+            pltpu.VMEM((2, comps, block_y, block_x, depth_z), jnp.float32),
+        ],
+    )
     return pl.pallas_call(
         step_kernel,
         out_shape=(
             jax.ShapeDtypeStruct(cur.shape, jnp.float32),
             jax.ShapeDtypeStruct(img.shape, jnp.float32),
         ),
-        in_specs=[vmem] * 7,
-        out_specs=(vmem, vmem),
-        scratch_shapes=[
-            pltpu.VMEM((comps, block_y + 2 * HALO, block_x, depth_z), jnp.float32),
-            pltpu.VMEM((2, comps, block_y, block_x, depth_z), jnp.float32),
-        ],
-        input_output_aliases={1: 0, 3: 1},
-        compiler_params=pltpu.CompilerParams(vmem_limit_bytes=48 * 1024 * 1024),
+        grid_spec=grid_spec,
+        input_output_aliases={2: 0, 4: 1},
+        compiler_params=pltpu.CompilerParams(vmem_limit_bytes=56 * 1024 * 1024),
         cost_estimate=pl.CostEstimate(
             flops=60 * cur.size, bytes_accessed=4 * 6 * cur.size, transcendentals=0
         ),
-    )(cur, prev, s, img, xlo, xhi, inj)
+    )(jnp.reshape(moment, (1,)).astype(jnp.int32), cur, prev, s, img, xlo, xhi, planes)
 
 
 def point_tables(cell_rows, x_start, cells_wide, depth_y):
@@ -99,10 +118,11 @@
 
 def spread_points(tables, amounts, depth_z):
     rows_y, places = tables
-    weighted = rows_y * amounts[:, None]
-    plane = jnp.einsum("ny,nc->yc", weighted, places, precision=lax.Precision.HIGHEST)
-    plane = plane.reshape(rows_y.shape[1], places.shape[1] // 4, 4)
-    return jnp.pad(plane, ((0, 0), (0, 0), (0, depth_z - 4)))
+    steps = amounts.shape[0]
+    weighted = places[:, None, :] * jnp.transpose(amounts)[:, :, None]
+    plane = jnp.einsum("ny,nsc->syc", rows_y, weighted, precision=lax.Precision.HIGHEST)
+    plane = plane.reshape(steps, rows_y.shape[1], places.shape[1] // 4, 4)
+    return jnp.pad(plane, ((0, 0), (0, 0), (0, 0), (0, depth_z - 4)))
 
 
 def shards(older_fields, fields_now, velocity, aperture, source_pos, wavelet, receiver_pos, traces):
@@ -122,17 +142,17 @@
     source_core = point_tables(source_pos, x_anchor, cells_x, depth_y)
     receiver_core = point_tables(receiver_pos, x_anchor, cells_x, depth_y)
 
+    planes = jnp.stack(
+        [
+            spread_points(source_core, wavelet, depth_z),
+            spread_points(receiver_core, traces, depth_z),
+        ],
+        axis=1,
+    )
+
     def advance(moment, previous, current, image_acc):
         low, high = with_halo(current, "dom", 2, HALO)
-        pulses = lax.dynamic_index_in_dim(wavelet, moment, 0, keepdims=False)
-        recorded = lax.dynamic_index_in_dim(traces, moment, 0, keepdims=False)
-        added = jnp.stack(
-            [
-                spread_points(source_core, pulses, depth_z),
-                spread_points(receiver_core, recorded, depth_z),
-            ]
-        )
-        return step_call(current, previous, speed_sq, image_acc, low, high, added)
+        return step_call(moment, current, previous, speed_sq, image_acc, low, high, planes)
 
     def pair(index, state_carry):
         previous, current, image_acc = state_carry

time: 594 us -> 591 us (level)
  local copies, waits for them, and re-layouts: 139 us -> 50.6 us
  starting transfers between devices: 148 us -> 230 us
  matrix products: 80.5 us -> 12.8 us
  waiting for transfers between devices: 14.2 us -> 68.7 us
  other arithmetic: 3.41 us -> 22.4 us
    ppermute x20, starting transfers between devices: 115 us -> 197 us  [with_halo(): low = lax.ppermute(tail, axis, [(i, (i + 1) % count) for i in range(ends)])]
    ppermute x20, waiting for transfers between devices: 0.05 us -> 68.6 us  [with_halo(): high = lax.ppermute(head, axis, [((i + 1) % count, i) for i in range(ends)])]
    dot_general x40 -> x2, matrix products: 79.8 us -> 12.1 us  [spread_points(): jnp.einsum('ny,nsc->syc', rows_y, weighted, precision=lax.Precision.HIGHEST)]
    reshape x40 -> x2, local copies, waits for them, and re-layouts: 41.4 us -> 10.9 us  [spread_points(): plane = plane.reshape(steps, rows_y.shape[1], places.shape[1] // 4, 4)]
    while x40 -> x0, local copies, waits for them, and re-layouts: 18.8 us -> none
    slice x20, local copies, waits for them, and re-layouts: 38.4 us -> 22.5 us  [with_halo(): head = lax.slice_in_dim(cells, 0, width, axis=dim)]
    another operation x20 -> x1, other arithmetic: 1.4 us -> 16.2 us  [shards(): jnp.stack([spread_points(source_core, wavelet, depth_z), spread_points(re...]
    all_to_all x1, waiting for transfers between devices: 14.1 us -> 0.01 us  [shards(): lax.all_to_all(chosen, 'dom', split_axis=1, concat_axis=0, tiled=True)]
  transfers between devices with their start and end apart: 41 -> 41, of which waited for: 1 -> 20; matrix products, arithmetic and copies ran while one was open for 27% -> 10% of each run, Pallas kernels for 0% -> 0%
where the time goes in v3:
time: 591 us; the launch traced here: 589 us
  starting transfers between devices  230 us (39%)
  Pallas kernels  178 us (30%)
  waiting for transfers between devices  68.7 us (12%)
  local copies, waits for them, and re-layouts  50.6 us (9%)
  blocking collectives  24.4 us (4%)
  other arithmetic  22.4 us (4%)
  matrix products  12.8 us (2%)
    ppermute x20, starting transfers between devices, with_halo(): low = lax.ppermute(tail, axis, [(i, (i + 1) % count) for i in range(ends)])  197 us
    pallas_call x20, Pallas kernels, step_call(): pl.pallas_call(step_kernel, out_shape=(jax.ShapeDtypeStruct(cur.shape, jn...  178 us
    ppermute x20, waiting for transfers between devices, with_halo(): high = lax.ppermute(head, axis, [((i + 1) % count, i) for i in range(ends)])  68.6 us
    ppermute x20, starting transfers between devices, with_halo(): high = lax.ppermute(head, axis, [((i + 1) % count, i) for i in range(ends)])  25.6 us
    all_to_all x1, blocking collectives, shards(): lax.all_to_all(outgoing, 'dom', split_axis=0, concat_axis=1, tiled=True)  24.4 us
    slice x20, local copies, waits for them, and re-layouts, with_halo(): head = lax.slice_in_dim(cells, 0, width, axis=dim)  22.5 us
    another operation x1, other arithmetic, shards(): jnp.stack([spread_points(source_core, wavelet, depth_z), spread_points(re...  16.2 us
    another operation x1, local copies, waits for them, and re-layouts, shards(): jnp.stack([spread_points(source_core, wavelet, depth_z), spread_points(re...  15.5 us
  transfers between devices with their start and end apart: 41, of which 20 were waited for; matrix products, arithmetic and copies ran while one was open for 10% of the time, Pallas kernels for 0%

profile of v3, /device:TPU:0, one launch (start us, length us, event | category | flops | bytes accessed | tf_op | source)
XLA Modules:
  0.0 588.6 jit_solution(16117598724649417387)
XLA Ops:
  14.8 11.6 %fusion = f32[20,32,128]{2,1,0:T(8,128)S(1)} fusion(f32[8192,20]{0,1:T(8,128)} %bitcast.67, f32[8192,32]{0,1:T(8,128)S(1)} %fusion.8, s32[8192]{0:T(1024)S(1)} %bitcast.65), kind=kOutput, calls=%fused_computation.2 | convolution fusion | flops 8059355136 | bytes 2064384 | tf_op jit(solution)/shard_map/ny,nsc->syc/dot_general | solution.py:123
  38.0 15.5 %pad_bitcast_fusion = (f32[20,1,128,8,128]{4,3,2,1,0:T(8,128)}, f32[20,1,128,8,128]{4,3,2,1,0:T(8,128)}) fusion(f32[20,128,8,4]{3,2,1,0:T(8,128)} %copy.25, f32[20,128,8,4]{3,2,1,0:T(8,128)} %copy.24), kind=kLoop, calls=%fused_computation.4 | loop fusion | bytes 21626880 | tf_op jit(solution)/shard_map/stack | solution.py:145
  53.5 16.2 %pad_maximum_fusion = f32[20,2,128,8,128]{4,3,2,1,0:T(8,128)} fusion(f32[20,1,128,8,128]{4,3,2,1,0:T(8,128)} %get-tuple-element.134, f32[20,1,128,8,128]{4,3,2,1,0:T(8,128)} %get-tuple-element.135), kind=kLoop, calls=%fused_computation.1 | loop fusion | flops 5242880 | bytes 41943040 | tf_op jit(solution)/shard_map/stack | solution.py:145
  69.8 492.6 %while.17 = (s32[]{:T(128)}, f32[2,128,8,128]{3,2,1,0:T(8,128)S(1)}, f32[2,128,8,128]{3,2,1,0:T(8,128)S(1)}, f32[128,8,128]{2,1,0:T(8,128)S(1)}, f32[128,8,128]{...) while((s32[]{:T(128)}, f32[2,128,8,128]{3,2,1,0:T(8,128)S(1)}, ...), condition=%wide.region_1.2_spmd, body=%wide.region_0.1_spmd.sunk | while | flops 31457284 | bytes 25166092 | solution.py:163
  78.5 8.9 %eval_jaxpr.10 = (f32[2,128,8,128]{3,2,1,0:T(8,128)S(1)}, f32[128,8,128]{2,1,0:T(8,128)S(1)}) custom-call(s32[1]{0:T(128)} %bitcast.56.moment_ref, f32[2,128,8,128]{3,2,1,0:T(8,128)S(1)} %get-tuple-element.199.cur_ref.prev_ref, f32[2,128,8,128]{3,2,1,0:T(8,128)S(1)} %get-tuple-element.198.prev_ref, ...), custom_call_target="tpu_custom_call", output_to_operand_aliasing={{0}: (2, {}), {1}: (4, {})} | custom-call | flops 15728640 | bytes 6291456 | tf_op jit(solution)/shard_map/while/body/eval_jaxpr/pallas_call | solution.py:91
  88.5 11.1 %collective-permute-start.2 = (f32[2,128,4,128]{3,2,1,0:T(4,128)}, f32[2,128,4,128]{3,2,1,0:T(4,128)}, u32[]{:S(2)}, u32[]{:S(2)}) collective-permute-start(f32[2,128,4,128]{3,2,1,0:T(4,128)} %get-tuple-element.185), channel_id=1, source_target_pairs={{0,1},{1,2},{2,3},{3,4},{4,5},{5,6},{6,7},{7,8},{8,9},{9,10},{10,1... | collective-permute-start | bytes 1572872 | tf_op jit(solution)/shard_map/while/body/eval_jaxpr/ppermute | solution.py:20
  105.0 8.9 %eval_jaxpr.11 = (f32[2,128,8,128]{3,2,1,0:T(8,128)S(1)}, f32[128,8,128]{2,1,0:T(8,128)S(1)}) custom-call(s32[1]{0:T(128)} %bitcast.57.moment_ref, f32[2,128,8,128]{3,2,1,0:T(8,128)S(1)} %get-tuple-element.206.cur_ref, f32[2,128,8,128]{3,2,1,0:T(8,128)S(1)} %get-tuple-element.199.cur_ref.prev_ref, ...), custom_call_target="tpu_custom_call", output_to_operand_aliasing={{0}: (2, {}), {1}: (4, {})} | custom-call | flops 15728640 | bytes 6291456 | tf_op jit(solution)/shard_map/while/body/eval_jaxpr/pallas_call | solution.py:91
  115.0 11.1 %collective-permute-start = (f32[2,128,4,128]{3,2,1,0:T(4,128)}, f32[2,128,4,128]{3,2,1,0:T(4,128)}, u32[]{:S(2)}, u32[]{:S(2)}) collective-permute-start(f32[2,128,4,128]{3,2,1,0:T(4,128)} %get-tuple-element.181), channel_id=1, source_target_pairs={{0,1},{1,2},{2,3},{3,4},{4,5},{5,6},{6,7},{7,8},{8,9},{9,10},{10,1... | collective-permute-start | bytes 1572872 | tf_op jit(solution)/shard_map/while/body/eval_jaxpr/ppermute | solution.py:20
  131.4 8.9 %eval_jaxpr.10 = (f32[2,128,8,128]{3,2,1,0:T(8,128)S(1)}, f32[128,8,128]{2,1,0:T(8,128)S(1)}) custom-call(s32[1]{0:T(128)} %bitcast.56.moment_ref, f32[2,128,8,128]{3,2,1,0:T(8,128)S(1)} %get-tuple-element.199.cur_ref.prev_ref, f32[2,128,8,128]{3,2,1,0:T(8,128)S(1)} %get-tuple-element.198.prev_ref, ...), custom_call_target="tpu_custom_call", output_to_operand_aliasing={{0}: (2, {}), {1}: (4, {})} | custom-call | flops 15728640 | bytes 6291456 | tf_op jit(solution)/shard_map/while/body/eval_jaxpr/pallas_call | solution.py:91
  141.5 11.1 %collective-permute-start.2 = (f32[2,128,4,128]{3,2,1,0:T(4,128)}, f32[2,128,4,128]{3,2,1,0:T(4,128)}, u32[]{:S(2)}, u32[]{:S(2)}) collective-permute-start(f32[2,128,4,128]{3,2,1,0:T(4,128)} %get-tuple-element.185), channel_id=1, source_target_pairs={{0,1},{1,2},{2,3},{3,4},{4,5},{5,6},{6,7},{7,8},{8,9},{9,10},{10,1... | collective-permute-start | bytes 1572872 | tf_op jit(solution)/shard_map/while/body/eval_jaxpr/ppermute | solution.py:20
  157.9 8.9 %eval_jaxpr.11 = (f32[2,128,8,128]{3,2,1,0:T(8,128)S(1)}, f32[128,8,128]{2,1,0:T(8,128)S(1)}) custom-call(s32[1]{0:T(128)} %bitcast.57.moment_ref, f32[2,128,8,128]{3,2,1,0:T(8,128)S(1)} %get-tuple-element.206.cur_ref, f32[2,128,8,128]{3,2,1,0:T(8,128)S(1)} %get-tuple-element.199.cur_ref.prev_ref, ...), custom_call_target="tpu_custom_call", output_to_operand_aliasing={{0}: (2, {}), {1}: (4, {})} | custom-call | flops 15728640 | bytes 6291456 | tf_op jit(solution)/shard_map/while/body/eval_jaxpr/pallas_call | solution.py:91
  167.9 11.1 %collective-permute-start = (f32[2,128,4,128]{3,2,1,0:T(4,128)}, f32[2,128,4,128]{3,2,1,0:T(4,128)}, u32[]{:S(2)}, u32[]{:S(2)}) collective-permute-start(f32[2,128,4,128]{3,2,1,0:T(4,128)} %get-tuple-element.181), channel_id=1, source_target_pairs={{0,1},{1,2},{2,3},{3,4},{4,5},{5,6},{6,7},{7,8},{8,9},{9,10},{10,1... | collective-permute-start | bytes 1572872 | tf_op jit(solution)/shard_map/while/body/eval_jaxpr/ppermute | solution.py:20
  184.4 8.9 %eval_jaxpr.10 = (f32[2,128,8,128]{3,2,1,0:T(8,128)S(1)}, f32[128,8,128]{2,1,0:T(8,128)S(1)}) custom-call(s32[1]{0:T(128)} %bitcast.56.moment_ref, f32[2,128,8,128]{3,2,1,0:T(8,128)S(1)} %get-tuple-element.199.cur_ref.prev_ref, f32[2,128,8,128]{3,2,1,0:T(8,128)S(1)} %get-tuple-element.198.prev_ref, ...), custom_call_target="tpu_custom_call", output_to_operand_aliasing={{0}: (2, {}), {1}: (4, {})} | custom-call | flops 15728640 | bytes 6291456 | tf_op jit(solution)/shard_map/while/body/eval_jaxpr/pallas_call | solution.py:91
  194.4 11.1 %collective-permute-start.2 = (f32[2,128,4,128]{3,2,1,0:T(4,128)}, f32[2,128,4,128]{3,2,1,0:T(4,128)}, u32[]{:S(2)}, u32[]{:S(2)}) collective-permute-start(f32[2,128,4,128]{3,2,1,0:T(4,128)} %get-tuple-element.185), channel_id=1, source_target_pairs={{0,1},{1,2},{2,3},{3,4},{4,5},{5,6},{6,7},{7,8},{8,9},{9,10},{10,1... | collective-permute-start | bytes 1572872 | tf_op jit(solution)/shard_map/while/body/eval_jaxpr/ppermute | solution.py:20
  220.9 11.1 %collective-permute-start = (f32[2,128,4,128]{3,2,1,0:T(4,128)}, f32[2,128,4,128]{3,2,1,0:T(4,128)}, u32[]{:S(2)}, u32[]{:S(2)}) collective-permute-start(f32[2,128,4,128]{3,2,1,0:T(4,128)} %get-tuple-element.181), channel_id=1, source_target_pairs={{0,1},{1,2},{2,3},{3,4},{4,5},{5,6},{6,7},{7,8},{8,9},{9,10},{10,1... | collective-permute-start | bytes 1572872 | tf_op jit(solution)/shard_map/while/body/eval_jaxpr/ppermute | solution.py:20
  247.3 10.7 %collective-permute-start.2 = (f32[2,128,4,128]{3,2,1,0:T(4,128)}, f32[2,128,4,128]{3,2,1,0:T(4,128)}, u32[]{:S(2)}, u32[]{:S(2)}) collective-permute-start(f32[2,128,4,128]{3,2,1,0:T(4,128)} %get-tuple-element.185), channel_id=1, source_target_pairs={{0,1},{1,2},{2,3},{3,4},{4,5},{5,6},{6,7},{7,8},{8,9},{9,10},{10,1... | collective-permute-start | bytes 1572872 | tf_op jit(solution)/shard_map/while/body/eval_jaxpr/ppermute | solution.py:20
  273.4 9.9 %collective-permute-start = (f32[2,128,4,128]{3,2,1,0:T(4,128)}, f32[2,128,4,128]{3,2,1,0:T(4,128)}, u32[]{:S(2)}, u32[]{:S(2)}) collective-permute-start(f32[2,128,4,128]{3,2,1,0:T(4,128)} %get-tuple-element.181), channel_id=1, source_target_pairs={{0,1},{1,2},{2,3},{3,4},{4,5},{5,6},{6,7},{7,8},{8,9},{9,10},{10,1... | collective-permute-start | bytes 1572872 | tf_op jit(solution)/shard_map/while/body/eval_jaxpr/ppermute | solution.py:20
  297.9 9.9 %collective-permute-start.2 = (f32[2,128,4,128]{3,2,1,0:T(4,128)}, f32[2,128,4,128]{3,2,1,0:T(4,128)}, u32[]{:S(2)}, u32[]{:S(2)}) collective-permute-start(f32[2,128,4,128]{3,2,1,0:T(4,128)} %get-tuple-element.185), channel_id=1, source_target_pairs={{0,1},{1,2},{2,3},{3,4},{4,5},{5,6},{6,7},{7,8},{8,9},{9,10},{10,1... | collective-permute-start | bytes 1572872 | tf_op jit(solution)/shard_map/while/body/eval_jaxpr/ppermute | solution.py:20
  322.0 9.6 %collective-permute-start = (f32[2,128,4,128]{3,2,1,0:T(4,128)}, f32[2,128,4,128]{3,2,1,0:T(4,128)}, u32[]{:S(2)}, u32[]{:S(2)}) collective-permute-start(f32[2,128,4,128]{3,2,1,0:T(4,128)} %get-tuple-element.181), channel_id=1, source_target_pairs={{0,1},{1,2},{2,3},{3,4},{4,5},{5,6},{6,7},{7,8},{8,9},{9,10},{10,1... | collective-permute-start | bytes 1572872 | tf_op jit(solution)/shard_map/while/body/eval_jaxpr/ppermute | solution.py:20
  346.3 9.9 %collective-permute-start.2 = (f32[2,128,4,128]{3,2,1,0:T(4,128)}, f32[2,128,4,128]{3,2,1,0:T(4,128)}, u32[]{:S(2)}, u32[]{:S(2)}) collective-permute-start(f32[2,128,4,128]{3,2,1,0:T(4,128)} %get-tuple-element.185), channel_id=1, source_target_pairs={{0,1},{1,2},{2,3},{3,4},{4,5},{5,6},{6,7},{7,8},{8,9},{9,10},{10,1... | collective-permute-start | bytes 1572872 | tf_op jit(solution)/shard_map/while/body/eval_jaxpr/ppermute | solution.py:20
  370.3 9.6 %collective-permute-start = (f32[2,128,4,128]{3,2,1,0:T(4,128)}, f32[2,128,4,128]{3,2,1,0:T(4,128)}, u32[]{:S(2)}, u32[]{:S(2)}) collective-permute-start(f32[2,128,4,128]{3,2,1,0:T(4,128)} %get-tuple-element.181), channel_id=1, source_target_pairs={{0,1},{1,2},{2,3},{3,4},{4,5},{5,6},{6,7},{7,8},{8,9},{9,10},{10,1... | collective-permute-start | bytes 1572872 | tf_op jit(solution)/shard_map/while/body/eval_jaxpr/ppermute | solution.py:20
  384.6 8.9 %eval_jaxpr.10 = (f32[2,128,8,128]{3,2,1,0:T(8,128)S(1)}, f32[128,8,128]{2,1,0:T(8,128)S(1)}) custom-call(s32[1]{0:T(128)} %bitcast.56.moment_ref, f32[2,128,8,128]{3,2,1,0:T(8,128)S(1)} %get-tuple-element.199.cur_ref.prev_ref, f32[2,128,8,128]{3,2,1,0:T(8,128)S(1)} %get-tuple-element.198.prev_ref, ...), custom_call_target="tpu_custom_call", output_to_operand_aliasing={{0}: (2, {}), {1}: (4, {})} | custom-call | flops 15728640 | bytes 6291456 | tf_op jit(solution)/shard_map/while/body/eval_jaxpr/pallas_call | solution.py:91
  394.6 9.9 %collective-permute-start.2 = (f32[2,128,4,128]{3,2,1,0:T(4,128)}, f32[2,128,4,128]{3,2,1,0:T(4,128)}, u32[]{:S(2)}, u32[]{:S(2)}) collective-permute-start(f32[2,128,4,128]{3,2,1,0:T(4,128)} %get-tuple-element.185), channel_id=1, source_target_pairs={{0,1},{1,2},{2,3},{3,4},{4,5},{5,6},{6,7},{7,8},{8,9},{9,10},{10,1... | collective-permute-start | bytes 1572872 | tf_op jit(solution)/shard_map/while/body/eval_jaxpr/ppermute | solution.py:20
  408.6 8.9 %eval_jaxpr.11 = (f32[2,128,8,128]{3,2,1,0:T(8,128)S(1)}, f32[128,8,128]{2,1,0:T(8,128)S(1)}) custom-call(s32[1]{0:T(128)} %bitcast.57.moment_ref, f32[2,128,8,128]{3,2,1,0:T(8,128)S(1)} %get-tuple-element.206.cur_ref, f32[2,128,8,128]{3,2,1,0:T(8,128)S(1)} %get-tuple-element.199.cur_ref.prev_ref, ...), custom_call_target="tpu_custom_call", output_to_operand_aliasing={{0}: (2, {}), {1}: (4, {})} | custom-call | flops 15728640 | bytes 6291456 | tf_op jit(solution)/shard_map/while/body/eval_jaxpr/pallas_call | solution.py:91
  418.6 9.6 %collective-permute-start = (f32[2,128,4,128]{3,2,1,0:T(4,128)}, f32[2,128,4,128]{3,2,1,0:T(4,128)}, u32[]{:S(2)}, u32[]{:S(2)}) collective-permute-start(f32[2,128,4,128]{3,2,1,0:T(4,128)} %get-tuple-element.181), channel_id=1, source_target_pairs={{0,1},{1,2},{2,3},{3,4},{4,5},{5,6},{6,7},{7,8},{8,9},{9,10},{10,1... | collective-permute-start | bytes 1572872 | tf_op jit(solution)/shard_map/while/body/eval_jaxpr/ppermute | solution.py:20
  442.9 9.9 %collective-permute-start.2 = (f32[2,128,4,128]{3,2,1,0:T(4,128)}, f32[2,128,4,128]{3,2,1,0:T(4,128)}, u32[]{:S(2)}, u32[]{:S(2)}) collective-permute-start(f32[2,128,4,128]{3,2,1,0:T(4,128)} %get-tuple-element.185), channel_id=1, source_target_pairs={{0,1},{1,2},{2,3},{3,4},{4,5},{5,6},{6,7},{7,8},{8,9},{9,10},{10,1... | collective-permute-start | bytes 1572872 | tf_op jit(solution)/shard_map/while/body/eval_jaxpr/ppermute | solution.py:20
  466.9 9.6 %collective-permute-start = (f32[2,128,4,128]{3,2,1,0:T(4,128)}, f32[2,128,4,128]{3,2,1,0:T(4,128)}, u32[]{:S(2)}, u32[]{:S(2)}) collective-permute-start(f32[2,128,4,128]{3,2,1,0:T(4,128)} %get-tuple-element.181), channel_id=1, source_target_pairs={{0,1},{1,2},{2,3},{3,4},{4,5},{5,6},{6,7},{7,8},{8,9},{9,10},{10,1... | collective-permute-start | bytes 1572872 | tf_op jit(solution)/shard_map/while/body/eval_jaxpr/ppermute | solution.py:20
  491.2 9.9 %collective-permute-start.2 = (f32[2,128,4,128]{3,2,1,0:T(4,128)}, f32[2,128,4,128]{3,2,1,0:T(4,128)}, u32[]{:S(2)}, u32[]{:S(2)}) collective-permute-start(f32[2,128,4,128]{3,2,1,0:T(4,128)} %get-tuple-element.185), channel_id=1, source_target_pairs={{0,1},{1,2},{2,3},{3,4},{4,5},{5,6},{6,7},{7,8},{8,9},{9,10},{10,1... | collective-permute-start | bytes 1572872 | tf_op jit(solution)/shard_map/while/body/eval_jaxpr/ppermute | solution.py:20
  515.3 9.6 %collective-permute-start = (f32[2,128,4,128]{3,2,1,0:T(4,128)}, f32[2,128,4,128]{3,2,1,0:T(4,128)}, u32[]{:S(2)}, u32[]{:S(2)}) collective-permute-start(f32[2,128,4,128]{3,2,1,0:T(4,128)} %get-tuple-element.181), channel_id=1, source_target_pairs={{0,1},{1,2},{2,3},{3,4},{4,5},{5,6},{6,7},{7,8},{8,9},{9,10},{10,1... | collective-permute-start | bytes 1572872 | tf_op jit(solution)/shard_map/while/body/eval_jaxpr/ppermute | solution.py:20
  529.5 8.9 %eval_jaxpr.10 = (f32[2,128,8,128]{3,2,1,0:T(8,128)S(1)}, f32[128,8,128]{2,1,0:T(8,128)S(1)}) custom-call(s32[1]{0:T(128)} %bitcast.56.moment_ref, f32[2,128,8,128]{3,2,1,0:T(8,128)S(1)} %get-tuple-element.199.cur_ref.prev_ref, f32[2,128,8,128]{3,2,1,0:T(8,128)S(1)} %get-tuple-element.198.prev_ref, ...), custom_call_target="tpu_custom_call", output_to_operand_aliasing={{0}: (2, {}), {1}: (4, {})} | custom-call | flops 15728640 | bytes 6291456 | tf_op jit(solution)/shard_map/while/body/eval_jaxpr/pallas_call | solution.py:91
  539.5 9.9 %collective-permute-start.2 = (f32[2,128,4,128]{3,2,1,0:T(4,128)}, f32[2,128,4,128]{3,2,1,0:T(4,128)}, u32[]{:S(2)}, u32[]{:S(2)}) collective-permute-start(f32[2,128,4,128]{3,2,1,0:T(4,128)} %get-tuple-element.185), channel_id=1, source_target_pairs={{0,1},{1,2},{2,3},{3,4},{4,5},{5,6},{6,7},{7,8},{8,9},{9,10},{10,1... | collective-permute-start | bytes 1572872 | tf_op jit(solution)/shard_map/while/body/eval_jaxpr/ppermute | solution.py:20
  562.5 24.4 %all_to_all.27 = f32[128,1,8,128]{3,2,1,0:T(8,128)S(1)} all-to-all(f32[128,1,8,128]{3,2,1,0:T(8,128)S(1)} %multiply_bitcast_fusion), channel_id=1, replica_groups=mesh['survey'=2,'dom'=16] {'dom'}, dimensions={0} | all-to-all | bytes 1048576 | tf_op jit(solution)/shard_map/all_to_all | solution.py:174
  (131 shorter events, 254.2 us)
Async XLA Ops:
  3.6 66.1 %all-to-all-start = ((f32[8,16,8,128]{3,2,0,1:T(8,128)}), f32[8,16,8,128]{3,2,0,1:T(8,128)S(1)}, u32[]{:S(2)}, u32[]{:S(2)}) async-start(f32[8,16,8,128]{3,2,0,1:T(8,128)} %select_bitcast_fusion), calls=%async_computation | async-start | bytes 1048576 | tf_op jit(solution)/shard_map/all_to_all | solution.py:138
  88.5 12.4 %collective-permute-start.2 = (f32[2,128,4,128]{3,2,1,0:T(4,128)}, f32[2,128,4,128]{3,2,1,0:T(4,128)}, u32[]{:S(2)}, u32[]{:S(2)}) collective-permute-start(f32[2,128,4,128]{3,2,1,0:T(4,128)} %get-tuple-element.185), channel_id=1, source_target_pairs={{0,1},{1,2},{2,3},{3,4},{4,5},{5,6},{6,7},{7,8},{8,9},{9,10},{10,1... | collective-permute-start | bytes 1572872 | tf_op jit(solution)/shard_map/while/body/eval_jaxpr/ppermute | solution.py:20
  99.6 5.3 collective-permute-start.3
  115.0 12.4 %collective-permute-start = (f32[2,128,4,128]{3,2,1,0:T(4,128)}, f32[2,128,4,128]{3,2,1,0:T(4,128)}, u32[]{:S(2)}, u32[]{:S(2)}) collective-permute-start(f32[2,128,4,128]{3,2,1,0:T(4,128)} %get-tuple-element.181), channel_id=1, source_target_pairs={{0,1},{1,2},{2,3},{3,4},{4,5},{5,6},{6,7},{7,8},{8,9},{9,10},{10,1... | collective-permute-start | bytes 1572872 | tf_op jit(solution)/shard_map/while/body/eval_jaxpr/ppermute | solution.py:20
  126.1 5.3 collective-permute-start.1
  141.5 12.4 %collective-permute-start.2 = (f32[2,128,4,128]{3,2,1,0:T(4,128)}, f32[2,128,4,128]{3,2,1,0:T(4,128)}, u32[]{:S(2)}, u32[]{:S(2)}) collective-permute-start(f32[2,128,4,128]{3,2,1,0:T(4,128)} %get-tuple-element.185), channel_id=1, source_target_pairs={{0,1},{1,2},{2,3},{3,4},{4,5},{5,6},{6,7},{7,8},{8,9},{9,10},{10,1... | collective-permute-start | bytes 1572872 | tf_op jit(solution)/shard_map/while/body/eval_jaxpr/ppermute | solution.py:20
  152.6 5.3 collective-permute-start.3
  167.9 12.4 %collective-permute-start = (f32[2,128,4,128]{3,2,1,0:T(4,128)}, f32[2,128,4,128]{3,2,1,0:T(4,128)}, u32[]{:S(2)}, u32[]{:S(2)}) collective-permute-start(f32[2,128,4,128]{3,2,1,0:T(4,128)} %get-tuple-element.181), channel_id=1, source_target_pairs={{0,1},{1,2},{2,3},{3,4},{4,5},{5,6},{6,7},{7,8},{8,9},{9,10},{10,1... | collective-permute-start | bytes 1572872 | tf_op jit(solution)/shard_map/while/body/eval_jaxpr/ppermute | solution.py:20
  179.0 5.3 collective-permute-start.1
  194.4 12.4 %collective-permute-start.2 = (f32[2,128,4,128]{3,2,1,0:T(4,128)}, f32[2,128,4,128]{3,2,1,0:T(4,128)}, u32[]{:S(2)}, u32[]{:S(2)}) collective-permute-start(f32[2,128,4,128]{3,2,1,0:T(4,128)} %get-tuple-element.185), channel_id=1, source_target_pairs={{0,1},{1,2},{2,3},{3,4},{4,5},{5,6},{6,7},{7,8},{8,9},{9,10},{10,1... | collective-permute-start | bytes 1572872 | tf_op jit(solution)/shard_map/while/body/eval_jaxpr/ppermute | solution.py:20
  205.5 5.3 collective-permute-start.3
  220.9 12.4 %collective-permute-start = (f32[2,128,4,128]{3,2,1,0:T(4,128)}, f32[2,128,4,128]{3,2,1,0:T(4,128)}, u32[]{:S(2)}, u32[]{:S(2)}) collective-permute-start(f32[2,128,4,128]{3,2,1,0:T(4,128)} %get-tuple-element.181), channel_id=1, source_target_pairs={{0,1},{1,2},{2,3},{3,4},{4,5},{5,6},{6,7},{7,8},{8,9},{9,10},{10,1... | collective-permute-start | bytes 1572872 | tf_op jit(solution)/shard_map/while/body/eval_jaxpr/ppermute | solution.py:20
  232.0 5.3 collective-permute-start.1
  247.3 12.0 %collective-permute-start.2 = (f32[2,128,4,128]{3,2,1,0:T(4,128)}, f32[2,128,4,128]{3,2,1,0:T(4,128)}, u32[]{:S(2)}, u32[]{:S(2)}) collective-permute-start(f32[2,128,4,128]{3,2,1,0:T(4,128)} %get-tuple-element.185), channel_id=1, source_target_pairs={{0,1},{1,2},{2,3},{3,4},{4,5},{5,6},{6,7},{7,8},{8,9},{9,10},{10,1... | collective-permute-start | bytes 1572872 | tf_op jit(solution)/shard_map/while/body/eval_jaxpr/ppermute | solution.py:20
  258.0 5.3 collective-permute-start.3
  273.4 11.1 %collective-permute-start = (f32[2,128,4,128]{3,2,1,0:T(4,128)}, f32[2,128,4,128]{3,2,1,0:T(4,128)}, u32[]{:S(2)}, u32[]{:S(2)}) collective-permute-start(f32[2,128,4,128]{3,2,1,0:T(4,128)} %get-tuple-element.181), channel_id=1, source_target_pairs={{0,1},{1,2},{2,3},{3,4},{4,5},{5,6},{6,7},{7,8},{8,9},{9,10},{10,1... | collective-permute-start | bytes 1572872 | tf_op jit(solution)/shard_map/while/body/eval_jaxpr/ppermute | solution.py:20
  283.3 4.7 collective-permute-start.1
  297.9 11.2 %collective-permute-start.2 = (f32[2,128,4,128]{3,2,1,0:T(4,128)}, f32[2,128,4,128]{3,2,1,0:T(4,128)}, u32[]{:S(2)}, u32[]{:S(2)}) collective-permute-start(f32[2,128,4,128]{3,2,1,0:T(4,128)} %get-tuple-element.185), channel_id=1, source_target_pairs={{0,1},{1,2},{2,3},{3,4},{4,5},{5,6},{6,7},{7,8},{8,9},{9,10},{10,1... | collective-permute-start | bytes 1572872 | tf_op jit(solution)/shard_map/while/body/eval_jaxpr/ppermute | solution.py:20
  322.0 10.9 %collective-permute-start = (f32[2,128,4,128]{3,2,1,0:T(4,128)}, f32[2,128,4,128]{3,2,1,0:T(4,128)}, u32[]{:S(2)}, u32[]{:S(2)}) collective-permute-start(f32[2,128,4,128]{3,2,1,0:T(4,128)} %get-tuple-element.181), channel_id=1, source_target_pairs={{0,1},{1,2},{2,3},{3,4},{4,5},{5,6},{6,7},{7,8},{8,9},{9,10},{10,1... | collective-permute-start | bytes 1572872 | tf_op jit(solution)/shard_map/while/body/eval_jaxpr/ppermute | solution.py:20
  331.6 4.7 collective-permute-start.1
  346.3 11.2 %collective-permute-start.2 = (f32[2,128,4,128]{3,2,1,0:T(4,128)}, f32[2,128,4,128]{3,2,1,0:T(4,128)}, u32[]{:S(2)}, u32[]{:S(2)}) collective-permute-start(f32[2,128,4,128]{3,2,1,0:T(4,128)} %get-tuple-element.185), channel_id=1, source_target_pairs={{0,1},{1,2},{2,3},{3,4},{4,5},{5,6},{6,7},{7,8},{8,9},{9,10},{10,1... | collective-permute-start | bytes 1572872 | tf_op jit(solution)/shard_map/while/body/eval_jaxpr/ppermute | solution.py:20
  370.3 10.9 %collective-permute-start = (f32[2,128,4,128]{3,2,1,0:T(4,128)}, f32[2,128,4,128]{3,2,1,0:T(4,128)}, u32[]{:S(2)}, u32[]{:S(2)}) collective-permute-start(f32[2,128,4,128]{3,2,1,0:T(4,128)} %get-tuple-element.181), channel_id=1, source_target_pairs={{0,1},{1,2},{2,3},{3,4},{4,5},{5,6},{6,7},{7,8},{8,9},{9,10},{10,1... | collective-permute-start | bytes 1572872 | tf_op jit(solution)/shard_map/while/body/eval_jaxpr/ppermute | solution.py:20
  379.9 4.7 collective-permute-start.1
  394.6 11.2 %collective-permute-start.2 = (f32[2,128,4,128]{3,2,1,0:T(4,128)}, f32[2,128,4,128]{3,2,1,0:T(4,128)}, u32[]{:S(2)}, u32[]{:S(2)}) collective-permute-start(f32[2,128,4,128]{3,2,1,0:T(4,128)} %get-tuple-element.185), channel_id=1, source_target_pairs={{0,1},{1,2},{2,3},{3,4},{4,5},{5,6},{6,7},{7,8},{8,9},{9,10},{10,1... | collective-permute-start | bytes 1572872 | tf_op jit(solution)/shard_map/while/body/eval_jaxpr/ppermute | solution.py:20
  418.6 10.9 %collective-permute-start = (f32[2,128,4,128]{3,2,1,0:T(4,128)}, f32[2,128,4,128]{3,2,1,0:T(4,128)}, u32[]{:S(2)}, u32[]{:S(2)}) collective-permute-start(f32[2,128,4,128]{3,2,1,0:T(4,128)} %get-tuple-element.181), channel_id=1, source_target_pairs={{0,1},{1,2},{2,3},{3,4},{4,5},{5,6},{6,7},{7,8},{8,9},{9,10},{10,1... | collective-permute-start | bytes 1572872 | tf_op jit(solution)/shard_map/while/body/eval_jaxpr/ppermute | solution.py:20
  442.9 11.2 %collective-permute-start.2 = (f32[2,128,4,128]{3,2,1,0:T(4,128)}, f32[2,128,4,128]{3,2,1,0:T(4,128)}, u32[]{:S(2)}, u32[]{:S(2)}) collective-permute-start(f32[2,128,4,128]{3,2,1,0:T(4,128)} %get-tuple-element.185), channel_id=1, source_target_pairs={{0,1},{1,2},{2,3},{3,4},{4,5},{5,6},{6,7},{7,8},{8,9},{9,10},{10,1... | collective-permute-start | bytes 1572872 | tf_op jit(solution)/shard_map/while/body/eval_jaxpr/ppermute | solution.py:20
  466.9 10.9 %collective-permute-start = (f32[2,128,4,128]{3,2,1,0:T(4,128)}, f32[2,128,4,128]{3,2,1,0:T(4,128)}, u32[]{:S(2)}, u32[]{:S(2)}) collective-permute-start(f32[2,128,4,128]{3,2,1,0:T(4,128)} %get-tuple-element.181), channel_id=1, source_target_pairs={{0,1},{1,2},{2,3},{3,4},{4,5},{5,6},{6,7},{7,8},{8,9},{9,10},{10,1... | collective-permute-start | bytes 1572872 | tf_op jit(solution)/shard_map/while/body/eval_jaxpr/ppermute | solution.py:20
  476.5 4.7 collective-permute-start.1
  491.2 11.2 %collective-permute-start.2 = (f32[2,128,4,128]{3,2,1,0:T(4,128)}, f32[2,128,4,128]{3,2,1,0:T(4,128)}, u32[]{:S(2)}, u32[]{:S(2)}) collective-permute-start(f32[2,128,4,128]{3,2,1,0:T(4,128)} %get-tuple-element.185), channel_id=1, source_target_pairs={{0,1},{1,2},{2,3},{3,4},{4,5},{5,6},{6,7},{7,8},{8,9},{9,10},{10,1... | collective-permute-start | bytes 1572872 | tf_op jit(solution)/shard_map/while/body/eval_jaxpr/ppermute | solution.py:20
  515.3 10.9 %collective-permute-start = (f32[2,128,4,128]{3,2,1,0:T(4,128)}, f32[2,128,4,128]{3,2,1,0:T(4,128)}, u32[]{:S(2)}, u32[]{:S(2)}) collective-permute-start(f32[2,128,4,128]{3,2,1,0:T(4,128)} %get-tuple-element.181), channel_id=1, source_target_pairs={{0,1},{1,2},{2,3},{3,4},{4,5},{5,6},{6,7},{7,8},{8,9},{9,10},{10,1... | collective-permute-start | bytes 1572872 | tf_op jit(solution)/shard_map/while/body/eval_jaxpr/ppermute | solution.py:20
  524.9 4.7 collective-permute-start.1
  539.5 11.2 %collective-permute-start.2 = (f32[2,128,4,128]{3,2,1,0:T(4,128)}, f32[2,128,4,128]{3,2,1,0:T(4,128)}, u32[]{:S(2)}, u32[]{:S(2)}) collective-permute-start(f32[2,128,4,128]{3,2,1,0:T(4,128)} %get-tuple-element.185), channel_id=1, source_target_pairs={{0,1},{1,2},{2,3},{3,4},{4,5},{5,6},{6,7},{7,8},{8,9},{9,10},{10,1... | collective-permute-start | bytes 1572872 | tf_op jit(solution)/shard_map/while/body/eval_jaxpr/ppermute | solution.py:20
  (17 other events, 684.8 us)

commit v4 on v3

--- a/solution.py
+++ b/solution.py
@@ -9,7 +9,6 @@
 stencil_weights = (8.0 / 5.0, -1.0 / 5.0, 8.0 / 315.0, -1.0 / 560.0)
 center_weight = 3.0 * (-205.0 / 72.0)
 HALO = 4
-XOFF = 8
 
 
 def with_halo(cells, axis, dim, width):
@@ -23,45 +22,66 @@
 
 
 def step_kernel(
-    moment_ref, cur_ref, prev_ref, s_ref, img_ref, xlo_ref, xhi_ref, inj_ref, out_ref, imgo_ref, ey_ref, hx_ref
+    moment_ref,
+    cur_ref,
+    prev_ref,
+    s_ref,
+    img_ref,
+    xlo_ref,
+    xhi_ref,
+    ylo_ref,
+    yhi_ref,
+    inj_ref,
+    out_ref,
+    imgo_ref,
+    ey_ref,
+    hx_ref,
 ):
     comps, block_y, block_x, depth_z = cur_ref.shape
-    zeros_y = jnp.zeros((comps, HALO, block_x, depth_z), jnp.float32)
-    ey_ref[:, 0:HALO] = zeros_y
-    ey_ref[:, HALO + block_y : 2 * HALO + block_y] = zeros_y
+    tiles = block_x // 8
+    ey_ref[:, 0:HALO] = ylo_ref[...]
+    ey_ref[:, HALO + block_y : 2 * HALO + block_y] = yhi_ref[...]
     ey_ref[:, HALO : HALO + block_y] = cur_ref[...]
-    hx_ref[0, :, :, block_x - HALO : block_x, :] = xlo_ref[...]
+    hx_ref[0, :, :, 8 - HALO : 8, :] = xlo_ref[...]
     hx_ref[1, :, :, 0:HALO, :] = xhi_ref[...]
-    lane = lax.broadcasted_iota(jnp.int32, (block_x, depth_z), 1)
-    sub = lax.broadcasted_iota(jnp.int32, (block_x, depth_z), 0)
+    lane = lax.broadcasted_iota(jnp.int32, (8, depth_z), 1)
+    sub = lax.broadcasted_iota(jnp.int32, (8, depth_z), 0)
 
     def row(y, carry):
         done = []
         for c in range(comps):
-            ctr = ey_ref[c, HALO + y]
-            left = hx_ref[0, c, y]
-            right = hx_ref[1, c, y]
-            acc = center_weight * ctr
-            for m in range(1, HALO + 1):
-                ahead = pltpu.roll(jnp.where(sub >= m, ctr, right), block_x - m, 0)
-                behind = pltpu.roll(jnp.where(sub < block_x - m, ctr, left), m, 0)
-                b = ahead + behind
-                b = b + ey_ref[c, HALO + y + m] + ey_ref[c, HALO + y - m]
-                up = jnp.where(lane < depth_z - m, pltpu.roll(ctr, depth_z - m, 1), 0.0)
-                down = jnp.where(lane >= m, pltpu.roll(ctr, m, 1), 0.0)
-                b = b + up + down
-                acc = acc + stencil_weights[m - 1] * b
-            lap = acc + inj_ref[c, y]
-            upd = 2.0 * ctr - prev_ref[c, y] + s_ref[y] * lap
-            out_ref[c, y] = upd
-            done.append(upd)
-        imgo_ref[y] = img_ref[y] + done[0] * done[1]
+            parts = [hx_ref[0, c, y]]
+            for t in range(tiles):
+                parts.append(ey_ref[c, HALO + y, 8 * t : 8 * t + 8])
+            parts.append(hx_ref[1, c, y])
+            ups = []
+            for t in range(tiles):
+                cols = slice(8 * t, 8 * t + 8)
+                ctr = parts[t + 1]
+                acc = center_weight * ctr
+                for m in range(1, HALO + 1):
+                    ahead = pltpu.roll(jnp.where(sub >= m, ctr, parts[t + 2]), 8 - m, 0)
+                    behind = pltpu.roll(jnp.where(sub < 8 - m, ctr, parts[t]), m, 0)
+                    b = ahead + behind
+                    b = b + ey_ref[c, HALO + y + m, cols] + ey_ref[c, HALO + y - m, cols]
+                    up = jnp.where(lane < depth_z - m, pltpu.roll(ctr, depth_z - m, 1), 0.0)
+                    down = jnp.where(lane >= m, pltpu.roll(ctr, m, 1), 0.0)
+                    b = b + up + down
+                    acc = acc + stencil_weights[m - 1] * b
+                lap = acc + inj_ref[c, y, cols]
+                upd = 2.0 * ctr - prev_ref[c, y, cols] + s_ref[y, cols] * lap
+                out_ref[c, y, cols] = upd
+                ups.append(upd)
+            done.append(ups)
+        for t in range(tiles):
+            cols = slice(8 * t, 8 * t + 8)
+            imgo_ref[y, cols] = img_ref[y, cols] + done[0][t] * done[1][t]
         return carry
 
-    lax.fori_loop(0, block_y, row, 0, unroll=2)
-
-
-def step_call(moment, cur, prev, s, img, xlo, xhi, planes):
+    lax.fori_loop(0, block_y, row, 0)
+
+
+def step_call(moment, cur, prev, s, img, xlo, xhi, ylo, yhi, planes):
     comps, block_y, block_x, depth_z = cur.shape
 
     def whole(shape):
@@ -80,12 +100,14 @@
             whole(img.shape),
             whole(xlo.shape),
             whole(xhi.shape),
+            whole(ylo.shape),
+            whole(yhi.shape),
             plane_spec,
         ],
         out_specs=(whole(cur.shape), whole(img.shape)),
         scratch_shapes=[
             pltpu.VMEM((comps, block_y + 2 * HALO, block_x, depth_z), jnp.float32),
-            pltpu.VMEM((2, comps, block_y, block_x, depth_z), jnp.float32),
+            pltpu.VMEM((2, comps, block_y, 8, depth_z), jnp.float32),
         ],
     )
     return pl.pallas_call(
@@ -100,13 +122,63 @@
         cost_estimate=pl.CostEstimate(
             flops=60 * cur.size, bytes_accessed=4 * 6 * cur.size, transcendentals=0
         ),
-    )(jnp.reshape(moment, (1,)).astype(jnp.int32), cur, prev, s, img, xlo, xhi, planes)
-
-
-def point_tables(cell_rows, x_start, cells_wide, depth_y):
+    )(jnp.reshape(moment, (1,)).astype(jnp.int32), cur, prev, s, img, xlo, xhi, ylo, yhi, planes)
+
+
+def group_pairs(count, pick):
+    return [pair for g in range(count // 4) for pair in pick(4 * g, g)]
+
+
+def to_blocks(a, count):
+    member = lax.axis_index("dom") % 4
+    ydim, xdim = a.ndim - 3, a.ndim - 2
+    half = a.shape[ydim] // 2
+    pieces = []
+    for sub in range(2):
+        got = []
+        for h in range(2):
+            part = lax.slice_in_dim(a, h * half, (h + 1) * half, axis=ydim)
+            pairs = group_pairs(count, lambda b, g: [(b + 2 * e + sub, b + 2 * h + e) for e in range(2)])
+            got.append(lax.ppermute(part, "dom", pairs))
+        pieces.append(jnp.where(member // 2 == 0, got[0], got[1]))
+    return jnp.concatenate(pieces, axis=xdim)
+
+
+def from_blocks(b, count):
+    member = lax.axis_index("dom") % 4
+    ydim, xdim = b.ndim - 3, b.ndim - 2
+    width = b.shape[xdim] // 2
+    halves = []
+    for h in range(2):
+        got = []
+        for sub in range(2):
+            part = lax.slice_in_dim(b, sub * width, (sub + 1) * width, axis=xdim)
+            pairs = group_pairs(count, lambda o, g: [(o + 2 * h + e, o + 2 * e + sub) for e in range(2)])
+            got.append(lax.ppermute(part, "dom", pairs))
+        halves.append(jnp.where(member % 2 == 0, got[0], got[1]))
+    return jnp.concatenate(halves, axis=ydim)
+
+
+def block_halos(cur, count):
+    groups = count // 4
+    low_pairs = group_pairs(count, lambda b, g: [(b + 2 * h, b + 2 * h + 1) for h in range(2)])
+    low_pairs += group_pairs(
+        count, lambda b, g: [(b + 2 * h + 1, b + 4 + 2 * h) for h in range(2) if g + 1 < groups]
+    )
+    high_pairs = [(dst, src) for src, dst in low_pairs]
+    xlo = lax.ppermute(cur[:, :, -HALO:], "dom", low_pairs)
+    xhi = lax.ppermute(cur[:, :, :HALO], "dom", high_pairs)
+    up_pairs = group_pairs(count, lambda b, g: [(b + e, b + 2 + e) for e in range(2)])
+    ylo = lax.ppermute(cur[:, -HALO:], "dom", up_pairs)
+    yhi = lax.ppermute(cur[:, :HALO], "dom", [(dst, src) for src, dst in up_pairs])
+    return xlo, xhi, ylo, yhi
+
+
+def point_tables(cell_rows, x_start, cells_wide, y_start, depth_y):
     local_x = cell_rows[0] - x_start
     inside = (local_x >= 0) & (local_x < cells_wide)
-    rows_y = (cell_rows[1][:, None] == jnp.arange(depth_y, dtype=jnp.int32)[None, :]).astype(
+    local_y = cell_rows[1] - y_start
+    rows_y = (local_y[:, None] == jnp.arange(depth_y, dtype=jnp.int32)[None, :]).astype(
         jnp.float32
     )
     column = local_x * 4 + cell_rows[2]
@@ -132,16 +204,23 @@
     depth_z = fields_now.shape[3]
     block_y = velocity.shape[0]
     steps_total = wavelet.shape[0]
-    x_anchor = lax.axis_index("dom") * cells_x
     bricks = velocity.reshape(block_y, slab_count, cells_x, depth_z)
     chosen = jnp.take(bricks, aperture, axis=1)
     arrived = lax.all_to_all(chosen, "dom", split_axis=1, concat_axis=0, tiled=True)
     scaled = courant * arrived.reshape(depth_y, cells_x, depth_z)
     speed_sq = scaled * scaled
-    image_zero = jnp.zeros((depth_y, cells_x, depth_z), jnp.float32)
-    source_core = point_tables(source_pos, x_anchor, cells_x, depth_y)
-    receiver_core = point_tables(receiver_pos, x_anchor, cells_x, depth_y)
-
+    member = lax.axis_index("dom") % 4
+    group = lax.axis_index("dom") // 4
+    speed_sq = to_blocks(speed_sq, slab_count)
+    older_fields = to_blocks(older_fields, slab_count)
+    fields_now = to_blocks(fields_now, slab_count)
+    block_rows = depth_y // 2
+    block_cols = 2 * cells_x
+    x_anchor = (4 * group + 2 * (member % 2)) * cells_x
+    y_anchor = (member // 2) * block_rows
+    image_zero = jnp.zeros((block_rows, block_cols, depth_z), jnp.float32)
+    source_core = point_tables(source_pos, x_anchor, block_cols, y_anchor, block_rows)
+    receiver_core = point_tables(receiver_pos, x_anchor, block_cols, y_anchor, block_rows)
     planes = jnp.stack(
         [
             spread_points(source_core, wavelet, depth_z),
@@ -151,8 +230,10 @@
     )
 
     def advance(moment, previous, current, image_acc):
-        low, high = with_halo(current, "dom", 2, HALO)
-        return step_call(moment, current, previous, speed_sq, image_acc, low, high, planes)
+        xlo, xhi, ylo, yhi = block_halos(current, slab_count)
+        return step_call(
+            moment, current, previous, speed_sq, image_acc, xlo, xhi, ylo, yhi, planes
+        )
 
     def pair(index, state_carry):
         previous, current, image_acc = state_carry
@@ -166,6 +247,9 @@
     if steps_total % 2:
         last, image_acc = advance(steps_total - 1, previous, current, image_acc)
         previous, current = current, last
+    previous = from_blocks(previous, slab_count)
+    current = from_blocks(current, slab_count)
+    image_acc = from_blocks(image_acc, slab_count)
     image_acc = image_acc * (1.0 / steps_total)
     outgoing = image_acc.reshape(depth_y, 1, cells_x, depth_z)
     one_hot = (aperture[None, :] == jnp.arange(slab_count, dtype=jnp.int32)[:, None]).astype(

time: 591 us -> 663 us (1.12); the launches traced: 589 us -> 654 us
  waiting for transfers between devices: 68.7 us -> 117 us
  blocking collectives: 24.4 us -> 0 us
  local copies, waits for them, and re-layouts: 50.6 us -> 71.7 us
  starting transfers between devices: 230 us -> 242 us
  matrix products: 12.8 us -> 22.8 us
    ppermute x40 -> x104, waiting for transfers between devices: 68.7 us -> 117 us  [the longest x20 83.3 us: block_halos(): lax.ppermute(cur[:, :HALO], 'dom', [(dst, src) for src, dst in up_pairs])]
    all_to_all x1 -> x0, blocking collectives: 24.4 us -> none  [shards(): lax.all_to_all(outgoing, 'dom', split_axis=0, concat_axis=1, tiled=True)]
    while x0 -> x120, local copies, waits for them, and re-layouts: none -> 14.1 us
    slice x20 -> x46, local copies, waits for them, and re-layouts: 22.5 us -> 35.4 us  [the longest x20 17.6 us: block_halos(): xhi = lax.ppermute(cur[:, :, :HALO], 'dom', high_pairs)]
    all_to_all x0 -> x1, starting transfers between devices: none -> 10.2 us  [shards(): lax.all_to_all(outgoing, 'dom', split_axis=0, concat_axis=1, tiled=True)]
    dot_general x2, matrix products: 12.1 us -> 22.1 us  [spread_points(): jnp.einsum('ny,nsc->syc', rows_y, weighted, precision=lax.Precision.HIGHEST)]
    another operation x1, other arithmetic: 16.2 us -> 7.33 us  [shards(): jnp.stack([spread_points(source_core, wavelet, depth_z), spread_points(re...]
    another operation x1, local copies, waits for them, and re-layouts: 15.5 us -> 8.01 us  [shards(): jnp.stack([spread_points(source_core, wavelet, depth_z), spread_points(re...]
  transfers between devices with their start and end apart: 41 -> 106, of which waited for: 20 -> 43; matrix products, arithmetic and copies ran while one was open for 10% -> 12% of each run, Pallas kernels for 0% -> 0%
where the time goes in v4:
time: 663 us; the launch traced here: 654 us
  starting transfers between devices  242 us (37%)
  Pallas kernels  175 us (26%)
  waiting for transfers between devices  117 us (18%)
  local copies, waits for them, and re-layouts  71.7 us (11%)
  matrix products  22.8 us (3%)
  other arithmetic  22.3 us (3%)
    pallas_call x20, Pallas kernels, step_call(): pl.pallas_call(step_kernel, out_shape=(jax.ShapeDtypeStruct(cur.shape, jn...  175 us
    ppermute x20, waiting for transfers between devices, block_halos(): lax.ppermute(cur[:, :HALO], 'dom', [(dst, src) for src, dst in up_pairs])  83.3 us
    ppermute x20, starting transfers between devices, block_halos(): xlo = lax.ppermute(cur[:, :, -HALO:], 'dom', low_pairs)  76.1 us
    ppermute x20, starting transfers between devices, block_halos(): ylo = lax.ppermute(cur[:, -HALO:], 'dom', up_pairs)  41.6 us
    ppermute x12, starting transfers between devices, to_blocks(): got.append(lax.ppermute(part, 'dom', pairs))  33.5 us
    ppermute x20, starting transfers between devices, block_halos(): xhi = lax.ppermute(cur[:, :, :HALO], 'dom', high_pairs)  25.8 us
    ppermute x20, starting transfers between devices, block_halos(): lax.ppermute(cur[:, :HALO], 'dom', [(dst, src) for src, dst in up_pairs])  25.8 us
    dot_general x2, matrix products, spread_points(): jnp.einsum('ny,nsc->syc', rows_y, weighted, precision=lax.Precision.HIGHEST)  22.1 us
  transfers between devices with their start and end apart: 106, of which 43 were waited for; matrix products, arithmetic and copies ran while one was open for 12% of the time, Pallas kernels for 0%

profile of v4, /device:TPU:0, one launch (start us, length us, event | category | flops | bytes accessed | tf_op | source)
XLA Modules:
  0.0 653.9 jit_solution(8775311008519851571)
XLA Ops:
  4.2 5.4 collective-permute-start.12
  16.6 8.1 %all-to-all-start = ((f32[8,16,8,128]{3,2,0,1:T(8,128)}), f32[8,16,8,128]{3,2,0,1:T(8,128)S(1)}, u32[]{:S(2)}, u32[]{:S(2)}) async-start(f32[8,16,8,128]{3,2,0,1:T(8,128)} %select_bitcast_fusion), calls=%async_computation | async-start | bytes 1048576 | tf_op jit(solution)/shard_map/all_to_all | solution.py:209
  29.8 21.3 %fusion = f32[20,64,64]{2,1,0:T(8,128)S(1)} fusion(f32[8192,20]{0,1:T(8,128)} %bitcast.80, f32[8192,64]{0,1:T(8,128)S(1)} %fusion.5, pred[8192,64,1]{0,1,2:T(32,128)(4,1)} %fusion.39), kind=kOutput, calls=%fused_computation.1 | convolution fusion | flops 8063549440 | bytes 3604480 | tf_op jit(solution)/shard_map/ny,nsc->syc/dot_general | solution.py:195
  51.2 6.3 copy.25
  58.4 6.2 copy.24
  64.6 8.0 %pad_bitcast_fusion = (f32[20,1,64,16,128]{4,3,2,1,0:T(8,128)S(1)}, f32[20,1,64,16,128]{4,3,2,1,0:T(8,128)S(1)}) fusion(f32[20,64,16,4]{3,2,1,0:T(8,128)} %copy.25, f32[20,64,16,4]{3,2,1,0:T(8,128)} %copy.24), kind=kLoop, calls=%fused_computation.6 | loop fusion | bytes 21626880 | tf_op jit(solution)/shard_map/stack | solution.py:224
  72.6 7.3 %pad_maximum_fusion = f32[20,2,64,16,128]{4,3,2,1,0:T(8,128)} fusion(f32[20,1,64,16,128]{4,3,2,1,0:T(8,128)S(1)} %get-tuple-element.150, f32[20,1,64,16,128]{4,3,2,1,0:T(8,128)S(1)} %get-tuple-element.151), kind=kLoop, calls=%fused_computation.3 | loop fusion | flops 5242880 | bytes 41943040 | tf_op jit(solution)/shard_map/stack | solution.py:224
  97.7 12.2 %collective-permute-start.17 = (f32[64,8,128]{2,1,0:T(8,128)S(1)}, f32[64,8,128]{2,1,0:T(8,128)S(1)}, u32[]{:S(2)}, u32[]{:S(2)}) collective-permute-start(f32[64,8,128]{2,1,0:T(8,128)S(1)} %bitcast.74), channel_id=1, source_target_pairs={{0,2},{2,3},{4,6},{6,7},{8,10},{10,11},{12,14},{14,15},{16,18},{18... | collective-permute-start | bytes 786440 | tf_op jit(solution)/shard_map/ppermute | solution.py:142
  113.9 492.5 %while.17 = (s32[]{:T(128)}, f32[2,64,16,128]{3,2,1,0:T(8,128)S(1)}, f32[2,64,16,128]{3,2,1,0:T(8,128)S(1)}, f32[64,16,128]{2,1,0:T(8,128)S(1)}, f32[64,16,128]{...) while((s32[]{:T(128)}, f32[2,64,16,128]{3,2,1,0:T(8,128)S(1)}, ...), condition=%wide.region_1.2_spmd, body=%wide.region_0.1_spmd.sunk | while | flops 31457284 | bytes 23593556 | solution.py:244
  129.5 8.8 %eval_jaxpr.10 = (f32[2,64,16,128]{3,2,1,0:T(8,128)S(1)}, f32[64,16,128]{2,1,0:T(8,128)S(1)}) custom-call(s32[1]{0:T(128)} %bitcast.66.moment_ref, f32[2,64,16,128]{3,2,1,0:T(8,128)S(1)} %get-tuple-element.223.cur_ref.prev_ref, f32[2,64,16,128]{3,2,1,0:T(8,128)S(1)} %get-tuple-element.222.prev_ref, ...), custom_call_target="tpu_custom_call", output_to_operand_aliasing={{0}: (2, {}), {1}: (4, {})} | custom-call | flops 15728640 | bytes 6291456 | tf_op jit(solution)/shard_map/while/body/eval_jaxpr/pallas_call | solution.py:113
  153.7 8.8 %eval_jaxpr.11 = (f32[2,64,16,128]{3,2,1,0:T(8,128)S(1)}, f32[64,16,128]{2,1,0:T(8,128)S(1)}) custom-call(s32[1]{0:T(128)} %bitcast.67.moment_ref, f32[2,64,16,128]{3,2,1,0:T(8,128)S(1)} %get-tuple-element.230.cur_ref, f32[2,64,16,128]{3,2,1,0:T(8,128)S(1)} %get-tuple-element.223.cur_ref.prev_ref, ...), custom_call_target="tpu_custom_call", output_to_operand_aliasing={{0}: (2, {}), {1}: (4, {})} | custom-call | flops 15728640 | bytes 6291456 | tf_op jit(solution)/shard_map/while/body/eval_jaxpr/pallas_call | solution.py:113
  178.3 8.8 %eval_jaxpr.10 = (f32[2,64,16,128]{3,2,1,0:T(8,128)S(1)}, f32[64,16,128]{2,1,0:T(8,128)S(1)}) custom-call(s32[1]{0:T(128)} %bitcast.66.moment_ref, f32[2,64,16,128]{3,2,1,0:T(8,128)S(1)} %get-tuple-element.223.cur_ref.prev_ref, f32[2,64,16,128]{3,2,1,0:T(8,128)S(1)} %get-tuple-element.222.prev_ref, ...), custom_call_target="tpu_custom_call", output_to_operand_aliasing={{0}: (2, {}), {1}: (4, {})} | custom-call | flops 15728640 | bytes 6291456 | tf_op jit(solution)/shard_map/while/body/eval_jaxpr/pallas_call | solution.py:113
  203.0 8.8 %eval_jaxpr.11 = (f32[2,64,16,128]{3,2,1,0:T(8,128)S(1)}, f32[64,16,128]{2,1,0:T(8,128)S(1)}) custom-call(s32[1]{0:T(128)} %bitcast.67.moment_ref, f32[2,64,16,128]{3,2,1,0:T(8,128)S(1)} %get-tuple-element.230.cur_ref, f32[2,64,16,128]{3,2,1,0:T(8,128)S(1)} %get-tuple-element.223.cur_ref.prev_ref, ...), custom_call_target="tpu_custom_call", output_to_operand_aliasing={{0}: (2, {}), {1}: (4, {})} | custom-call | flops 15728640 | bytes 6291456 | tf_op jit(solution)/shard_map/while/body/eval_jaxpr/pallas_call | solution.py:113
  227.7 8.8 %eval_jaxpr.10 = (f32[2,64,16,128]{3,2,1,0:T(8,128)S(1)}, f32[64,16,128]{2,1,0:T(8,128)S(1)}) custom-call(s32[1]{0:T(128)} %bitcast.66.moment_ref, f32[2,64,16,128]{3,2,1,0:T(8,128)S(1)} %get-tuple-element.223.cur_ref.prev_ref, f32[2,64,16,128]{3,2,1,0:T(8,128)S(1)} %get-tuple-element.222.prev_ref, ...), custom_call_target="tpu_custom_call", output_to_operand_aliasing={{0}: (2, {}), {1}: (4, {})} | custom-call | flops 15728640 | bytes 6291456 | tf_op jit(solution)/shard_map/while/body/eval_jaxpr/pallas_call | solution.py:113
  252.3 8.8 %eval_jaxpr.11 = (f32[2,64,16,128]{3,2,1,0:T(8,128)S(1)}, f32[64,16,128]{2,1,0:T(8,128)S(1)}) custom-call(s32[1]{0:T(128)} %bitcast.67.moment_ref, f32[2,64,16,128]{3,2,1,0:T(8,128)S(1)} %get-tuple-element.230.cur_ref, f32[2,64,16,128]{3,2,1,0:T(8,128)S(1)} %get-tuple-element.223.cur_ref.prev_ref, ...), custom_call_target="tpu_custom_call", output_to_operand_aliasing={{0}: (2, {}), {1}: (4, {})} | custom-call | flops 15728640 | bytes 6291456 | tf_op jit(solution)/shard_map/while/body/eval_jaxpr/pallas_call | solution.py:113
  277.0 8.8 %eval_jaxpr.10 = (f32[2,64,16,128]{3,2,1,0:T(8,128)S(1)}, f32[64,16,128]{2,1,0:T(8,128)S(1)}) custom-call(s32[1]{0:T(128)} %bitcast.66.moment_ref, f32[2,64,16,128]{3,2,1,0:T(8,128)S(1)} %get-tuple-element.223.cur_ref.prev_ref, f32[2,64,16,128]{3,2,1,0:T(8,128)S(1)} %get-tuple-element.222.prev_ref, ...), custom_call_target="tpu_custom_call", output_to_operand_aliasing={{0}: (2, {}), {1}: (4, {})} | custom-call | flops 15728640 | bytes 6291456 | tf_op jit(solution)/shard_map/while/body/eval_jaxpr/pallas_call | solution.py:113
  301.6 8.8 %eval_jaxpr.11 = (f32[2,64,16,128]{3,2,1,0:T(8,128)S(1)}, f32[64,16,128]{2,1,0:T(8,128)S(1)}) custom-call(s32[1]{0:T(128)} %bitcast.67.moment_ref, f32[2,64,16,128]{3,2,1,0:T(8,128)S(1)} %get-tuple-element.230.cur_ref, f32[2,64,16,128]{3,2,1,0:T(8,128)S(1)} %get-tuple-element.223.cur_ref.prev_ref, ...), custom_call_target="tpu_custom_call", output_to_operand_aliasing={{0}: (2, {}), {1}: (4, {})} | custom-call | flops 15728640 | bytes 6291456 | tf_op jit(solution)/shard_map/while/body/eval_jaxpr/pallas_call | solution.py:113
  326.3 8.8 %eval_jaxpr.10 = (f32[2,64,16,128]{3,2,1,0:T(8,128)S(1)}, f32[64,16,128]{2,1,0:T(8,128)S(1)}) custom-call(s32[1]{0:T(128)} %bitcast.66.moment_ref, f32[2,64,16,128]{3,2,1,0:T(8,128)S(1)} %get-tuple-element.223.cur_ref.prev_ref, f32[2,64,16,128]{3,2,1,0:T(8,128)S(1)} %get-tuple-element.222.prev_ref, ...), custom_call_target="tpu_custom_call", output_to_operand_aliasing={{0}: (2, {}), {1}: (4, {})} | custom-call | flops 15728640 | bytes 6291456 | tf_op jit(solution)/shard_map/while/body/eval_jaxpr/pallas_call | solution.py:113
  351.0 8.8 %eval_jaxpr.11 = (f32[2,64,16,128]{3,2,1,0:T(8,128)S(1)}, f32[64,16,128]{2,1,0:T(8,128)S(1)}) custom-call(s32[1]{0:T(128)} %bitcast.67.moment_ref, f32[2,64,16,128]{3,2,1,0:T(8,128)S(1)} %get-tuple-element.230.cur_ref, f32[2,64,16,128]{3,2,1,0:T(8,128)S(1)} %get-tuple-element.223.cur_ref.prev_ref, ...), custom_call_target="tpu_custom_call", output_to_operand_aliasing={{0}: (2, {}), {1}: (4, {})} | custom-call | flops 15728640 | bytes 6291456 | tf_op jit(solution)/shard_map/while/body/eval_jaxpr/pallas_call | solution.py:113
  375.6 8.8 %eval_jaxpr.10 = (f32[2,64,16,128]{3,2,1,0:T(8,128)S(1)}, f32[64,16,128]{2,1,0:T(8,128)S(1)}) custom-call(s32[1]{0:T(128)} %bitcast.66.moment_ref, f32[2,64,16,128]{3,2,1,0:T(8,128)S(1)} %get-tuple-element.223.cur_ref.prev_ref, f32[2,64,16,128]{3,2,1,0:T(8,128)S(1)} %get-tuple-element.222.prev_ref, ...), custom_call_target="tpu_custom_call", output_to_operand_aliasing={{0}: (2, {}), {1}: (4, {})} | custom-call | flops 15728640 | bytes 6291456 | tf_op jit(solution)/shard_map/while/body/eval_jaxpr/pallas_call | solution.py:113
  400.3 8.8 %eval_jaxpr.11 = (f32[2,64,16,128]{3,2,1,0:T(8,128)S(1)}, f32[64,16,128]{2,1,0:T(8,128)S(1)}) custom-call(s32[1]{0:T(128)} %bitcast.67.moment_ref, f32[2,64,16,128]{3,2,1,0:T(8,128)S(1)} %get-tuple-element.230.cur_ref, f32[2,64,16,128]{3,2,1,0:T(8,128)S(1)} %get-tuple-element.223.cur_ref.prev_ref, ...), custom_call_target="tpu_custom_call", output_to_operand_aliasing={{0}: (2, {}), {1}: (4, {})} | custom-call | flops 15728640 | bytes 6291456 | tf_op jit(solution)/shard_map/while/body/eval_jaxpr/pallas_call | solution.py:113
  425.0 8.8 %eval_jaxpr.10 = (f32[2,64,16,128]{3,2,1,0:T(8,128)S(1)}, f32[64,16,128]{2,1,0:T(8,128)S(1)}) custom-call(s32[1]{0:T(128)} %bitcast.66.moment_ref, f32[2,64,16,128]{3,2,1,0:T(8,128)S(1)} %get-tuple-element.223.cur_ref.prev_ref, f32[2,64,16,128]{3,2,1,0:T(8,128)S(1)} %get-tuple-element.222.prev_ref, ...), custom_call_target="tpu_custom_call", output_to_operand_aliasing={{0}: (2, {}), {1}: (4, {})} | custom-call | flops 15728640 | bytes 6291456 | tf_op jit(solution)/shard_map/while/body/eval_jaxpr/pallas_call | solution.py:113
  449.6 8.8 %eval_jaxpr.11 = (f32[2,64,16,128]{3,2,1,0:T(8,128)S(1)}, f32[64,16,128]{2,1,0:T(8,128)S(1)}) custom-call(s32[1]{0:T(128)} %bitcast.67.moment_ref, f32[2,64,16,128]{3,2,1,0:T(8,128)S(1)} %get-tuple-element.230.cur_ref, f32[2,64,16,128]{3,2,1,0:T(8,128)S(1)} %get-tuple-element.223.cur_ref.prev_ref, ...), custom_call_target="tpu_custom_call", output_to_operand_aliasing={{0}: (2, {}), {1}: (4, {})} | custom-call | flops 15728640 | bytes 6291456 | tf_op jit(solution)/shard_map/while/body/eval_jaxpr/pallas_call | solution.py:113
  474.3 8.8 %eval_jaxpr.10 = (f32[2,64,16,128]{3,2,1,0:T(8,128)S(1)}, f32[64,16,128]{2,1,0:T(8,128)S(1)}) custom-call(s32[1]{0:T(128)} %bitcast.66.moment_ref, f32[2,64,16,128]{3,2,1,0:T(8,128)S(1)} %get-tuple-element.223.cur_ref.prev_ref, f32[2,64,16,128]{3,2,1,0:T(8,128)S(1)} %get-tuple-element.222.prev_ref, ...), custom_call_target="tpu_custom_call", output_to_operand_aliasing={{0}: (2, {}), {1}: (4, {})} | custom-call | flops 15728640 | bytes 6291456 | tf_op jit(solution)/shard_map/while/body/eval_jaxpr/pallas_call | solution.py:113
  498.9 8.8 %eval_jaxpr.11 = (f32[2,64,16,128]{3,2,1,0:T(8,128)S(1)}, f32[64,16,128]{2,1,0:T(8,128)S(1)}) custom-call(s32[1]{0:T(128)} %bitcast.67.moment_ref, f32[2,64,16,128]{3,2,1,0:T(8,128)S(1)} %get-tuple-element.230.cur_ref, f32[2,64,16,128]{3,2,1,0:T(8,128)S(1)} %get-tuple-element.223.cur_ref.prev_ref, ...), custom_call_target="tpu_custom_call", output_to_operand_aliasing={{0}: (2, {}), {1}: (4, {})} | custom-call | flops 15728640 | bytes 6291456 | tf_op jit(solution)/shard_map/while/body/eval_jaxpr/pallas_call | solution.py:113
  523.6 8.8 %eval_jaxpr.10 = (f32[2,64,16,128]{3,2,1,0:T(8,128)S(1)}, f32[64,16,128]{2,1,0:T(8,128)S(1)}) custom-call(s32[1]{0:T(128)} %bitcast.66.moment_ref, f32[2,64,16,128]{3,2,1,0:T(8,128)S(1)} %get-tuple-element.223.cur_ref.prev_ref, f32[2,64,16,128]{3,2,1,0:T(8,128)S(1)} %get-tuple-element.222.prev_ref, ...), custom_call_target="tpu_custom_call", output_to_operand_aliasing={{0}: (2, {}), {1}: (4, {})} | custom-call | flops 15728640 | bytes 6291456 | tf_op jit(solution)/shard_map/while/body/eval_jaxpr/pallas_call | solution.py:113
  548.3 8.8 %eval_jaxpr.11 = (f32[2,64,16,128]{3,2,1,0:T(8,128)S(1)}, f32[64,16,128]{2,1,0:T(8,128)S(1)}) custom-call(s32[1]{0:T(128)} %bitcast.67.moment_ref, f32[2,64,16,128]{3,2,1,0:T(8,128)S(1)} %get-tuple-element.230.cur_ref, f32[2,64,16,128]{3,2,1,0:T(8,128)S(1)} %get-tuple-element.223.cur_ref.prev_ref, ...), custom_call_target="tpu_custom_call", output_to_operand_aliasing={{0}: (2, {}), {1}: (4, {})} | custom-call | flops 15728640 | bytes 6291456 | tf_op jit(solution)/shard_map/while/body/eval_jaxpr/pallas_call | solution.py:113
  572.9 8.8 %eval_jaxpr.10 = (f32[2,64,16,128]{3,2,1,0:T(8,128)S(1)}, f32[64,16,128]{2,1,0:T(8,128)S(1)}) custom-call(s32[1]{0:T(128)} %bitcast.66.moment_ref, f32[2,64,16,128]{3,2,1,0:T(8,128)S(1)} %get-tuple-element.223.cur_ref.prev_ref, f32[2,64,16,128]{3,2,1,0:T(8,128)S(1)} %get-tuple-element.222.prev_ref, ...), custom_call_target="tpu_custom_call", output_to_operand_aliasing={{0}: (2, {}), {1}: (4, {})} | custom-call | flops 15728640 | bytes 6291456 | tf_op jit(solution)/shard_map/while/body/eval_jaxpr/pallas_call | solution.py:113
  597.6 8.8 %eval_jaxpr.11 = (f32[2,64,16,128]{3,2,1,0:T(8,128)S(1)}, f32[64,16,128]{2,1,0:T(8,128)S(1)}) custom-call(s32[1]{0:T(128)} %bitcast.67.moment_ref, f32[2,64,16,128]{3,2,1,0:T(8,128)S(1)} %get-tuple-element.230.cur_ref, f32[2,64,16,128]{3,2,1,0:T(8,128)S(1)} %get-tuple-element.223.cur_ref.prev_ref, ...), custom_call_target="tpu_custom_call", output_to_operand_aliasing={{0}: (2, {}), {1}: (4, {})} | custom-call | flops 15728640 | bytes 6291456 | tf_op jit(solution)/shard_map/while/body/eval_jaxpr/pallas_call | solution.py:113
  618.3 5.3 collective-permute-start.25
  627.0 10.2 %all-to-all-start.1 = ((f32[128,1,8,128]{3,2,1,0:T(8,128)}), f32[128,1,8,128]{3,2,1,0:T(8,128)S(1)}, u32[]{:S(2)}, u32[]{:S(2)}) async-start(f32[128,1,8,128]{3,2,1,0:T(8,128)} %maximum_multiply_fusion), calls=%async_computation.1 | async-start | bytes 1048576 | tf_op jit(solution)/shard_map/all_to_all | solution.py:258
  642.3 8.9 %collective-permute-done.22 = f32[2,64,8,128]{3,2,1,0:T(8,128)S(1)} collective-permute-done((f32[2,64,8,128]{3,2,1,0:T(8,128)}, f32[2,64,8,128]{3,2,1,0:T(8,128)S(1)}, u32[]{:S(2)}, u32[]{:S(2)}) %collective-permute-start.22) | collective-permute-done | bytes 524320 | tf_op jit(solution)/shard_map/ppermute | solution.py:157
  (418 shorter events, 376.8 us)
Async XLA Ops:
  2.9 77.8 %collective-permute-start.14 = (f32[2,64,8,128]{3,2,1,0:T(8,128)}, f32[2,64,8,128]{3,2,1,0:T(8,128)}, u32[]{:S(2)}, u32[]{:S(2)}) collective-permute-start(f32[2,64,8,128]{3,2,1,0:T(8,128)} %get-tuple-element.139), channel_id=1, source_target_pairs={{1,0},{3,1},{5,4},{7,5},{9,8},{11,9},{13,12},{15,13},{17,16},{19,1... | collective-permute-start | bytes 1572872 | tf_op jit(solution)/shard_map/ppermute | solution.py:142
  4.2 84.1 %collective-permute-start.12 = (f32[2,64,8,128]{3,2,1,0:T(8,128)}, f32[2,64,8,128]{3,2,1,0:T(8,128)}, u32[]{:S(2)}, u32[]{:S(2)}) collective-permute-start(f32[2,64,8,128]{3,2,1,0:T(8,128)} %get-tuple-element.139), channel_id=1, source_target_pairs={{0,0},{2,1},{4,4},{6,5},{8,8},{10,9},{12,12},{14,13},{16,16},{18,1... | collective-permute-start | bytes 1572872 | tf_op jit(solution)/shard_map/ppermute | solution.py:142
  9.6 76.3 %collective-permute-start.15 = (f32[2,64,8,128]{3,2,1,0:T(8,128)}, f32[2,64,8,128]{3,2,1,0:T(8,128)}, u32[]{:S(2)}, u32[]{:S(2)}) collective-permute-start(f32[2,64,8,128]{3,2,1,0:T(8,128)} %get-tuple-element.138), channel_id=1, source_target_pairs={{1,2},{3,3},{5,6},{7,7},{9,10},{11,11},{13,14},{15,15},{17,18},{19... | collective-permute-start | bytes 1572872 | tf_op jit(solution)/shard_map/ppermute | solution.py:142
  11.1 77.9 %collective-permute-start.13 = (f32[2,64,8,128]{3,2,1,0:T(8,128)}, f32[2,64,8,128]{3,2,1,0:T(8,128)}, u32[]{:S(2)}, u32[]{:S(2)}) collective-permute-start(f32[2,64,8,128]{3,2,1,0:T(8,128)} %get-tuple-element.138), channel_id=1, source_target_pairs={{0,2},{2,3},{4,6},{6,7},{8,10},{10,11},{12,14},{14,15},{16,18},{18... | collective-permute-start | bytes 1572872 | tf_op jit(solution)/shard_map/ppermute | solution.py:142
  16.6 78.2 %all-to-all-start = ((f32[8,16,8,128]{3,2,0,1:T(8,128)}), f32[8,16,8,128]{3,2,0,1:T(8,128)S(1)}, u32[]{:S(2)}, u32[]{:S(2)}) async-start(f32[8,16,8,128]{3,2,0,1:T(8,128)} %select_bitcast_fusion), calls=%async_computation | async-start | bytes 1048576 | tf_op jit(solution)/shard_map/all_to_all | solution.py:209
  94.9 16.1 %collective-permute-start.18 = (f32[64,8,128]{2,1,0:T(8,128)S(1)}, f32[64,8,128]{2,1,0:T(8,128)S(1)}, u32[]{:S(2)}, u32[]{:S(2)}) collective-permute-start(f32[64,8,128]{2,1,0:T(8,128)S(1)} %bitcast.75), channel_id=1, source_target_pairs={{1,0},{3,1},{5,4},{7,5},{9,8},{11,9},{13,12},{15,13},{17,16},{19,1... | collective-permute-start | bytes 786440 | tf_op jit(solution)/shard_map/ppermute | solution.py:142
  96.2 14.8 %collective-permute-start.19 = (f32[64,8,128]{2,1,0:T(8,128)S(1)}, f32[64,8,128]{2,1,0:T(8,128)S(1)}, u32[]{:S(2)}, u32[]{:S(2)}) collective-permute-start(f32[64,8,128]{2,1,0:T(8,128)S(1)} %bitcast.73), channel_id=1, source_target_pairs={{1,2},{3,3},{5,6},{7,7},{9,10},{11,11},{13,14},{15,15},{17,18},{19... | collective-permute-start | bytes 786440 | tf_op jit(solution)/shard_map/ppermute | solution.py:142
  97.7 16.1 %collective-permute-start.17 = (f32[64,8,128]{2,1,0:T(8,128)S(1)}, f32[64,8,128]{2,1,0:T(8,128)S(1)}, u32[]{:S(2)}, u32[]{:S(2)}) collective-permute-start(f32[64,8,128]{2,1,0:T(8,128)S(1)} %bitcast.74), channel_id=1, source_target_pairs={{0,2},{2,3},{4,6},{6,7},{8,10},{10,11},{12,14},{14,15},{16,18},{18... | collective-permute-start | bytes 786440 | tf_op jit(solution)/shard_map/ppermute | solution.py:142
  163.3 14.3 %collective-permute-start = (f32[2,64,4,128]{3,2,1,0:T(4,128)}, f32[2,64,4,128]{3,2,1,0:T(4,128)S(1)}, u32[]{:S(2)}, u32[]{:S(2)}) collective-permute-start(f32[2,64,4,128]{3,2,1,0:T(4,128)} %get-tuple-element.201), channel_id=1, source_target_pairs={{0,1},{2,3},{4,5},{6,7},{8,9},{10,11},{12,13},{14,15},{1,4},{3,6},... | collective-permute-start | bytes 786440 | tf_op jit(solution)/shard_map/while/body/eval_jaxpr/ppermute | solution.py:169
  188.0 14.3 %collective-permute-start.4 = (f32[2,64,4,128]{3,2,1,0:T(4,128)}, f32[2,64,4,128]{3,2,1,0:T(4,128)S(1)}, u32[]{:S(2)}, u32[]{:S(2)}) collective-permute-start(f32[2,64,4,128]{3,2,1,0:T(4,128)} %get-tuple-element.207), channel_id=1, source_target_pairs={{0,1},{2,3},{4,5},{6,7},{8,9},{10,11},{12,13},{14,15},{1,4},{3,6},... | collective-permute-start | bytes 786440 | tf_op jit(solution)/shard_map/while/body/eval_jaxpr/ppermute | solution.py:169
  212.7 14.3 %collective-permute-start = (f32[2,64,4,128]{3,2,1,0:T(4,128)}, f32[2,64,4,128]{3,2,1,0:T(4,128)S(1)}, u32[]{:S(2)}, u32[]{:S(2)}) collective-permute-start(f32[2,64,4,128]{3,2,1,0:T(4,128)} %get-tuple-element.201), channel_id=1, source_target_pairs={{0,1},{2,3},{4,5},{6,7},{8,9},{10,11},{12,13},{14,15},{1,4},{3,6},... | collective-permute-start | bytes 786440 | tf_op jit(solution)/shard_map/while/body/eval_jaxpr/ppermute | solution.py:169
  237.3 14.3 %collective-permute-start.4 = (f32[2,64,4,128]{3,2,1,0:T(4,128)}, f32[2,64,4,128]{3,2,1,0:T(4,128)S(1)}, u32[]{:S(2)}, u32[]{:S(2)}) collective-permute-start(f32[2,64,4,128]{3,2,1,0:T(4,128)} %get-tuple-element.207), channel_id=1, source_target_pairs={{0,1},{2,3},{4,5},{6,7},{8,9},{10,11},{12,13},{14,15},{1,4},{3,6},... | collective-permute-start | bytes 786440 | tf_op jit(solution)/shard_map/while/body/eval_jaxpr/ppermute | solution.py:169
  262.0 14.3 %collective-permute-start = (f32[2,64,4,128]{3,2,1,0:T(4,128)}, f32[2,64,4,128]{3,2,1,0:T(4,128)S(1)}, u32[]{:S(2)}, u32[]{:S(2)}) collective-permute-start(f32[2,64,4,128]{3,2,1,0:T(4,128)} %get-tuple-element.201), channel_id=1, source_target_pairs={{0,1},{2,3},{4,5},{6,7},{8,9},{10,11},{12,13},{14,15},{1,4},{3,6},... | collective-permute-start | bytes 786440 | tf_op jit(solution)/shard_map/while/body/eval_jaxpr/ppermute | solution.py:169
  286.6 14.3 %collective-permute-start.4 = (f32[2,64,4,128]{3,2,1,0:T(4,128)}, f32[2,64,4,128]{3,2,1,0:T(4,128)S(1)}, u32[]{:S(2)}, u32[]{:S(2)}) collective-permute-start(f32[2,64,4,128]{3,2,1,0:T(4,128)} %get-tuple-element.207), channel_id=1, source_target_pairs={{0,1},{2,3},{4,5},{6,7},{8,9},{10,11},{12,13},{14,15},{1,4},{3,6},... | collective-permute-start | bytes 786440 | tf_op jit(solution)/shard_map/while/body/eval_jaxpr/ppermute | solution.py:169
  311.3 14.3 %collective-permute-start = (f32[2,64,4,128]{3,2,1,0:T(4,128)}, f32[2,64,4,128]{3,2,1,0:T(4,128)S(1)}, u32[]{:S(2)}, u32[]{:S(2)}) collective-permute-start(f32[2,64,4,128]{3,2,1,0:T(4,128)} %get-tuple-element.201), channel_id=1, source_target_pairs={{0,1},{2,3},{4,5},{6,7},{8,9},{10,11},{12,13},{14,15},{1,4},{3,6},... | collective-permute-start | bytes 786440 | tf_op jit(solution)/shard_map/while/body/eval_jaxpr/ppermute | solution.py:169
  336.0 14.3 %collective-permute-start.4 = (f32[2,64,4,128]{3,2,1,0:T(4,128)}, f32[2,64,4,128]{3,2,1,0:T(4,128)S(1)}, u32[]{:S(2)}, u32[]{:S(2)}) collective-permute-start(f32[2,64,4,128]{3,2,1,0:T(4,128)} %get-tuple-element.207), channel_id=1, source_target_pairs={{0,1},{2,3},{4,5},{6,7},{8,9},{10,11},{12,13},{14,15},{1,4},{3,6},... | collective-permute-start | bytes 786440 | tf_op jit(solution)/shard_map/while/body/eval_jaxpr/ppermute | solution.py:169
  360.6 14.3 %collective-permute-start = (f32[2,64,4,128]{3,2,1,0:T(4,128)}, f32[2,64,4,128]{3,2,1,0:T(4,128)S(1)}, u32[]{:S(2)}, u32[]{:S(2)}) collective-permute-start(f32[2,64,4,128]{3,2,1,0:T(4,128)} %get-tuple-element.201), channel_id=1, source_target_pairs={{0,1},{2,3},{4,5},{6,7},{8,9},{10,11},{12,13},{14,15},{1,4},{3,6},... | collective-permute-start | bytes 786440 | tf_op jit(solution)/shard_map/while/body/eval_jaxpr/ppermute | solution.py:169
  385.3 14.3 %collective-permute-start.4 = (f32[2,64,4,128]{3,2,1,0:T(4,128)}, f32[2,64,4,128]{3,2,1,0:T(4,128)S(1)}, u32[]{:S(2)}, u32[]{:S(2)}) collective-permute-start(f32[2,64,4,128]{3,2,1,0:T(4,128)} %get-tuple-element.207), channel_id=1, source_target_pairs={{0,1},{2,3},{4,5},{6,7},{8,9},{10,11},{12,13},{14,15},{1,4},{3,6},... | collective-permute-start | bytes 786440 | tf_op jit(solution)/shard_map/while/body/eval_jaxpr/ppermute | solution.py:169
  410.0 14.3 %collective-permute-start = (f32[2,64,4,128]{3,2,1,0:T(4,128)}, f32[2,64,4,128]{3,2,1,0:T(4,128)S(1)}, u32[]{:S(2)}, u32[]{:S(2)}) collective-permute-start(f32[2,64,4,128]{3,2,1,0:T(4,128)} %get-tuple-element.201), channel_id=1, source_target_pairs={{0,1},{2,3},{4,5},{6,7},{8,9},{10,11},{12,13},{14,15},{1,4},{3,6},... | collective-permute-start | bytes 786440 | tf_op jit(solution)/shard_map/while/body/eval_jaxpr/ppermute | solution.py:169
  434.6 14.3 %collective-permute-start.4 = (f32[2,64,4,128]{3,2,1,0:T(4,128)}, f32[2,64,4,128]{3,2,1,0:T(4,128)S(1)}, u32[]{:S(2)}, u32[]{:S(2)}) collective-permute-start(f32[2,64,4,128]{3,2,1,0:T(4,128)} %get-tuple-element.207), channel_id=1, source_target_pairs={{0,1},{2,3},{4,5},{6,7},{8,9},{10,11},{12,13},{14,15},{1,4},{3,6},... | collective-permute-start | bytes 786440 | tf_op jit(solution)/shard_map/while/body/eval_jaxpr/ppermute | solution.py:169
  459.3 14.3 %collective-permute-start = (f32[2,64,4,128]{3,2,1,0:T(4,128)}, f32[2,64,4,128]{3,2,1,0:T(4,128)S(1)}, u32[]{:S(2)}, u32[]{:S(2)}) collective-permute-start(f32[2,64,4,128]{3,2,1,0:T(4,128)} %get-tuple-element.201), channel_id=1, source_target_pairs={{0,1},{2,3},{4,5},{6,7},{8,9},{10,11},{12,13},{14,15},{1,4},{3,6},... | collective-permute-start | bytes 786440 | tf_op jit(solution)/shard_map/while/body/eval_jaxpr/ppermute | solution.py:169
  483.9 14.3 %collective-permute-start.4 = (f32[2,64,4,128]{3,2,1,0:T(4,128)}, f32[2,64,4,128]{3,2,1,0:T(4,128)S(1)}, u32[]{:S(2)}, u32[]{:S(2)}) collective-permute-start(f32[2,64,4,128]{3,2,1,0:T(4,128)} %get-tuple-element.207), channel_id=1, source_target_pairs={{0,1},{2,3},{4,5},{6,7},{8,9},{10,11},{12,13},{14,15},{1,4},{3,6},... | collective-permute-start | bytes 786440 | tf_op jit(solution)/shard_map/while/body/eval_jaxpr/ppermute | solution.py:169
  508.6 14.3 %collective-permute-start = (f32[2,64,4,128]{3,2,1,0:T(4,128)}, f32[2,64,4,128]{3,2,1,0:T(4,128)S(1)}, u32[]{:S(2)}, u32[]{:S(2)}) collective-permute-start(f32[2,64,4,128]{3,2,1,0:T(4,128)} %get-tuple-element.201), channel_id=1, source_target_pairs={{0,1},{2,3},{4,5},{6,7},{8,9},{10,11},{12,13},{14,15},{1,4},{3,6},... | collective-permute-start | bytes 786440 | tf_op jit(solution)/shard_map/while/body/eval_jaxpr/ppermute | solution.py:169
  533.3 14.3 %collective-permute-start.4 = (f32[2,64,4,128]{3,2,1,0:T(4,128)}, f32[2,64,4,128]{3,2,1,0:T(4,128)S(1)}, u32[]{:S(2)}, u32[]{:S(2)}) collective-permute-start(f32[2,64,4,128]{3,2,1,0:T(4,128)} %get-tuple-element.207), channel_id=1, source_target_pairs={{0,1},{2,3},{4,5},{6,7},{8,9},{10,11},{12,13},{14,15},{1,4},{3,6},... | collective-permute-start | bytes 786440 | tf_op jit(solution)/shard_map/while/body/eval_jaxpr/ppermute | solution.py:169
  557.9 14.3 %collective-permute-start = (f32[2,64,4,128]{3,2,1,0:T(4,128)}, f32[2,64,4,128]{3,2,1,0:T(4,128)S(1)}, u32[]{:S(2)}, u32[]{:S(2)}) collective-permute-start(f32[2,64,4,128]{3,2,1,0:T(4,128)} %get-tuple-element.201), channel_id=1, source_target_pairs={{0,1},{2,3},{4,5},{6,7},{8,9},{10,11},{12,13},{14,15},{1,4},{3,6},... | collective-permute-start | bytes 786440 | tf_op jit(solution)/shard_map/while/body/eval_jaxpr/ppermute | solution.py:169
  607.3 16.4 %collective-permute-start.30 = (f32[64,8,128]{2,1,0:T(8,128)S(1)}, f32[64,8,128]{2,1,0:T(8,128)S(1)}, u32[]{:S(2)}, u32[]{:S(2)}) collective-permute-start(f32[64,8,128]{2,1,0:T(8,128)S(1)} %get-tuple-element.143), channel_id=1, source_target_pairs={{2,0},{3,2},{6,4},{7,6},{10,8},{11,10},{14,12},{15,14},{18,16},{19... | collective-permute-start | bytes 786440 | tf_op jit(solution)/shard_map/ppermute | solution.py:157
  614.3 22.9 %collective-permute-start.24 = (f32[2,64,8,128]{3,2,1,0:T(8,128)}, f32[2,64,8,128]{3,2,1,0:T(8,128)S(1)}, u32[]{:S(2)}, u32[]{:S(2)}) collective-permute-start(f32[2,64,8,128]{3,2,1,0:T(8,128)} %get-tuple-element.135), channel_id=1, source_target_pairs={{0,0},{1,2},{4,4},{5,6},{8,8},{9,10},{12,12},{13,14},{16,16},{17,1... | collective-permute-start | bytes 1572872 | tf_op jit(solution)/shard_map/ppermute | solution.py:157
  617.0 23.3 %collective-permute-start.26 = (f32[2,64,8,128]{3,2,1,0:T(8,128)}, f32[2,64,8,128]{3,2,1,0:T(8,128)S(1)}, u32[]{:S(2)}, u32[]{:S(2)}) collective-permute-start(f32[2,64,8,128]{3,2,1,0:T(8,128)} %get-tuple-element.135), channel_id=1, source_target_pairs={{2,0},{3,2},{6,4},{7,6},{10,8},{11,10},{14,12},{15,14},{18,16},{19... | collective-permute-start | bytes 1572872 | tf_op jit(solution)/shard_map/ppermute | solution.py:157
  618.3 20.2 %collective-permute-start.25 = (f32[2,64,8,128]{3,2,1,0:T(8,128)}, f32[2,64,8,128]{3,2,1,0:T(8,128)}, u32[]{:S(2)}, u32[]{:S(2)}) collective-permute-start(f32[2,64,8,128]{3,2,1,0:T(8,128)} %get-tuple-element.134), channel_id=1, source_target_pairs={{0,1},{1,3},{4,5},{5,7},{8,9},{9,11},{12,13},{13,15},{16,17},{17,1... | collective-permute-start | bytes 1572872 | tf_op jit(solution)/shard_map/ppermute | solution.py:157
  623.7 17.4 %collective-permute-start.27 = (f32[2,64,8,128]{3,2,1,0:T(8,128)}, f32[2,64,8,128]{3,2,1,0:T(8,128)S(1)}, u32[]{:S(2)}, u32[]{:S(2)}) collective-permute-start(f32[2,64,8,128]{3,2,1,0:T(8,128)} %get-tuple-element.134), channel_id=1, source_target_pairs={{2,1},{3,3},{6,5},{7,7},{10,9},{11,11},{14,13},{15,15},{18,17},{19... | collective-permute-start | bytes 1572872 | tf_op jit(solution)/shard_map/ppermute | solution.py:157
  624.4 17.8 %collective-permute-start.20 = (f32[2,64,8,128]{3,2,1,0:T(8,128)}, f32[2,64,8,128]{3,2,1,0:T(8,128)S(1)}, u32[]{:S(2)}, u32[]{:S(2)}) collective-permute-start(f32[2,64,8,128]{3,2,1,0:T(8,128)} %get-tuple-element.137), channel_id=1, source_target_pairs={{0,0},{1,2},{4,4},{5,6},{8,8},{9,10},{12,12},{13,14},{16,16},{17,1... | collective-permute-start | bytes 1572872 | tf_op jit(solution)/shard_map/ppermute | solution.py:157
  627.0 25.3 %all-to-all-start.1 = ((f32[128,1,8,128]{3,2,1,0:T(8,128)}), f32[128,1,8,128]{3,2,1,0:T(8,128)S(1)}, u32[]{:S(2)}, u32[]{:S(2)}) async-start(f32[128,1,8,128]{3,2,1,0:T(8,128)} %maximum_multiply_fusion), calls=%async_computation.1 | async-start | bytes 1048576 | tf_op jit(solution)/shard_map/all_to_all | solution.py:258
  (139 other events, 806.7 us)

commit v5 on v3

--- a/solution.py
+++ b/solution.py
@@ -12,35 +12,54 @@
 XOFF = 8
 
 
-def with_halo(cells, axis, dim, width):
+def trade_halos(head, tail, axis):
     count = lax.axis_size(axis)
     ends = count - 1
-    head = lax.slice_in_dim(cells, 0, width, axis=dim)
-    tail = lax.slice_in_dim(cells, cells.shape[dim] - width, cells.shape[dim], axis=dim)
     low = lax.ppermute(tail, axis, [(i, (i + 1) % count) for i in range(ends)])
     high = lax.ppermute(head, axis, [((i + 1) % count, i) for i in range(ends)])
     return low, high
 
 
 def step_kernel(
-    moment_ref, cur_ref, prev_ref, s_ref, img_ref, xlo_ref, xhi_ref, inj_ref, out_ref, imgo_ref, ey_ref, hx_ref
+    moment_ref,
+    cur_ref,
+    prev_ref,
+    s_ref,
+    img_ref,
+    xlo_ref,
+    xhi_ref,
+    inj_ref,
+    out_ref,
+    imgo_ref,
+    head_ref,
+    tail_ref,
+    ey_ref,
+    hx_ref,
 ):
     comps, block_y, block_x, depth_z = cur_ref.shape
-    zeros_y = jnp.zeros((comps, HALO, block_x, depth_z), jnp.float32)
-    ey_ref[:, 0:HALO] = zeros_y
-    ey_ref[:, HALO + block_y : 2 * HALO + block_y] = zeros_y
-    ey_ref[:, HALO : HALO + block_y] = cur_ref[...]
+    chunk = prev_ref.shape[1]
+    index = pl.program_id(0)
+
+    @pl.when(index == 0)
+    def _():
+        zeros_y = jnp.zeros((comps, HALO, block_x, depth_z), jnp.float32)
+        ey_ref[:, 0:HALO] = zeros_y
+        ey_ref[:, HALO + block_y : 2 * HALO + block_y] = zeros_y
+        ey_ref[:, HALO : HALO + block_y] = cur_ref[...]
+
     hx_ref[0, :, :, block_x - HALO : block_x, :] = xlo_ref[...]
     hx_ref[1, :, :, 0:HALO, :] = xhi_ref[...]
     lane = lax.broadcasted_iota(jnp.int32, (block_x, depth_z), 1)
     sub = lax.broadcasted_iota(jnp.int32, (block_x, depth_z), 0)
-
-    def row(y, carry):
+    base = index * chunk
+
+    def row(r, carry):
+        y = base + r
         done = []
         for c in range(comps):
             ctr = ey_ref[c, HALO + y]
-            left = hx_ref[0, c, y]
-            right = hx_ref[1, c, y]
+            left = hx_ref[0, c, r]
+            right = hx_ref[1, c, r]
             acc = center_weight * ctr
             for m in range(1, HALO + 1):
                 ahead = pltpu.roll(jnp.where(sub >= m, ctr, right), block_x - m, 0)
@@ -51,52 +70,66 @@
                 down = jnp.where(lane >= m, pltpu.roll(ctr, m, 1), 0.0)
                 b = b + up + down
                 acc = acc + stencil_weights[m - 1] * b
-            lap = acc + inj_ref[c, y]
-            upd = 2.0 * ctr - prev_ref[c, y] + s_ref[y] * lap
-            out_ref[c, y] = upd
+            lap = acc + inj_ref[c, r]
+            upd = 2.0 * ctr - prev_ref[c, r] + s_ref[r] * lap
+            out_ref[c, r] = upd
+            head_ref[c, r] = upd[0:HALO]
+            tail_ref[c, r] = upd[block_x - HALO : block_x]
             done.append(upd)
-        imgo_ref[y] = img_ref[y] + done[0] * done[1]
+        imgo_ref[r] = img_ref[r] + done[0] * done[1]
         return carry
 
-    lax.fori_loop(0, block_y, row, 0, unroll=2)
-
-
-def step_call(moment, cur, prev, s, img, xlo, xhi, planes):
+    lax.fori_loop(0, chunk, row, 0, unroll=2)
+
+
+def step_call(moment, cur, prev, s, img, xlo, xhi, planes, chunks=8):
     comps, block_y, block_x, depth_z = cur.shape
+    chunk = block_y // chunks
 
     def whole(shape):
         return pl.BlockSpec(shape, lambda i, k: (0,) * len(shape))
 
+    def rows(shape):
+        return pl.BlockSpec(shape, lambda i, k: (0, i) + (0,) * (len(shape) - 2))
+
+    field_rows = rows((comps, chunk, block_x, depth_z))
+    halo_rows = rows((comps, chunk, HALO, depth_z))
+    flat_rows = pl.BlockSpec((chunk, block_x, depth_z), lambda i, k: (i, 0, 0))
     plane_spec = pl.BlockSpec(
-        (None, comps, block_y, block_x, depth_z), lambda i, k: (k[0], 0, 0, 0, 0)
+        (None, comps, chunk, block_x, depth_z), lambda i, k: (k[0], 0, i, 0, 0)
     )
     grid_spec = pltpu.PrefetchScalarGridSpec(
         num_scalar_prefetch=1,
-        grid=(1,),
+        grid=(chunks,),
         in_specs=[
             whole(cur.shape),
-            whole(prev.shape),
-            whole(s.shape),
-            whole(img.shape),
-            whole(xlo.shape),
-            whole(xhi.shape),
+            field_rows,
+            flat_rows,
+            flat_rows,
+            halo_rows,
+            halo_rows,
             plane_spec,
         ],
-        out_specs=(whole(cur.shape), whole(img.shape)),
+        out_specs=(field_rows, flat_rows, halo_rows, halo_rows),
         scratch_shapes=[
             pltpu.VMEM((comps, block_y + 2 * HALO, block_x, depth_z), jnp.float32),
-            pltpu.VMEM((2, comps, block_y, block_x, depth_z), jnp.float32),
+            pltpu.VMEM((2, comps, chunk, block_x, depth_z), jnp.float32),
         ],
     )
+    halo_shape = jax.ShapeDtypeStruct((comps, block_y, HALO, depth_z), jnp.float32)
     return pl.pallas_call(
         step_kernel,
         out_shape=(
             jax.ShapeDtypeStruct(cur.shape, jnp.float32),
             jax.ShapeDtypeStruct(img.shape, jnp.float32),
+            halo_shape,
+            halo_shape,
         ),
         grid_spec=grid_spec,
         input_output_aliases={2: 0, 4: 1},
-        compiler_params=pltpu.CompilerParams(vmem_limit_bytes=56 * 1024 * 1024),
+        compiler_params=pltpu.CompilerParams(
+            dimension_semantics=("arbitrary",), vmem_limit_bytes=48 * 1024 * 1024
+        ),
         cost_estimate=pl.CostEstimate(
             flops=60 * cur.size, bytes_accessed=4 * 6 * cur.size, transcendentals=0
         ),
@@ -116,13 +149,10 @@
     return (rows_y, places.astype(jnp.float32))
 
 
-def spread_points(tables, amounts, depth_z):
+def spread_points(tables, amounts):
     rows_y, places = tables
-    steps = amounts.shape[0]
     weighted = places[:, None, :] * jnp.transpose(amounts)[:, :, None]
-    plane = jnp.einsum("ny,nsc->syc", rows_y, weighted, precision=lax.Precision.HIGHEST)
-    plane = plane.reshape(steps, rows_y.shape[1], places.shape[1] // 4, 4)
-    return jnp.pad(plane, ((0, 0), (0, 0), (0, 0), (0, depth_z - 4)))
+    return jnp.einsum("ny,nsc->syc", rows_y, weighted, precision=lax.Precision.HIGHEST)
 
 
 def shards(older_fields, fields_now, velocity, aperture, source_pos, wavelet, receiver_pos, traces):
@@ -143,28 +173,33 @@
     receiver_core = point_tables(receiver_pos, x_anchor, cells_x, depth_y)
 
     planes = jnp.stack(
-        [
-            spread_points(source_core, wavelet, depth_z),
-            spread_points(receiver_core, traces, depth_z),
-        ],
-        axis=1,
-    )
-
-    def advance(moment, previous, current, image_acc):
-        low, high = with_halo(current, "dom", 2, HALO)
+        [spread_points(source_core, wavelet), spread_points(receiver_core, traces)], axis=1
+    )
+    planes = planes.reshape(steps_total, 2, depth_y, cells_x, 4)
+    planes = jnp.pad(planes, ((0, 0), (0, 0), (0, 0), (0, 0), (0, depth_z - 4)))
+
+    def advance(moment, previous, current, head, tail, image_acc):
+        low, high = trade_halos(head, tail, "dom")
         return step_call(moment, current, previous, speed_sq, image_acc, low, high, planes)
 
     def pair(index, state_carry):
-        previous, current, image_acc = state_carry
-        first, image_acc = advance(2 * index, previous, current, image_acc)
-        second, image_acc = advance(2 * index + 1, current, first, image_acc)
-        return (first, second, image_acc)
-
-    previous, current, image_acc = lax.fori_loop(
-        0, steps_total // 2, pair, (older_fields, fields_now, image_zero)
-    )
+        previous, current, head, tail, image_acc = state_carry
+        first, image_acc, head, tail = advance(2 * index, previous, current, head, tail, image_acc)
+        second, image_acc, head, tail = advance(2 * index + 1, current, first, head, tail, image_acc)
+        return (first, second, head, tail, image_acc)
+
+    start = (
+        older_fields,
+        fields_now,
+        fields_now[:, :, :HALO],
+        fields_now[:, :, cells_x - HALO :],
+        image_zero,
+    )
+    previous, current, head, tail, image_acc = lax.fori_loop(0, steps_total // 2, pair, start)
     if steps_total % 2:
-        last, image_acc = advance(steps_total - 1, previous, current, image_acc)
+        last, image_acc, head, tail = advance(
+            steps_total - 1, previous, current, head, tail, image_acc
+        )
         previous, current = current, last
     image_acc = image_acc * (1.0 / steps_total)
     outgoing = image_acc.reshape(depth_y, 1, cells_x, depth_z)

time: 591 us -> 577 us (0.976)
  Pallas kernels: 178 us -> 200 us
  local copies, waits for them, and re-layouts: 50.6 us -> 34.4 us
  other arithmetic: 22.4 us -> 7.07 us
  starting transfers between devices: 230 us -> 217 us
  waiting for transfers between devices: 68.7 us -> 75.3 us
    pallas_call x20, Pallas kernels: 178 us -> 200 us  [step_call(): pl.pallas_call(step_kernel, out_shape=(jax.ShapeDtypeStruct(cur.shape, jn...]
    slice x20 -> x1, local copies, waits for them, and re-layouts: 22.5 us -> 1.72 us  [shards(): fields_now[:, :, cells_x - HALO:]]
    another operation x1, other arithmetic: 16.2 us -> 0.06 us  [shards(): jnp.stack([spread_points(source_core, wavelet), spread_points(receiver_co...]
    pad x0 -> x1, local copies, waits for them, and re-layouts: none -> 15.5 us  [shards(): planes = jnp.pad(planes, ((0, 0), (0, 0), (0, 0), (0, 0), (0, depth_z - 4)))]
    another operation x1 -> x2, local copies, waits for them, and re-layouts: 15.5 us -> 0.05 us  [shards(): jnp.stack([spread_points(source_core, wavelet), spread_points(receiver_co...]
    unnamed x16 -> x7, local copies, waits for them, and re-layouts: 0.05 us -> 14.7 us
    ppermute x40, starting transfers between devices: 223 us -> 210 us  [the longest x20 184 us: trade_halos(): low = lax.ppermute(tail, axis, [(i, (i + 1) % count) for i in range(ends)])]
    reshape x2 -> x0, local copies, waits for them, and re-layouts: 10.9 us -> none  [spread_points(): plane = plane.reshape(steps, rows_y.shape[1], places.shape[1] // 4, 4)]
  transfers between devices with their start and end apart: 41 -> 41, of which waited for: 20 -> 40; matrix products, arithmetic and copies ran while one was open for 10% -> 8% of each run, Pallas kernels for 0% -> 0%
where the time goes in v5:
time: 577 us; the launch traced here: 572 us
  starting transfers between devices  217 us (38%)
  Pallas kernels  200 us (35%)
  waiting for transfers between devices  75.3 us (13%)
  local copies, waits for them, and re-layouts  34.4 us (6%)
  blocking collectives  24.5 us (4%)
  matrix products  12.8 us (2%)
  other arithmetic  7.07 us (1%)
    pallas_call x20, Pallas kernels, step_call(): pl.pallas_call(step_kernel, out_shape=(jax.ShapeDtypeStruct(cur.shape, jn...  200 us
    ppermute x20, starting transfers between devices, trade_halos(): low = lax.ppermute(tail, axis, [(i, (i + 1) % count) for i in range(ends)])  184 us
    ppermute x20, waiting for transfers between devices, trade_halos(): high = lax.ppermute(head, axis, [((i + 1) % count, i) for i in range(ends)])  71.6 us
    ppermute x20, starting transfers between devices, trade_halos(): high = lax.ppermute(head, axis, [((i + 1) % count, i) for i in range(ends)])  25.8 us
    all_to_all x1, blocking collectives, shards(): lax.all_to_all(outgoing, 'dom', split_axis=0, concat_axis=1, tiled=True)  24.5 us
    pad x1, local copies, waits for them, and re-layouts, shards(): planes = jnp.pad(planes, ((0, 0), (0, 0), (0, 0), (0, 0), (0, depth_z - 4)))  15.5 us
    unnamed x7, local copies, waits for them, and re-layouts  14.7 us
    dot_general x2, matrix products, spread_points(): jnp.einsum('ny,nsc->syc', rows_y, weighted, precision=lax.Precision.HIGHEST)  12.1 us
  transfers between devices with their start and end apart: 41, of which 40 were waited for; matrix products, arithmetic and copies ran while one was open for 8% of the time, Pallas kernels for 0%

profile of v5, /device:TPU:0, one launch (start us, length us, event | category | flops | bytes accessed | tf_op | source)
XLA Modules:
  0.0 572.2 jit_solution(4767483976746285519)
XLA Ops:
  17.8 11.6 %fusion = f32[20,32,128]{2,1,0:T(8,128)S(1)} fusion(f32[8192,20]{0,1:T(8,128)} %bitcast.63, f32[8192,32]{0,1:T(8,128)S(1)} %fusion.8, s32[8192]{0:T(1024)S(1)} %bitcast.61), kind=kOutput, calls=%fused_computation.1 | convolution fusion | flops 8059355136 | bytes 2064384 | tf_op jit(solution)/shard_map/ny,nsc->syc/dot_general | solution.py:155
  32.4 10.1 %copy.30 = f32[20,2,128,8,4]{4,3,2,1,0:T(8,128)} copy(f32[20,2,128,8,4]{2,3,4,1,0:T(8,128)S(1)} %pad_maximum_fusion) | data formatting | bytes 1310720
  42.6 15.5 %pad.4.clone = f32[20,2,128,8,128]{4,3,2,1,0:T(8,128)} pad(f32[20,2,128,8,4]{4,3,2,1,0:T(8,128)} %copy.30, f32[]{:T(128)} %constant.44.clone.1), padding=0_0x0_0x0_0x0_0x0_124 | pad | bytes 21626884 | tf_op jit(solution)/shard_map/jit(_pad)/pad | solution.py:179
  60.7 485.3 %while.21 = (s32[]{:T(128)}, f32[2,128,8,128]{3,2,1,0:T(8,128)}, f32[2,128,8,128]{3,2,1,0:T(8,128)}, f32[2,128,4,128]{3,2,1,0:T(4,128)S(1)}, f32[2,128,4,128]{3,...) while((s32[]{:T(128)}, f32[2,128,8,128]{3,2,1,0:T(8,128)}, ...), condition=%wide.region_1.2_spmd, body=%wide.region_0.1_spmd.sunk | while | flops 31457284 | bytes 20971804 | solution.py:198
  68.0 10.0 %eval_jaxpr.10 = (f32[2,128,8,128]{3,2,1,0:T(8,128)}, f32[128,8,128]{2,1,0:T(8,128)S(1)}, f32[2,128,4,128]{3,2,1,0:T(4,128)S(1)}, f32[2,128,4,128]{3,2,1,0:T(4,128)S(1)}) custom-call(s32[1]{0:T(128)} %bitcast.52.moment_ref, f32[2,128,8,128]{3,2,1,0:T(8,128)} %get-tuple-element.259.cur_ref.prev_ref, ...), custom_call_target="tpu_custom_call", output_to_operand_aliasing={{0}: (2, {}), {1}: (4, {})} | custom-call | flops 15728640 | bytes 6291456 | tf_op jit(solution)/shard_map/while/body/eval_jaxpr/pallas_call | solution.py:120
  78.0 10.3 %collective-permute-start.2 = (f32[2,128,4,128]{3,2,1,0:T(4,128)S(1)}, f32[2,128,4,128]{3,2,1,0:T(4,128)S(1)}, u32[]{:S(2)}, u32[]{:S(2)}) collective-permute-start(f32[2,128,4,128]{3,2,1,0:T(4,128)S(1)} %get-tuple-element.241), channel_id=1, source_target_pairs={{0,1},{1,2},{2,3},{3,4},{4,5},{5,6},{6,7},{7,8},{8,9},{9,10},{10,1... | collective-permute-start | bytes 1572872 | tf_op jit(solution)/shard_map/while/body/eval_jaxpr/ppermute | solution.py:18
  94.1 10.0 %eval_jaxpr.11 = (f32[2,128,8,128]{3,2,1,0:T(8,128)}, f32[128,8,128]{2,1,0:T(8,128)S(1)}, f32[2,128,4,128]{3,2,1,0:T(4,128)S(1)}, f32[2,128,4,128]{3,2,1,0:T(4,128)S(1)}) custom-call(s32[1]{0:T(128)} %bitcast.53.moment_ref, f32[2,128,8,128]{3,2,1,0:T(8,128)} %get-tuple-element.268.cur_ref, ...), custom_call_target="tpu_custom_call", output_to_operand_aliasing={{0}: (2, {}), {1}: (4, {})} | custom-call | flops 15728640 | bytes 6291456 | tf_op jit(solution)/shard_map/while/body/eval_jaxpr/pallas_call | solution.py:120
  104.1 10.3 %collective-permute-start = (f32[2,128,4,128]{3,2,1,0:T(4,128)S(1)}, f32[2,128,4,128]{3,2,1,0:T(4,128)S(1)}, u32[]{:S(2)}, u32[]{:S(2)}) collective-permute-start(f32[2,128,4,128]{3,2,1,0:T(4,128)S(1)} %get-tuple-element.261), channel_id=1, source_target_pairs={{0,1},{1,2},{2,3},{3,4},{4,5},{5,6},{6,7},{7,8},{8,9},{9,10},{10,1... | collective-permute-start | bytes 1572872 | tf_op jit(solution)/shard_map/while/body/eval_jaxpr/ppermute | solution.py:18
  120.2 10.0 %eval_jaxpr.10 = (f32[2,128,8,128]{3,2,1,0:T(8,128)}, f32[128,8,128]{2,1,0:T(8,128)S(1)}, f32[2,128,4,128]{3,2,1,0:T(4,128)S(1)}, f32[2,128,4,128]{3,2,1,0:T(4,128)S(1)}) custom-call(s32[1]{0:T(128)} %bitcast.52.moment_ref, f32[2,128,8,128]{3,2,1,0:T(8,128)} %get-tuple-element.259.cur_ref.prev_ref, ...), custom_call_target="tpu_custom_call", output_to_operand_aliasing={{0}: (2, {}), {1}: (4, {})} | custom-call | flops 15728640 | bytes 6291456 | tf_op jit(solution)/shard_map/while/body/eval_jaxpr/pallas_call | solution.py:120
  130.2 10.3 %collective-permute-start.2 = (f32[2,128,4,128]{3,2,1,0:T(4,128)S(1)}, f32[2,128,4,128]{3,2,1,0:T(4,128)S(1)}, u32[]{:S(2)}, u32[]{:S(2)}) collective-permute-start(f32[2,128,4,128]{3,2,1,0:T(4,128)S(1)} %get-tuple-element.241), channel_id=1, source_target_pairs={{0,1},{1,2},{2,3},{3,4},{4,5},{5,6},{6,7},{7,8},{8,9},{9,10},{10,1... | collective-permute-start | bytes 1572872 | tf_op jit(solution)/shard_map/while/body/eval_jaxpr/ppermute | solution.py:18
  146.3 10.0 %eval_jaxpr.11 = (f32[2,128,8,128]{3,2,1,0:T(8,128)}, f32[128,8,128]{2,1,0:T(8,128)S(1)}, f32[2,128,4,128]{3,2,1,0:T(4,128)S(1)}, f32[2,128,4,128]{3,2,1,0:T(4,128)S(1)}) custom-call(s32[1]{0:T(128)} %bitcast.53.moment_ref, f32[2,128,8,128]{3,2,1,0:T(8,128)} %get-tuple-element.268.cur_ref, ...), custom_call_target="tpu_custom_call", output_to_operand_aliasing={{0}: (2, {}), {1}: (4, {})} | custom-call | flops 15728640 | bytes 6291456 | tf_op jit(solution)/shard_map/while/body/eval_jaxpr/pallas_call | solution.py:120
  156.3 10.3 %collective-permute-start = (f32[2,128,4,128]{3,2,1,0:T(4,128)S(1)}, f32[2,128,4,128]{3,2,1,0:T(4,128)S(1)}, u32[]{:S(2)}, u32[]{:S(2)}) collective-permute-start(f32[2,128,4,128]{3,2,1,0:T(4,128)S(1)} %get-tuple-element.261), channel_id=1, source_target_pairs={{0,1},{1,2},{2,3},{3,4},{4,5},{5,6},{6,7},{7,8},{8,9},{9,10},{10,1... | collective-permute-start | bytes 1572872 | tf_op jit(solution)/shard_map/while/body/eval_jaxpr/ppermute | solution.py:18
  172.4 10.0 %eval_jaxpr.10 = (f32[2,128,8,128]{3,2,1,0:T(8,128)}, f32[128,8,128]{2,1,0:T(8,128)S(1)}, f32[2,128,4,128]{3,2,1,0:T(4,128)S(1)}, f32[2,128,4,128]{3,2,1,0:T(4,128)S(1)}) custom-call(s32[1]{0:T(128)} %bitcast.52.moment_ref, f32[2,128,8,128]{3,2,1,0:T(8,128)} %get-tuple-element.259.cur_ref.prev_ref, ...), custom_call_target="tpu_custom_call", output_to_operand_aliasing={{0}: (2, {}), {1}: (4, {})} | custom-call | flops 15728640 | bytes 6291456 | tf_op jit(solution)/shard_map/while/body/eval_jaxpr/pallas_call | solution.py:120
  182.4 10.3 %collective-permute-start.2 = (f32[2,128,4,128]{3,2,1,0:T(4,128)S(1)}, f32[2,128,4,128]{3,2,1,0:T(4,128)S(1)}, u32[]{:S(2)}, u32[]{:S(2)}) collective-permute-start(f32[2,128,4,128]{3,2,1,0:T(4,128)S(1)} %get-tuple-element.241), channel_id=1, source_target_pairs={{0,1},{1,2},{2,3},{3,4},{4,5},{5,6},{6,7},{7,8},{8,9},{9,10},{10,1... | collective-permute-start | bytes 1572872 | tf_op jit(solution)/shard_map/while/body/eval_jaxpr/ppermute | solution.py:18
  198.5 10.0 %eval_jaxpr.11 = (f32[2,128,8,128]{3,2,1,0:T(8,128)}, f32[128,8,128]{2,1,0:T(8,128)S(1)}, f32[2,128,4,128]{3,2,1,0:T(4,128)S(1)}, f32[2,128,4,128]{3,2,1,0:T(4,128)S(1)}) custom-call(s32[1]{0:T(128)} %bitcast.53.moment_ref, f32[2,128,8,128]{3,2,1,0:T(8,128)} %get-tuple-element.268.cur_ref, ...), custom_call_target="tpu_custom_call", output_to_operand_aliasing={{0}: (2, {}), {1}: (4, {})} | custom-call | flops 15728640 | bytes 6291456 | tf_op jit(solution)/shard_map/while/body/eval_jaxpr/pallas_call | solution.py:120
  208.5 10.3 %collective-permute-start = (f32[2,128,4,128]{3,2,1,0:T(4,128)S(1)}, f32[2,128,4,128]{3,2,1,0:T(4,128)S(1)}, u32[]{:S(2)}, u32[]{:S(2)}) collective-permute-start(f32[2,128,4,128]{3,2,1,0:T(4,128)S(1)} %get-tuple-element.261), channel_id=1, source_target_pairs={{0,1},{1,2},{2,3},{3,4},{4,5},{5,6},{6,7},{7,8},{8,9},{9,10},{10,1... | collective-permute-start | bytes 1572872 | tf_op jit(solution)/shard_map/while/body/eval_jaxpr/ppermute | solution.py:18
  224.6 10.0 %eval_jaxpr.10 = (f32[2,128,8,128]{3,2,1,0:T(8,128)}, f32[128,8,128]{2,1,0:T(8,128)S(1)}, f32[2,128,4,128]{3,2,1,0:T(4,128)S(1)}, f32[2,128,4,128]{3,2,1,0:T(4,128)S(1)}) custom-call(s32[1]{0:T(128)} %bitcast.52.moment_ref, f32[2,128,8,128]{3,2,1,0:T(8,128)} %get-tuple-element.259.cur_ref.prev_ref, ...), custom_call_target="tpu_custom_call", output_to_operand_aliasing={{0}: (2, {}), {1}: (4, {})} | custom-call | flops 15728640 | bytes 6291456 | tf_op jit(solution)/shard_map/while/body/eval_jaxpr/pallas_call | solution.py:120
  234.6 9.9 %collective-permute-start.2 = (f32[2,128,4,128]{3,2,1,0:T(4,128)S(1)}, f32[2,128,4,128]{3,2,1,0:T(4,128)S(1)}, u32[]{:S(2)}, u32[]{:S(2)}) collective-permute-start(f32[2,128,4,128]{3,2,1,0:T(4,128)S(1)} %get-tuple-element.241), channel_id=1, source_target_pairs={{0,1},{1,2},{2,3},{3,4},{4,5},{5,6},{6,7},{7,8},{8,9},{9,10},{10,1... | collective-permute-start | bytes 1572872 | tf_op jit(solution)/shard_map/while/body/eval_jaxpr/ppermute | solution.py:18
  250.3 10.0 %eval_jaxpr.11 = (f32[2,128,8,128]{3,2,1,0:T(8,128)}, f32[128,8,128]{2,1,0:T(8,128)S(1)}, f32[2,128,4,128]{3,2,1,0:T(4,128)S(1)}, f32[2,128,4,128]{3,2,1,0:T(4,128)S(1)}) custom-call(s32[1]{0:T(128)} %bitcast.53.moment_ref, f32[2,128,8,128]{3,2,1,0:T(8,128)} %get-tuple-element.268.cur_ref, ...), custom_call_target="tpu_custom_call", output_to_operand_aliasing={{0}: (2, {}), {1}: (4, {})} | custom-call | flops 15728640 | bytes 6291456 | tf_op jit(solution)/shard_map/while/body/eval_jaxpr/pallas_call | solution.py:120
  274.5 10.0 %eval_jaxpr.10 = (f32[2,128,8,128]{3,2,1,0:T(8,128)}, f32[128,8,128]{2,1,0:T(8,128)S(1)}, f32[2,128,4,128]{3,2,1,0:T(4,128)S(1)}, f32[2,128,4,128]{3,2,1,0:T(4,128)S(1)}) custom-call(s32[1]{0:T(128)} %bitcast.52.moment_ref, f32[2,128,8,128]{3,2,1,0:T(8,128)} %get-tuple-element.259.cur_ref.prev_ref, ...), custom_call_target="tpu_custom_call", output_to_operand_aliasing={{0}: (2, {}), {1}: (4, {})} | custom-call | flops 15728640 | bytes 6291456 | tf_op jit(solution)/shard_map/while/body/eval_jaxpr/pallas_call | solution.py:120
  297.9 10.0 %eval_jaxpr.11 = (f32[2,128,8,128]{3,2,1,0:T(8,128)}, f32[128,8,128]{2,1,0:T(8,128)S(1)}, f32[2,128,4,128]{3,2,1,0:T(4,128)S(1)}, f32[2,128,4,128]{3,2,1,0:T(4,128)S(1)}) custom-call(s32[1]{0:T(128)} %bitcast.53.moment_ref, f32[2,128,8,128]{3,2,1,0:T(8,128)} %get-tuple-element.268.cur_ref, ...), custom_call_target="tpu_custom_call", output_to_operand_aliasing={{0}: (2, {}), {1}: (4, {})} | custom-call | flops 15728640 | bytes 6291456 | tf_op jit(solution)/shard_map/while/body/eval_jaxpr/pallas_call | solution.py:120
  322.1 10.0 %eval_jaxpr.10 = (f32[2,128,8,128]{3,2,1,0:T(8,128)}, f32[128,8,128]{2,1,0:T(8,128)S(1)}, f32[2,128,4,128]{3,2,1,0:T(4,128)S(1)}, f32[2,128,4,128]{3,2,1,0:T(4,128)S(1)}) custom-call(s32[1]{0:T(128)} %bitcast.52.moment_ref, f32[2,128,8,128]{3,2,1,0:T(8,128)} %get-tuple-element.259.cur_ref.prev_ref, ...), custom_call_target="tpu_custom_call", output_to_operand_aliasing={{0}: (2, {}), {1}: (4, {})} | custom-call | flops 15728640 | bytes 6291456 | tf_op jit(solution)/shard_map/while/body/eval_jaxpr/pallas_call | solution.py:120
  345.5 10.0 %eval_jaxpr.11 = (f32[2,128,8,128]{3,2,1,0:T(8,128)}, f32[128,8,128]{2,1,0:T(8,128)S(1)}, f32[2,128,4,128]{3,2,1,0:T(4,128)S(1)}, f32[2,128,4,128]{3,2,1,0:T(4,128)S(1)}) custom-call(s32[1]{0:T(128)} %bitcast.53.moment_ref, f32[2,128,8,128]{3,2,1,0:T(8,128)} %get-tuple-element.268.cur_ref, ...), custom_call_target="tpu_custom_call", output_to_operand_aliasing={{0}: (2, {}), {1}: (4, {})} | custom-call | flops 15728640 | bytes 6291456 | tf_op jit(solution)/shard_map/while/body/eval_jaxpr/pallas_call | solution.py:120
  369.7 10.0 %eval_jaxpr.10 = (f32[2,128,8,128]{3,2,1,0:T(8,128)}, f32[128,8,128]{2,1,0:T(8,128)S(1)}, f32[2,128,4,128]{3,2,1,0:T(4,128)S(1)}, f32[2,128,4,128]{3,2,1,0:T(4,128)S(1)}) custom-call(s32[1]{0:T(128)} %bitcast.52.moment_ref, f32[2,128,8,128]{3,2,1,0:T(8,128)} %get-tuple-element.259.cur_ref.prev_ref, ...), custom_call_target="tpu_custom_call", output_to_operand_aliasing={{0}: (2, {}), {1}: (4, {})} | custom-call | flops 15728640 | bytes 6291456 | tf_op jit(solution)/shard_map/while/body/eval_jaxpr/pallas_call | solution.py:120
  393.1 10.0 %eval_jaxpr.11 = (f32[2,128,8,128]{3,2,1,0:T(8,128)}, f32[128,8,128]{2,1,0:T(8,128)S(1)}, f32[2,128,4,128]{3,2,1,0:T(4,128)S(1)}, f32[2,128,4,128]{3,2,1,0:T(4,128)S(1)}) custom-call(s32[1]{0:T(128)} %bitcast.53.moment_ref, f32[2,128,8,128]{3,2,1,0:T(8,128)} %get-tuple-element.268.cur_ref, ...), custom_call_target="tpu_custom_call", output_to_operand_aliasing={{0}: (2, {}), {1}: (4, {})} | custom-call | flops 15728640 | bytes 6291456 | tf_op jit(solution)/shard_map/while/body/eval_jaxpr/pallas_call | solution.py:120
  417.3 10.0 %eval_jaxpr.10 = (f32[2,128,8,128]{3,2,1,0:T(8,128)}, f32[128,8,128]{2,1,0:T(8,128)S(1)}, f32[2,128,4,128]{3,2,1,0:T(4,128)S(1)}, f32[2,128,4,128]{3,2,1,0:T(4,128)S(1)}) custom-call(s32[1]{0:T(128)} %bitcast.52.moment_ref, f32[2,128,8,128]{3,2,1,0:T(8,128)} %get-tuple-element.259.cur_ref.prev_ref, ...), custom_call_target="tpu_custom_call", output_to_operand_aliasing={{0}: (2, {}), {1}: (4, {})} | custom-call | flops 15728640 | bytes 6291456 | tf_op jit(solution)/shard_map/while/body/eval_jaxpr/pallas_call | solution.py:120
  440.8 10.0 %eval_jaxpr.11 = (f32[2,128,8,128]{3,2,1,0:T(8,128)}, f32[128,8,128]{2,1,0:T(8,128)S(1)}, f32[2,128,4,128]{3,2,1,0:T(4,128)S(1)}, f32[2,128,4,128]{3,2,1,0:T(4,128)S(1)}) custom-call(s32[1]{0:T(128)} %bitcast.53.moment_ref, f32[2,128,8,128]{3,2,1,0:T(8,128)} %get-tuple-element.268.cur_ref, ...), custom_call_target="tpu_custom_call", output_to_operand_aliasing={{0}: (2, {}), {1}: (4, {})} | custom-call | flops 15728640 | bytes 6291456 | tf_op jit(solution)/shard_map/while/body/eval_jaxpr/pallas_call | solution.py:120
  464.9 10.0 %eval_jaxpr.10 = (f32[2,128,8,128]{3,2,1,0:T(8,128)}, f32[128,8,128]{2,1,0:T(8,128)S(1)}, f32[2,128,4,128]{3,2,1,0:T(4,128)S(1)}, f32[2,128,4,128]{3,2,1,0:T(4,128)S(1)}) custom-call(s32[1]{0:T(128)} %bitcast.52.moment_ref, f32[2,128,8,128]{3,2,1,0:T(8,128)} %get-tuple-element.259.cur_ref.prev_ref, ...), custom_call_target="tpu_custom_call", output_to_operand_aliasing={{0}: (2, {}), {1}: (4, {})} | custom-call | flops 15728640 | bytes 6291456 | tf_op jit(solution)/shard_map/while/body/eval_jaxpr/pallas_call | solution.py:120
  488.4 10.0 %eval_jaxpr.11 = (f32[2,128,8,128]{3,2,1,0:T(8,128)}, f32[128,8,128]{2,1,0:T(8,128)S(1)}, f32[2,128,4,128]{3,2,1,0:T(4,128)S(1)}, f32[2,128,4,128]{3,2,1,0:T(4,128)S(1)}) custom-call(s32[1]{0:T(128)} %bitcast.53.moment_ref, f32[2,128,8,128]{3,2,1,0:T(8,128)} %get-tuple-element.268.cur_ref, ...), custom_call_target="tpu_custom_call", output_to_operand_aliasing={{0}: (2, {}), {1}: (4, {})} | custom-call | flops 15728640 | bytes 6291456 | tf_op jit(solution)/shard_map/while/body/eval_jaxpr/pallas_call | solution.py:120
  512.6 10.0 %eval_jaxpr.10 = (f32[2,128,8,128]{3,2,1,0:T(8,128)}, f32[128,8,128]{2,1,0:T(8,128)S(1)}, f32[2,128,4,128]{3,2,1,0:T(4,128)S(1)}, f32[2,128,4,128]{3,2,1,0:T(4,128)S(1)}) custom-call(s32[1]{0:T(128)} %bitcast.52.moment_ref, f32[2,128,8,128]{3,2,1,0:T(8,128)} %get-tuple-element.259.cur_ref.prev_ref, ...), custom_call_target="tpu_custom_call", output_to_operand_aliasing={{0}: (2, {}), {1}: (4, {})} | custom-call | flops 15728640 | bytes 6291456 | tf_op jit(solution)/shard_map/while/body/eval_jaxpr/pallas_call | solution.py:120
  536.0 10.0 %eval_jaxpr.11 = (f32[2,128,8,128]{3,2,1,0:T(8,128)}, f32[128,8,128]{2,1,0:T(8,128)S(1)}, f32[2,128,4,128]{3,2,1,0:T(4,128)S(1)}, f32[2,128,4,128]{3,2,1,0:T(4,128)S(1)}) custom-call(s32[1]{0:T(128)} %bitcast.53.moment_ref, f32[2,128,8,128]{3,2,1,0:T(8,128)} %get-tuple-element.268.cur_ref, ...), custom_call_target="tpu_custom_call", output_to_operand_aliasing={{0}: (2, {}), {1}: (4, {})} | custom-call | flops 15728640 | bytes 6291456 | tf_op jit(solution)/shard_map/while/body/eval_jaxpr/pallas_call | solution.py:120
  546.0 24.5 %all_to_all.27 = f32[128,1,8,128]{3,2,1,0:T(8,128)S(1)} all-to-all(f32[128,1,8,128]{3,2,1,0:T(8,128)S(1)} %multiply_bitcast_fusion), channel_id=1, replica_groups=mesh['survey'=2,'dom'=16] {'dom'}, dimensions={0} | all-to-all | bytes 1048576 | tf_op jit(solution)/shard_map/all_to_all | solution.py:209
  (103 shorter events, 237.3 us)
Async XLA Ops:
  8.1 51.7 %all-to-all-start = ((f32[8,16,8,128]{3,2,0,1:T(8,128)}), f32[8,16,8,128]{3,2,0,1:T(8,128)S(1)}, u32[]{:S(2)}, u32[]{:S(2)}) async-start(f32[8,16,8,128]{3,2,0,1:T(8,128)} %select_bitcast_fusion), calls=%async_computation | async-start | bytes 1048576 | tf_op jit(solution)/shard_map/all_to_all | solution.py:168
  78.0 11.8 %collective-permute-start.2 = (f32[2,128,4,128]{3,2,1,0:T(4,128)S(1)}, f32[2,128,4,128]{3,2,1,0:T(4,128)S(1)}, u32[]{:S(2)}, u32[]{:S(2)}) collective-permute-start(f32[2,128,4,128]{3,2,1,0:T(4,128)S(1)} %get-tuple-element.241), channel_id=1, source_target_pairs={{0,1},{1,2},{2,3},{3,4},{4,5},{5,6},{6,7},{7,8},{8,9},{9,10},{10,1... | collective-permute-start | bytes 1572872 | tf_op jit(solution)/shard_map/while/body/eval_jaxpr/ppermute | solution.py:18
  88.3 5.8 %collective-permute-start.3 = (f32[2,128,4,128]{3,2,1,0:T(4,128)S(1)}, f32[2,128,4,128]{3,2,1,0:T(4,128)S(1)}, u32[]{:S(2)}, u32[]{:S(2)}) collective-permute-start(f32[2,128,4,128]{3,2,1,0:T(4,128)S(1)} %get-tuple-element.242), channel_id=1, source_target_pairs={{1,0},{2,1},{3,2},{4,3},{5,4},{6,5},{7,6},{8,7},{9,8},{10,9},{11,1... | collective-permute-start | bytes 1572872 | tf_op jit(solution)/shard_map/while/body/eval_jaxpr/ppermute | solution.py:19
  104.1 11.8 %collective-permute-start = (f32[2,128,4,128]{3,2,1,0:T(4,128)S(1)}, f32[2,128,4,128]{3,2,1,0:T(4,128)S(1)}, u32[]{:S(2)}, u32[]{:S(2)}) collective-permute-start(f32[2,128,4,128]{3,2,1,0:T(4,128)S(1)} %get-tuple-element.261), channel_id=1, source_target_pairs={{0,1},{1,2},{2,3},{3,4},{4,5},{5,6},{6,7},{7,8},{8,9},{9,10},{10,1... | collective-permute-start | bytes 1572872 | tf_op jit(solution)/shard_map/while/body/eval_jaxpr/ppermute | solution.py:18
  114.4 5.8 %collective-permute-start.1 = (f32[2,128,4,128]{3,2,1,0:T(4,128)S(1)}, f32[2,128,4,128]{3,2,1,0:T(4,128)S(1)}, u32[]{:S(2)}, u32[]{:S(2)}) collective-permute-start(f32[2,128,4,128]{3,2,1,0:T(4,128)S(1)} %get-tuple-element.260), channel_id=1, source_target_pairs={{1,0},{2,1},{3,2},{4,3},{5,4},{6,5},{7,6},{8,7},{9,8},{10,9},{11,1... | collective-permute-start | bytes 1572872 | tf_op jit(solution)/shard_map/while/body/eval_jaxpr/ppermute | solution.py:19
  130.2 11.8 %collective-permute-start.2 = (f32[2,128,4,128]{3,2,1,0:T(4,128)S(1)}, f32[2,128,4,128]{3,2,1,0:T(4,128)S(1)}, u32[]{:S(2)}, u32[]{:S(2)}) collective-permute-start(f32[2,128,4,128]{3,2,1,0:T(4,128)S(1)} %get-tuple-element.241), channel_id=1, source_target_pairs={{0,1},{1,2},{2,3},{3,4},{4,5},{5,6},{6,7},{7,8},{8,9},{9,10},{10,1... | collective-permute-start | bytes 1572872 | tf_op jit(solution)/shard_map/while/body/eval_jaxpr/ppermute | solution.py:18
  140.5 5.8 %collective-permute-start.3 = (f32[2,128,4,128]{3,2,1,0:T(4,128)S(1)}, f32[2,128,4,128]{3,2,1,0:T(4,128)S(1)}, u32[]{:S(2)}, u32[]{:S(2)}) collective-permute-start(f32[2,128,4,128]{3,2,1,0:T(4,128)S(1)} %get-tuple-element.242), channel_id=1, source_target_pairs={{1,0},{2,1},{3,2},{4,3},{5,4},{6,5},{7,6},{8,7},{9,8},{10,9},{11,1... | collective-permute-start | bytes 1572872 | tf_op jit(solution)/shard_map/while/body/eval_jaxpr/ppermute | solution.py:19
  156.3 11.8 %collective-permute-start = (f32[2,128,4,128]{3,2,1,0:T(4,128)S(1)}, f32[2,128,4,128]{3,2,1,0:T(4,128)S(1)}, u32[]{:S(2)}, u32[]{:S(2)}) collective-permute-start(f32[2,128,4,128]{3,2,1,0:T(4,128)S(1)} %get-tuple-element.261), channel_id=1, source_target_pairs={{0,1},{1,2},{2,3},{3,4},{4,5},{5,6},{6,7},{7,8},{8,9},{9,10},{10,1... | collective-permute-start | bytes 1572872 | tf_op jit(solution)/shard_map/while/body/eval_jaxpr/ppermute | solution.py:18
  166.6 5.8 %collective-permute-start.1 = (f32[2,128,4,128]{3,2,1,0:T(4,128)S(1)}, f32[2,128,4,128]{3,2,1,0:T(4,128)S(1)}, u32[]{:S(2)}, u32[]{:S(2)}) collective-permute-start(f32[2,128,4,128]{3,2,1,0:T(4,128)S(1)} %get-tuple-element.260), channel_id=1, source_target_pairs={{1,0},{2,1},{3,2},{4,3},{5,4},{6,5},{7,6},{8,7},{9,8},{10,9},{11,1... | collective-permute-start | bytes 1572872 | tf_op jit(solution)/shard_map/while/body/eval_jaxpr/ppermute | solution.py:19
  182.4 11.8 %collective-permute-start.2 = (f32[2,128,4,128]{3,2,1,0:T(4,128)S(1)}, f32[2,128,4,128]{3,2,1,0:T(4,128)S(1)}, u32[]{:S(2)}, u32[]{:S(2)}) collective-permute-start(f32[2,128,4,128]{3,2,1,0:T(4,128)S(1)} %get-tuple-element.241), channel_id=1, source_target_pairs={{0,1},{1,2},{2,3},{3,4},{4,5},{5,6},{6,7},{7,8},{8,9},{9,10},{10,1... | collective-permute-start | bytes 1572872 | tf_op jit(solution)/shard_map/while/body/eval_jaxpr/ppermute | solution.py:18
  192.7 5.8 %collective-permute-start.3 = (f32[2,128,4,128]{3,2,1,0:T(4,128)S(1)}, f32[2,128,4,128]{3,2,1,0:T(4,128)S(1)}, u32[]{:S(2)}, u32[]{:S(2)}) collective-permute-start(f32[2,128,4,128]{3,2,1,0:T(4,128)S(1)} %get-tuple-element.242), channel_id=1, source_target_pairs={{1,0},{2,1},{3,2},{4,3},{5,4},{6,5},{7,6},{8,7},{9,8},{10,9},{11,1... | collective-permute-start | bytes 1572872 | tf_op jit(solution)/shard_map/while/body/eval_jaxpr/ppermute | solution.py:19
  208.5 11.8 %collective-permute-start = (f32[2,128,4,128]{3,2,1,0:T(4,128)S(1)}, f32[2,128,4,128]{3,2,1,0:T(4,128)S(1)}, u32[]{:S(2)}, u32[]{:S(2)}) collective-permute-start(f32[2,128,4,128]{3,2,1,0:T(4,128)S(1)} %get-tuple-element.261), channel_id=1, source_target_pairs={{0,1},{1,2},{2,3},{3,4},{4,5},{5,6},{6,7},{7,8},{8,9},{9,10},{10,1... | collective-permute-start | bytes 1572872 | tf_op jit(solution)/shard_map/while/body/eval_jaxpr/ppermute | solution.py:18
  218.8 5.8 %collective-permute-start.1 = (f32[2,128,4,128]{3,2,1,0:T(4,128)S(1)}, f32[2,128,4,128]{3,2,1,0:T(4,128)S(1)}, u32[]{:S(2)}, u32[]{:S(2)}) collective-permute-start(f32[2,128,4,128]{3,2,1,0:T(4,128)S(1)} %get-tuple-element.260), channel_id=1, source_target_pairs={{1,0},{2,1},{3,2},{4,3},{5,4},{6,5},{7,6},{8,7},{9,8},{10,9},{11,1... | collective-permute-start | bytes 1572872 | tf_op jit(solution)/shard_map/while/body/eval_jaxpr/ppermute | solution.py:19
  234.6 11.4 %collective-permute-start.2 = (f32[2,128,4,128]{3,2,1,0:T(4,128)S(1)}, f32[2,128,4,128]{3,2,1,0:T(4,128)S(1)}, u32[]{:S(2)}, u32[]{:S(2)}) collective-permute-start(f32[2,128,4,128]{3,2,1,0:T(4,128)S(1)} %get-tuple-element.241), channel_id=1, source_target_pairs={{0,1},{1,2},{2,3},{3,4},{4,5},{5,6},{6,7},{7,8},{8,9},{9,10},{10,1... | collective-permute-start | bytes 1572872 | tf_op jit(solution)/shard_map/while/body/eval_jaxpr/ppermute | solution.py:18
  244.6 5.8 %collective-permute-start.3 = (f32[2,128,4,128]{3,2,1,0:T(4,128)S(1)}, f32[2,128,4,128]{3,2,1,0:T(4,128)S(1)}, u32[]{:S(2)}, u32[]{:S(2)}) collective-permute-start(f32[2,128,4,128]{3,2,1,0:T(4,128)S(1)} %get-tuple-element.242), channel_id=1, source_target_pairs={{1,0},{2,1},{3,2},{4,3},{5,4},{6,5},{7,6},{8,7},{9,8},{10,9},{11,1... | collective-permute-start | bytes 1572872 | tf_op jit(solution)/shard_map/while/body/eval_jaxpr/ppermute | solution.py:19
  260.3 10.6 %collective-permute-start = (f32[2,128,4,128]{3,2,1,0:T(4,128)S(1)}, f32[2,128,4,128]{3,2,1,0:T(4,128)S(1)}, u32[]{:S(2)}, u32[]{:S(2)}) collective-permute-start(f32[2,128,4,128]{3,2,1,0:T(4,128)S(1)} %get-tuple-element.261), channel_id=1, source_target_pairs={{0,1},{1,2},{2,3},{3,4},{4,5},{5,6},{6,7},{7,8},{8,9},{9,10},{10,1... | collective-permute-start | bytes 1572872 | tf_op jit(solution)/shard_map/while/body/eval_jaxpr/ppermute | solution.py:18
  269.4 5.1 collective-permute-start.1
  284.5 10.6 %collective-permute-start.2 = (f32[2,128,4,128]{3,2,1,0:T(4,128)S(1)}, f32[2,128,4,128]{3,2,1,0:T(4,128)S(1)}, u32[]{:S(2)}, u32[]{:S(2)}) collective-permute-start(f32[2,128,4,128]{3,2,1,0:T(4,128)S(1)} %get-tuple-element.241), channel_id=1, source_target_pairs={{0,1},{1,2},{2,3},{3,4},{4,5},{5,6},{6,7},{7,8},{8,9},{9,10},{10,1... | collective-permute-start | bytes 1572872 | tf_op jit(solution)/shard_map/while/body/eval_jaxpr/ppermute | solution.py:18
  307.9 10.6 %collective-permute-start = (f32[2,128,4,128]{3,2,1,0:T(4,128)S(1)}, f32[2,128,4,128]{3,2,1,0:T(4,128)S(1)}, u32[]{:S(2)}, u32[]{:S(2)}) collective-permute-start(f32[2,128,4,128]{3,2,1,0:T(4,128)S(1)} %get-tuple-element.261), channel_id=1, source_target_pairs={{0,1},{1,2},{2,3},{3,4},{4,5},{5,6},{6,7},{7,8},{8,9},{9,10},{10,1... | collective-permute-start | bytes 1572872 | tf_op jit(solution)/shard_map/while/body/eval_jaxpr/ppermute | solution.py:18
  317.0 5.1 collective-permute-start.1
  332.1 10.6 %collective-permute-start.2 = (f32[2,128,4,128]{3,2,1,0:T(4,128)S(1)}, f32[2,128,4,128]{3,2,1,0:T(4,128)S(1)}, u32[]{:S(2)}, u32[]{:S(2)}) collective-permute-start(f32[2,128,4,128]{3,2,1,0:T(4,128)S(1)} %get-tuple-element.241), channel_id=1, source_target_pairs={{0,1},{1,2},{2,3},{3,4},{4,5},{5,6},{6,7},{7,8},{8,9},{9,10},{10,1... | collective-permute-start | bytes 1572872 | tf_op jit(solution)/shard_map/while/body/eval_jaxpr/ppermute | solution.py:18
  355.5 10.6 %collective-permute-start = (f32[2,128,4,128]{3,2,1,0:T(4,128)S(1)}, f32[2,128,4,128]{3,2,1,0:T(4,128)S(1)}, u32[]{:S(2)}, u32[]{:S(2)}) collective-permute-start(f32[2,128,4,128]{3,2,1,0:T(4,128)S(1)} %get-tuple-element.261), channel_id=1, source_target_pairs={{0,1},{1,2},{2,3},{3,4},{4,5},{5,6},{6,7},{7,8},{8,9},{9,10},{10,1... | collective-permute-start | bytes 1572872 | tf_op jit(solution)/shard_map/while/body/eval_jaxpr/ppermute | solution.py:18
  364.7 5.1 collective-permute-start.1
  379.7 10.6 %collective-permute-start.2 = (f32[2,128,4,128]{3,2,1,0:T(4,128)S(1)}, f32[2,128,4,128]{3,2,1,0:T(4,128)S(1)}, u32[]{:S(2)}, u32[]{:S(2)}) collective-permute-start(f32[2,128,4,128]{3,2,1,0:T(4,128)S(1)} %get-tuple-element.241), channel_id=1, source_target_pairs={{0,1},{1,2},{2,3},{3,4},{4,5},{5,6},{6,7},{7,8},{8,9},{9,10},{10,1... | collective-permute-start | bytes 1572872 | tf_op jit(solution)/shard_map/while/body/eval_jaxpr/ppermute | solution.py:18
  403.1 10.6 %collective-permute-start = (f32[2,128,4,128]{3,2,1,0:T(4,128)S(1)}, f32[2,128,4,128]{3,2,1,0:T(4,128)S(1)}, u32[]{:S(2)}, u32[]{:S(2)}) collective-permute-start(f32[2,128,4,128]{3,2,1,0:T(4,128)S(1)} %get-tuple-element.261), channel_id=1, source_target_pairs={{0,1},{1,2},{2,3},{3,4},{4,5},{5,6},{6,7},{7,8},{8,9},{9,10},{10,1... | collective-permute-start | bytes 1572872 | tf_op jit(solution)/shard_map/while/body/eval_jaxpr/ppermute | solution.py:18
  412.3 5.1 collective-permute-start.1
  427.3 10.6 %collective-permute-start.2 = (f32[2,128,4,128]{3,2,1,0:T(4,128)S(1)}, f32[2,128,4,128]{3,2,1,0:T(4,128)S(1)}, u32[]{:S(2)}, u32[]{:S(2)}) collective-permute-start(f32[2,128,4,128]{3,2,1,0:T(4,128)S(1)} %get-tuple-element.241), channel_id=1, source_target_pairs={{0,1},{1,2},{2,3},{3,4},{4,5},{5,6},{6,7},{7,8},{8,9},{9,10},{10,1... | collective-permute-start | bytes 1572872 | tf_op jit(solution)/shard_map/while/body/eval_jaxpr/ppermute | solution.py:18
  450.8 10.6 %collective-permute-start = (f32[2,128,4,128]{3,2,1,0:T(4,128)S(1)}, f32[2,128,4,128]{3,2,1,0:T(4,128)S(1)}, u32[]{:S(2)}, u32[]{:S(2)}) collective-permute-start(f32[2,128,4,128]{3,2,1,0:T(4,128)S(1)} %get-tuple-element.261), channel_id=1, source_target_pairs={{0,1},{1,2},{2,3},{3,4},{4,5},{5,6},{6,7},{7,8},{8,9},{9,10},{10,1... | collective-permute-start | bytes 1572872 | tf_op jit(solution)/shard_map/while/body/eval_jaxpr/ppermute | solution.py:18
  474.9 10.6 %collective-permute-start.2 = (f32[2,128,4,128]{3,2,1,0:T(4,128)S(1)}, f32[2,128,4,128]{3,2,1,0:T(4,128)S(1)}, u32[]{:S(2)}, u32[]{:S(2)}) collective-permute-start(f32[2,128,4,128]{3,2,1,0:T(4,128)S(1)} %get-tuple-element.241), channel_id=1, source_target_pairs={{0,1},{1,2},{2,3},{3,4},{4,5},{5,6},{6,7},{7,8},{8,9},{9,10},{10,1... | collective-permute-start | bytes 1572872 | tf_op jit(solution)/shard_map/while/body/eval_jaxpr/ppermute | solution.py:18
  498.4 10.6 %collective-permute-start = (f32[2,128,4,128]{3,2,1,0:T(4,128)S(1)}, f32[2,128,4,128]{3,2,1,0:T(4,128)S(1)}, u32[]{:S(2)}, u32[]{:S(2)}) collective-permute-start(f32[2,128,4,128]{3,2,1,0:T(4,128)S(1)} %get-tuple-element.261), channel_id=1, source_target_pairs={{0,1},{1,2},{2,3},{3,4},{4,5},{5,6},{6,7},{7,8},{8,9},{9,10},{10,1... | collective-permute-start | bytes 1572872 | tf_op jit(solution)/shard_map/while/body/eval_jaxpr/ppermute | solution.py:18
  507.5 5.1 collective-permute-start.1
  522.6 10.6 %collective-permute-start.2 = (f32[2,128,4,128]{3,2,1,0:T(4,128)S(1)}, f32[2,128,4,128]{3,2,1,0:T(4,128)S(1)}, u32[]{:S(2)}, u32[]{:S(2)}) collective-permute-start(f32[2,128,4,128]{3,2,1,0:T(4,128)S(1)} %get-tuple-element.241), channel_id=1, source_target_pairs={{0,1},{1,2},{2,3},{3,4},{4,5},{5,6},{6,7},{7,8},{8,9},{9,10},{10,1... | collective-permute-start | bytes 1572872 | tf_op jit(solution)/shard_map/while/body/eval_jaxpr/ppermute | solution.py:18
  (11 other events, 555.4 us)

commit v6 on v3

v6 whole, which is shorter than its diff:
```python
import functools

import jax
import jax.numpy as jnp
from jax import lax
from jax.experimental import pallas as pl
from jax.experimental.pallas import tpu as pltpu
from jax.sharding import PartitionSpec as P

courant = 0.09
stencil_weights = (8.0 / 5.0, -1.0 / 5.0, 8.0 / 315.0, -1.0 / 560.0)
center_weight = 3.0 * (-205.0 / 72.0)
HALO = 4
XOFF = 8


def trade_halos(head, tail, axis):
    count = lax.axis_size(axis)
    ends = count - 1
    low = lax.ppermute(tail, axis, [(i, (i + 1) % count) for i in range(ends)])
    high = lax.ppermute(head, axis, [((i + 1) % count, i) for i in range(ends)])
    return low, high


def wave_kernel(with_image, moment_ref, cur_ref, prev_ref, s_ref, xlo_ref, xhi_ref, inj_ref, *rest):
    if with_image:
        other_ref, img_ref, out_ref, head_ref, tail_ref, imgo_ref, ey_ref, hx_ref = rest
    else:
        out_ref, head_ref, tail_ref, ey_ref, hx_ref = rest
    block_y, block_x, depth_z = cur_ref.shape
    zeros_y = jnp.zeros((HALO, block_x, depth_z), jnp.float32)
    ey_ref[0:HALO] = zeros_y
    ey_ref[HALO + block_y : 2 * HALO + block_y] = zeros_y
    ey_ref[HALO : HALO + block_y] = cur_ref[...]
    hx_ref[0, :, block_x - HALO : block_x, :] = xlo_ref[...]
    hx_ref[1, :, 0:HALO, :] = xhi_ref[...]
    lane = lax.broadcasted_iota(jnp.int32, (block_x, depth_z), 1)
    sub = lax.broadcasted_iota(jnp.int32, (block_x, depth_z), 0)

    def row(y, carry):
        ctr = ey_ref[HALO + y]
        left = hx_ref[0, y]
        right = hx_ref[1, y]
        acc = center_weight * ctr
        for m in range(1, HALO + 1):
            ahead = pltpu.roll(jnp.where(sub >= m, ctr, right), block_x - m, 0)
            behind = pltpu.roll(jnp.where(sub < block_x - m, ctr, left), m, 0)
            b = ahead + behind
            b = b + ey_ref[HALO + y + m] + ey_ref[HALO + y - m]
            up = jnp.where(lane < depth_z - m, pltpu.roll(ctr, depth_z - m, 1), 0.0)
            down = jnp.where(lane >= m, pltpu.roll(ctr, m, 1), 0.0)
            b = b + up + down
            acc = acc + stencil_weights[m - 1] * b
        lap = acc + inj_ref[y]
        upd = 2.0 * ctr - prev_ref[y] + s_ref[y] * lap
        out_ref[y] = upd
        head_ref[y] = upd[0:HALO]
        tail_ref[y] = upd[block_x - HALO : block_x]
        if with_image:
            imgo_ref[y] = img_ref[y] + other_ref[y] * upd
        return carry

    lax.fori_loop(0, block_y, row, 0, unroll=2)


def wave_call(component, moment, cur, prev, s, xlo, xhi, planes, other=None, img=None):
    block_y, block_x, depth_z = cur.shape
    with_image = img is not None

    def whole(shape):
        return pl.BlockSpec(shape, lambda i, k: (0,) * len(shape))

    plane_spec = pl.BlockSpec(
        (None, None, block_y, block_x, depth_z), lambda i, k: (k[0], component, 0, 0, 0)
    )
    in_specs = [whole(cur.shape), whole(prev.shape), whole(s.shape), whole(xlo.shape), whole(xhi.shape), plane_spec]
    operands = [cur, prev, s, xlo, xhi, planes]
    halo_shape = jax.ShapeDtypeStruct(xlo.shape, jnp.float32)
    out_shape = [jax.ShapeDtypeStruct(cur.shape, jnp.float32), halo_shape, halo_shape]
    out_specs = [whole(cur.shape), whole(xlo.shape), whole(xlo.shape)]
    aliases = {2: 0}
    if with_image:
        in_specs += [whole(other.shape), whole(img.shape)]
        operands += [other, img]
        out_shape.append(jax.ShapeDtypeStruct(img.shape, jnp.float32))
        out_specs.append(whole(img.shape))
        aliases[8] = 3
    grid_spec = pltpu.PrefetchScalarGridSpec(
        num_scalar_prefetch=1,
        grid=(1,),
        in_specs=in_specs,
        out_specs=tuple(out_specs),
        scratch_shapes=[
            pltpu.VMEM((block_y + 2 * HALO, block_x, depth_z), jnp.float32),
            pltpu.VMEM((2, block_y, block_x, depth_z), jnp.float32),
        ],
    )
    return pl.pallas_call(
        functools.partial(wave_kernel, with_image),
        out_shape=tuple(out_shape),
        grid_spec=grid_spec,
        input_output_aliases=aliases,
        compiler_params=pltpu.CompilerParams(vmem_limit_bytes=48 * 1024 * 1024),
        cost_estimate=pl.CostEstimate(
            flops=60 * cur.size, bytes_accessed=4 * 6 * cur.size, transcendentals=0
        ),
    )(jnp.reshape(moment, (1,)).astype(jnp.int32), *operands)


def point_tables(cell_rows, x_start, cells_wide, depth_y):
    local_x = cell_rows[0] - x_start
    inside = (local_x >= 0) & (local_x < cells_wide)
    rows_y = (cell_rows[1][:, None] == jnp.arange(depth_y, dtype=jnp.int32)[None, :]).astype(
        jnp.float32
    )
    column = local_x * 4 + cell_rows[2]
    places = (column[:, None] == jnp.arange(cells_wide * 4, dtype=jnp.int32)[None, :]) & inside[
        :, None
    ]
    return (rows_y, places.astype(jnp.float32))


def spread_points(tables, amounts):
    rows_y, places = tables
    weighted = places[:, None, :] * jnp.transpose(amounts)[:, :, None]
    return jnp.einsum("ny,nsc->syc", rows_y, weighted, precision=lax.Precision.HIGHEST)


def shards(older_fields, fields_now, velocity, aperture, source_pos, wavelet, receiver_pos, traces):
    slab_count = lax.axis_size("dom")
    depth_y = fields_now.shape[1]
    cells_x = fields_now.shape[2]
    depth_z = fields_now.shape[3]
    block_y = velocity.shape[0]
    steps_total = wavelet.shape[0]
    x_anchor = lax.axis_index("dom") * cells_x
    bricks = velocity.reshape(block_y, slab_count, cells_x, depth_z)
    chosen = jnp.take(bricks, aperture, axis=1)
    arrived = lax.all_to_all(chosen, "dom", split_axis=1, concat_axis=0, tiled=True)
    scaled = courant * arrived.reshape(depth_y, cells_x, depth_z)
    speed_sq = scaled * scaled
    image_zero = jnp.zeros((depth_y, cells_x, depth_z), jnp.float32)
    source_core = point_tables(source_pos, x_anchor, cells_x, depth_y)
    receiver_core = point_tables(receiver_pos, x_anchor, cells_x, depth_y)

    planes = jnp.stack(
        [spread_points(source_core, wavelet), spread_points(receiver_core, traces)], axis=1
    )
    planes = planes.reshape(steps_total, 2, depth_y, cells_x, 4)
    planes = jnp.pad(planes, ((0, 0), (0, 0), (0, 0), (0, 0), (0, depth_z - 4)))

    def advance(moment, state):
        (prev0, cur0, head0, tail0), (prev1, cur1, head1, tail1), image_acc = state
        low0, high0 = trade_halos(head0, tail0, "dom")
        low1, high1 = trade_halos(head1, tail1, "dom")
        new0, head0, tail0 = wave_call(0, moment, cur0, prev0, speed_sq, low0, high0, planes)
        new1, head1, tail1, image_acc = wave_call(
            1, moment, cur1, prev1, speed_sq, low1, high1, planes, new0, image_acc
        )
        return (cur0, new0, head0, tail0), (cur1, new1, head1, tail1), image_acc

    def pair(index, state):
        return advance(2 * index + 1, advance(2 * index, state))

    def edges(field):
        return (field[:, :HALO], field[:, cells_x - HALO :])

    start = (
        (older_fields[0], fields_now[0]) + edges(fields_now[0]),
        (older_fields[1], fields_now[1]) + edges(fields_now[1]),
        image_zero,
    )
    state = lax.fori_loop(0, steps_total // 2, pair, start)
    if steps_total % 2:
        state = advance(steps_total - 1, state)
    (prev0, cur0, _, _), (prev1, cur1, _, _), image_acc = state
    previous = jnp.stack([prev0, prev1])
    current = jnp.stack([cur0, cur1])
    image_acc = image_acc * (1.0 / steps_total)
    outgoing = image_acc.reshape(depth_y, 1, cells_x, depth_z)
    one_hot = (aperture[None, :] == jnp.arange(slab_count, dtype=jnp.int32)[:, None]).astype(
        jnp.float32
    )
    received = lax.all_to_all(outgoing, "dom", split_axis=0, concat_axis=1, tiled=True)
    summed = jnp.einsum("mj,yjcz->ymcz", one_hot, received, precision=lax.Precision.HIGHEST)
    image_model = summed.reshape(received.shape[0], slab_count * cells_x, received.shape[3])
    return (previous, current, image_model)


def solution(mesh):
    in_specs = (
        P(None, "survey", "dom", None),
        P(None, "survey", "dom", None),
        P("dom", "survey", None),
        P("survey"),
        P(None, "survey"),
        P(None, "survey"),
        P(None, "survey"),
        P(None, "survey"),
    )
    out_specs = (
        P(None, "survey", "dom", None),
        P(None, "survey", "dom", None),
        P("dom", "survey", None),
    )
    return jax.shard_map(shards, mesh=mesh, in_specs=in_specs, out_specs=out_specs, check_vma=False)
```

time: 591 us -> 675 us (1.14)
  Pallas kernels: 178 us -> 320 us
  waiting for transfers between devices: 68.7 us -> 10.4 us
  starting transfers between devices: 230 us -> 271 us
  blocking collectives: 24.4 us -> 0 us
  other arithmetic: 22.4 us -> 12.5 us
  local copies, waits for them, and re-layouts: 50.6 us -> 41.8 us
    pallas_call x20 -> x40, Pallas kernels: 178 us -> 320 us  [wave_call(): pl.pallas_call(functools.partial(wave_kernel, with_image), out_shape=tupl...]
    ppermute x40 -> x80, waiting for transfers between devices: 68.7 us -> 0.21 us  [the longest x40 0.11 us: trade_halos(): high = lax.ppermute(head, axis, [((i + 1) % count, i) for i in range(ends)])]
    ppermute x40 -> x80, starting transfers between devices: 223 us -> 251 us  [the longest x40 199 us: trade_halos(): low = lax.ppermute(tail, axis, [(i, (i + 1) % count) for i in range(ends)])]
    all_to_all x1 -> x0, blocking collectives: 24.4 us -> none  [shards(): lax.all_to_all(outgoing, 'dom', split_axis=0, concat_axis=1, tiled=True)]
    slice x20 -> x1, local copies, waits for them, and re-layouts: 22.5 us -> 0.86 us  [edges(): return (field[:, :HALO], field[:, cells_x - HALO:])]
    pad x0 -> x1, local copies, waits for them, and re-layouts: none -> 16.2 us  [shards(): planes = jnp.pad(planes, ((0, 0), (0, 0), (0, 0), (0, 0), (0, depth_z - 4)))]
    another operation x1 -> x2, local copies, waits for them, and re-layouts: 15.5 us -> 0.05 us  [shards(): jnp.stack([spread_points(source_core, wavelet), spread_points(receiver_co...]
    all_to_all x0 -> x1, starting transfers between devices: none -> 12.6 us  [shards(): lax.all_to_all(outgoing, 'dom', split_axis=0, concat_axis=1, tiled=True)]
  transfers between devices with their start and end apart: 41 -> 82, of which waited for: 20 -> 1; matrix products, arithmetic and copies ran while one was open for 10% -> 7% of each run, Pallas kernels for 0% -> 36%
where the time goes in v6:
time: 675 us; the launch traced here: 671 us
  Pallas kernels  320 us (47%)
  starting transfers between devices  271 us (40%)
  local copies, waits for them, and re-layouts  41.8 us (6%)
  matrix products  12.8 us (2%)
  other arithmetic  12.5 us (2%)
  waiting for transfers between devices  10.4 us (2%)
    pallas_call x40, Pallas kernels, wave_call(): pl.pallas_call(functools.partial(wave_kernel, with_image), out_shape=tupl...  320 us
    ppermute x40, starting transfers between devices, trade_halos(): low = lax.ppermute(tail, axis, [(i, (i + 1) % count) for i in range(ends)])  199 us
    ppermute x40, starting transfers between devices, trade_halos(): high = lax.ppermute(head, axis, [((i + 1) % count, i) for i in range(ends)])  51.7 us
    pad x1, local copies, waits for them, and re-layouts, shards(): planes = jnp.pad(planes, ((0, 0), (0, 0), (0, 0), (0, 0), (0, depth_z - 4)))  16.2 us
  transfers between devices with their start and end apart: 82, of which 1 were waited for; matrix products, arithmetic and copies ran while one was open for 7% of the time, Pallas kernels for 36%

profile of v6, /device:TPU:0, one launch (start us, length us, event | category | flops | bytes accessed | tf_op | source)
XLA Modules:
  0.0 671.4 jit_solution(10560400509342153632)
XLA Ops:
  15.6 11.6 %fusion = f32[20,32,128]{2,1,0:T(8,128)S(1)} fusion(f32[8192,20]{0,1:T(8,128)} %bitcast.79, f32[8192,32]{0,1:T(8,128)S(1)} %fusion.8, s32[8192]{0:T(1024)S(1)} %bitcast.77), kind=kOutput, calls=%fused_computation.1 | convolution fusion | flops 8059355136 | bytes 2064384 | tf_op jit(solution)/shard_map/ny,nsc->syc/dot_general | solution.py:126
  27.9 10.1 %copy.32 = f32[20,2,128,8,4]{4,3,2,1,0:T(8,128)} copy(f32[20,2,128,8,4]{2,3,4,1,0:T(8,128)S(1)} %pad_maximum_fusion.2) | data formatting | bytes 1310720
  38.0 16.2 %pad.4.clone = f32[20,2,128,8,128]{4,3,2,1,0:T(8,128)} pad(f32[20,2,128,8,4]{4,3,2,1,0:T(8,128)} %copy.32, f32[]{:T(128)} %constant.44.clone.1), padding=0_0x0_0x0_0x0_0x0_124 | pad | bytes 21626884 | tf_op jit(solution)/shard_map/jit(_pad)/pad | solution.py:150
  57.2 583.6 %while.29 = (s32[]{:T(128)}, f32[128,8,128]{2,1,0:T(8,128)}, f32[128,8,128]{2,1,0:T(8,128)S(1)}, f32[128,4,128]{2,1,0:T(4,128)S(1)}, f32[128,4,128]{2,1,0:T(4,12...) while((s32[]{:T(128)}, f32[128,8,128]{2,1,0:T(8,128)}, ...), condition=%wide.region_1.2_spmd, body=%wide.region_0.1_spmd.sunk | while | flops 31457284 | bytes 47186760 | solution.py:173
  66.4 8.1 %eval_jaxpr.20 = (f32[128,8,128]{2,1,0:T(8,128)}, f32[128,4,128]{2,1,0:T(4,128)S(1)}, f32[128,4,128]{2,1,0:T(4,128)S(1)}) custom-call(s32[1]{0:T(128)} %bitcast.64.moment_ref, f32[128,8,128]{2,1,0:T(8,128)S(1)} %get-tuple-element.391.cur_ref.prev_ref, f32[128,8,128]{2,1,0:T(8,128)} %get-tuple-element.390.prev_ref, ...), custom_call_target="tpu_custom_call", output_to_operand_aliasing={{0}: (2, {})} | custom-call | flops 7864320 | bytes 3145728 | tf_op jit(solution)/shard_map/while/body/eval_jaxpr/pallas_call | solution.py:98
  93.2 8.4 %eval_jaxpr.21 = (f32[128,8,128]{2,1,0:T(8,128)}, f32[128,4,128]{2,1,0:T(4,128)}, f32[128,4,128]{2,1,0:T(4,128)S(1)}) custom-call(s32[1]{0:T(128)} %bitcast.65.moment_ref, f32[128,8,128]{2,1,0:T(8,128)} %get-tuple-element.404.cur_ref.rest_0_, f32[128,8,128]{2,1,0:T(8,128)} %copy-done.1, ...), custom_call_target="tpu_custom_call", output_to_operand_aliasing={{0}: (2, {})} | custom-call | flops 7864320 | bytes 3145728 | tf_op jit(solution)/shard_map/while/body/eval_jaxpr/pallas_call | solution.py:98
  101.6 8.1 %eval_jaxpr.23 = (f32[128,8,128]{2,1,0:T(8,128)S(1)}, f32[128,4,128]{2,1,0:T(4,128)}, f32[128,4,128]{2,1,0:T(4,128)S(1)}, f32[128,8,128]{2,1,0:T(8,128)S(1)}) custom-call(s32[1]{0:T(128)} %bitcast.65.moment_ref, f32[128,8,128]{2,1,0:T(8,128)S(1)} %copy-done.9, f32[128,8,128]{2,1,0:T(8,128)S(1)} %copy-done.5, ...), custom_call_target="tpu_custom_call", output_to_operand_aliasing={{0}: (2, {}), {3}: (8, {})} | custom-call | flops 7864320 | bytes 3145728 | tf_op jit(solution)/shard_map/while/body/eval_jaxpr/pallas_call | solution.py:98
  121.9 8.1 %eval_jaxpr.20 = (f32[128,8,128]{2,1,0:T(8,128)}, f32[128,4,128]{2,1,0:T(4,128)S(1)}, f32[128,4,128]{2,1,0:T(4,128)S(1)}) custom-call(s32[1]{0:T(128)} %bitcast.64.moment_ref, f32[128,8,128]{2,1,0:T(8,128)S(1)} %get-tuple-element.391.cur_ref.prev_ref, f32[128,8,128]{2,1,0:T(8,128)} %get-tuple-element.390.prev_ref, ...), custom_call_target="tpu_custom_call", output_to_operand_aliasing={{0}: (2, {})} | custom-call | flops 7864320 | bytes 3145728 | tf_op jit(solution)/shard_map/while/body/eval_jaxpr/pallas_call | solution.py:98
  150.4 8.4 %eval_jaxpr.21 = (f32[128,8,128]{2,1,0:T(8,128)}, f32[128,4,128]{2,1,0:T(4,128)}, f32[128,4,128]{2,1,0:T(4,128)S(1)}) custom-call(s32[1]{0:T(128)} %bitcast.65.moment_ref, f32[128,8,128]{2,1,0:T(8,128)} %get-tuple-element.404.cur_ref.rest_0_, f32[128,8,128]{2,1,0:T(8,128)} %copy-done.1, ...), custom_call_target="tpu_custom_call", output_to_operand_aliasing={{0}: (2, {})} | custom-call | flops 7864320 | bytes 3145728 | tf_op jit(solution)/shard_map/while/body/eval_jaxpr/pallas_call | solution.py:98
  158.9 8.1 %eval_jaxpr.23 = (f32[128,8,128]{2,1,0:T(8,128)S(1)}, f32[128,4,128]{2,1,0:T(4,128)}, f32[128,4,128]{2,1,0:T(4,128)S(1)}, f32[128,8,128]{2,1,0:T(8,128)S(1)}) custom-call(s32[1]{0:T(128)} %bitcast.65.moment_ref, f32[128,8,128]{2,1,0:T(8,128)S(1)} %copy-done.9, f32[128,8,128]{2,1,0:T(8,128)S(1)} %copy-done.5, ...), custom_call_target="tpu_custom_call", output_to_operand_aliasing={{0}: (2, {}), {3}: (8, {})} | custom-call | flops 7864320 | bytes 3145728 | tf_op jit(solution)/shard_map/while/body/eval_jaxpr/pallas_call | solution.py:98
  181.0 8.1 %eval_jaxpr.20 = (f32[128,8,128]{2,1,0:T(8,128)}, f32[128,4,128]{2,1,0:T(4,128)S(1)}, f32[128,4,128]{2,1,0:T(4,128)S(1)}) custom-call(s32[1]{0:T(128)} %bitcast.64.moment_ref, f32[128,8,128]{2,1,0:T(8,128)S(1)} %get-tuple-element.391.cur_ref.prev_ref, f32[128,8,128]{2,1,0:T(8,128)} %get-tuple-element.390.prev_ref, ...), custom_call_target="tpu_custom_call", output_to_operand_aliasing={{0}: (2, {})} | custom-call | flops 7864320 | bytes 3145728 | tf_op jit(solution)/shard_map/while/body/eval_jaxpr/pallas_call | solution.py:98
  209.5 8.4 %eval_jaxpr.21 = (f32[128,8,128]{2,1,0:T(8,128)}, f32[128,4,128]{2,1,0:T(4,128)}, f32[128,4,128]{2,1,0:T(4,128)S(1)}) custom-call(s32[1]{0:T(128)} %bitcast.65.moment_ref, f32[128,8,128]{2,1,0:T(8,128)} %get-tuple-element.404.cur_ref.rest_0_, f32[128,8,128]{2,1,0:T(8,128)} %copy-done.1, ...), custom_call_target="tpu_custom_call", output_to_operand_aliasing={{0}: (2, {})} | custom-call | flops 7864320 | bytes 3145728 | tf_op jit(solution)/shard_map/while/body/eval_jaxpr/pallas_call | solution.py:98
  218.0 8.1 %eval_jaxpr.23 = (f32[128,8,128]{2,1,0:T(8,128)S(1)}, f32[128,4,128]{2,1,0:T(4,128)}, f32[128,4,128]{2,1,0:T(4,128)S(1)}, f32[128,8,128]{2,1,0:T(8,128)S(1)}) custom-call(s32[1]{0:T(128)} %bitcast.65.moment_ref, f32[128,8,128]{2,1,0:T(8,128)S(1)} %copy-done.9, f32[128,8,128]{2,1,0:T(8,128)S(1)} %copy-done.5, ...), custom_call_target="tpu_custom_call", output_to_operand_aliasing={{0}: (2, {}), {3}: (8, {})} | custom-call | flops 7864320 | bytes 3145728 | tf_op jit(solution)/shard_map/while/body/eval_jaxpr/pallas_call | solution.py:98
  240.1 8.1 %eval_jaxpr.20 = (f32[128,8,128]{2,1,0:T(8,128)}, f32[128,4,128]{2,1,0:T(4,128)S(1)}, f32[128,4,128]{2,1,0:T(4,128)S(1)}) custom-call(s32[1]{0:T(128)} %bitcast.64.moment_ref, f32[128,8,128]{2,1,0:T(8,128)S(1)} %get-tuple-element.391.cur_ref.prev_ref, f32[128,8,128]{2,1,0:T(8,128)} %get-tuple-element.390.prev_ref, ...), custom_call_target="tpu_custom_call", output_to_operand_aliasing={{0}: (2, {})} | custom-call | flops 7864320 | bytes 3145728 | tf_op jit(solution)/shard_map/while/body/eval_jaxpr/pallas_call | solution.py:98
  268.6 8.4 %eval_jaxpr.21 = (f32[128,8,128]{2,1,0:T(8,128)}, f32[128,4,128]{2,1,0:T(4,128)}, f32[128,4,128]{2,1,0:T(4,128)S(1)}) custom-call(s32[1]{0:T(128)} %bitcast.65.moment_ref, f32[128,8,128]{2,1,0:T(8,128)} %get-tuple-element.404.cur_ref.rest_0_, f32[128,8,128]{2,1,0:T(8,128)} %copy-done.1, ...), custom_call_target="tpu_custom_call", output_to_operand_aliasing={{0}: (2, {})} | custom-call | flops 7864320 | bytes 3145728 | tf_op jit(solution)/shard_map/while/body/eval_jaxpr/pallas_call | solution.py:98
  277.1 8.1 %eval_jaxpr.23 = (f32[128,8,128]{2,1,0:T(8,128)S(1)}, f32[128,4,128]{2,1,0:T(4,128)}, f32[128,4,128]{2,1,0:T(4,128)S(1)}, f32[128,8,128]{2,1,0:T(8,128)S(1)}) custom-call(s32[1]{0:T(128)} %bitcast.65.moment_ref, f32[128,8,128]{2,1,0:T(8,128)S(1)} %copy-done.9, f32[128,8,128]{2,1,0:T(8,128)S(1)} %copy-done.5, ...), custom_call_target="tpu_custom_call", output_to_operand_aliasing={{0}: (2, {}), {3}: (8, {})} | custom-call | flops 7864320 | bytes 3145728 | tf_op jit(solution)/shard_map/while/body/eval_jaxpr/pallas_call | solution.py:98
  299.2 8.1 %eval_jaxpr.20 = (f32[128,8,128]{2,1,0:T(8,128)}, f32[128,4,128]{2,1,0:T(4,128)S(1)}, f32[128,4,128]{2,1,0:T(4,128)S(1)}) custom-call(s32[1]{0:T(128)} %bitcast.64.moment_ref, f32[128,8,128]{2,1,0:T(8,128)S(1)} %get-tuple-element.391.cur_ref.prev_ref, f32[128,8,128]{2,1,0:T(8,128)} %get-tuple-element.390.prev_ref, ...), custom_call_target="tpu_custom_call", output_to_operand_aliasing={{0}: (2, {})} | custom-call | flops 7864320 | bytes 3145728 | tf_op jit(solution)/shard_map/while/body/eval_jaxpr/pallas_call | solution.py:98
  327.8 8.4 %eval_jaxpr.21 = (f32[128,8,128]{2,1,0:T(8,128)}, f32[128,4,128]{2,1,0:T(4,128)}, f32[128,4,128]{2,1,0:T(4,128)S(1)}) custom-call(s32[1]{0:T(128)} %bitcast.65.moment_ref, f32[128,8,128]{2,1,0:T(8,128)} %get-tuple-element.404.cur_ref.rest_0_, f32[128,8,128]{2,1,0:T(8,128)} %copy-done.1, ...), custom_call_target="tpu_custom_call", output_to_operand_aliasing={{0}: (2, {})} | custom-call | flops 7864320 | bytes 3145728 | tf_op jit(solution)/shard_map/while/body/eval_jaxpr/pallas_call | solution.py:98
  336.2 8.1 %eval_jaxpr.23 = (f32[128,8,128]{2,1,0:T(8,128)S(1)}, f32[128,4,128]{2,1,0:T(4,128)}, f32[128,4,128]{2,1,0:T(4,128)S(1)}, f32[128,8,128]{2,1,0:T(8,128)S(1)}) custom-call(s32[1]{0:T(128)} %bitcast.65.moment_ref, f32[128,8,128]{2,1,0:T(8,128)S(1)} %copy-done.9, f32[128,8,128]{2,1,0:T(8,128)S(1)} %copy-done.5, ...), custom_call_target="tpu_custom_call", output_to_operand_aliasing={{0}: (2, {}), {3}: (8, {})} | custom-call | flops 7864320 | bytes 3145728 | tf_op jit(solution)/shard_map/while/body/eval_jaxpr/pallas_call | solution.py:98
  358.3 8.1 %eval_jaxpr.20 = (f32[128,8,128]{2,1,0:T(8,128)}, f32[128,4,128]{2,1,0:T(4,128)S(1)}, f32[128,4,128]{2,1,0:T(4,128)S(1)}) custom-call(s32[1]{0:T(128)} %bitcast.64.moment_ref, f32[128,8,128]{2,1,0:T(8,128)S(1)} %get-tuple-element.391.cur_ref.prev_ref, f32[128,8,128]{2,1,0:T(8,128)} %get-tuple-element.390.prev_ref, ...), custom_call_target="tpu_custom_call", output_to_operand_aliasing={{0}: (2, {})} | custom-call | flops 7864320 | bytes 3145728 | tf_op jit(solution)/shard_map/while/body/eval_jaxpr/pallas_call | solution.py:98
  386.9 8.4 %eval_jaxpr.21 = (f32[128,8,128]{2,1,0:T(8,128)}, f32[128,4,128]{2,1,0:T(4,128)}, f32[128,4,128]{2,1,0:T(4,128)S(1)}) custom-call(s32[1]{0:T(128)} %bitcast.65.moment_ref, f32[128,8,128]{2,1,0:T(8,128)} %get-tuple-element.404.cur_ref.rest_0_, f32[128,8,128]{2,1,0:T(8,128)} %copy-done.1, ...), custom_call_target="tpu_custom_call", output_to_operand_aliasing={{0}: (2, {})} | custom-call | flops 7864320 | bytes 3145728 | tf_op jit(solution)/shard_map/while/body/eval_jaxpr/pallas_call | solution.py:98
  417.4 8.1 %eval_jaxpr.20 = (f32[128,8,128]{2,1,0:T(8,128)}, f32[128,4,128]{2,1,0:T(4,128)S(1)}, f32[128,4,128]{2,1,0:T(4,128)S(1)}) custom-call(s32[1]{0:T(128)} %bitcast.64.moment_ref, f32[128,8,128]{2,1,0:T(8,128)S(1)} %get-tuple-element.391.cur_ref.prev_ref, f32[128,8,128]{2,1,0:T(8,128)} %get-tuple-element.390.prev_ref, ...), custom_call_target="tpu_custom_call", output_to_operand_aliasing={{0}: (2, {})} | custom-call | flops 7864320 | bytes 3145728 | tf_op jit(solution)/shard_map/while/body/eval_jaxpr/pallas_call | solution.py:98
  446.0 8.4 %eval_jaxpr.21 = (f32[128,8,128]{2,1,0:T(8,128)}, f32[128,4,128]{2,1,0:T(4,128)}, f32[128,4,128]{2,1,0:T(4,128)S(1)}) custom-call(s32[1]{0:T(128)} %bitcast.65.moment_ref, f32[128,8,128]{2,1,0:T(8,128)} %get-tuple-element.404.cur_ref.rest_0_, f32[128,8,128]{2,1,0:T(8,128)} %copy-done.1, ...), custom_call_target="tpu_custom_call", output_to_operand_aliasing={{0}: (2, {})} | custom-call | flops 7864320 | bytes 3145728 | tf_op jit(solution)/shard_map/while/body/eval_jaxpr/pallas_call | solution.py:98
  476.5 8.1 %eval_jaxpr.20 = (f32[128,8,128]{2,1,0:T(8,128)}, f32[128,4,128]{2,1,0:T(4,128)S(1)}, f32[128,4,128]{2,1,0:T(4,128)S(1)}) custom-call(s32[1]{0:T(128)} %bitcast.64.moment_ref, f32[128,8,128]{2,1,0:T(8,128)S(1)} %get-tuple-element.391.cur_ref.prev_ref, f32[128,8,128]{2,1,0:T(8,128)} %get-tuple-element.390.prev_ref, ...), custom_call_target="tpu_custom_call", output_to_operand_aliasing={{0}: (2, {})} | custom-call | flops 7864320 | bytes 3145728 | tf_op jit(solution)/shard_map/while/body/eval_jaxpr/pallas_call | solution.py:98
  505.1 8.4 %eval_jaxpr.21 = (f32[128,8,128]{2,1,0:T(8,128)}, f32[128,4,128]{2,1,0:T(4,128)}, f32[128,4,128]{2,1,0:T(4,128)S(1)}) custom-call(s32[1]{0:T(128)} %bitcast.65.moment_ref, f32[128,8,128]{2,1,0:T(8,128)} %get-tuple-element.404.cur_ref.rest_0_, f32[128,8,128]{2,1,0:T(8,128)} %copy-done.1, ...), custom_call_target="tpu_custom_call", output_to_operand_aliasing={{0}: (2, {})} | custom-call | flops 7864320 | bytes 3145728 | tf_op jit(solution)/shard_map/while/body/eval_jaxpr/pallas_call | solution.py:98
  535.6 8.1 %eval_jaxpr.20 = (f32[128,8,128]{2,1,0:T(8,128)}, f32[128,4,128]{2,1,0:T(4,128)S(1)}, f32[128,4,128]{2,1,0:T(4,128)S(1)}) custom-call(s32[1]{0:T(128)} %bitcast.64.moment_ref, f32[128,8,128]{2,1,0:T(8,128)S(1)} %get-tuple-element.391.cur_ref.prev_ref, f32[128,8,128]{2,1,0:T(8,128)} %get-tuple-element.390.prev_ref, ...), custom_call_target="tpu_custom_call", output_to_operand_aliasing={{0}: (2, {})} | custom-call | flops 7864320 | bytes 3145728 | tf_op jit(solution)/shard_map/while/body/eval_jaxpr/pallas_call | solution.py:98
  564.2 8.4 %eval_jaxpr.21 = (f32[128,8,128]{2,1,0:T(8,128)}, f32[128,4,128]{2,1,0:T(4,128)}, f32[128,4,128]{2,1,0:T(4,128)S(1)}) custom-call(s32[1]{0:T(128)} %bitcast.65.moment_ref, f32[128,8,128]{2,1,0:T(8,128)} %get-tuple-element.404.cur_ref.rest_0_, f32[128,8,128]{2,1,0:T(8,128)} %copy-done.1, ...), custom_call_target="tpu_custom_call", output_to_operand_aliasing={{0}: (2, {})} | custom-call | flops 7864320 | bytes 3145728 | tf_op jit(solution)/shard_map/while/body/eval_jaxpr/pallas_call | solution.py:98
  594.7 8.1 %eval_jaxpr.20 = (f32[128,8,128]{2,1,0:T(8,128)}, f32[128,4,128]{2,1,0:T(4,128)S(1)}, f32[128,4,128]{2,1,0:T(4,128)S(1)}) custom-call(s32[1]{0:T(128)} %bitcast.64.moment_ref, f32[128,8,128]{2,1,0:T(8,128)S(1)} %get-tuple-element.391.cur_ref.prev_ref, f32[128,8,128]{2,1,0:T(8,128)} %get-tuple-element.390.prev_ref, ...), custom_call_target="tpu_custom_call", output_to_operand_aliasing={{0}: (2, {})} | custom-call | flops 7864320 | bytes 3145728 | tf_op jit(solution)/shard_map/while/body/eval_jaxpr/pallas_call | solution.py:98
  623.3 8.4 %eval_jaxpr.21 = (f32[128,8,128]{2,1,0:T(8,128)}, f32[128,4,128]{2,1,0:T(4,128)}, f32[128,4,128]{2,1,0:T(4,128)S(1)}) custom-call(s32[1]{0:T(128)} %bitcast.65.moment_ref, f32[128,8,128]{2,1,0:T(8,128)} %get-tuple-element.404.cur_ref.rest_0_, f32[128,8,128]{2,1,0:T(8,128)} %copy-done.1, ...), custom_call_target="tpu_custom_call", output_to_operand_aliasing={{0}: (2, {})} | custom-call | flops 7864320 | bytes 3145728 | tf_op jit(solution)/shard_map/while/body/eval_jaxpr/pallas_call | solution.py:98
  631.7 8.1 %eval_jaxpr.23 = (f32[128,8,128]{2,1,0:T(8,128)S(1)}, f32[128,4,128]{2,1,0:T(4,128)}, f32[128,4,128]{2,1,0:T(4,128)S(1)}, f32[128,8,128]{2,1,0:T(8,128)S(1)}) custom-call(s32[1]{0:T(128)} %bitcast.65.moment_ref, f32[128,8,128]{2,1,0:T(8,128)S(1)} %copy-done.9, f32[128,8,128]{2,1,0:T(8,128)S(1)} %copy-done.5, ...), custom_call_target="tpu_custom_call", output_to_operand_aliasing={{0}: (2, {}), {3}: (8, {})} | custom-call | flops 7864320 | bytes 3145728 | tf_op jit(solution)/shard_map/while/body/eval_jaxpr/pallas_call | solution.py:98
  642.7 12.6 %all-to-all-start.1 = ((f32[128,1,8,128]{3,2,1,0:T(8,128)}), f32[128,1,8,128]{3,2,1,0:T(8,128)S(1)}, u32[]{:S(2)}, u32[]{:S(2)}) async-start(f32[128,1,8,128]{3,2,1,0:T(8,128)} %multiply_bitcast_fusion), calls=%async_computation.1 | async-start | bytes 1048576 | tf_op jit(solution)/shard_map/all_to_all | solution.py:184
  659.6 10.1 %all-to-all-done.1 = f32[128,1,8,128]{3,2,1,0:T(8,128)S(1)} async-done(((f32[128,1,8,128]{3,2,1,0:T(8,128)}), f32[128,1,8,128]{3,2,1,0:T(8,128)S(1)}, u32[]{:S(2)}, u32[]{:S(2)}) %all-to-all-start.1) | async-done | bytes 524320 | tf_op jit(solution)/shard_map/all_to_all | solution.py:184
  (472 shorter events, 393.7 us)
Async XLA Ops:
  3.6 52.7 %all-to-all-start = ((f32[8,16,8,128]{3,2,0,1:T(8,128)}), f32[8,16,8,128]{3,2,0,1:T(8,128)S(1)}, u32[]{:S(2)}, u32[]{:S(2)}) async-start(f32[8,16,8,128]{3,2,0,1:T(8,128)} %select_bitcast_fusion), calls=%async_computation | async-start | bytes 1048576 | tf_op jit(solution)/shard_map/all_to_all | solution.py:139
  60.9 19.3 %collective-permute-start.4 = (f32[128,4,128]{2,1,0:T(4,128)S(1)}, f32[128,4,128]{2,1,0:T(4,128)S(1)}, u32[]{:S(2)}, u32[]{:S(2)}) collective-permute-start(f32[128,4,128]{2,1,0:T(4,128)S(1)} %get-tuple-element.397), channel_id=1, source_target_pairs={{0,1},{1,2},{2,3},{3,4},{4,5},{5,6},{6,7},{7,8},{8,9},{9,10},{10,1... | collective-permute-start | bytes 786440 | tf_op jit(solution)/shard_map/while/body/eval_jaxpr/ppermute | solution.py:20
  74.6 18.6 %collective-permute-start.2 = (f32[128,4,128]{2,1,0:T(4,128)S(1)}, f32[128,4,128]{2,1,0:T(4,128)S(1)}, u32[]{:S(2)}, u32[]{:S(2)}) collective-permute-start(f32[128,4,128]{2,1,0:T(4,128)S(1)} %get-tuple-element.362), channel_id=1, source_target_pairs={{0,1},{1,2},{2,3},{3,4},{4,5},{5,6},{6,7},{7,8},{8,9},{9,10},{10,1... | collective-permute-start | bytes 786440 | tf_op jit(solution)/shard_map/while/body/eval_jaxpr/ppermute | solution.py:20
  116.3 20.2 %collective-permute-start.4 = (f32[128,4,128]{2,1,0:T(4,128)S(1)}, f32[128,4,128]{2,1,0:T(4,128)S(1)}, u32[]{:S(2)}, u32[]{:S(2)}) collective-permute-start(f32[128,4,128]{2,1,0:T(4,128)S(1)} %get-tuple-element.397), channel_id=1, source_target_pairs={{0,1},{1,2},{2,3},{3,4},{4,5},{5,6},{6,7},{7,8},{8,9},{9,10},{10,1... | collective-permute-start | bytes 786440 | tf_op jit(solution)/shard_map/while/body/eval_jaxpr/ppermute | solution.py:20
  120.6 16.0 %collective-permute-start.5 = (f32[128,4,128]{2,1,0:T(4,128)}, f32[128,4,128]{2,1,0:T(4,128)S(1)}, u32[]{:S(2)}, u32[]{:S(2)}) collective-permute-start(f32[128,4,128]{2,1,0:T(4,128)} %get-tuple-element.396), channel_id=1, source_target_pairs={{1,0},{2,1},{3,2},{4,3},{5,4},{6,5},{7,6},{8,7},{9,8},{10,9},{11,1... | collective-permute-start | bytes 786440 | tf_op jit(solution)/shard_map/while/body/eval_jaxpr/ppermute | solution.py:21
  130.1 20.4 %collective-permute-start.2 = (f32[128,4,128]{2,1,0:T(4,128)S(1)}, f32[128,4,128]{2,1,0:T(4,128)S(1)}, u32[]{:S(2)}, u32[]{:S(2)}) collective-permute-start(f32[128,4,128]{2,1,0:T(4,128)S(1)} %get-tuple-element.362), channel_id=1, source_target_pairs={{0,1},{1,2},{2,3},{3,4},{4,5},{5,6},{6,7},{7,8},{8,9},{9,10},{10,1... | collective-permute-start | bytes 786440 | tf_op jit(solution)/shard_map/while/body/eval_jaxpr/ppermute | solution.py:20
  174.7 21.0 %collective-permute-start.4 = (f32[128,4,128]{2,1,0:T(4,128)S(1)}, f32[128,4,128]{2,1,0:T(4,128)S(1)}, u32[]{:S(2)}, u32[]{:S(2)}) collective-permute-start(f32[128,4,128]{2,1,0:T(4,128)S(1)} %get-tuple-element.397), channel_id=1, source_target_pairs={{0,1},{1,2},{2,3},{3,4},{4,5},{5,6},{6,7},{7,8},{8,9},{9,10},{10,1... | collective-permute-start | bytes 786440 | tf_op jit(solution)/shard_map/while/body/eval_jaxpr/ppermute | solution.py:20
  179.6 16.1 %collective-permute-start.5 = (f32[128,4,128]{2,1,0:T(4,128)}, f32[128,4,128]{2,1,0:T(4,128)S(1)}, u32[]{:S(2)}, u32[]{:S(2)}) collective-permute-start(f32[128,4,128]{2,1,0:T(4,128)} %get-tuple-element.396), channel_id=1, source_target_pairs={{1,0},{2,1},{3,2},{4,3},{5,4},{6,5},{7,6},{8,7},{9,8},{10,9},{11,1... | collective-permute-start | bytes 786440 | tf_op jit(solution)/shard_map/while/body/eval_jaxpr/ppermute | solution.py:21
  189.1 20.4 %collective-permute-start.2 = (f32[128,4,128]{2,1,0:T(4,128)S(1)}, f32[128,4,128]{2,1,0:T(4,128)S(1)}, u32[]{:S(2)}, u32[]{:S(2)}) collective-permute-start(f32[128,4,128]{2,1,0:T(4,128)S(1)} %get-tuple-element.362), channel_id=1, source_target_pairs={{0,1},{1,2},{2,3},{3,4},{4,5},{5,6},{6,7},{7,8},{8,9},{9,10},{10,1... | collective-permute-start | bytes 786440 | tf_op jit(solution)/shard_map/while/body/eval_jaxpr/ppermute | solution.py:20
  194.3 15.2 %collective-permute-start.3 = (f32[128,4,128]{2,1,0:T(4,128)S(1)}, f32[128,4,128]{2,1,0:T(4,128)S(1)}, u32[]{:S(2)}, u32[]{:S(2)}) collective-permute-start(f32[128,4,128]{2,1,0:T(4,128)S(1)} %get-tuple-element.363), channel_id=1, source_target_pairs={{1,0},{2,1},{3,2},{4,3},{5,4},{6,5},{7,6},{8,7},{9,8},{10,9},{11,1... | collective-permute-start | bytes 786440 | tf_op jit(solution)/shard_map/while/body/eval_jaxpr/ppermute | solution.py:21
  233.8 21.0 %collective-permute-start.4 = (f32[128,4,128]{2,1,0:T(4,128)S(1)}, f32[128,4,128]{2,1,0:T(4,128)S(1)}, u32[]{:S(2)}, u32[]{:S(2)}) collective-permute-start(f32[128,4,128]{2,1,0:T(4,128)S(1)} %get-tuple-element.397), channel_id=1, source_target_pairs={{0,1},{1,2},{2,3},{3,4},{4,5},{5,6},{6,7},{7,8},{8,9},{9,10},{10,1... | collective-permute-start | bytes 786440 | tf_op jit(solution)/shard_map/while/body/eval_jaxpr/ppermute | solution.py:20
  238.7 16.1 %collective-permute-start.5 = (f32[128,4,128]{2,1,0:T(4,128)}, f32[128,4,128]{2,1,0:T(4,128)S(1)}, u32[]{:S(2)}, u32[]{:S(2)}) collective-permute-start(f32[128,4,128]{2,1,0:T(4,128)} %get-tuple-element.396), channel_id=1, source_target_pairs={{1,0},{2,1},{3,2},{4,3},{5,4},{6,5},{7,6},{8,7},{9,8},{10,9},{11,1... | collective-permute-start | bytes 786440 | tf_op jit(solution)/shard_map/while/body/eval_jaxpr/ppermute | solution.py:21
  248.2 20.4 %collective-permute-start.2 = (f32[128,4,128]{2,1,0:T(4,128)S(1)}, f32[128,4,128]{2,1,0:T(4,128)S(1)}, u32[]{:S(2)}, u32[]{:S(2)}) collective-permute-start(f32[128,4,128]{2,1,0:T(4,128)S(1)} %get-tuple-element.362), channel_id=1, source_target_pairs={{0,1},{1,2},{2,3},{3,4},{4,5},{5,6},{6,7},{7,8},{8,9},{9,10},{10,1... | collective-permute-start | bytes 786440 | tf_op jit(solution)/shard_map/while/body/eval_jaxpr/ppermute | solution.py:20
  292.9 21.0 %collective-permute-start.4 = (f32[128,4,128]{2,1,0:T(4,128)S(1)}, f32[128,4,128]{2,1,0:T(4,128)S(1)}, u32[]{:S(2)}, u32[]{:S(2)}) collective-permute-start(f32[128,4,128]{2,1,0:T(4,128)S(1)} %get-tuple-element.397), channel_id=1, source_target_pairs={{0,1},{1,2},{2,3},{3,4},{4,5},{5,6},{6,7},{7,8},{8,9},{9,10},{10,1... | collective-permute-start | bytes 786440 | tf_op jit(solution)/shard_map/while/body/eval_jaxpr/ppermute | solution.py:20
  297.8 16.1 %collective-permute-start.5 = (f32[128,4,128]{2,1,0:T(4,128)}, f32[128,4,128]{2,1,0:T(4,128)S(1)}, u32[]{:S(2)}, u32[]{:S(2)}) collective-permute-start(f32[128,4,128]{2,1,0:T(4,128)} %get-tuple-element.396), channel_id=1, source_target_pairs={{1,0},{2,1},{3,2},{4,3},{5,4},{6,5},{7,6},{8,7},{9,8},{10,9},{11,1... | collective-permute-start | bytes 786440 | tf_op jit(solution)/shard_map/while/body/eval_jaxpr/ppermute | solution.py:21
  307.3 20.4 %collective-permute-start.2 = (f32[128,4,128]{2,1,0:T(4,128)S(1)}, f32[128,4,128]{2,1,0:T(4,128)S(1)}, u32[]{:S(2)}, u32[]{:S(2)}) collective-permute-start(f32[128,4,128]{2,1,0:T(4,128)S(1)} %get-tuple-element.362), channel_id=1, source_target_pairs={{0,1},{1,2},{2,3},{3,4},{4,5},{5,6},{6,7},{7,8},{8,9},{9,10},{10,1... | collective-permute-start | bytes 786440 | tf_op jit(solution)/shard_map/while/body/eval_jaxpr/ppermute | solution.py:20
  352.0 21.0 %collective-permute-start.4 = (f32[128,4,128]{2,1,0:T(4,128)S(1)}, f32[128,4,128]{2,1,0:T(4,128)S(1)}, u32[]{:S(2)}, u32[]{:S(2)}) collective-permute-start(f32[128,4,128]{2,1,0:T(4,128)S(1)} %get-tuple-element.397), channel_id=1, source_target_pairs={{0,1},{1,2},{2,3},{3,4},{4,5},{5,6},{6,7},{7,8},{8,9},{9,10},{10,1... | collective-permute-start | bytes 786440 | tf_op jit(solution)/shard_map/while/body/eval_jaxpr/ppermute | solution.py:20
  356.9 16.1 %collective-permute-start.5 = (f32[128,4,128]{2,1,0:T(4,128)}, f32[128,4,128]{2,1,0:T(4,128)S(1)}, u32[]{:S(2)}, u32[]{:S(2)}) collective-permute-start(f32[128,4,128]{2,1,0:T(4,128)} %get-tuple-element.396), channel_id=1, source_target_pairs={{1,0},{2,1},{3,2},{4,3},{5,4},{6,5},{7,6},{8,7},{9,8},{10,9},{11,1... | collective-permute-start | bytes 786440 | tf_op jit(solution)/shard_map/while/body/eval_jaxpr/ppermute | solution.py:21
  366.4 20.4 %collective-permute-start.2 = (f32[128,4,128]{2,1,0:T(4,128)S(1)}, f32[128,4,128]{2,1,0:T(4,128)S(1)}, u32[]{:S(2)}, u32[]{:S(2)}) collective-permute-start(f32[128,4,128]{2,1,0:T(4,128)S(1)} %get-tuple-element.362), channel_id=1, source_target_pairs={{0,1},{1,2},{2,3},{3,4},{4,5},{5,6},{6,7},{7,8},{8,9},{9,10},{10,1... | collective-permute-start | bytes 786440 | tf_op jit(solution)/shard_map/while/body/eval_jaxpr/ppermute | solution.py:20
  411.1 21.0 %collective-permute-start.4 = (f32[128,4,128]{2,1,0:T(4,128)S(1)}, f32[128,4,128]{2,1,0:T(4,128)S(1)}, u32[]{:S(2)}, u32[]{:S(2)}) collective-permute-start(f32[128,4,128]{2,1,0:T(4,128)S(1)} %get-tuple-element.397), channel_id=1, source_target_pairs={{0,1},{1,2},{2,3},{3,4},{4,5},{5,6},{6,7},{7,8},{8,9},{9,10},{10,1... | collective-permute-start | bytes 786440 | tf_op jit(solution)/shard_map/while/body/eval_jaxpr/ppermute | solution.py:20
  416.0 16.1 %collective-permute-start.5 = (f32[128,4,128]{2,1,0:T(4,128)}, f32[128,4,128]{2,1,0:T(4,128)S(1)}, u32[]{:S(2)}, u32[]{:S(2)}) collective-permute-start(f32[128,4,128]{2,1,0:T(4,128)} %get-tuple-element.396), channel_id=1, source_target_pairs={{1,0},{2,1},{3,2},{4,3},{5,4},{6,5},{7,6},{8,7},{9,8},{10,9},{11,1... | collective-permute-start | bytes 786440 | tf_op jit(solution)/shard_map/while/body/eval_jaxpr/ppermute | solution.py:21
  425.5 20.4 %collective-permute-start.2 = (f32[128,4,128]{2,1,0:T(4,128)S(1)}, f32[128,4,128]{2,1,0:T(4,128)S(1)}, u32[]{:S(2)}, u32[]{:S(2)}) collective-permute-start(f32[128,4,128]{2,1,0:T(4,128)S(1)} %get-tuple-element.362), channel_id=1, source_target_pairs={{0,1},{1,2},{2,3},{3,4},{4,5},{5,6},{6,7},{7,8},{8,9},{9,10},{10,1... | collective-permute-start | bytes 786440 | tf_op jit(solution)/shard_map/while/body/eval_jaxpr/ppermute | solution.py:20
  470.2 21.0 %collective-permute-start.4 = (f32[128,4,128]{2,1,0:T(4,128)S(1)}, f32[128,4,128]{2,1,0:T(4,128)S(1)}, u32[]{:S(2)}, u32[]{:S(2)}) collective-permute-start(f32[128,4,128]{2,1,0:T(4,128)S(1)} %get-tuple-element.397), channel_id=1, source_target_pairs={{0,1},{1,2},{2,3},{3,4},{4,5},{5,6},{6,7},{7,8},{8,9},{9,10},{10,1... | collective-permute-start | bytes 786440 | tf_op jit(solution)/shard_map/while/body/eval_jaxpr/ppermute | solution.py:20
  475.1 16.1 %collective-permute-start.5 = (f32[128,4,128]{2,1,0:T(4,128)}, f32[128,4,128]{2,1,0:T(4,128)S(1)}, u32[]{:S(2)}, u32[]{:S(2)}) collective-permute-start(f32[128,4,128]{2,1,0:T(4,128)} %get-tuple-element.396), channel_id=1, source_target_pairs={{1,0},{2,1},{3,2},{4,3},{5,4},{6,5},{7,6},{8,7},{9,8},{10,9},{11,1... | collective-permute-start | bytes 786440 | tf_op jit(solution)/shard_map/while/body/eval_jaxpr/ppermute | solution.py:21
  484.6 20.4 %collective-permute-start.2 = (f32[128,4,128]{2,1,0:T(4,128)S(1)}, f32[128,4,128]{2,1,0:T(4,128)S(1)}, u32[]{:S(2)}, u32[]{:S(2)}) collective-permute-start(f32[128,4,128]{2,1,0:T(4,128)S(1)} %get-tuple-element.362), channel_id=1, source_target_pairs={{0,1},{1,2},{2,3},{3,4},{4,5},{5,6},{6,7},{7,8},{8,9},{9,10},{10,1... | collective-permute-start | bytes 786440 | tf_op jit(solution)/shard_map/while/body/eval_jaxpr/ppermute | solution.py:20
  529.3 21.0 %collective-permute-start.4 = (f32[128,4,128]{2,1,0:T(4,128)S(1)}, f32[128,4,128]{2,1,0:T(4,128)S(1)}, u32[]{:S(2)}, u32[]{:S(2)}) collective-permute-start(f32[128,4,128]{2,1,0:T(4,128)S(1)} %get-tuple-element.397), channel_id=1, source_target_pairs={{0,1},{1,2},{2,3},{3,4},{4,5},{5,6},{6,7},{7,8},{8,9},{9,10},{10,1... | collective-permute-start | bytes 786440 | tf_op jit(solution)/shard_map/while/body/eval_jaxpr/ppermute | solution.py:20
  534.2 16.1 %collective-permute-start.5 = (f32[128,4,128]{2,1,0:T(4,128)}, f32[128,4,128]{2,1,0:T(4,128)S(1)}, u32[]{:S(2)}, u32[]{:S(2)}) collective-permute-start(f32[128,4,128]{2,1,0:T(4,128)} %get-tuple-element.396), channel_id=1, source_target_pairs={{1,0},{2,1},{3,2},{4,3},{5,4},{6,5},{7,6},{8,7},{9,8},{10,9},{11,1... | collective-permute-start | bytes 786440 | tf_op jit(solution)/shard_map/while/body/eval_jaxpr/ppermute | solution.py:21
  543.7 20.4 %collective-permute-start.2 = (f32[128,4,128]{2,1,0:T(4,128)S(1)}, f32[128,4,128]{2,1,0:T(4,128)S(1)}, u32[]{:S(2)}, u32[]{:S(2)}) collective-permute-start(f32[128,4,128]{2,1,0:T(4,128)S(1)} %get-tuple-element.362), channel_id=1, source_target_pairs={{0,1},{1,2},{2,3},{3,4},{4,5},{5,6},{6,7},{7,8},{8,9},{9,10},{10,1... | collective-permute-start | bytes 786440 | tf_op jit(solution)/shard_map/while/body/eval_jaxpr/ppermute | solution.py:20
  588.4 21.0 %collective-permute-start.4 = (f32[128,4,128]{2,1,0:T(4,128)S(1)}, f32[128,4,128]{2,1,0:T(4,128)S(1)}, u32[]{:S(2)}, u32[]{:S(2)}) collective-permute-start(f32[128,4,128]{2,1,0:T(4,128)S(1)} %get-tuple-element.397), channel_id=1, source_target_pairs={{0,1},{1,2},{2,3},{3,4},{4,5},{5,6},{6,7},{7,8},{8,9},{9,10},{10,1... | collective-permute-start | bytes 786440 | tf_op jit(solution)/shard_map/while/body/eval_jaxpr/ppermute | solution.py:20
  593.3 16.1 %collective-permute-start.5 = (f32[128,4,128]{2,1,0:T(4,128)}, f32[128,4,128]{2,1,0:T(4,128)S(1)}, u32[]{:S(2)}, u32[]{:S(2)}) collective-permute-start(f32[128,4,128]{2,1,0:T(4,128)} %get-tuple-element.396), channel_id=1, source_target_pairs={{1,0},{2,1},{3,2},{4,3},{5,4},{6,5},{7,6},{8,7},{9,8},{10,9},{11,1... | collective-permute-start | bytes 786440 | tf_op jit(solution)/shard_map/while/body/eval_jaxpr/ppermute | solution.py:21
  602.8 20.4 %collective-permute-start.2 = (f32[128,4,128]{2,1,0:T(4,128)S(1)}, f32[128,4,128]{2,1,0:T(4,128)S(1)}, u32[]{:S(2)}, u32[]{:S(2)}) collective-permute-start(f32[128,4,128]{2,1,0:T(4,128)S(1)} %get-tuple-element.362), channel_id=1, source_target_pairs={{0,1},{1,2},{2,3},{3,4},{4,5},{5,6},{6,7},{7,8},{8,9},{9,10},{10,1... | collective-permute-start | bytes 786440 | tf_op jit(solution)/shard_map/while/body/eval_jaxpr/ppermute | solution.py:20
  642.7 27.1 %all-to-all-start.1 = ((f32[128,1,8,128]{3,2,1,0:T(8,128)}), f32[128,1,8,128]{3,2,1,0:T(8,128)S(1)}, u32[]{:S(2)}, u32[]{:S(2)}) async-start(f32[128,1,8,128]{3,2,1,0:T(8,128)} %multiply_bitcast_fusion), calls=%async_computation.1 | async-start | bytes 1048576 | tf_op jit(solution)/shard_map/all_to_all | solution.py:184
  (185 other events, 2506.7 us)

commit v7 on v6

--- a/solution.py
+++ b/solution.py
@@ -11,6 +11,7 @@
 stencil_weights = (8.0 / 5.0, -1.0 / 5.0, 8.0 / 315.0, -1.0 / 560.0)
 center_weight = 3.0 * (-205.0 / 72.0)
 HALO = 4
+ROWS = 8
 XOFF = 8
 
 
@@ -34,33 +35,35 @@
     ey_ref[HALO : HALO + block_y] = cur_ref[...]
     hx_ref[0, :, block_x - HALO : block_x, :] = xlo_ref[...]
     hx_ref[1, :, 0:HALO, :] = xhi_ref[...]
-    lane = lax.broadcasted_iota(jnp.int32, (block_x, depth_z), 1)
-    sub = lax.broadcasted_iota(jnp.int32, (block_x, depth_z), 0)
-
-    def row(y, carry):
-        ctr = ey_ref[HALO + y]
-        left = hx_ref[0, y]
-        right = hx_ref[1, y]
+    rows = ROWS
+    lane = lax.broadcasted_iota(jnp.int32, (rows, block_x, depth_z), 2)
+    sub = lax.broadcasted_iota(jnp.int32, (rows, block_x, depth_z), 1)
+
+    def chunk(index, carry):
+        y = pl.multiple_of(index * rows, rows)
+        ctr = ey_ref[pl.ds(HALO + y, rows)]
+        left = hx_ref[0, pl.ds(y, rows)]
+        right = hx_ref[1, pl.ds(y, rows)]
         acc = center_weight * ctr
         for m in range(1, HALO + 1):
-            ahead = pltpu.roll(jnp.where(sub >= m, ctr, right), block_x - m, 0)
-            behind = pltpu.roll(jnp.where(sub < block_x - m, ctr, left), m, 0)
+            ahead = pltpu.roll(jnp.where(sub >= m, ctr, right), block_x - m, 1)
+            behind = pltpu.roll(jnp.where(sub < block_x - m, ctr, left), m, 1)
             b = ahead + behind
-            b = b + ey_ref[HALO + y + m] + ey_ref[HALO + y - m]
-            up = jnp.where(lane < depth_z - m, pltpu.roll(ctr, depth_z - m, 1), 0.0)
-            down = jnp.where(lane >= m, pltpu.roll(ctr, m, 1), 0.0)
+            b = b + ey_ref[pl.ds(HALO + y + m, rows)] + ey_ref[pl.ds(HALO + y - m, rows)]
+            up = jnp.where(lane < depth_z - m, pltpu.roll(ctr, depth_z - m, 2), 0.0)
+            down = jnp.where(lane >= m, pltpu.roll(ctr, m, 2), 0.0)
             b = b + up + down
             acc = acc + stencil_weights[m - 1] * b
-        lap = acc + inj_ref[y]
-        upd = 2.0 * ctr - prev_ref[y] + s_ref[y] * lap
-        out_ref[y] = upd
-        head_ref[y] = upd[0:HALO]
-        tail_ref[y] = upd[block_x - HALO : block_x]
+        lap = acc + inj_ref[pl.ds(y, rows)]
+        upd = 2.0 * ctr - prev_ref[pl.ds(y, rows)] + s_ref[pl.ds(y, rows)] * lap
+        out_ref[pl.ds(y, rows)] = upd
+        head_ref[pl.ds(y, rows)] = upd[:, 0:HALO]
+        tail_ref[pl.ds(y, rows)] = upd[:, block_x - HALO : block_x]
         if with_image:
-            imgo_ref[y] = img_ref[y] + other_ref[y] * upd
+            imgo_ref[pl.ds(y, rows)] = img_ref[pl.ds(y, rows)] + other_ref[pl.ds(y, rows)] * upd
         return carry
 
-    lax.fori_loop(0, block_y, row, 0, unroll=2)
+    lax.fori_loop(0, block_y // rows, chunk, 0)
 
 
 def wave_call(component, moment, cur, prev, s, xlo, xhi, planes, other=None, img=None):

time: 675 us -> 530 us (0.79)
  Pallas kernels: 320 us -> 174 us
    pallas_call x40, Pallas kernels: 320 us -> 174 us  [wave_call(): pl.pallas_call(functools.partial(wave_kernel, with_image), out_shape=tupl...]
  transfers between devices with their start and end apart: 82 -> 82, of which waited for: 1 -> 1; matrix products, arithmetic and copies ran while one was open for 7% -> 9% of each run, Pallas kernels for 36% -> 25%
where the time goes in v7:
time: 530 us; the launch traced here: 526 us
  starting transfers between devices  271 us (51%)
  Pallas kernels  174 us (33%)
  local copies, waits for them, and re-layouts  41.8 us (8%)
  matrix products  12.8 us (2%)
  other arithmetic  12.5 us (2%)
  waiting for transfers between devices  10.4 us (2%)
    ppermute x40, starting transfers between devices, trade_halos(): low = lax.ppermute(tail, axis, [(i, (i + 1) % count) for i in range(ends)])  200 us
    pallas_call x40, Pallas kernels, wave_call(): pl.pallas_call(functools.partial(wave_kernel, with_image), out_shape=tupl...  174 us
    ppermute x40, starting transfers between devices, trade_halos(): high = lax.ppermute(head, axis, [((i + 1) % count, i) for i in range(ends)])  51.7 us
    pad x1, local copies, waits for them, and re-layouts, shards(): planes = jnp.pad(planes, ((0, 0), (0, 0), (0, 0), (0, 0), (0, depth_z - 4)))  16.2 us
    dot_general x2, matrix products, spread_points(): jnp.einsum('ny,nsc->syc', rows_y, weighted, precision=lax.Precision.HIGHEST)  12.1 us
    all_to_all x1, starting transfers between devices, shards(): lax.all_to_all(outgoing, 'dom', split_axis=0, concat_axis=1, tiled=True)  12.1 us
  transfers between devices with their start and end apart: 82, of which 1 were waited for; matrix products, arithmetic and copies ran while one was open for 9% of the time, Pallas kernels for 25%

profile of v7, /device:TPU:0, one launch (start us, length us, event | category | flops | bytes accessed | tf_op | source)
XLA Modules:
  0.0 526.3 jit_solution(17628372496086288856)
XLA Ops:
  3.6 7.4 %all-to-all-start = ((f32[8,16,8,128]{3,2,0,1:T(8,128)}), f32[8,16,8,128]{3,2,0,1:T(8,128)S(1)}, u32[]{:S(2)}, u32[]{:S(2)}) async-start(f32[8,16,8,128]{3,2,0,1:T(8,128)} %select_bitcast_fusion), calls=%async_computation | async-start | bytes 1048576 | tf_op jit(solution)/shard_map/all_to_all | solution.py:142
  15.6 11.6 %fusion = f32[20,32,128]{2,1,0:T(8,128)S(1)} fusion(f32[8192,20]{0,1:T(8,128)} %bitcast.79, f32[8192,32]{0,1:T(8,128)S(1)} %fusion.8, s32[8192]{0:T(1024)S(1)} %bitcast.77), kind=kOutput, calls=%fused_computation.1 | convolution fusion | flops 8059355136 | bytes 2064384 | tf_op jit(solution)/shard_map/ny,nsc->syc/dot_general | solution.py:129
  27.9 10.1 %copy.32 = f32[20,2,128,8,4]{4,3,2,1,0:T(8,128)} copy(f32[20,2,128,8,4]{2,3,4,1,0:T(8,128)S(1)} %pad_maximum_fusion.2) | data formatting | bytes 1310720
  38.0 16.2 %pad.4.clone = f32[20,2,128,8,128]{4,3,2,1,0:T(8,128)} pad(f32[20,2,128,8,4]{4,3,2,1,0:T(8,128)} %copy.32, f32[]{:T(128)} %constant.44.clone.1), padding=0_0x0_0x0_0x0_0x0_124 | pad | bytes 21626884 | tf_op jit(solution)/shard_map/jit(_pad)/pad | solution.py:153
  57.2 439.0 %while.29 = (s32[]{:T(128)}, f32[128,8,128]{2,1,0:T(8,128)}, f32[128,8,128]{2,1,0:T(8,128)S(1)}, f32[128,4,128]{2,1,0:T(4,128)S(1)}, f32[128,4,128]{2,1,0:T(4,12...) while((s32[]{:T(128)}, f32[128,8,128]{2,1,0:T(8,128)}, ...), condition=%wide.region_1.2_spmd, body=%wide.region_0.1_spmd.sunk | while | flops 31457284 | bytes 47186760 | solution.py:176
  86.0 4.8 eval_jaxpr.21
  96.2 5.2 collective-permute-start
  111.9 7.0 %collective-permute-start.2 = (f32[128,4,128]{2,1,0:T(4,128)S(1)}, f32[128,4,128]{2,1,0:T(4,128)S(1)}, u32[]{:S(2)}, u32[]{:S(2)}) collective-permute-start(f32[128,4,128]{2,1,0:T(4,128)S(1)} %get-tuple-element.362), channel_id=1, source_target_pairs={{0,1},{1,2},{2,3},{3,4},{4,5},{5,6},{6,7},{7,8},{8,9},{9,10},{10,1... | collective-permute-start | bytes 786440 | tf_op jit(solution)/shard_map/while/body/eval_jaxpr/ppermute | solution.py:21
  129.5 4.8 eval_jaxpr.21
  139.8 6.1 %collective-permute-start = (f32[128,4,128]{2,1,0:T(4,128)S(1)}, f32[128,4,128]{2,1,0:T(4,128)S(1)}, u32[]{:S(2)}, u32[]{:S(2)}) collective-permute-start(f32[128,4,128]{2,1,0:T(4,128)S(1)} %get-tuple-element.393), channel_id=1, source_target_pairs={{0,1},{1,2},{2,3},{3,4},{4,5},{5,6},{6,7},{7,8},{8,9},{9,10},{10,1... | collective-permute-start | bytes 786440 | tf_op jit(solution)/shard_map/while/body/eval_jaxpr/ppermute | solution.py:21
  156.4 7.0 %collective-permute-start.2 = (f32[128,4,128]{2,1,0:T(4,128)S(1)}, f32[128,4,128]{2,1,0:T(4,128)S(1)}, u32[]{:S(2)}, u32[]{:S(2)}) collective-permute-start(f32[128,4,128]{2,1,0:T(4,128)S(1)} %get-tuple-element.362), channel_id=1, source_target_pairs={{0,1},{1,2},{2,3},{3,4},{4,5},{5,6},{6,7},{7,8},{8,9},{9,10},{10,1... | collective-permute-start | bytes 786440 | tf_op jit(solution)/shard_map/while/body/eval_jaxpr/ppermute | solution.py:21
  174.1 4.8 eval_jaxpr.21
  184.3 6.1 %collective-permute-start = (f32[128,4,128]{2,1,0:T(4,128)S(1)}, f32[128,4,128]{2,1,0:T(4,128)S(1)}, u32[]{:S(2)}, u32[]{:S(2)}) collective-permute-start(f32[128,4,128]{2,1,0:T(4,128)S(1)} %get-tuple-element.393), channel_id=1, source_target_pairs={{0,1},{1,2},{2,3},{3,4},{4,5},{5,6},{6,7},{7,8},{8,9},{9,10},{10,1... | collective-permute-start | bytes 786440 | tf_op jit(solution)/shard_map/while/body/eval_jaxpr/ppermute | solution.py:21
  201.0 7.0 %collective-permute-start.2 = (f32[128,4,128]{2,1,0:T(4,128)S(1)}, f32[128,4,128]{2,1,0:T(4,128)S(1)}, u32[]{:S(2)}, u32[]{:S(2)}) collective-permute-start(f32[128,4,128]{2,1,0:T(4,128)S(1)} %get-tuple-element.362), channel_id=1, source_target_pairs={{0,1},{1,2},{2,3},{3,4},{4,5},{5,6},{6,7},{7,8},{8,9},{9,10},{10,1... | collective-permute-start | bytes 786440 | tf_op jit(solution)/shard_map/while/body/eval_jaxpr/ppermute | solution.py:21
  218.6 4.8 eval_jaxpr.21
  228.9 6.1 %collective-permute-start = (f32[128,4,128]{2,1,0:T(4,128)S(1)}, f32[128,4,128]{2,1,0:T(4,128)S(1)}, u32[]{:S(2)}, u32[]{:S(2)}) collective-permute-start(f32[128,4,128]{2,1,0:T(4,128)S(1)} %get-tuple-element.393), channel_id=1, source_target_pairs={{0,1},{1,2},{2,3},{3,4},{4,5},{5,6},{6,7},{7,8},{8,9},{9,10},{10,1... | collective-permute-start | bytes 786440 | tf_op jit(solution)/shard_map/while/body/eval_jaxpr/ppermute | solution.py:21
  245.5 7.0 %collective-permute-start.2 = (f32[128,4,128]{2,1,0:T(4,128)S(1)}, f32[128,4,128]{2,1,0:T(4,128)S(1)}, u32[]{:S(2)}, u32[]{:S(2)}) collective-permute-start(f32[128,4,128]{2,1,0:T(4,128)S(1)} %get-tuple-element.362), channel_id=1, source_target_pairs={{0,1},{1,2},{2,3},{3,4},{4,5},{5,6},{6,7},{7,8},{8,9},{9,10},{10,1... | collective-permute-start | bytes 786440 | tf_op jit(solution)/shard_map/while/body/eval_jaxpr/ppermute | solution.py:21
  263.2 4.8 eval_jaxpr.21
  273.4 6.1 %collective-permute-start = (f32[128,4,128]{2,1,0:T(4,128)S(1)}, f32[128,4,128]{2,1,0:T(4,128)S(1)}, u32[]{:S(2)}, u32[]{:S(2)}) collective-permute-start(f32[128,4,128]{2,1,0:T(4,128)S(1)} %get-tuple-element.393), channel_id=1, source_target_pairs={{0,1},{1,2},{2,3},{3,4},{4,5},{5,6},{6,7},{7,8},{8,9},{9,10},{10,1... | collective-permute-start | bytes 786440 | tf_op jit(solution)/shard_map/while/body/eval_jaxpr/ppermute | solution.py:21
  290.1 7.0 %collective-permute-start.2 = (f32[128,4,128]{2,1,0:T(4,128)S(1)}, f32[128,4,128]{2,1,0:T(4,128)S(1)}, u32[]{:S(2)}, u32[]{:S(2)}) collective-permute-start(f32[128,4,128]{2,1,0:T(4,128)S(1)} %get-tuple-element.362), channel_id=1, source_target_pairs={{0,1},{1,2},{2,3},{3,4},{4,5},{5,6},{6,7},{7,8},{8,9},{9,10},{10,1... | collective-permute-start | bytes 786440 | tf_op jit(solution)/shard_map/while/body/eval_jaxpr/ppermute | solution.py:21
  307.7 4.8 eval_jaxpr.21
  318.0 6.1 %collective-permute-start = (f32[128,4,128]{2,1,0:T(4,128)S(1)}, f32[128,4,128]{2,1,0:T(4,128)S(1)}, u32[]{:S(2)}, u32[]{:S(2)}) collective-permute-start(f32[128,4,128]{2,1,0:T(4,128)S(1)} %get-tuple-element.393), channel_id=1, source_target_pairs={{0,1},{1,2},{2,3},{3,4},{4,5},{5,6},{6,7},{7,8},{8,9},{9,10},{10,1... | collective-permute-start | bytes 786440 | tf_op jit(solution)/shard_map/while/body/eval_jaxpr/ppermute | solution.py:21
  334.6 7.0 %collective-permute-start.2 = (f32[128,4,128]{2,1,0:T(4,128)S(1)}, f32[128,4,128]{2,1,0:T(4,128)S(1)}, u32[]{:S(2)}, u32[]{:S(2)}) collective-permute-start(f32[128,4,128]{2,1,0:T(4,128)S(1)} %get-tuple-element.362), channel_id=1, source_target_pairs={{0,1},{1,2},{2,3},{3,4},{4,5},{5,6},{6,7},{7,8},{8,9},{9,10},{10,1... | collective-permute-start | bytes 786440 | tf_op jit(solution)/shard_map/while/body/eval_jaxpr/ppermute | solution.py:21
  362.5 6.1 %collective-permute-start = (f32[128,4,128]{2,1,0:T(4,128)S(1)}, f32[128,4,128]{2,1,0:T(4,128)S(1)}, u32[]{:S(2)}, u32[]{:S(2)}) collective-permute-start(f32[128,4,128]{2,1,0:T(4,128)S(1)} %get-tuple-element.393), channel_id=1, source_target_pairs={{0,1},{1,2},{2,3},{3,4},{4,5},{5,6},{6,7},{7,8},{8,9},{9,10},{10,1... | collective-permute-start | bytes 786440 | tf_op jit(solution)/shard_map/while/body/eval_jaxpr/ppermute | solution.py:21
  379.2 7.0 %collective-permute-start.2 = (f32[128,4,128]{2,1,0:T(4,128)S(1)}, f32[128,4,128]{2,1,0:T(4,128)S(1)}, u32[]{:S(2)}, u32[]{:S(2)}) collective-permute-start(f32[128,4,128]{2,1,0:T(4,128)S(1)} %get-tuple-element.362), channel_id=1, source_target_pairs={{0,1},{1,2},{2,3},{3,4},{4,5},{5,6},{6,7},{7,8},{8,9},{9,10},{10,1... | collective-permute-start | bytes 786440 | tf_op jit(solution)/shard_map/while/body/eval_jaxpr/ppermute | solution.py:21
  407.1 6.1 %collective-permute-start = (f32[128,4,128]{2,1,0:T(4,128)S(1)}, f32[128,4,128]{2,1,0:T(4,128)S(1)}, u32[]{:S(2)}, u32[]{:S(2)}) collective-permute-start(f32[128,4,128]{2,1,0:T(4,128)S(1)} %get-tuple-element.393), channel_id=1, source_target_pairs={{0,1},{1,2},{2,3},{3,4},{4,5},{5,6},{6,7},{7,8},{8,9},{9,10},{10,1... | collective-permute-start | bytes 786440 | tf_op jit(solution)/shard_map/while/body/eval_jaxpr/ppermute | solution.py:21
  423.7 7.0 %collective-permute-start.2 = (f32[128,4,128]{2,1,0:T(4,128)S(1)}, f32[128,4,128]{2,1,0:T(4,128)S(1)}, u32[]{:S(2)}, u32[]{:S(2)}) collective-permute-start(f32[128,4,128]{2,1,0:T(4,128)S(1)} %get-tuple-element.362), channel_id=1, source_target_pairs={{0,1},{1,2},{2,3},{3,4},{4,5},{5,6},{6,7},{7,8},{8,9},{9,10},{10,1... | collective-permute-start | bytes 786440 | tf_op jit(solution)/shard_map/while/body/eval_jaxpr/ppermute | solution.py:21
  451.6 6.1 %collective-permute-start = (f32[128,4,128]{2,1,0:T(4,128)S(1)}, f32[128,4,128]{2,1,0:T(4,128)S(1)}, u32[]{:S(2)}, u32[]{:S(2)}) collective-permute-start(f32[128,4,128]{2,1,0:T(4,128)S(1)} %get-tuple-element.393), channel_id=1, source_target_pairs={{0,1},{1,2},{2,3},{3,4},{4,5},{5,6},{6,7},{7,8},{8,9},{9,10},{10,1... | collective-permute-start | bytes 786440 | tf_op jit(solution)/shard_map/while/body/eval_jaxpr/ppermute | solution.py:21
  468.3 7.0 %collective-permute-start.2 = (f32[128,4,128]{2,1,0:T(4,128)S(1)}, f32[128,4,128]{2,1,0:T(4,128)S(1)}, u32[]{:S(2)}, u32[]{:S(2)}) collective-permute-start(f32[128,4,128]{2,1,0:T(4,128)S(1)} %get-tuple-element.362), channel_id=1, source_target_pairs={{0,1},{1,2},{2,3},{3,4},{4,5},{5,6},{6,7},{7,8},{8,9},{9,10},{10,1... | collective-permute-start | bytes 786440 | tf_op jit(solution)/shard_map/while/body/eval_jaxpr/ppermute | solution.py:21
  486.0 4.8 eval_jaxpr.21
  498.1 12.1 %all-to-all-start.1 = ((f32[128,1,8,128]{3,2,1,0:T(8,128)}), f32[128,1,8,128]{3,2,1,0:T(8,128)S(1)}, u32[]{:S(2)}, u32[]{:S(2)}) async-start(f32[128,1,8,128]{3,2,1,0:T(8,128)} %multiply_bitcast_fusion), calls=%async_computation.1 | async-start | bytes 1048576 | tf_op jit(solution)/shard_map/all_to_all | solution.py:187
  514.5 10.1 %all-to-all-done.1 = f32[128,1,8,128]{3,2,1,0:T(8,128)S(1)} async-done(((f32[128,1,8,128]{3,2,1,0:T(8,128)}), f32[128,1,8,128]{3,2,1,0:T(8,128)S(1)}, u32[]{:S(2)}, u32[]{:S(2)}) %all-to-all-start.1) | async-done | bytes 524320 | tf_op jit(solution)/shard_map/all_to_all | solution.py:187
  (472 shorter events, 305.0 us)
Async XLA Ops:
  3.6 52.7 %all-to-all-start = ((f32[8,16,8,128]{3,2,0,1:T(8,128)}), f32[8,16,8,128]{3,2,0,1:T(8,128)S(1)}, u32[]{:S(2)}, u32[]{:S(2)}) async-start(f32[8,16,8,128]{3,2,0,1:T(8,128)} %select_bitcast_fusion), calls=%async_computation | async-start | bytes 1048576 | tf_op jit(solution)/shard_map/all_to_all | solution.py:142
  60.9 15.7 %collective-permute-start.4 = (f32[128,4,128]{2,1,0:T(4,128)S(1)}, f32[128,4,128]{2,1,0:T(4,128)S(1)}, u32[]{:S(2)}, u32[]{:S(2)}) collective-permute-start(f32[128,4,128]{2,1,0:T(4,128)S(1)} %get-tuple-element.397), channel_id=1, source_target_pairs={{0,1},{1,2},{2,3},{3,4},{4,5},{5,6},{6,7},{7,8},{8,9},{9,10},{10,1... | collective-permute-start | bytes 786440 | tf_op jit(solution)/shard_map/while/body/eval_jaxpr/ppermute | solution.py:21
  71.0 15.0 %collective-permute-start.2 = (f32[128,4,128]{2,1,0:T(4,128)S(1)}, f32[128,4,128]{2,1,0:T(4,128)S(1)}, u32[]{:S(2)}, u32[]{:S(2)}) collective-permute-start(f32[128,4,128]{2,1,0:T(4,128)S(1)} %get-tuple-element.362), channel_id=1, source_target_pairs={{0,1},{1,2},{2,3},{3,4},{4,5},{5,6},{6,7},{7,8},{8,9},{9,10},{10,1... | collective-permute-start | bytes 786440 | tf_op jit(solution)/shard_map/while/body/eval_jaxpr/ppermute | solution.py:21
  102.7 17.5 %collective-permute-start.4 = (f32[128,4,128]{2,1,0:T(4,128)S(1)}, f32[128,4,128]{2,1,0:T(4,128)S(1)}, u32[]{:S(2)}, u32[]{:S(2)}) collective-permute-start(f32[128,4,128]{2,1,0:T(4,128)S(1)} %get-tuple-element.397), channel_id=1, source_target_pairs={{0,1},{1,2},{2,3},{3,4},{4,5},{5,6},{6,7},{7,8},{8,9},{9,10},{10,1... | collective-permute-start | bytes 786440 | tf_op jit(solution)/shard_map/while/body/eval_jaxpr/ppermute | solution.py:21
  106.0 14.2 %collective-permute-start.5 = (f32[128,4,128]{2,1,0:T(4,128)}, f32[128,4,128]{2,1,0:T(4,128)S(1)}, u32[]{:S(2)}, u32[]{:S(2)}) collective-permute-start(f32[128,4,128]{2,1,0:T(4,128)} %get-tuple-element.396), channel_id=1, source_target_pairs={{1,0},{2,1},{3,2},{4,3},{5,4},{6,5},{7,6},{8,7},{9,8},{10,9},{11,1... | collective-permute-start | bytes 786440 | tf_op jit(solution)/shard_map/while/body/eval_jaxpr/ppermute | solution.py:22
  111.9 17.6 %collective-permute-start.2 = (f32[128,4,128]{2,1,0:T(4,128)S(1)}, f32[128,4,128]{2,1,0:T(4,128)S(1)}, u32[]{:S(2)}, u32[]{:S(2)}) collective-permute-start(f32[128,4,128]{2,1,0:T(4,128)S(1)} %get-tuple-element.362), channel_id=1, source_target_pairs={{0,1},{1,2},{2,3},{3,4},{4,5},{5,6},{6,7},{7,8},{8,9},{9,10},{10,1... | collective-permute-start | bytes 786440 | tf_op jit(solution)/shard_map/while/body/eval_jaxpr/ppermute | solution.py:21
  147.1 17.6 %collective-permute-start.4 = (f32[128,4,128]{2,1,0:T(4,128)S(1)}, f32[128,4,128]{2,1,0:T(4,128)S(1)}, u32[]{:S(2)}, u32[]{:S(2)}) collective-permute-start(f32[128,4,128]{2,1,0:T(4,128)S(1)} %get-tuple-element.397), channel_id=1, source_target_pairs={{0,1},{1,2},{2,3},{3,4},{4,5},{5,6},{6,7},{7,8},{8,9},{9,10},{10,1... | collective-permute-start | bytes 786440 | tf_op jit(solution)/shard_map/while/body/eval_jaxpr/ppermute | solution.py:21
  150.5 14.3 %collective-permute-start.5 = (f32[128,4,128]{2,1,0:T(4,128)}, f32[128,4,128]{2,1,0:T(4,128)S(1)}, u32[]{:S(2)}, u32[]{:S(2)}) collective-permute-start(f32[128,4,128]{2,1,0:T(4,128)} %get-tuple-element.396), channel_id=1, source_target_pairs={{1,0},{2,1},{3,2},{4,3},{5,4},{6,5},{7,6},{8,7},{9,8},{10,9},{11,1... | collective-permute-start | bytes 786440 | tf_op jit(solution)/shard_map/while/body/eval_jaxpr/ppermute | solution.py:22
  156.4 17.7 %collective-permute-start.2 = (f32[128,4,128]{2,1,0:T(4,128)S(1)}, f32[128,4,128]{2,1,0:T(4,128)S(1)}, u32[]{:S(2)}, u32[]{:S(2)}) collective-permute-start(f32[128,4,128]{2,1,0:T(4,128)S(1)} %get-tuple-element.362), channel_id=1, source_target_pairs={{0,1},{1,2},{2,3},{3,4},{4,5},{5,6},{6,7},{7,8},{8,9},{9,10},{10,1... | collective-permute-start | bytes 786440 | tf_op jit(solution)/shard_map/while/body/eval_jaxpr/ppermute | solution.py:21
  184.3 12.1 %collective-permute-start = (f32[128,4,128]{2,1,0:T(4,128)S(1)}, f32[128,4,128]{2,1,0:T(4,128)S(1)}, u32[]{:S(2)}, u32[]{:S(2)}) collective-permute-start(f32[128,4,128]{2,1,0:T(4,128)S(1)} %get-tuple-element.393), channel_id=1, source_target_pairs={{0,1},{1,2},{2,3},{3,4},{4,5},{5,6},{6,7},{7,8},{8,9},{9,10},{10,1... | collective-permute-start | bytes 786440 | tf_op jit(solution)/shard_map/while/body/eval_jaxpr/ppermute | solution.py:21
  191.7 17.6 %collective-permute-start.4 = (f32[128,4,128]{2,1,0:T(4,128)S(1)}, f32[128,4,128]{2,1,0:T(4,128)S(1)}, u32[]{:S(2)}, u32[]{:S(2)}) collective-permute-start(f32[128,4,128]{2,1,0:T(4,128)S(1)} %get-tuple-element.397), channel_id=1, source_target_pairs={{0,1},{1,2},{2,3},{3,4},{4,5},{5,6},{6,7},{7,8},{8,9},{9,10},{10,1... | collective-permute-start | bytes 786440 | tf_op jit(solution)/shard_map/while/body/eval_jaxpr/ppermute | solution.py:21
  195.1 14.3 %collective-permute-start.5 = (f32[128,4,128]{2,1,0:T(4,128)}, f32[128,4,128]{2,1,0:T(4,128)S(1)}, u32[]{:S(2)}, u32[]{:S(2)}) collective-permute-start(f32[128,4,128]{2,1,0:T(4,128)} %get-tuple-element.396), channel_id=1, source_target_pairs={{1,0},{2,1},{3,2},{4,3},{5,4},{6,5},{7,6},{8,7},{9,8},{10,9},{11,1... | collective-permute-start | bytes 786440 | tf_op jit(solution)/shard_map/while/body/eval_jaxpr/ppermute | solution.py:22
  201.0 17.7 %collective-permute-start.2 = (f32[128,4,128]{2,1,0:T(4,128)S(1)}, f32[128,4,128]{2,1,0:T(4,128)S(1)}, u32[]{:S(2)}, u32[]{:S(2)}) collective-permute-start(f32[128,4,128]{2,1,0:T(4,128)S(1)} %get-tuple-element.362), channel_id=1, source_target_pairs={{0,1},{1,2},{2,3},{3,4},{4,5},{5,6},{6,7},{7,8},{8,9},{9,10},{10,1... | collective-permute-start | bytes 786440 | tf_op jit(solution)/shard_map/while/body/eval_jaxpr/ppermute | solution.py:21
  236.2 17.6 %collective-permute-start.4 = (f32[128,4,128]{2,1,0:T(4,128)S(1)}, f32[128,4,128]{2,1,0:T(4,128)S(1)}, u32[]{:S(2)}, u32[]{:S(2)}) collective-permute-start(f32[128,4,128]{2,1,0:T(4,128)S(1)} %get-tuple-element.397), channel_id=1, source_target_pairs={{0,1},{1,2},{2,3},{3,4},{4,5},{5,6},{6,7},{7,8},{8,9},{9,10},{10,1... | collective-permute-start | bytes 786440 | tf_op jit(solution)/shard_map/while/body/eval_jaxpr/ppermute | solution.py:21
  239.6 14.3 %collective-permute-start.5 = (f32[128,4,128]{2,1,0:T(4,128)}, f32[128,4,128]{2,1,0:T(4,128)S(1)}, u32[]{:S(2)}, u32[]{:S(2)}) collective-permute-start(f32[128,4,128]{2,1,0:T(4,128)} %get-tuple-element.396), channel_id=1, source_target_pairs={{1,0},{2,1},{3,2},{4,3},{5,4},{6,5},{7,6},{8,7},{9,8},{10,9},{11,1... | collective-permute-start | bytes 786440 | tf_op jit(solution)/shard_map/while/body/eval_jaxpr/ppermute | solution.py:22
  245.5 17.7 %collective-permute-start.2 = (f32[128,4,128]{2,1,0:T(4,128)S(1)}, f32[128,4,128]{2,1,0:T(4,128)S(1)}, u32[]{:S(2)}, u32[]{:S(2)}) collective-permute-start(f32[128,4,128]{2,1,0:T(4,128)S(1)} %get-tuple-element.362), channel_id=1, source_target_pairs={{0,1},{1,2},{2,3},{3,4},{4,5},{5,6},{6,7},{7,8},{8,9},{9,10},{10,1... | collective-permute-start | bytes 786440 | tf_op jit(solution)/shard_map/while/body/eval_jaxpr/ppermute | solution.py:21
  280.8 17.6 %collective-permute-start.4 = (f32[128,4,128]{2,1,0:T(4,128)S(1)}, f32[128,4,128]{2,1,0:T(4,128)S(1)}, u32[]{:S(2)}, u32[]{:S(2)}) collective-permute-start(f32[128,4,128]{2,1,0:T(4,128)S(1)} %get-tuple-element.397), channel_id=1, source_target_pairs={{0,1},{1,2},{2,3},{3,4},{4,5},{5,6},{6,7},{7,8},{8,9},{9,10},{10,1... | collective-permute-start | bytes 786440 | tf_op jit(solution)/shard_map/while/body/eval_jaxpr/ppermute | solution.py:21
  284.2 14.3 %collective-permute-start.5 = (f32[128,4,128]{2,1,0:T(4,128)}, f32[128,4,128]{2,1,0:T(4,128)S(1)}, u32[]{:S(2)}, u32[]{:S(2)}) collective-permute-start(f32[128,4,128]{2,1,0:T(4,128)} %get-tuple-element.396), channel_id=1, source_target_pairs={{1,0},{2,1},{3,2},{4,3},{5,4},{6,5},{7,6},{8,7},{9,8},{10,9},{11,1... | collective-permute-start | bytes 786440 | tf_op jit(solution)/shard_map/while/body/eval_jaxpr/ppermute | solution.py:22
  290.1 17.7 %collective-permute-start.2 = (f32[128,4,128]{2,1,0:T(4,128)S(1)}, f32[128,4,128]{2,1,0:T(4,128)S(1)}, u32[]{:S(2)}, u32[]{:S(2)}) collective-permute-start(f32[128,4,128]{2,1,0:T(4,128)S(1)} %get-tuple-element.362), channel_id=1, source_target_pairs={{0,1},{1,2},{2,3},{3,4},{4,5},{5,6},{6,7},{7,8},{8,9},{9,10},{10,1... | collective-permute-start | bytes 786440 | tf_op jit(solution)/shard_map/while/body/eval_jaxpr/ppermute | solution.py:21
  325.3 17.6 %collective-permute-start.4 = (f32[128,4,128]{2,1,0:T(4,128)S(1)}, f32[128,4,128]{2,1,0:T(4,128)S(1)}, u32[]{:S(2)}, u32[]{:S(2)}) collective-permute-start(f32[128,4,128]{2,1,0:T(4,128)S(1)} %get-tuple-element.397), channel_id=1, source_target_pairs={{0,1},{1,2},{2,3},{3,4},{4,5},{5,6},{6,7},{7,8},{8,9},{9,10},{10,1... | collective-permute-start | bytes 786440 | tf_op jit(solution)/shard_map/while/body/eval_jaxpr/ppermute | solution.py:21
  328.7 14.3 %collective-permute-start.5 = (f32[128,4,128]{2,1,0:T(4,128)}, f32[128,4,128]{2,1,0:T(4,128)S(1)}, u32[]{:S(2)}, u32[]{:S(2)}) collective-permute-start(f32[128,4,128]{2,1,0:T(4,128)} %get-tuple-element.396), channel_id=1, source_target_pairs={{1,0},{2,1},{3,2},{4,3},{5,4},{6,5},{7,6},{8,7},{9,8},{10,9},{11,1... | collective-permute-start | bytes 786440 | tf_op jit(solution)/shard_map/while/body/eval_jaxpr/ppermute | solution.py:22
  334.6 17.7 %collective-permute-start.2 = (f32[128,4,128]{2,1,0:T(4,128)S(1)}, f32[128,4,128]{2,1,0:T(4,128)S(1)}, u32[]{:S(2)}, u32[]{:S(2)}) collective-permute-start(f32[128,4,128]{2,1,0:T(4,128)S(1)} %get-tuple-element.362), channel_id=1, source_target_pairs={{0,1},{1,2},{2,3},{3,4},{4,5},{5,6},{6,7},{7,8},{8,9},{9,10},{10,1... | collective-permute-start | bytes 786440 | tf_op jit(solution)/shard_map/while/body/eval_jaxpr/ppermute | solution.py:21
  369.9 17.6 %collective-permute-start.4 = (f32[128,4,128]{2,1,0:T(4,128)S(1)}, f32[128,4,128]{2,1,0:T(4,128)S(1)}, u32[]{:S(2)}, u32[]{:S(2)}) collective-permute-start(f32[128,4,128]{2,1,0:T(4,128)S(1)} %get-tuple-element.397), channel_id=1, source_target_pairs={{0,1},{1,2},{2,3},{3,4},{4,5},{5,6},{6,7},{7,8},{8,9},{9,10},{10,1... | collective-permute-start | bytes 786440 | tf_op jit(solution)/shard_map/while/body/eval_jaxpr/ppermute | solution.py:21
  373.3 14.3 %collective-permute-start.5 = (f32[128,4,128]{2,1,0:T(4,128)}, f32[128,4,128]{2,1,0:T(4,128)S(1)}, u32[]{:S(2)}, u32[]{:S(2)}) collective-permute-start(f32[128,4,128]{2,1,0:T(4,128)} %get-tuple-element.396), channel_id=1, source_target_pairs={{1,0},{2,1},{3,2},{4,3},{5,4},{6,5},{7,6},{8,7},{9,8},{10,9},{11,1... | collective-permute-start | bytes 786440 | tf_op jit(solution)/shard_map/while/body/eval_jaxpr/ppermute | solution.py:22
  379.2 17.7 %collective-permute-start.2 = (f32[128,4,128]{2,1,0:T(4,128)S(1)}, f32[128,4,128]{2,1,0:T(4,128)S(1)}, u32[]{:S(2)}, u32[]{:S(2)}) collective-permute-start(f32[128,4,128]{2,1,0:T(4,128)S(1)} %get-tuple-element.362), channel_id=1, source_target_pairs={{0,1},{1,2},{2,3},{3,4},{4,5},{5,6},{6,7},{7,8},{8,9},{9,10},{10,1... | collective-permute-start | bytes 786440 | tf_op jit(solution)/shard_map/while/body/eval_jaxpr/ppermute | solution.py:21
  414.5 17.6 %collective-permute-start.4 = (f32[128,4,128]{2,1,0:T(4,128)S(1)}, f32[128,4,128]{2,1,0:T(4,128)S(1)}, u32[]{:S(2)}, u32[]{:S(2)}) collective-permute-start(f32[128,4,128]{2,1,0:T(4,128)S(1)} %get-tuple-element.397), channel_id=1, source_target_pairs={{0,1},{1,2},{2,3},{3,4},{4,5},{5,6},{6,7},{7,8},{8,9},{9,10},{10,1... | collective-permute-start | bytes 786440 | tf_op jit(solution)/shard_map/while/body/eval_jaxpr/ppermute | solution.py:21
  417.8 14.3 %collective-permute-start.5 = (f32[128,4,128]{2,1,0:T(4,128)}, f32[128,4,128]{2,1,0:T(4,128)S(1)}, u32[]{:S(2)}, u32[]{:S(2)}) collective-permute-start(f32[128,4,128]{2,1,0:T(4,128)} %get-tuple-element.396), channel_id=1, source_target_pairs={{1,0},{2,1},{3,2},{4,3},{5,4},{6,5},{7,6},{8,7},{9,8},{10,9},{11,1... | collective-permute-start | bytes 786440 | tf_op jit(solution)/shard_map/while/body/eval_jaxpr/ppermute | solution.py:22
  423.7 17.7 %collective-permute-start.2 = (f32[128,4,128]{2,1,0:T(4,128)S(1)}, f32[128,4,128]{2,1,0:T(4,128)S(1)}, u32[]{:S(2)}, u32[]{:S(2)}) collective-permute-start(f32[128,4,128]{2,1,0:T(4,128)S(1)} %get-tuple-element.362), channel_id=1, source_target_pairs={{0,1},{1,2},{2,3},{3,4},{4,5},{5,6},{6,7},{7,8},{8,9},{9,10},{10,1... | collective-permute-start | bytes 786440 | tf_op jit(solution)/shard_map/while/body/eval_jaxpr/ppermute | solution.py:21
  459.0 17.6 %collective-permute-start.4 = (f32[128,4,128]{2,1,0:T(4,128)S(1)}, f32[128,4,128]{2,1,0:T(4,128)S(1)}, u32[]{:S(2)}, u32[]{:S(2)}) collective-permute-start(f32[128,4,128]{2,1,0:T(4,128)S(1)} %get-tuple-element.397), channel_id=1, source_target_pairs={{0,1},{1,2},{2,3},{3,4},{4,5},{5,6},{6,7},{7,8},{8,9},{9,10},{10,1... | collective-permute-start | bytes 786440 | tf_op jit(solution)/shard_map/while/body/eval_jaxpr/ppermute | solution.py:21
  462.4 14.3 %collective-permute-start.5 = (f32[128,4,128]{2,1,0:T(4,128)}, f32[128,4,128]{2,1,0:T(4,128)S(1)}, u32[]{:S(2)}, u32[]{:S(2)}) collective-permute-start(f32[128,4,128]{2,1,0:T(4,128)} %get-tuple-element.396), channel_id=1, source_target_pairs={{1,0},{2,1},{3,2},{4,3},{5,4},{6,5},{7,6},{8,7},{9,8},{10,9},{11,1... | collective-permute-start | bytes 786440 | tf_op jit(solution)/shard_map/while/body/eval_jaxpr/ppermute | solution.py:22
  468.3 17.7 %collective-permute-start.2 = (f32[128,4,128]{2,1,0:T(4,128)S(1)}, f32[128,4,128]{2,1,0:T(4,128)S(1)}, u32[]{:S(2)}, u32[]{:S(2)}) collective-permute-start(f32[128,4,128]{2,1,0:T(4,128)S(1)} %get-tuple-element.362), channel_id=1, source_target_pairs={{0,1},{1,2},{2,3},{3,4},{4,5},{5,6},{6,7},{7,8},{8,9},{9,10},{10,1... | collective-permute-start | bytes 786440 | tf_op jit(solution)/shard_map/while/body/eval_jaxpr/ppermute | solution.py:21
  498.1 26.6 %all-to-all-start.1 = ((f32[128,1,8,128]{3,2,1,0:T(8,128)}), f32[128,1,8,128]{3,2,1,0:T(8,128)S(1)}, u32[]{:S(2)}, u32[]{:S(2)}) async-start(f32[128,1,8,128]{3,2,1,0:T(8,128)} %multiply_bitcast_fusion), calls=%async_computation.1 | async-start | bytes 1048576 | tf_op jit(solution)/shard_map/all_to_all | solution.py:187
  (185 other events, 1931.8 us)

commit v8 on v7

--- a/solution.py
+++ b/solution.py
@@ -54,7 +54,9 @@
             down = jnp.where(lane >= m, pltpu.roll(ctr, m, 2), 0.0)
             b = b + up + down
             acc = acc + stencil_weights[m - 1] * b
-        lap = acc + inj_ref[pl.ds(y, rows)]
+        spread = jnp.broadcast_to(inj_ref[pl.ds(y, rows)], (rows, block_x, depth_z))
+        spread = pltpu.roll(spread, 0, 2, stride=4, stride_axis=1)
+        lap = acc + jnp.where(lane < 4, spread, 0.0)
         upd = 2.0 * ctr - prev_ref[pl.ds(y, rows)] + s_ref[pl.ds(y, rows)] * lap
         out_ref[pl.ds(y, rows)] = upd
         head_ref[pl.ds(y, rows)] = upd[:, 0:HALO]
@@ -74,7 +76,7 @@
         return pl.BlockSpec(shape, lambda i, k: (0,) * len(shape))
 
     plane_spec = pl.BlockSpec(
-        (None, None, block_y, block_x, depth_z), lambda i, k: (k[0], component, 0, 0, 0)
+        (None, None, block_y, 1, depth_z), lambda i, k: (k[0], component, 0, 0, 0)
     )
     in_specs = [whole(cur.shape), whole(prev.shape), whole(s.shape), whole(xlo.shape), whole(xhi.shape), plane_spec]
     operands = [cur, prev, s, xlo, xhi, planes]
@@ -150,7 +152,10 @@
         [spread_points(source_core, wavelet), spread_points(receiver_core, traces)], axis=1
     )
     planes = planes.reshape(steps_total, 2, depth_y, cells_x, 4)
-    planes = jnp.pad(planes, ((0, 0), (0, 0), (0, 0), (0, 0), (0, depth_z - 4)))
+    gap = jnp.zeros((steps_total, 2, depth_y, depth_z - 4 * cells_x), jnp.float32)
+    tail = planes[:, :, :, :0:-1].reshape(steps_total, 2, depth_y, 4 * (cells_x - 1))
+    planes = jnp.concatenate([planes[:, :, :, 0], gap, tail], axis=3)
+    planes = planes.reshape(steps_total, 2, depth_y, 1, depth_z)
 
     def advance(moment, state):
         (prev0, cur0, head0, tail0), (prev1, cur1, head1, tail1), image_acc = state

time: 530 us -> 507 us (0.957)
  local copies, waits for them, and re-layouts: 41.8 us -> 23.2 us
    pad x1 -> x0, local copies, waits for them, and re-layouts: 16.2 us -> none  [shards(): planes = jnp.pad(planes, ((0, 0), (0, 0), (0, 0), (0, 0), (0, depth_z - 4)))]
    unnamed x11 -> x23, local copies, waits for them, and re-layouts: 10.1 us -> 0.07 us
  transfers between devices with their start and end apart: 82 -> 82, of which waited for: 1 -> 1; matrix products, arithmetic and copies ran while one was open for 9% -> 5% of each run, Pallas kernels for 25% -> 26%
where the time goes in v8:
time: 507 us; the launch traced here: 504 us
  starting transfers between devices  271 us (53%)
  Pallas kernels  172 us (34%)
  local copies, waits for them, and re-layouts  23.2 us (5%)
  matrix products  11.7 us (2%)
  waiting for transfers between devices  11.6 us (2%)
  other arithmetic  10.1 us (2%)
    ppermute x40, starting transfers between devices, trade_halos(): low = lax.ppermute(tail, axis, [(i, (i + 1) % count) for i in range(ends)])  200 us
    pallas_call x40, Pallas kernels, wave_call(): pl.pallas_call(functools.partial(wave_kernel, with_image), out_shape=tupl...  172 us
    ppermute x40, starting transfers between devices, trade_halos(): high = lax.ppermute(head, axis, [((i + 1) % count, i) for i in range(ends)])  51.7 us
    all_to_all x1, starting transfers between devices, shards(): lax.all_to_all(outgoing, 'dom', split_axis=0, concat_axis=1, tiled=True)  12.2 us
    all_to_all x1, waiting for transfers between devices, shards(): lax.all_to_all(outgoing, 'dom', split_axis=0, concat_axis=1, tiled=True)  11.3 us
    dot_general x2, matrix products, spread_points(): jnp.einsum('ny,nsc->syc', rows_y, weighted, precision=lax.Precision.HIGHEST)  11 us
    while x280, local copies, waits for them, and re-layouts  10.3 us
  transfers between devices with their start and end apart: 82, of which 1 were waited for; matrix products, arithmetic and copies ran while one was open for 5% of the time, Pallas kernels for 26%

profile of v8, /device:TPU:0, one launch (start us, length us, event | category | flops | bytes accessed | tf_op | source)
XLA Modules:
  0.0 504.0 jit_solution(3518692226708572894)
XLA Ops:
  3.6 7.4 %all-to-all-start = ((f32[8,16,8,128]{3,2,0,1:T(8,128)}), f32[8,16,8,128]{3,2,0,1:T(8,128)S(1)}, u32[]{:S(2)}, u32[]{:S(2)}) async-start(f32[8,16,8,128]{3,2,0,1:T(8,128)} %select_bitcast_fusion), calls=%async_computation | async-start | bytes 1048576 | tf_op jit(solution)/shard_map/all_to_all | solution.py:144
  12.2 10.5 %fusion = f32[20,32,128]{2,1,0:T(8,128)S(1)} fusion(f32[8192,20]{0,1:T(8,128)S(1)} %bitcast.85, f32[8192,32]{0,1:T(8,128)S(1)} %fusion.8, s32[8192]{0:T(1024)S(1)} %bitcast.83), kind=kOutput, calls=%fused_computation.1 | convolution fusion | flops 8059355136 | bytes 2064384 | tf_op jit(solution)/shard_map/ny,nsc->syc/dot_general | solution.py:131
  36.2 437.4 %while.29 = (s32[]{:T(128)}, f32[128,8,128]{2,1,0:T(8,128)}, f32[128,8,128]{2,1,0:T(8,128)S(1)}, f32[128,4,128]{2,1,0:T(4,128)}, f32[128,4,128]{2,1,0:T(4,128)},...) while((s32[]{:T(128)}, f32[128,8,128]{2,1,0:T(8,128)}, ...), condition=%wide.region_1.2_spmd, body=%wide.region_0.1_spmd.sunk | while | flops 31457284 | bytes 67109736 | solution.py:181
  64.8 4.8 eval_jaxpr.21
  75.0 5.1 %collective-permute-start = (f32[128,4,128]{2,1,0:T(4,128)}, f32[128,4,128]{2,1,0:T(4,128)S(1)}, u32[]{:S(2)}, u32[]{:S(2)}) collective-permute-start(f32[128,4,128]{2,1,0:T(4,128)} %get-tuple-element.381), channel_id=1, source_target_pairs={{0,1},{1,2},{2,3},{3,4},{4,5},{5,6},{6,7},{7,8},{8,9},{9,10},{10,1... | collective-permute-start | bytes 786440 | tf_op jit(solution)/shard_map/while/body/eval_jaxpr/ppermute | solution.py:21
  90.7 7.2 %collective-permute-start.2 = (f32[128,4,128]{2,1,0:T(4,128)S(1)}, f32[128,4,128]{2,1,0:T(4,128)S(1)}, u32[]{:S(2)}, u32[]{:S(2)}) collective-permute-start(f32[128,4,128]{2,1,0:T(4,128)S(1)} %get-tuple-element.350), channel_id=1, source_target_pairs={{0,1},{1,2},{2,3},{3,4},{4,5},{5,6},{6,7},{7,8},{8,9},{9,10},{10,1... | collective-permute-start | bytes 786440 | tf_op jit(solution)/shard_map/while/body/eval_jaxpr/ppermute | solution.py:21
  108.1 4.8 eval_jaxpr.21
  118.4 6.1 %collective-permute-start = (f32[128,4,128]{2,1,0:T(4,128)}, f32[128,4,128]{2,1,0:T(4,128)S(1)}, u32[]{:S(2)}, u32[]{:S(2)}) collective-permute-start(f32[128,4,128]{2,1,0:T(4,128)} %get-tuple-element.381), channel_id=1, source_target_pairs={{0,1},{1,2},{2,3},{3,4},{4,5},{5,6},{6,7},{7,8},{8,9},{9,10},{10,1... | collective-permute-start | bytes 786440 | tf_op jit(solution)/shard_map/while/body/eval_jaxpr/ppermute | solution.py:21
  135.0 7.3 %collective-permute-start.2 = (f32[128,4,128]{2,1,0:T(4,128)S(1)}, f32[128,4,128]{2,1,0:T(4,128)S(1)}, u32[]{:S(2)}, u32[]{:S(2)}) collective-permute-start(f32[128,4,128]{2,1,0:T(4,128)S(1)} %get-tuple-element.350), channel_id=1, source_target_pairs={{0,1},{1,2},{2,3},{3,4},{4,5},{5,6},{6,7},{7,8},{8,9},{9,10},{10,1... | collective-permute-start | bytes 786440 | tf_op jit(solution)/shard_map/while/body/eval_jaxpr/ppermute | solution.py:21
  152.6 4.8 eval_jaxpr.21
  162.8 6.1 %collective-permute-start = (f32[128,4,128]{2,1,0:T(4,128)}, f32[128,4,128]{2,1,0:T(4,128)S(1)}, u32[]{:S(2)}, u32[]{:S(2)}) collective-permute-start(f32[128,4,128]{2,1,0:T(4,128)} %get-tuple-element.381), channel_id=1, source_target_pairs={{0,1},{1,2},{2,3},{3,4},{4,5},{5,6},{6,7},{7,8},{8,9},{9,10},{10,1... | collective-permute-start | bytes 786440 | tf_op jit(solution)/shard_map/while/body/eval_jaxpr/ppermute | solution.py:21
  179.4 7.3 %collective-permute-start.2 = (f32[128,4,128]{2,1,0:T(4,128)S(1)}, f32[128,4,128]{2,1,0:T(4,128)S(1)}, u32[]{:S(2)}, u32[]{:S(2)}) collective-permute-start(f32[128,4,128]{2,1,0:T(4,128)S(1)} %get-tuple-element.350), channel_id=1, source_target_pairs={{0,1},{1,2},{2,3},{3,4},{4,5},{5,6},{6,7},{7,8},{8,9},{9,10},{10,1... | collective-permute-start | bytes 786440 | tf_op jit(solution)/shard_map/while/body/eval_jaxpr/ppermute | solution.py:21
  197.0 4.8 eval_jaxpr.21
  207.2 6.1 %collective-permute-start = (f32[128,4,128]{2,1,0:T(4,128)}, f32[128,4,128]{2,1,0:T(4,128)S(1)}, u32[]{:S(2)}, u32[]{:S(2)}) collective-permute-start(f32[128,4,128]{2,1,0:T(4,128)} %get-tuple-element.381), channel_id=1, source_target_pairs={{0,1},{1,2},{2,3},{3,4},{4,5},{5,6},{6,7},{7,8},{8,9},{9,10},{10,1... | collective-permute-start | bytes 786440 | tf_op jit(solution)/shard_map/while/body/eval_jaxpr/ppermute | solution.py:21
  223.8 7.3 %collective-permute-start.2 = (f32[128,4,128]{2,1,0:T(4,128)S(1)}, f32[128,4,128]{2,1,0:T(4,128)S(1)}, u32[]{:S(2)}, u32[]{:S(2)}) collective-permute-start(f32[128,4,128]{2,1,0:T(4,128)S(1)} %get-tuple-element.350), channel_id=1, source_target_pairs={{0,1},{1,2},{2,3},{3,4},{4,5},{5,6},{6,7},{7,8},{8,9},{9,10},{10,1... | collective-permute-start | bytes 786440 | tf_op jit(solution)/shard_map/while/body/eval_jaxpr/ppermute | solution.py:21
  241.4 4.8 eval_jaxpr.21
  251.6 6.1 %collective-permute-start = (f32[128,4,128]{2,1,0:T(4,128)}, f32[128,4,128]{2,1,0:T(4,128)S(1)}, u32[]{:S(2)}, u32[]{:S(2)}) collective-permute-start(f32[128,4,128]{2,1,0:T(4,128)} %get-tuple-element.381), channel_id=1, source_target_pairs={{0,1},{1,2},{2,3},{3,4},{4,5},{5,6},{6,7},{7,8},{8,9},{9,10},{10,1... | collective-permute-start | bytes 786440 | tf_op jit(solution)/shard_map/while/body/eval_jaxpr/ppermute | solution.py:21
  268.3 7.3 %collective-permute-start.2 = (f32[128,4,128]{2,1,0:T(4,128)S(1)}, f32[128,4,128]{2,1,0:T(4,128)S(1)}, u32[]{:S(2)}, u32[]{:S(2)}) collective-permute-start(f32[128,4,128]{2,1,0:T(4,128)S(1)} %get-tuple-element.350), channel_id=1, source_target_pairs={{0,1},{1,2},{2,3},{3,4},{4,5},{5,6},{6,7},{7,8},{8,9},{9,10},{10,1... | collective-permute-start | bytes 786440 | tf_op jit(solution)/shard_map/while/body/eval_jaxpr/ppermute | solution.py:21
  285.8 4.8 eval_jaxpr.21
  296.0 6.1 %collective-permute-start = (f32[128,4,128]{2,1,0:T(4,128)}, f32[128,4,128]{2,1,0:T(4,128)S(1)}, u32[]{:S(2)}, u32[]{:S(2)}) collective-permute-start(f32[128,4,128]{2,1,0:T(4,128)} %get-tuple-element.381), channel_id=1, source_target_pairs={{0,1},{1,2},{2,3},{3,4},{4,5},{5,6},{6,7},{7,8},{8,9},{9,10},{10,1... | collective-permute-start | bytes 786440 | tf_op jit(solution)/shard_map/while/body/eval_jaxpr/ppermute | solution.py:21
  312.7 7.3 %collective-permute-start.2 = (f32[128,4,128]{2,1,0:T(4,128)S(1)}, f32[128,4,128]{2,1,0:T(4,128)S(1)}, u32[]{:S(2)}, u32[]{:S(2)}) collective-permute-start(f32[128,4,128]{2,1,0:T(4,128)S(1)} %get-tuple-element.350), channel_id=1, source_target_pairs={{0,1},{1,2},{2,3},{3,4},{4,5},{5,6},{6,7},{7,8},{8,9},{9,10},{10,1... | collective-permute-start | bytes 786440 | tf_op jit(solution)/shard_map/while/body/eval_jaxpr/ppermute | solution.py:21
  330.2 4.8 eval_jaxpr.21
  340.4 6.1 %collective-permute-start = (f32[128,4,128]{2,1,0:T(4,128)}, f32[128,4,128]{2,1,0:T(4,128)S(1)}, u32[]{:S(2)}, u32[]{:S(2)}) collective-permute-start(f32[128,4,128]{2,1,0:T(4,128)} %get-tuple-element.381), channel_id=1, source_target_pairs={{0,1},{1,2},{2,3},{3,4},{4,5},{5,6},{6,7},{7,8},{8,9},{9,10},{10,1... | collective-permute-start | bytes 786440 | tf_op jit(solution)/shard_map/while/body/eval_jaxpr/ppermute | solution.py:21
  357.1 7.3 %collective-permute-start.2 = (f32[128,4,128]{2,1,0:T(4,128)S(1)}, f32[128,4,128]{2,1,0:T(4,128)S(1)}, u32[]{:S(2)}, u32[]{:S(2)}) collective-permute-start(f32[128,4,128]{2,1,0:T(4,128)S(1)} %get-tuple-element.350), channel_id=1, source_target_pairs={{0,1},{1,2},{2,3},{3,4},{4,5},{5,6},{6,7},{7,8},{8,9},{9,10},{10,1... | collective-permute-start | bytes 786440 | tf_op jit(solution)/shard_map/while/body/eval_jaxpr/ppermute | solution.py:21
  374.6 4.8 eval_jaxpr.21
  384.8 6.1 %collective-permute-start = (f32[128,4,128]{2,1,0:T(4,128)}, f32[128,4,128]{2,1,0:T(4,128)S(1)}, u32[]{:S(2)}, u32[]{:S(2)}) collective-permute-start(f32[128,4,128]{2,1,0:T(4,128)} %get-tuple-element.381), channel_id=1, source_target_pairs={{0,1},{1,2},{2,3},{3,4},{4,5},{5,6},{6,7},{7,8},{8,9},{9,10},{10,1... | collective-permute-start | bytes 786440 | tf_op jit(solution)/shard_map/while/body/eval_jaxpr/ppermute | solution.py:21
  401.5 7.3 %collective-permute-start.2 = (f32[128,4,128]{2,1,0:T(4,128)S(1)}, f32[128,4,128]{2,1,0:T(4,128)S(1)}, u32[]{:S(2)}, u32[]{:S(2)}) collective-permute-start(f32[128,4,128]{2,1,0:T(4,128)S(1)} %get-tuple-element.350), channel_id=1, source_target_pairs={{0,1},{1,2},{2,3},{3,4},{4,5},{5,6},{6,7},{7,8},{8,9},{9,10},{10,1... | collective-permute-start | bytes 786440 | tf_op jit(solution)/shard_map/while/body/eval_jaxpr/ppermute | solution.py:21
  419.1 4.8 eval_jaxpr.21
  429.3 6.1 %collective-permute-start = (f32[128,4,128]{2,1,0:T(4,128)}, f32[128,4,128]{2,1,0:T(4,128)S(1)}, u32[]{:S(2)}, u32[]{:S(2)}) collective-permute-start(f32[128,4,128]{2,1,0:T(4,128)} %get-tuple-element.381), channel_id=1, source_target_pairs={{0,1},{1,2},{2,3},{3,4},{4,5},{5,6},{6,7},{7,8},{8,9},{9,10},{10,1... | collective-permute-start | bytes 786440 | tf_op jit(solution)/shard_map/while/body/eval_jaxpr/ppermute | solution.py:21
  445.9 7.3 %collective-permute-start.2 = (f32[128,4,128]{2,1,0:T(4,128)S(1)}, f32[128,4,128]{2,1,0:T(4,128)S(1)}, u32[]{:S(2)}, u32[]{:S(2)}) collective-permute-start(f32[128,4,128]{2,1,0:T(4,128)S(1)} %get-tuple-element.350), channel_id=1, source_target_pairs={{0,1},{1,2},{2,3},{3,4},{4,5},{5,6},{6,7},{7,8},{8,9},{9,10},{10,1... | collective-permute-start | bytes 786440 | tf_op jit(solution)/shard_map/while/body/eval_jaxpr/ppermute | solution.py:21
  475.7 12.2 %all-to-all-start.1 = ((f32[128,1,8,128]{3,2,1,0:T(8,128)}), f32[128,1,8,128]{3,2,1,0:T(8,128)S(1)}, u32[]{:S(2)}, u32[]{:S(2)}) async-start(f32[128,1,8,128]{3,2,1,0:T(8,128)} %multiply_bitcast_fusion), calls=%async_computation.1 | async-start | bytes 1048576 | tf_op jit(solution)/shard_map/all_to_all | solution.py:192
  491.0 11.3 %all-to-all-done.1 = f32[128,1,8,128]{3,2,1,0:T(8,128)S(1)} async-done(((f32[128,1,8,128]{3,2,1,0:T(8,128)}), f32[128,1,8,128]{3,2,1,0:T(8,128)S(1)}, u32[]{:S(2)}, u32[]{:S(2)}) %all-to-all-start.1) | async-done | bytes 524320 | tf_op jit(solution)/shard_map/all_to_all | solution.py:192
  (510 shorter events, 296.4 us)
Async XLA Ops:
  3.6 31.7 %all-to-all-start = ((f32[8,16,8,128]{3,2,0,1:T(8,128)}), f32[8,16,8,128]{3,2,0,1:T(8,128)S(1)}, u32[]{:S(2)}, u32[]{:S(2)}) async-start(f32[8,16,8,128]{3,2,0,1:T(8,128)} %select_bitcast_fusion), calls=%async_computation | async-start | bytes 1048576 | tf_op jit(solution)/shard_map/all_to_all | solution.py:144
  39.8 16.0 %collective-permute-start.4 = (f32[128,4,128]{2,1,0:T(4,128)S(1)}, f32[128,4,128]{2,1,0:T(4,128)S(1)}, u32[]{:S(2)}, u32[]{:S(2)}) collective-permute-start(f32[128,4,128]{2,1,0:T(4,128)S(1)} %get-tuple-element.385), channel_id=1, source_target_pairs={{0,1},{1,2},{2,3},{3,4},{4,5},{5,6},{6,7},{7,8},{8,9},{9,10},{10,1... | collective-permute-start | bytes 786440 | tf_op jit(solution)/shard_map/while/body/eval_jaxpr/ppermute | solution.py:21
  49.9 14.9 %collective-permute-start.2 = (f32[128,4,128]{2,1,0:T(4,128)S(1)}, f32[128,4,128]{2,1,0:T(4,128)S(1)}, u32[]{:S(2)}, u32[]{:S(2)}) collective-permute-start(f32[128,4,128]{2,1,0:T(4,128)S(1)} %get-tuple-element.350), channel_id=1, source_target_pairs={{0,1},{1,2},{2,3},{3,4},{4,5},{5,6},{6,7},{7,8},{8,9},{9,10},{10,1... | collective-permute-start | bytes 786440 | tf_op jit(solution)/shard_map/while/body/eval_jaxpr/ppermute | solution.py:21
  81.4 17.8 %collective-permute-start.4 = (f32[128,4,128]{2,1,0:T(4,128)S(1)}, f32[128,4,128]{2,1,0:T(4,128)S(1)}, u32[]{:S(2)}, u32[]{:S(2)}) collective-permute-start(f32[128,4,128]{2,1,0:T(4,128)S(1)} %get-tuple-element.385), channel_id=1, source_target_pairs={{0,1},{1,2},{2,3},{3,4},{4,5},{5,6},{6,7},{7,8},{8,9},{9,10},{10,1... | collective-permute-start | bytes 786440 | tf_op jit(solution)/shard_map/while/body/eval_jaxpr/ppermute | solution.py:21
  84.8 14.3 %collective-permute-start.5 = (f32[128,4,128]{2,1,0:T(4,128)}, f32[128,4,128]{2,1,0:T(4,128)S(1)}, u32[]{:S(2)}, u32[]{:S(2)}) collective-permute-start(f32[128,4,128]{2,1,0:T(4,128)} %get-tuple-element.384), channel_id=1, source_target_pairs={{1,0},{2,1},{3,2},{4,3},{5,4},{6,5},{7,6},{8,7},{9,8},{10,9},{11,1... | collective-permute-start | bytes 786440 | tf_op jit(solution)/shard_map/while/body/eval_jaxpr/ppermute | solution.py:22
  90.7 17.4 %collective-permute-start.2 = (f32[128,4,128]{2,1,0:T(4,128)S(1)}, f32[128,4,128]{2,1,0:T(4,128)S(1)}, u32[]{:S(2)}, u32[]{:S(2)}) collective-permute-start(f32[128,4,128]{2,1,0:T(4,128)S(1)} %get-tuple-element.350), channel_id=1, source_target_pairs={{0,1},{1,2},{2,3},{3,4},{4,5},{5,6},{6,7},{7,8},{8,9},{9,10},{10,1... | collective-permute-start | bytes 786440 | tf_op jit(solution)/shard_map/while/body/eval_jaxpr/ppermute | solution.py:21
  125.7 17.9 %collective-permute-start.4 = (f32[128,4,128]{2,1,0:T(4,128)S(1)}, f32[128,4,128]{2,1,0:T(4,128)S(1)}, u32[]{:S(2)}, u32[]{:S(2)}) collective-permute-start(f32[128,4,128]{2,1,0:T(4,128)S(1)} %get-tuple-element.385), channel_id=1, source_target_pairs={{0,1},{1,2},{2,3},{3,4},{4,5},{5,6},{6,7},{7,8},{8,9},{9,10},{10,1... | collective-permute-start | bytes 786440 | tf_op jit(solution)/shard_map/while/body/eval_jaxpr/ppermute | solution.py:21
  129.2 14.4 %collective-permute-start.5 = (f32[128,4,128]{2,1,0:T(4,128)}, f32[128,4,128]{2,1,0:T(4,128)S(1)}, u32[]{:S(2)}, u32[]{:S(2)}) collective-permute-start(f32[128,4,128]{2,1,0:T(4,128)} %get-tuple-element.384), channel_id=1, source_target_pairs={{1,0},{2,1},{3,2},{4,3},{5,4},{6,5},{7,6},{8,7},{9,8},{10,9},{11,1... | collective-permute-start | bytes 786440 | tf_op jit(solution)/shard_map/while/body/eval_jaxpr/ppermute | solution.py:22
  135.0 17.5 %collective-permute-start.2 = (f32[128,4,128]{2,1,0:T(4,128)S(1)}, f32[128,4,128]{2,1,0:T(4,128)S(1)}, u32[]{:S(2)}, u32[]{:S(2)}) collective-permute-start(f32[128,4,128]{2,1,0:T(4,128)S(1)} %get-tuple-element.350), channel_id=1, source_target_pairs={{0,1},{1,2},{2,3},{3,4},{4,5},{5,6},{6,7},{7,8},{8,9},{9,10},{10,1... | collective-permute-start | bytes 786440 | tf_op jit(solution)/shard_map/while/body/eval_jaxpr/ppermute | solution.py:21
  170.1 17.9 %collective-permute-start.4 = (f32[128,4,128]{2,1,0:T(4,128)S(1)}, f32[128,4,128]{2,1,0:T(4,128)S(1)}, u32[]{:S(2)}, u32[]{:S(2)}) collective-permute-start(f32[128,4,128]{2,1,0:T(4,128)S(1)} %get-tuple-element.385), channel_id=1, source_target_pairs={{0,1},{1,2},{2,3},{3,4},{4,5},{5,6},{6,7},{7,8},{8,9},{9,10},{10,1... | collective-permute-start | bytes 786440 | tf_op jit(solution)/shard_map/while/body/eval_jaxpr/ppermute | solution.py:21
  173.6 14.4 %collective-permute-start.5 = (f32[128,4,128]{2,1,0:T(4,128)}, f32[128,4,128]{2,1,0:T(4,128)S(1)}, u32[]{:S(2)}, u32[]{:S(2)}) collective-permute-start(f32[128,4,128]{2,1,0:T(4,128)} %get-tuple-element.384), channel_id=1, source_target_pairs={{1,0},{2,1},{3,2},{4,3},{5,4},{6,5},{7,6},{8,7},{9,8},{10,9},{11,1... | collective-permute-start | bytes 786440 | tf_op jit(solution)/shard_map/while/body/eval_jaxpr/ppermute | solution.py:22
  179.4 17.5 %collective-permute-start.2 = (f32[128,4,128]{2,1,0:T(4,128)S(1)}, f32[128,4,128]{2,1,0:T(4,128)S(1)}, u32[]{:S(2)}, u32[]{:S(2)}) collective-permute-start(f32[128,4,128]{2,1,0:T(4,128)S(1)} %get-tuple-element.350), channel_id=1, source_target_pairs={{0,1},{1,2},{2,3},{3,4},{4,5},{5,6},{6,7},{7,8},{8,9},{9,10},{10,1... | collective-permute-start | bytes 786440 | tf_op jit(solution)/shard_map/while/body/eval_jaxpr/ppermute | solution.py:21
  214.6 17.9 %collective-permute-start.4 = (f32[128,4,128]{2,1,0:T(4,128)S(1)}, f32[128,4,128]{2,1,0:T(4,128)S(1)}, u32[]{:S(2)}, u32[]{:S(2)}) collective-permute-start(f32[128,4,128]{2,1,0:T(4,128)S(1)} %get-tuple-element.385), channel_id=1, source_target_pairs={{0,1},{1,2},{2,3},{3,4},{4,5},{5,6},{6,7},{7,8},{8,9},{9,10},{10,1... | collective-permute-start | bytes 786440 | tf_op jit(solution)/shard_map/while/body/eval_jaxpr/ppermute | solution.py:21
  218.0 14.4 %collective-permute-start.5 = (f32[128,4,128]{2,1,0:T(4,128)}, f32[128,4,128]{2,1,0:T(4,128)S(1)}, u32[]{:S(2)}, u32[]{:S(2)}) collective-permute-start(f32[128,4,128]{2,1,0:T(4,128)} %get-tuple-element.384), channel_id=1, source_target_pairs={{1,0},{2,1},{3,2},{4,3},{5,4},{6,5},{7,6},{8,7},{9,8},{10,9},{11,1... | collective-permute-start | bytes 786440 | tf_op jit(solution)/shard_map/while/body/eval_jaxpr/ppermute | solution.py:22
  223.8 17.5 %collective-permute-start.2 = (f32[128,4,128]{2,1,0:T(4,128)S(1)}, f32[128,4,128]{2,1,0:T(4,128)S(1)}, u32[]{:S(2)}, u32[]{:S(2)}) collective-permute-start(f32[128,4,128]{2,1,0:T(4,128)S(1)} %get-tuple-element.350), channel_id=1, source_target_pairs={{0,1},{1,2},{2,3},{3,4},{4,5},{5,6},{6,7},{7,8},{8,9},{9,10},{10,1... | collective-permute-start | bytes 786440 | tf_op jit(solution)/shard_map/while/body/eval_jaxpr/ppermute | solution.py:21
  251.6 12.2 %collective-permute-start = (f32[128,4,128]{2,1,0:T(4,128)}, f32[128,4,128]{2,1,0:T(4,128)S(1)}, u32[]{:S(2)}, u32[]{:S(2)}) collective-permute-start(f32[128,4,128]{2,1,0:T(4,128)} %get-tuple-element.381), channel_id=1, source_target_pairs={{0,1},{1,2},{2,3},{3,4},{4,5},{5,6},{6,7},{7,8},{8,9},{9,10},{10,1... | collective-permute-start | bytes 786440 | tf_op jit(solution)/shard_map/while/body/eval_jaxpr/ppermute | solution.py:21
  259.0 17.9 %collective-permute-start.4 = (f32[128,4,128]{2,1,0:T(4,128)S(1)}, f32[128,4,128]{2,1,0:T(4,128)S(1)}, u32[]{:S(2)}, u32[]{:S(2)}) collective-permute-start(f32[128,4,128]{2,1,0:T(4,128)S(1)} %get-tuple-element.385), channel_id=1, source_target_pairs={{0,1},{1,2},{2,3},{3,4},{4,5},{5,6},{6,7},{7,8},{8,9},{9,10},{10,1... | collective-permute-start | bytes 786440 | tf_op jit(solution)/shard_map/while/body/eval_jaxpr/ppermute | solution.py:21
  262.4 14.4 %collective-permute-start.5 = (f32[128,4,128]{2,1,0:T(4,128)}, f32[128,4,128]{2,1,0:T(4,128)S(1)}, u32[]{:S(2)}, u32[]{:S(2)}) collective-permute-start(f32[128,4,128]{2,1,0:T(4,128)} %get-tuple-element.384), channel_id=1, source_target_pairs={{1,0},{2,1},{3,2},{4,3},{5,4},{6,5},{7,6},{8,7},{9,8},{10,9},{11,1... | collective-permute-start | bytes 786440 | tf_op jit(solution)/shard_map/while/body/eval_jaxpr/ppermute | solution.py:22
  268.3 17.5 %collective-permute-start.2 = (f32[128,4,128]{2,1,0:T(4,128)S(1)}, f32[128,4,128]{2,1,0:T(4,128)S(1)}, u32[]{:S(2)}, u32[]{:S(2)}) collective-permute-start(f32[128,4,128]{2,1,0:T(4,128)S(1)} %get-tuple-element.350), channel_id=1, source_target_pairs={{0,1},{1,2},{2,3},{3,4},{4,5},{5,6},{6,7},{7,8},{8,9},{9,10},{10,1... | collective-permute-start | bytes 786440 | tf_op jit(solution)/shard_map/while/body/eval_jaxpr/ppermute | solution.py:21
  303.4 17.9 %collective-permute-start.4 = (f32[128,4,128]{2,1,0:T(4,128)S(1)}, f32[128,4,128]{2,1,0:T(4,128)S(1)}, u32[]{:S(2)}, u32[]{:S(2)}) collective-permute-start(f32[128,4,128]{2,1,0:T(4,128)S(1)} %get-tuple-element.385), channel_id=1, source_target_pairs={{0,1},{1,2},{2,3},{3,4},{4,5},{5,6},{6,7},{7,8},{8,9},{9,10},{10,1... | collective-permute-start | bytes 786440 | tf_op jit(solution)/shard_map/while/body/eval_jaxpr/ppermute | solution.py:21
  306.8 14.4 %collective-permute-start.5 = (f32[128,4,128]{2,1,0:T(4,128)}, f32[128,4,128]{2,1,0:T(4,128)S(1)}, u32[]{:S(2)}, u32[]{:S(2)}) collective-permute-start(f32[128,4,128]{2,1,0:T(4,128)} %get-tuple-element.384), channel_id=1, source_target_pairs={{1,0},{2,1},{3,2},{4,3},{5,4},{6,5},{7,6},{8,7},{9,8},{10,9},{11,1... | collective-permute-start | bytes 786440 | tf_op jit(solution)/shard_map/while/body/eval_jaxpr/ppermute | solution.py:22
  312.7 17.5 %collective-permute-start.2 = (f32[128,4,128]{2,1,0:T(4,128)S(1)}, f32[128,4,128]{2,1,0:T(4,128)S(1)}, u32[]{:S(2)}, u32[]{:S(2)}) collective-permute-start(f32[128,4,128]{2,1,0:T(4,128)S(1)} %get-tuple-element.350), channel_id=1, source_target_pairs={{0,1},{1,2},{2,3},{3,4},{4,5},{5,6},{6,7},{7,8},{8,9},{9,10},{10,1... | collective-permute-start | bytes 786440 | tf_op jit(solution)/shard_map/while/body/eval_jaxpr/ppermute | solution.py:21
  347.8 17.9 %collective-permute-start.4 = (f32[128,4,128]{2,1,0:T(4,128)S(1)}, f32[128,4,128]{2,1,0:T(4,128)S(1)}, u32[]{:S(2)}, u32[]{:S(2)}) collective-permute-start(f32[128,4,128]{2,1,0:T(4,128)S(1)} %get-tuple-element.385), channel_id=1, source_target_pairs={{0,1},{1,2},{2,3},{3,4},{4,5},{5,6},{6,7},{7,8},{8,9},{9,10},{10,1... | collective-permute-start | bytes 786440 | tf_op jit(solution)/shard_map/while/body/eval_jaxpr/ppermute | solution.py:21
  351.2 14.4 %collective-permute-start.5 = (f32[128,4,128]{2,1,0:T(4,128)}, f32[128,4,128]{2,1,0:T(4,128)S(1)}, u32[]{:S(2)}, u32[]{:S(2)}) collective-permute-start(f32[128,4,128]{2,1,0:T(4,128)} %get-tuple-element.384), channel_id=1, source_target_pairs={{1,0},{2,1},{3,2},{4,3},{5,4},{6,5},{7,6},{8,7},{9,8},{10,9},{11,1... | collective-permute-start | bytes 786440 | tf_op jit(solution)/shard_map/while/body/eval_jaxpr/ppermute | solution.py:22
  357.1 17.5 %collective-permute-start.2 = (f32[128,4,128]{2,1,0:T(4,128)S(1)}, f32[128,4,128]{2,1,0:T(4,128)S(1)}, u32[]{:S(2)}, u32[]{:S(2)}) collective-permute-start(f32[128,4,128]{2,1,0:T(4,128)S(1)} %get-tuple-element.350), channel_id=1, source_target_pairs={{0,1},{1,2},{2,3},{3,4},{4,5},{5,6},{6,7},{7,8},{8,9},{9,10},{10,1... | collective-permute-start | bytes 786440 | tf_op jit(solution)/shard_map/while/body/eval_jaxpr/ppermute | solution.py:21
  392.2 17.9 %collective-permute-start.4 = (f32[128,4,128]{2,1,0:T(4,128)S(1)}, f32[128,4,128]{2,1,0:T(4,128)S(1)}, u32[]{:S(2)}, u32[]{:S(2)}) collective-permute-start(f32[128,4,128]{2,1,0:T(4,128)S(1)} %get-tuple-element.385), channel_id=1, source_target_pairs={{0,1},{1,2},{2,3},{3,4},{4,5},{5,6},{6,7},{7,8},{8,9},{9,10},{10,1... | collective-permute-start | bytes 786440 | tf_op jit(solution)/shard_map/while/body/eval_jaxpr/ppermute | solution.py:21
  395.6 14.4 %collective-permute-start.5 = (f32[128,4,128]{2,1,0:T(4,128)}, f32[128,4,128]{2,1,0:T(4,128)S(1)}, u32[]{:S(2)}, u32[]{:S(2)}) collective-permute-start(f32[128,4,128]{2,1,0:T(4,128)} %get-tuple-element.384), channel_id=1, source_target_pairs={{1,0},{2,1},{3,2},{4,3},{5,4},{6,5},{7,6},{8,7},{9,8},{10,9},{11,1... | collective-permute-start | bytes 786440 | tf_op jit(solution)/shard_map/while/body/eval_jaxpr/ppermute | solution.py:22
  401.5 17.5 %collective-permute-start.2 = (f32[128,4,128]{2,1,0:T(4,128)S(1)}, f32[128,4,128]{2,1,0:T(4,128)S(1)}, u32[]{:S(2)}, u32[]{:S(2)}) collective-permute-start(f32[128,4,128]{2,1,0:T(4,128)S(1)} %get-tuple-element.350), channel_id=1, source_target_pairs={{0,1},{1,2},{2,3},{3,4},{4,5},{5,6},{6,7},{7,8},{8,9},{9,10},{10,1... | collective-permute-start | bytes 786440 | tf_op jit(solution)/shard_map/while/body/eval_jaxpr/ppermute | solution.py:21
  436.6 17.9 %collective-permute-start.4 = (f32[128,4,128]{2,1,0:T(4,128)S(1)}, f32[128,4,128]{2,1,0:T(4,128)S(1)}, u32[]{:S(2)}, u32[]{:S(2)}) collective-permute-start(f32[128,4,128]{2,1,0:T(4,128)S(1)} %get-tuple-element.385), channel_id=1, source_target_pairs={{0,1},{1,2},{2,3},{3,4},{4,5},{5,6},{6,7},{7,8},{8,9},{9,10},{10,1... | collective-permute-start | bytes 786440 | tf_op jit(solution)/shard_map/while/body/eval_jaxpr/ppermute | solution.py:21
  440.1 14.4 %collective-permute-start.5 = (f32[128,4,128]{2,1,0:T(4,128)}, f32[128,4,128]{2,1,0:T(4,128)S(1)}, u32[]{:S(2)}, u32[]{:S(2)}) collective-permute-start(f32[128,4,128]{2,1,0:T(4,128)} %get-tuple-element.384), channel_id=1, source_target_pairs={{1,0},{2,1},{3,2},{4,3},{5,4},{6,5},{7,6},{8,7},{9,8},{10,9},{11,1... | collective-permute-start | bytes 786440 | tf_op jit(solution)/shard_map/while/body/eval_jaxpr/ppermute | solution.py:22
  445.9 17.5 %collective-permute-start.2 = (f32[128,4,128]{2,1,0:T(4,128)S(1)}, f32[128,4,128]{2,1,0:T(4,128)S(1)}, u32[]{:S(2)}, u32[]{:S(2)}) collective-permute-start(f32[128,4,128]{2,1,0:T(4,128)S(1)} %get-tuple-element.350), channel_id=1, source_target_pairs={{0,1},{1,2},{2,3},{3,4},{4,5},{5,6},{6,7},{7,8},{8,9},{9,10},{10,1... | collective-permute-start | bytes 786440 | tf_op jit(solution)/shard_map/while/body/eval_jaxpr/ppermute | solution.py:21
  475.7 26.7 %all-to-all-start.1 = ((f32[128,1,8,128]{3,2,1,0:T(8,128)}), f32[128,1,8,128]{3,2,1,0:T(8,128)S(1)}, u32[]{:S(2)}, u32[]{:S(2)}) async-start(f32[128,1,8,128]{3,2,1,0:T(8,128)} %multiply_bitcast_fusion), calls=%async_computation.1 | async-start | bytes 1048576 | tf_op jit(solution)/shard_map/all_to_all | solution.py:192
  (201 other events, 1668.4 us)

commit v9 on v8

--- a/solution.py
+++ b/solution.py
@@ -12,6 +12,7 @@
 center_weight = 3.0 * (-205.0 / 72.0)
 HALO = 4
 ROWS = 8
+PARTS = 4
 XOFF = 8
 
 
@@ -29,21 +30,29 @@
     else:
         out_ref, head_ref, tail_ref, ey_ref, hx_ref = rest
     block_y, block_x, depth_z = cur_ref.shape
-    zeros_y = jnp.zeros((HALO, block_x, depth_z), jnp.float32)
-    ey_ref[0:HALO] = zeros_y
-    ey_ref[HALO + block_y : 2 * HALO + block_y] = zeros_y
-    ey_ref[HALO : HALO + block_y] = cur_ref[...]
+    part = prev_ref.shape[0]
+    index = pl.program_id(0)
+
+    @pl.when(index == 0)
+    def _():
+        zeros_y = jnp.zeros((HALO, block_x, depth_z), jnp.float32)
+        ey_ref[0:HALO] = zeros_y
+        ey_ref[HALO + block_y : 2 * HALO + block_y] = zeros_y
+        ey_ref[HALO : HALO + block_y] = cur_ref[...]
+
     hx_ref[0, :, block_x - HALO : block_x, :] = xlo_ref[...]
     hx_ref[1, :, 0:HALO, :] = xhi_ref[...]
     rows = ROWS
+    base = index * part
     lane = lax.broadcasted_iota(jnp.int32, (rows, block_x, depth_z), 2)
     sub = lax.broadcasted_iota(jnp.int32, (rows, block_x, depth_z), 1)
 
-    def chunk(index, carry):
-        y = pl.multiple_of(index * rows, rows)
+    def chunk(step, carry):
+        r = pl.multiple_of(step * rows, rows)
+        y = base + r
         ctr = ey_ref[pl.ds(HALO + y, rows)]
-        left = hx_ref[0, pl.ds(y, rows)]
-        right = hx_ref[1, pl.ds(y, rows)]
+        left = hx_ref[0, pl.ds(r, rows)]
+        right = hx_ref[1, pl.ds(r, rows)]
         acc = center_weight * ctr
         for m in range(1, HALO + 1):
             ahead = pltpu.roll(jnp.where(sub >= m, ctr, right), block_x - m, 1)
@@ -54,50 +63,62 @@
             down = jnp.where(lane >= m, pltpu.roll(ctr, m, 2), 0.0)
             b = b + up + down
             acc = acc + stencil_weights[m - 1] * b
-        spread = jnp.broadcast_to(inj_ref[pl.ds(y, rows)], (rows, block_x, depth_z))
+        spread = jnp.broadcast_to(inj_ref[pl.ds(r, rows)], (rows, block_x, depth_z))
         spread = pltpu.roll(spread, 0, 2, stride=4, stride_axis=1)
         lap = acc + jnp.where(lane < 4, spread, 0.0)
-        upd = 2.0 * ctr - prev_ref[pl.ds(y, rows)] + s_ref[pl.ds(y, rows)] * lap
-        out_ref[pl.ds(y, rows)] = upd
-        head_ref[pl.ds(y, rows)] = upd[:, 0:HALO]
-        tail_ref[pl.ds(y, rows)] = upd[:, block_x - HALO : block_x]
+        upd = 2.0 * ctr - prev_ref[pl.ds(r, rows)] + s_ref[pl.ds(r, rows)] * lap
+        out_ref[pl.ds(r, rows)] = upd
+        head_ref[pl.ds(r, rows)] = upd[:, 0:HALO]
+        tail_ref[pl.ds(r, rows)] = upd[:, block_x - HALO : block_x]
         if with_image:
-            imgo_ref[pl.ds(y, rows)] = img_ref[pl.ds(y, rows)] + other_ref[pl.ds(y, rows)] * upd
+            imgo_ref[pl.ds(r, rows)] = img_ref[pl.ds(r, rows)] + other_ref[pl.ds(r, rows)] * upd
         return carry
 
-    lax.fori_loop(0, block_y // rows, chunk, 0)
+    lax.fori_loop(0, part // rows, chunk, 0)
 
 
 def wave_call(component, moment, cur, prev, s, xlo, xhi, planes, other=None, img=None):
     block_y, block_x, depth_z = cur.shape
     with_image = img is not None
+    parts = PARTS
+    part = block_y // parts
 
     def whole(shape):
         return pl.BlockSpec(shape, lambda i, k: (0,) * len(shape))
 
+    def chunked(shape):
+        return pl.BlockSpec((part,) + shape[1:], lambda i, k: (i,) + (0,) * (len(shape) - 1))
+
     plane_spec = pl.BlockSpec(
-        (None, None, block_y, 1, depth_z), lambda i, k: (k[0], component, 0, 0, 0)
-    )
-    in_specs = [whole(cur.shape), whole(prev.shape), whole(s.shape), whole(xlo.shape), whole(xhi.shape), plane_spec]
+        (None, None, part, 1, depth_z), lambda i, k: (k[0], component, i, 0, 0)
+    )
+    in_specs = [
+        whole(cur.shape),
+        chunked(prev.shape),
+        chunked(s.shape),
+        chunked(xlo.shape),
+        chunked(xhi.shape),
+        plane_spec,
+    ]
     operands = [cur, prev, s, xlo, xhi, planes]
     halo_shape = jax.ShapeDtypeStruct(xlo.shape, jnp.float32)
     out_shape = [jax.ShapeDtypeStruct(cur.shape, jnp.float32), halo_shape, halo_shape]
-    out_specs = [whole(cur.shape), whole(xlo.shape), whole(xlo.shape)]
+    out_specs = [chunked(cur.shape), chunked(xlo.shape), chunked(xlo.shape)]
     aliases = {2: 0}
     if with_image:
-        in_specs += [whole(other.shape), whole(img.shape)]
+        in_specs += [chunked(other.shape), chunked(img.shape)]
         operands += [other, img]
         out_shape.append(jax.ShapeDtypeStruct(img.shape, jnp.float32))
-        out_specs.append(whole(img.shape))
+        out_specs.append(chunked(img.shape))
         aliases[8] = 3
     grid_spec = pltpu.PrefetchScalarGridSpec(
         num_scalar_prefetch=1,
-        grid=(1,),
+        grid=(parts,),
         in_specs=in_specs,
         out_specs=tuple(out_specs),
         scratch_shapes=[
             pltpu.VMEM((block_y + 2 * HALO, block_x, depth_z), jnp.float32),
-            pltpu.VMEM((2, block_y, block_x, depth_z), jnp.float32),
+            pltpu.VMEM((2, part, block_x, depth_z), jnp.float32),
         ],
     )
     return pl.pallas_call(
@@ -105,7 +126,9 @@
         out_shape=tuple(out_shape),
         grid_spec=grid_spec,
         input_output_aliases=aliases,
-        compiler_params=pltpu.CompilerParams(vmem_limit_bytes=48 * 1024 * 1024),
+        compiler_params=pltpu.CompilerParams(
+            dimension_semantics=("arbitrary",), vmem_limit_bytes=48 * 1024 * 1024
+        ),
         cost_estimate=pl.CostEstimate(
             flops=60 * cur.size, bytes_accessed=4 * 6 * cur.size, transcendentals=0
         ),

time: 507 us -> 516 us (1.018)
  Pallas kernels: 172 us -> 180 us
    pallas_call x40, Pallas kernels: 172 us -> 180 us  [wave_call(): pl.pallas_call(functools.partial(wave_kernel, with_image), out_shape=tupl...]
where the time goes in v9:
time: 516 us; the launch traced here: 512 us
  starting transfers between devices  271 us (53%)
  Pallas kernels  180 us (35%)
  local copies, waits for them, and re-layouts  23.2 us (4%)
  matrix products  11.7 us (2%)
  waiting for transfers between devices  11.6 us (2%)
  other arithmetic  10.1 us (2%)
    ppermute x40, starting transfers between devices, trade_halos(): low = lax.ppermute(tail, axis, [(i, (i + 1) % count) for i in range(ends)])  200 us
    pallas_call x40, Pallas kernels, wave_call(): pl.pallas_call(functools.partial(wave_kernel, with_image), out_shape=tupl...  180 us
    ppermute x40, starting transfers between devices, trade_halos(): high = lax.ppermute(head, axis, [((i + 1) % count, i) for i in range(ends)])  51.7 us
    all_to_all x1, starting transfers between devices, shards(): lax.all_to_all(outgoing, 'dom', split_axis=0, concat_axis=1, tiled=True)  12.2 us
    all_to_all x1, waiting for transfers between devices, shards(): lax.all_to_all(outgoing, 'dom', split_axis=0, concat_axis=1, tiled=True)  11.3 us
    dot_general x2, matrix products, spread_points(): jnp.einsum('ny,nsc->syc', rows_y, weighted, precision=lax.Precision.HIGHEST)  11 us
  transfers between devices with their start and end apart: 82, of which 1 were waited for; matrix products, arithmetic and copies ran while one was open for 5% of the time, Pallas kernels for 26%

profile of v9, /device:TPU:0, one launch (start us, length us, event | category | flops | bytes accessed | tf_op | source)
XLA Modules:
  0.0 511.6 jit_solution(9957350904354406583)
XLA Ops:
  3.6 7.4 %all-to-all-start = ((f32[8,16,8,128]{3,2,0,1:T(8,128)}), f32[8,16,8,128]{3,2,0,1:T(8,128)S(1)}, u32[]{:S(2)}, u32[]{:S(2)}) async-start(f32[8,16,8,128]{3,2,0,1:T(8,128)} %select_bitcast_fusion), calls=%async_computation | async-start | bytes 1048576 | tf_op jit(solution)/shard_map/all_to_all | solution.py:167
  12.2 10.5 %fusion = f32[20,32,128]{2,1,0:T(8,128)S(1)} fusion(f32[8192,20]{0,1:T(8,128)S(1)} %bitcast.85, f32[8192,32]{0,1:T(8,128)S(1)} %fusion.8, s32[8192]{0:T(1024)S(1)} %bitcast.83), kind=kOutput, calls=%fused_computation.1 | convolution fusion | flops 8059355136 | bytes 2064384 | tf_op jit(solution)/shard_map/ny,nsc->syc/dot_general | solution.py:154
  36.2 445.1 %while.29 = (s32[]{:T(128)}, f32[128,8,128]{2,1,0:T(8,128)}, f32[128,8,128]{2,1,0:T(8,128)S(1)}, f32[128,4,128]{2,1,0:T(4,128)}, f32[128,4,128]{2,1,0:T(4,128)},...) while((s32[]{:T(128)}, f32[128,8,128]{2,1,0:T(8,128)}, ...), condition=%wide.region_1.2_spmd, body=%wide.region_0.1_spmd.sunk | while | flops 31457284 | bytes 67109736 | solution.py:204
  65.2 5.0 eval_jaxpr.21
  91.6 7.0 %collective-permute-start.2 = (f32[128,4,128]{2,1,0:T(4,128)S(1)}, f32[128,4,128]{2,1,0:T(4,128)S(1)}, u32[]{:S(2)}, u32[]{:S(2)}) collective-permute-start(f32[128,4,128]{2,1,0:T(4,128)S(1)} %get-tuple-element.350), channel_id=1, source_target_pairs={{0,1},{1,2},{2,3},{3,4},{4,5},{5,6},{6,7},{7,8},{8,9},{9,10},{10,1... | collective-permute-start | bytes 786440 | tf_op jit(solution)/shard_map/while/body/eval_jaxpr/ppermute | solution.py:22
  109.2 5.0 eval_jaxpr.21
  119.8 6.1 %collective-permute-start = (f32[128,4,128]{2,1,0:T(4,128)}, f32[128,4,128]{2,1,0:T(4,128)S(1)}, u32[]{:S(2)}, u32[]{:S(2)}) collective-permute-start(f32[128,4,128]{2,1,0:T(4,128)} %get-tuple-element.381), channel_id=1, source_target_pairs={{0,1},{1,2},{2,3},{3,4},{4,5},{5,6},{6,7},{7,8},{8,9},{9,10},{10,1... | collective-permute-start | bytes 786440 | tf_op jit(solution)/shard_map/while/body/eval_jaxpr/ppermute | solution.py:22
  136.7 7.1 %collective-permute-start.2 = (f32[128,4,128]{2,1,0:T(4,128)S(1)}, f32[128,4,128]{2,1,0:T(4,128)S(1)}, u32[]{:S(2)}, u32[]{:S(2)}) collective-permute-start(f32[128,4,128]{2,1,0:T(4,128)S(1)} %get-tuple-element.350), channel_id=1, source_target_pairs={{0,1},{1,2},{2,3},{3,4},{4,5},{5,6},{6,7},{7,8},{8,9},{9,10},{10,1... | collective-permute-start | bytes 786440 | tf_op jit(solution)/shard_map/while/body/eval_jaxpr/ppermute | solution.py:22
  154.4 5.0 eval_jaxpr.21
  164.9 6.1 %collective-permute-start = (f32[128,4,128]{2,1,0:T(4,128)}, f32[128,4,128]{2,1,0:T(4,128)S(1)}, u32[]{:S(2)}, u32[]{:S(2)}) collective-permute-start(f32[128,4,128]{2,1,0:T(4,128)} %get-tuple-element.381), channel_id=1, source_target_pairs={{0,1},{1,2},{2,3},{3,4},{4,5},{5,6},{6,7},{7,8},{8,9},{9,10},{10,1... | collective-permute-start | bytes 786440 | tf_op jit(solution)/shard_map/while/body/eval_jaxpr/ppermute | solution.py:22
  181.9 7.1 %collective-permute-start.2 = (f32[128,4,128]{2,1,0:T(4,128)S(1)}, f32[128,4,128]{2,1,0:T(4,128)S(1)}, u32[]{:S(2)}, u32[]{:S(2)}) collective-permute-start(f32[128,4,128]{2,1,0:T(4,128)S(1)} %get-tuple-element.350), channel_id=1, source_target_pairs={{0,1},{1,2},{2,3},{3,4},{4,5},{5,6},{6,7},{7,8},{8,9},{9,10},{10,1... | collective-permute-start | bytes 786440 | tf_op jit(solution)/shard_map/while/body/eval_jaxpr/ppermute | solution.py:22
  199.6 5.0 eval_jaxpr.21
  210.1 6.1 %collective-permute-start = (f32[128,4,128]{2,1,0:T(4,128)}, f32[128,4,128]{2,1,0:T(4,128)S(1)}, u32[]{:S(2)}, u32[]{:S(2)}) collective-permute-start(f32[128,4,128]{2,1,0:T(4,128)} %get-tuple-element.381), channel_id=1, source_target_pairs={{0,1},{1,2},{2,3},{3,4},{4,5},{5,6},{6,7},{7,8},{8,9},{9,10},{10,1... | collective-permute-start | bytes 786440 | tf_op jit(solution)/shard_map/while/body/eval_jaxpr/ppermute | solution.py:22
  227.1 7.1 %collective-permute-start.2 = (f32[128,4,128]{2,1,0:T(4,128)S(1)}, f32[128,4,128]{2,1,0:T(4,128)S(1)}, u32[]{:S(2)}, u32[]{:S(2)}) collective-permute-start(f32[128,4,128]{2,1,0:T(4,128)S(1)} %get-tuple-element.350), channel_id=1, source_target_pairs={{0,1},{1,2},{2,3},{3,4},{4,5},{5,6},{6,7},{7,8},{8,9},{9,10},{10,1... | collective-permute-start | bytes 786440 | tf_op jit(solution)/shard_map/while/body/eval_jaxpr/ppermute | solution.py:22
  244.8 5.0 eval_jaxpr.21
  255.3 6.1 %collective-permute-start = (f32[128,4,128]{2,1,0:T(4,128)}, f32[128,4,128]{2,1,0:T(4,128)S(1)}, u32[]{:S(2)}, u32[]{:S(2)}) collective-permute-start(f32[128,4,128]{2,1,0:T(4,128)} %get-tuple-element.381), channel_id=1, source_target_pairs={{0,1},{1,2},{2,3},{3,4},{4,5},{5,6},{6,7},{7,8},{8,9},{9,10},{10,1... | collective-permute-start | bytes 786440 | tf_op jit(solution)/shard_map/while/body/eval_jaxpr/ppermute | solution.py:22
  272.3 7.1 %collective-permute-start.2 = (f32[128,4,128]{2,1,0:T(4,128)S(1)}, f32[128,4,128]{2,1,0:T(4,128)S(1)}, u32[]{:S(2)}, u32[]{:S(2)}) collective-permute-start(f32[128,4,128]{2,1,0:T(4,128)S(1)} %get-tuple-element.350), channel_id=1, source_target_pairs={{0,1},{1,2},{2,3},{3,4},{4,5},{5,6},{6,7},{7,8},{8,9},{9,10},{10,1... | collective-permute-start | bytes 786440 | tf_op jit(solution)/shard_map/while/body/eval_jaxpr/ppermute | solution.py:22
  290.0 5.0 eval_jaxpr.21
  300.5 6.1 %collective-permute-start = (f32[128,4,128]{2,1,0:T(4,128)}, f32[128,4,128]{2,1,0:T(4,128)S(1)}, u32[]{:S(2)}, u32[]{:S(2)}) collective-permute-start(f32[128,4,128]{2,1,0:T(4,128)} %get-tuple-element.381), channel_id=1, source_target_pairs={{0,1},{1,2},{2,3},{3,4},{4,5},{5,6},{6,7},{7,8},{8,9},{9,10},{10,1... | collective-permute-start | bytes 786440 | tf_op jit(solution)/shard_map/while/body/eval_jaxpr/ppermute | solution.py:22
  317.5 7.1 %collective-permute-start.2 = (f32[128,4,128]{2,1,0:T(4,128)S(1)}, f32[128,4,128]{2,1,0:T(4,128)S(1)}, u32[]{:S(2)}, u32[]{:S(2)}) collective-permute-start(f32[128,4,128]{2,1,0:T(4,128)S(1)} %get-tuple-element.350), channel_id=1, source_target_pairs={{0,1},{1,2},{2,3},{3,4},{4,5},{5,6},{6,7},{7,8},{8,9},{9,10},{10,1... | collective-permute-start | bytes 786440 | tf_op jit(solution)/shard_map/while/body/eval_jaxpr/ppermute | solution.py:22
  335.2 5.0 eval_jaxpr.21
  345.7 6.1 %collective-permute-start = (f32[128,4,128]{2,1,0:T(4,128)}, f32[128,4,128]{2,1,0:T(4,128)S(1)}, u32[]{:S(2)}, u32[]{:S(2)}) collective-permute-start(f32[128,4,128]{2,1,0:T(4,128)} %get-tuple-element.381), channel_id=1, source_target_pairs={{0,1},{1,2},{2,3},{3,4},{4,5},{5,6},{6,7},{7,8},{8,9},{9,10},{10,1... | collective-permute-start | bytes 786440 | tf_op jit(solution)/shard_map/while/body/eval_jaxpr/ppermute | solution.py:22
  362.7 7.1 %collective-permute-start.2 = (f32[128,4,128]{2,1,0:T(4,128)S(1)}, f32[128,4,128]{2,1,0:T(4,128)S(1)}, u32[]{:S(2)}, u32[]{:S(2)}) collective-permute-start(f32[128,4,128]{2,1,0:T(4,128)S(1)} %get-tuple-element.350), channel_id=1, source_target_pairs={{0,1},{1,2},{2,3},{3,4},{4,5},{5,6},{6,7},{7,8},{8,9},{9,10},{10,1... | collective-permute-start | bytes 786440 | tf_op jit(solution)/shard_map/while/body/eval_jaxpr/ppermute | solution.py:22
  380.4 5.0 eval_jaxpr.21
  390.9 6.1 %collective-permute-start = (f32[128,4,128]{2,1,0:T(4,128)}, f32[128,4,128]{2,1,0:T(4,128)S(1)}, u32[]{:S(2)}, u32[]{:S(2)}) collective-permute-start(f32[128,4,128]{2,1,0:T(4,128)} %get-tuple-element.381), channel_id=1, source_target_pairs={{0,1},{1,2},{2,3},{3,4},{4,5},{5,6},{6,7},{7,8},{8,9},{9,10},{10,1... | collective-permute-start | bytes 786440 | tf_op jit(solution)/shard_map/while/body/eval_jaxpr/ppermute | solution.py:22
  407.9 7.1 %collective-permute-start.2 = (f32[128,4,128]{2,1,0:T(4,128)S(1)}, f32[128,4,128]{2,1,0:T(4,128)S(1)}, u32[]{:S(2)}, u32[]{:S(2)}) collective-permute-start(f32[128,4,128]{2,1,0:T(4,128)S(1)} %get-tuple-element.350), channel_id=1, source_target_pairs={{0,1},{1,2},{2,3},{3,4},{4,5},{5,6},{6,7},{7,8},{8,9},{9,10},{10,1... | collective-permute-start | bytes 786440 | tf_op jit(solution)/shard_map/while/body/eval_jaxpr/ppermute | solution.py:22
  425.5 5.0 eval_jaxpr.21
  436.1 6.1 %collective-permute-start = (f32[128,4,128]{2,1,0:T(4,128)}, f32[128,4,128]{2,1,0:T(4,128)S(1)}, u32[]{:S(2)}, u32[]{:S(2)}) collective-permute-start(f32[128,4,128]{2,1,0:T(4,128)} %get-tuple-element.381), channel_id=1, source_target_pairs={{0,1},{1,2},{2,3},{3,4},{4,5},{5,6},{6,7},{7,8},{8,9},{9,10},{10,1... | collective-permute-start | bytes 786440 | tf_op jit(solution)/shard_map/while/body/eval_jaxpr/ppermute | solution.py:22
  453.1 7.1 %collective-permute-start.2 = (f32[128,4,128]{2,1,0:T(4,128)S(1)}, f32[128,4,128]{2,1,0:T(4,128)S(1)}, u32[]{:S(2)}, u32[]{:S(2)}) collective-permute-start(f32[128,4,128]{2,1,0:T(4,128)S(1)} %get-tuple-element.350), channel_id=1, source_target_pairs={{0,1},{1,2},{2,3},{3,4},{4,5},{5,6},{6,7},{7,8},{8,9},{9,10},{10,1... | collective-permute-start | bytes 786440 | tf_op jit(solution)/shard_map/while/body/eval_jaxpr/ppermute | solution.py:22
  470.7 5.0 eval_jaxpr.21
  483.3 12.2 %all-to-all-start.1 = ((f32[128,1,8,128]{3,2,1,0:T(8,128)}), f32[128,1,8,128]{3,2,1,0:T(8,128)S(1)}, u32[]{:S(2)}, u32[]{:S(2)}) async-start(f32[128,1,8,128]{3,2,1,0:T(8,128)} %multiply_bitcast_fusion), calls=%async_computation.1 | async-start | bytes 1048576 | tf_op jit(solution)/shard_map/all_to_all | solution.py:215
  498.6 11.3 %all-to-all-done.1 = f32[128,1,8,128]{3,2,1,0:T(8,128)S(1)} async-done(((f32[128,1,8,128]{3,2,1,0:T(8,128)}), f32[128,1,8,128]{3,2,1,0:T(8,128)S(1)}, u32[]{:S(2)}, u32[]{:S(2)}) %all-to-all-start.1) | async-done | bytes 524320 | tf_op jit(solution)/shard_map/all_to_all | solution.py:215
  (510 shorter events, 304.3 us)
Async XLA Ops:
  3.6 31.7 %all-to-all-start = ((f32[8,16,8,128]{3,2,0,1:T(8,128)}), f32[8,16,8,128]{3,2,0,1:T(8,128)S(1)}, u32[]{:S(2)}, u32[]{:S(2)}) async-start(f32[8,16,8,128]{3,2,0,1:T(8,128)} %select_bitcast_fusion), calls=%async_computation | async-start | bytes 1048576 | tf_op jit(solution)/shard_map/all_to_all | solution.py:167
  39.8 16.1 %collective-permute-start.4 = (f32[128,4,128]{2,1,0:T(4,128)S(1)}, f32[128,4,128]{2,1,0:T(4,128)S(1)}, u32[]{:S(2)}, u32[]{:S(2)}) collective-permute-start(f32[128,4,128]{2,1,0:T(4,128)S(1)} %get-tuple-element.385), channel_id=1, source_target_pairs={{0,1},{1,2},{2,3},{3,4},{4,5},{5,6},{6,7},{7,8},{8,9},{9,10},{10,1... | collective-permute-start | bytes 786440 | tf_op jit(solution)/shard_map/while/body/eval_jaxpr/ppermute | solution.py:22
  50.0 15.2 %collective-permute-start.2 = (f32[128,4,128]{2,1,0:T(4,128)S(1)}, f32[128,4,128]{2,1,0:T(4,128)S(1)}, u32[]{:S(2)}, u32[]{:S(2)}) collective-permute-start(f32[128,4,128]{2,1,0:T(4,128)S(1)} %get-tuple-element.350), channel_id=1, source_target_pairs={{0,1},{1,2},{2,3},{3,4},{4,5},{5,6},{6,7},{7,8},{8,9},{9,10},{10,1... | collective-permute-start | bytes 786440 | tf_op jit(solution)/shard_map/while/body/eval_jaxpr/ppermute | solution.py:22
  82.0 17.9 %collective-permute-start.4 = (f32[128,4,128]{2,1,0:T(4,128)S(1)}, f32[128,4,128]{2,1,0:T(4,128)S(1)}, u32[]{:S(2)}, u32[]{:S(2)}) collective-permute-start(f32[128,4,128]{2,1,0:T(4,128)S(1)} %get-tuple-element.385), channel_id=1, source_target_pairs={{0,1},{1,2},{2,3},{3,4},{4,5},{5,6},{6,7},{7,8},{8,9},{9,10},{10,1... | collective-permute-start | bytes 786440 | tf_op jit(solution)/shard_map/while/body/eval_jaxpr/ppermute | solution.py:22
  85.6 14.3 %collective-permute-start.5 = (f32[128,4,128]{2,1,0:T(4,128)}, f32[128,4,128]{2,1,0:T(4,128)S(1)}, u32[]{:S(2)}, u32[]{:S(2)}) collective-permute-start(f32[128,4,128]{2,1,0:T(4,128)} %get-tuple-element.384), channel_id=1, source_target_pairs={{1,0},{2,1},{3,2},{4,3},{5,4},{6,5},{7,6},{8,7},{9,8},{10,9},{11,1... | collective-permute-start | bytes 786440 | tf_op jit(solution)/shard_map/while/body/eval_jaxpr/ppermute | solution.py:23
  91.6 17.5 %collective-permute-start.2 = (f32[128,4,128]{2,1,0:T(4,128)S(1)}, f32[128,4,128]{2,1,0:T(4,128)S(1)}, u32[]{:S(2)}, u32[]{:S(2)}) collective-permute-start(f32[128,4,128]{2,1,0:T(4,128)S(1)} %get-tuple-element.350), channel_id=1, source_target_pairs={{0,1},{1,2},{2,3},{3,4},{4,5},{5,6},{6,7},{7,8},{8,9},{9,10},{10,1... | collective-permute-start | bytes 786440 | tf_op jit(solution)/shard_map/while/body/eval_jaxpr/ppermute | solution.py:22
  127.1 18.0 %collective-permute-start.4 = (f32[128,4,128]{2,1,0:T(4,128)S(1)}, f32[128,4,128]{2,1,0:T(4,128)S(1)}, u32[]{:S(2)}, u32[]{:S(2)}) collective-permute-start(f32[128,4,128]{2,1,0:T(4,128)S(1)} %get-tuple-element.385), channel_id=1, source_target_pairs={{0,1},{1,2},{2,3},{3,4},{4,5},{5,6},{6,7},{7,8},{8,9},{9,10},{10,1... | collective-permute-start | bytes 786440 | tf_op jit(solution)/shard_map/while/body/eval_jaxpr/ppermute | solution.py:22
  130.7 14.4 %collective-permute-start.5 = (f32[128,4,128]{2,1,0:T(4,128)}, f32[128,4,128]{2,1,0:T(4,128)S(1)}, u32[]{:S(2)}, u32[]{:S(2)}) collective-permute-start(f32[128,4,128]{2,1,0:T(4,128)} %get-tuple-element.384), channel_id=1, source_target_pairs={{1,0},{2,1},{3,2},{4,3},{5,4},{6,5},{7,6},{8,7},{9,8},{10,9},{11,1... | collective-permute-start | bytes 786440 | tf_op jit(solution)/shard_map/while/body/eval_jaxpr/ppermute | solution.py:23
  136.7 17.6 %collective-permute-start.2 = (f32[128,4,128]{2,1,0:T(4,128)S(1)}, f32[128,4,128]{2,1,0:T(4,128)S(1)}, u32[]{:S(2)}, u32[]{:S(2)}) collective-permute-start(f32[128,4,128]{2,1,0:T(4,128)S(1)} %get-tuple-element.350), channel_id=1, source_target_pairs={{0,1},{1,2},{2,3},{3,4},{4,5},{5,6},{6,7},{7,8},{8,9},{9,10},{10,1... | collective-permute-start | bytes 786440 | tf_op jit(solution)/shard_map/while/body/eval_jaxpr/ppermute | solution.py:22
  172.3 18.0 %collective-permute-start.4 = (f32[128,4,128]{2,1,0:T(4,128)S(1)}, f32[128,4,128]{2,1,0:T(4,128)S(1)}, u32[]{:S(2)}, u32[]{:S(2)}) collective-permute-start(f32[128,4,128]{2,1,0:T(4,128)S(1)} %get-tuple-element.385), channel_id=1, source_target_pairs={{0,1},{1,2},{2,3},{3,4},{4,5},{5,6},{6,7},{7,8},{8,9},{9,10},{10,1... | collective-permute-start | bytes 786440 | tf_op jit(solution)/shard_map/while/body/eval_jaxpr/ppermute | solution.py:22
  175.9 14.4 %collective-permute-start.5 = (f32[128,4,128]{2,1,0:T(4,128)}, f32[128,4,128]{2,1,0:T(4,128)S(1)}, u32[]{:S(2)}, u32[]{:S(2)}) collective-permute-start(f32[128,4,128]{2,1,0:T(4,128)} %get-tuple-element.384), channel_id=1, source_target_pairs={{1,0},{2,1},{3,2},{4,3},{5,4},{6,5},{7,6},{8,7},{9,8},{10,9},{11,1... | collective-permute-start | bytes 786440 | tf_op jit(solution)/shard_map/while/body/eval_jaxpr/ppermute | solution.py:23
  181.9 17.6 %collective-permute-start.2 = (f32[128,4,128]{2,1,0:T(4,128)S(1)}, f32[128,4,128]{2,1,0:T(4,128)S(1)}, u32[]{:S(2)}, u32[]{:S(2)}) collective-permute-start(f32[128,4,128]{2,1,0:T(4,128)S(1)} %get-tuple-element.350), channel_id=1, source_target_pairs={{0,1},{1,2},{2,3},{3,4},{4,5},{5,6},{6,7},{7,8},{8,9},{9,10},{10,1... | collective-permute-start | bytes 786440 | tf_op jit(solution)/shard_map/while/body/eval_jaxpr/ppermute | solution.py:22
  217.5 18.0 %collective-permute-start.4 = (f32[128,4,128]{2,1,0:T(4,128)S(1)}, f32[128,4,128]{2,1,0:T(4,128)S(1)}, u32[]{:S(2)}, u32[]{:S(2)}) collective-permute-start(f32[128,4,128]{2,1,0:T(4,128)S(1)} %get-tuple-element.385), channel_id=1, source_target_pairs={{0,1},{1,2},{2,3},{3,4},{4,5},{5,6},{6,7},{7,8},{8,9},{9,10},{10,1... | collective-permute-start | bytes 786440 | tf_op jit(solution)/shard_map/while/body/eval_jaxpr/ppermute | solution.py:22
  221.1 14.4 %collective-permute-start.5 = (f32[128,4,128]{2,1,0:T(4,128)}, f32[128,4,128]{2,1,0:T(4,128)S(1)}, u32[]{:S(2)}, u32[]{:S(2)}) collective-permute-start(f32[128,4,128]{2,1,0:T(4,128)} %get-tuple-element.384), channel_id=1, source_target_pairs={{1,0},{2,1},{3,2},{4,3},{5,4},{6,5},{7,6},{8,7},{9,8},{10,9},{11,1... | collective-permute-start | bytes 786440 | tf_op jit(solution)/shard_map/while/body/eval_jaxpr/ppermute | solution.py:23
  227.1 17.6 %collective-permute-start.2 = (f32[128,4,128]{2,1,0:T(4,128)S(1)}, f32[128,4,128]{2,1,0:T(4,128)S(1)}, u32[]{:S(2)}, u32[]{:S(2)}) collective-permute-start(f32[128,4,128]{2,1,0:T(4,128)S(1)} %get-tuple-element.350), channel_id=1, source_target_pairs={{0,1},{1,2},{2,3},{3,4},{4,5},{5,6},{6,7},{7,8},{8,9},{9,10},{10,1... | collective-permute-start | bytes 786440 | tf_op jit(solution)/shard_map/while/body/eval_jaxpr/ppermute | solution.py:22
  262.7 18.0 %collective-permute-start.4 = (f32[128,4,128]{2,1,0:T(4,128)S(1)}, f32[128,4,128]{2,1,0:T(4,128)S(1)}, u32[]{:S(2)}, u32[]{:S(2)}) collective-permute-start(f32[128,4,128]{2,1,0:T(4,128)S(1)} %get-tuple-element.385), channel_id=1, source_target_pairs={{0,1},{1,2},{2,3},{3,4},{4,5},{5,6},{6,7},{7,8},{8,9},{9,10},{10,1... | collective-permute-start | bytes 786440 | tf_op jit(solution)/shard_map/while/body/eval_jaxpr/ppermute | solution.py:22
  266.3 14.4 %collective-permute-start.5 = (f32[128,4,128]{2,1,0:T(4,128)}, f32[128,4,128]{2,1,0:T(4,128)S(1)}, u32[]{:S(2)}, u32[]{:S(2)}) collective-permute-start(f32[128,4,128]{2,1,0:T(4,128)} %get-tuple-element.384), channel_id=1, source_target_pairs={{1,0},{2,1},{3,2},{4,3},{5,4},{6,5},{7,6},{8,7},{9,8},{10,9},{11,1... | collective-permute-start | bytes 786440 | tf_op jit(solution)/shard_map/while/body/eval_jaxpr/ppermute | solution.py:23
  272.3 17.6 %collective-permute-start.2 = (f32[128,4,128]{2,1,0:T(4,128)S(1)}, f32[128,4,128]{2,1,0:T(4,128)S(1)}, u32[]{:S(2)}, u32[]{:S(2)}) collective-permute-start(f32[128,4,128]{2,1,0:T(4,128)S(1)} %get-tuple-element.350), channel_id=1, source_target_pairs={{0,1},{1,2},{2,3},{3,4},{4,5},{5,6},{6,7},{7,8},{8,9},{9,10},{10,1... | collective-permute-start | bytes 786440 | tf_op jit(solution)/shard_map/while/body/eval_jaxpr/ppermute | solution.py:22
  300.5 12.3 %collective-permute-start = (f32[128,4,128]{2,1,0:T(4,128)}, f32[128,4,128]{2,1,0:T(4,128)S(1)}, u32[]{:S(2)}, u32[]{:S(2)}) collective-permute-start(f32[128,4,128]{2,1,0:T(4,128)} %get-tuple-element.381), channel_id=1, source_target_pairs={{0,1},{1,2},{2,3},{3,4},{4,5},{5,6},{6,7},{7,8},{8,9},{9,10},{10,1... | collective-permute-start | bytes 786440 | tf_op jit(solution)/shard_map/while/body/eval_jaxpr/ppermute | solution.py:22
  307.9 18.0 %collective-permute-start.4 = (f32[128,4,128]{2,1,0:T(4,128)S(1)}, f32[128,4,128]{2,1,0:T(4,128)S(1)}, u32[]{:S(2)}, u32[]{:S(2)}) collective-permute-start(f32[128,4,128]{2,1,0:T(4,128)S(1)} %get-tuple-element.385), channel_id=1, source_target_pairs={{0,1},{1,2},{2,3},{3,4},{4,5},{5,6},{6,7},{7,8},{8,9},{9,10},{10,1... | collective-permute-start | bytes 786440 | tf_op jit(solution)/shard_map/while/body/eval_jaxpr/ppermute | solution.py:22
  311.5 14.4 %collective-permute-start.5 = (f32[128,4,128]{2,1,0:T(4,128)}, f32[128,4,128]{2,1,0:T(4,128)S(1)}, u32[]{:S(2)}, u32[]{:S(2)}) collective-permute-start(f32[128,4,128]{2,1,0:T(4,128)} %get-tuple-element.384), channel_id=1, source_target_pairs={{1,0},{2,1},{3,2},{4,3},{5,4},{6,5},{7,6},{8,7},{9,8},{10,9},{11,1... | collective-permute-start | bytes 786440 | tf_op jit(solution)/shard_map/while/body/eval_jaxpr/ppermute | solution.py:23
  317.5 17.6 %collective-permute-start.2 = (f32[128,4,128]{2,1,0:T(4,128)S(1)}, f32[128,4,128]{2,1,0:T(4,128)S(1)}, u32[]{:S(2)}, u32[]{:S(2)}) collective-permute-start(f32[128,4,128]{2,1,0:T(4,128)S(1)} %get-tuple-element.350), channel_id=1, source_target_pairs={{0,1},{1,2},{2,3},{3,4},{4,5},{5,6},{6,7},{7,8},{8,9},{9,10},{10,1... | collective-permute-start | bytes 786440 | tf_op jit(solution)/shard_map/while/body/eval_jaxpr/ppermute | solution.py:22
  353.1 18.0 %collective-permute-start.4 = (f32[128,4,128]{2,1,0:T(4,128)S(1)}, f32[128,4,128]{2,1,0:T(4,128)S(1)}, u32[]{:S(2)}, u32[]{:S(2)}) collective-permute-start(f32[128,4,128]{2,1,0:T(4,128)S(1)} %get-tuple-element.385), channel_id=1, source_target_pairs={{0,1},{1,2},{2,3},{3,4},{4,5},{5,6},{6,7},{7,8},{8,9},{9,10},{10,1... | collective-permute-start | bytes 786440 | tf_op jit(solution)/shard_map/while/body/eval_jaxpr/ppermute | solution.py:22
  356.7 14.4 %collective-permute-start.5 = (f32[128,4,128]{2,1,0:T(4,128)}, f32[128,4,128]{2,1,0:T(4,128)S(1)}, u32[]{:S(2)}, u32[]{:S(2)}) collective-permute-start(f32[128,4,128]{2,1,0:T(4,128)} %get-tuple-element.384), channel_id=1, source_target_pairs={{1,0},{2,1},{3,2},{4,3},{5,4},{6,5},{7,6},{8,7},{9,8},{10,9},{11,1... | collective-permute-start | bytes 786440 | tf_op jit(solution)/shard_map/while/body/eval_jaxpr/ppermute | solution.py:23
  362.7 17.6 %collective-permute-start.2 = (f32[128,4,128]{2,1,0:T(4,128)S(1)}, f32[128,4,128]{2,1,0:T(4,128)S(1)}, u32[]{:S(2)}, u32[]{:S(2)}) collective-permute-start(f32[128,4,128]{2,1,0:T(4,128)S(1)} %get-tuple-element.350), channel_id=1, source_target_pairs={{0,1},{1,2},{2,3},{3,4},{4,5},{5,6},{6,7},{7,8},{8,9},{9,10},{10,1... | collective-permute-start | bytes 786440 | tf_op jit(solution)/shard_map/while/body/eval_jaxpr/ppermute | solution.py:22
  398.3 18.0 %collective-permute-start.4 = (f32[128,4,128]{2,1,0:T(4,128)S(1)}, f32[128,4,128]{2,1,0:T(4,128)S(1)}, u32[]{:S(2)}, u32[]{:S(2)}) collective-permute-start(f32[128,4,128]{2,1,0:T(4,128)S(1)} %get-tuple-element.385), channel_id=1, source_target_pairs={{0,1},{1,2},{2,3},{3,4},{4,5},{5,6},{6,7},{7,8},{8,9},{9,10},{10,1... | collective-permute-start | bytes 786440 | tf_op jit(solution)/shard_map/while/body/eval_jaxpr/ppermute | solution.py:22
  401.9 14.4 %collective-permute-start.5 = (f32[128,4,128]{2,1,0:T(4,128)}, f32[128,4,128]{2,1,0:T(4,128)S(1)}, u32[]{:S(2)}, u32[]{:S(2)}) collective-permute-start(f32[128,4,128]{2,1,0:T(4,128)} %get-tuple-element.384), channel_id=1, source_target_pairs={{1,0},{2,1},{3,2},{4,3},{5,4},{6,5},{7,6},{8,7},{9,8},{10,9},{11,1... | collective-permute-start | bytes 786440 | tf_op jit(solution)/shard_map/while/body/eval_jaxpr/ppermute | solution.py:23
  407.9 17.6 %collective-permute-start.2 = (f32[128,4,128]{2,1,0:T(4,128)S(1)}, f32[128,4,128]{2,1,0:T(4,128)S(1)}, u32[]{:S(2)}, u32[]{:S(2)}) collective-permute-start(f32[128,4,128]{2,1,0:T(4,128)S(1)} %get-tuple-element.350), channel_id=1, source_target_pairs={{0,1},{1,2},{2,3},{3,4},{4,5},{5,6},{6,7},{7,8},{8,9},{9,10},{10,1... | collective-permute-start | bytes 786440 | tf_op jit(solution)/shard_map/while/body/eval_jaxpr/ppermute | solution.py:22
  443.5 18.0 %collective-permute-start.4 = (f32[128,4,128]{2,1,0:T(4,128)S(1)}, f32[128,4,128]{2,1,0:T(4,128)S(1)}, u32[]{:S(2)}, u32[]{:S(2)}) collective-permute-start(f32[128,4,128]{2,1,0:T(4,128)S(1)} %get-tuple-element.385), channel_id=1, source_target_pairs={{0,1},{1,2},{2,3},{3,4},{4,5},{5,6},{6,7},{7,8},{8,9},{9,10},{10,1... | collective-permute-start | bytes 786440 | tf_op jit(solution)/shard_map/while/body/eval_jaxpr/ppermute | solution.py:22
  447.1 14.4 %collective-permute-start.5 = (f32[128,4,128]{2,1,0:T(4,128)}, f32[128,4,128]{2,1,0:T(4,128)S(1)}, u32[]{:S(2)}, u32[]{:S(2)}) collective-permute-start(f32[128,4,128]{2,1,0:T(4,128)} %get-tuple-element.384), channel_id=1, source_target_pairs={{1,0},{2,1},{3,2},{4,3},{5,4},{6,5},{7,6},{8,7},{9,8},{10,9},{11,1... | collective-permute-start | bytes 786440 | tf_op jit(solution)/shard_map/while/body/eval_jaxpr/ppermute | solution.py:23
  453.1 17.6 %collective-permute-start.2 = (f32[128,4,128]{2,1,0:T(4,128)S(1)}, f32[128,4,128]{2,1,0:T(4,128)S(1)}, u32[]{:S(2)}, u32[]{:S(2)}) collective-permute-start(f32[128,4,128]{2,1,0:T(4,128)S(1)} %get-tuple-element.350), channel_id=1, source_target_pairs={{0,1},{1,2},{2,3},{3,4},{4,5},{5,6},{6,7},{7,8},{8,9},{9,10},{10,1... | collective-permute-start | bytes 786440 | tf_op jit(solution)/shard_map/while/body/eval_jaxpr/ppermute | solution.py:22
  483.3 26.7 %all-to-all-start.1 = ((f32[128,1,8,128]{3,2,1,0:T(8,128)}), f32[128,1,8,128]{3,2,1,0:T(8,128)S(1)}, u32[]{:S(2)}, u32[]{:S(2)}) async-start(f32[128,1,8,128]{3,2,1,0:T(8,128)} %multiply_bitcast_fusion), calls=%async_computation.1 | async-start | bytes 1048576 | tf_op jit(solution)/shard_map/all_to_all | solution.py:215
  (201 other events, 1687.4 us)

commit v10 on v8

--- a/solution.py
+++ b/solution.py
@@ -11,7 +11,7 @@
 stencil_weights = (8.0 / 5.0, -1.0 / 5.0, 8.0 / 315.0, -1.0 / 560.0)
 center_weight = 3.0 * (-205.0 / 72.0)
 HALO = 4
-ROWS = 8
+ROWS = 4
 XOFF = 8
 
 

time: 507 us -> 554 us (1.093)
  Pallas kernels: 172 us -> 219 us
    pallas_call x40, Pallas kernels: 172 us -> 219 us  [wave_call(): pl.pallas_call(functools.partial(wave_kernel, with_image), out_shape=tupl...]
  transfers between devices with their start and end apart: 82 -> 82, of which waited for: 1 -> 1; matrix products, arithmetic and copies ran while one was open for 5% -> 5% of each run, Pallas kernels for 26% -> 30%
where the time goes in v10:
time: 554 us; the launch traced here: 551 us
  starting transfers between devices  271 us (49%)
  Pallas kernels  219 us (40%)
  local copies, waits for them, and re-layouts  23.2 us (4%)
  matrix products  11.7 us (2%)
  waiting for transfers between devices  11.6 us (2%)
  other arithmetic  10.1 us (2%)
    pallas_call x40, Pallas kernels, wave_call(): pl.pallas_call(functools.partial(wave_kernel, with_image), out_shape=tupl...  219 us
    ppermute x40, starting transfers between devices, trade_halos(): low = lax.ppermute(tail, axis, [(i, (i + 1) % count) for i in range(ends)])  199 us
    ppermute x40, starting transfers between devices, trade_halos(): high = lax.ppermute(head, axis, [((i + 1) % count, i) for i in range(ends)])  51.7 us
    all_to_all x1, starting transfers between devices, shards(): lax.all_to_all(outgoing, 'dom', split_axis=0, concat_axis=1, tiled=True)  12.8 us
    all_to_all x1, waiting for transfers between devices, shards(): lax.all_to_all(outgoing, 'dom', split_axis=0, concat_axis=1, tiled=True)  11.3 us
  transfers between devices with their start and end apart: 82, of which 1 were waited for; matrix products, arithmetic and copies ran while one was open for 5% of the time, Pallas kernels for 30%

profile of v10, /device:TPU:0, one launch (start us, length us, event | category | flops | bytes accessed | tf_op | source)
XLA Modules:
  0.0 550.6 jit_solution(6460306038400372621)
XLA Ops:
  3.6 7.4 %all-to-all-start = ((f32[8,16,8,128]{3,2,0,1:T(8,128)}), f32[8,16,8,128]{3,2,0,1:T(8,128)S(1)}, u32[]{:S(2)}, u32[]{:S(2)}) async-start(f32[8,16,8,128]{3,2,0,1:T(8,128)} %select_bitcast_fusion), calls=%async_computation | async-start | bytes 1048576 | tf_op jit(solution)/shard_map/all_to_all | solution.py:144
  12.2 10.5 %fusion = f32[20,32,128]{2,1,0:T(8,128)S(1)} fusion(f32[8192,20]{0,1:T(8,128)S(1)} %bitcast.85, f32[8192,32]{0,1:T(8,128)S(1)} %fusion.8, s32[8192]{0:T(1024)S(1)} %bitcast.83), kind=kOutput, calls=%fused_computation.1 | convolution fusion | flops 8059355136 | bytes 2064384 | tf_op jit(solution)/shard_map/ny,nsc->syc/dot_general | solution.py:131
  36.2 483.5 %while.29 = (s32[]{:T(128)}, f32[128,8,128]{2,1,0:T(8,128)}, f32[128,8,128]{2,1,0:T(8,128)S(1)}, f32[128,4,128]{2,1,0:T(4,128)}, f32[128,4,128]{2,1,0:T(4,128)},...) while((s32[]{:T(128)}, f32[128,8,128]{2,1,0:T(8,128)}, ...), condition=%wide.region_1.2_spmd, body=%wide.region_0.1_spmd.sunk | while | flops 31457284 | bytes 67109736 | solution.py:181
  67.1 6.0 %eval_jaxpr.21 = (f32[128,8,128]{2,1,0:T(8,128)}, f32[128,4,128]{2,1,0:T(4,128)}, f32[128,4,128]{2,1,0:T(4,128)}) custom-call(s32[1]{0:T(128)} %bitcast.68.moment_ref, f32[128,8,128]{2,1,0:T(8,128)} %get-tuple-element.392.cur_ref.rest_0_, f32[128,8,128]{2,1,0:T(8,128)} %copy-done.3, ...), custom_call_target="tpu_custom_call", output_to_operand_aliasing={{0}: (2, {})} | custom-call | flops 7864320 | bytes 3145728 | tf_op jit(solution)/shard_map/while/body/eval_jaxpr/pallas_call | solution.py:103
  96.5 6.0 %collective-permute-start.2 = (f32[128,4,128]{2,1,0:T(4,128)S(1)}, f32[128,4,128]{2,1,0:T(4,128)S(1)}, u32[]{:S(2)}, u32[]{:S(2)}) collective-permute-start(f32[128,4,128]{2,1,0:T(4,128)S(1)} %get-tuple-element.350), channel_id=1, source_target_pairs={{0,1},{1,2},{2,3},{3,4},{4,5},{5,6},{6,7},{7,8},{8,9},{9,10},{10,1... | collective-permute-start | bytes 786440 | tf_op jit(solution)/shard_map/while/body/eval_jaxpr/ppermute | solution.py:21
  114.3 6.0 %eval_jaxpr.21 = (f32[128,8,128]{2,1,0:T(8,128)}, f32[128,4,128]{2,1,0:T(4,128)}, f32[128,4,128]{2,1,0:T(4,128)}) custom-call(s32[1]{0:T(128)} %bitcast.68.moment_ref, f32[128,8,128]{2,1,0:T(8,128)} %get-tuple-element.392.cur_ref.rest_0_, f32[128,8,128]{2,1,0:T(8,128)} %copy-done.3, ...), custom_call_target="tpu_custom_call", output_to_operand_aliasing={{0}: (2, {})} | custom-call | flops 7864320 | bytes 3145728 | tf_op jit(solution)/shard_map/while/body/eval_jaxpr/pallas_call | solution.py:103
  126.9 5.7 %collective-permute-start = (f32[128,4,128]{2,1,0:T(4,128)}, f32[128,4,128]{2,1,0:T(4,128)S(1)}, u32[]{:S(2)}, u32[]{:S(2)}) collective-permute-start(f32[128,4,128]{2,1,0:T(4,128)} %get-tuple-element.381), channel_id=1, source_target_pairs={{0,1},{1,2},{2,3},{3,4},{4,5},{5,6},{6,7},{7,8},{8,9},{9,10},{10,1... | collective-permute-start | bytes 786440 | tf_op jit(solution)/shard_map/while/body/eval_jaxpr/ppermute | solution.py:21
  145.6 6.1 %collective-permute-start.2 = (f32[128,4,128]{2,1,0:T(4,128)S(1)}, f32[128,4,128]{2,1,0:T(4,128)S(1)}, u32[]{:S(2)}, u32[]{:S(2)}) collective-permute-start(f32[128,4,128]{2,1,0:T(4,128)S(1)} %get-tuple-element.350), channel_id=1, source_target_pairs={{0,1},{1,2},{2,3},{3,4},{4,5},{5,6},{6,7},{7,8},{8,9},{9,10},{10,1... | collective-permute-start | bytes 786440 | tf_op jit(solution)/shard_map/while/body/eval_jaxpr/ppermute | solution.py:21
  163.4 6.0 %eval_jaxpr.21 = (f32[128,8,128]{2,1,0:T(8,128)}, f32[128,4,128]{2,1,0:T(4,128)}, f32[128,4,128]{2,1,0:T(4,128)}) custom-call(s32[1]{0:T(128)} %bitcast.68.moment_ref, f32[128,8,128]{2,1,0:T(8,128)} %get-tuple-element.392.cur_ref.rest_0_, f32[128,8,128]{2,1,0:T(8,128)} %copy-done.3, ...), custom_call_target="tpu_custom_call", output_to_operand_aliasing={{0}: (2, {})} | custom-call | flops 7864320 | bytes 3145728 | tf_op jit(solution)/shard_map/while/body/eval_jaxpr/pallas_call | solution.py:103
  176.0 5.7 %collective-permute-start = (f32[128,4,128]{2,1,0:T(4,128)}, f32[128,4,128]{2,1,0:T(4,128)S(1)}, u32[]{:S(2)}, u32[]{:S(2)}) collective-permute-start(f32[128,4,128]{2,1,0:T(4,128)} %get-tuple-element.381), channel_id=1, source_target_pairs={{0,1},{1,2},{2,3},{3,4},{4,5},{5,6},{6,7},{7,8},{8,9},{9,10},{10,1... | collective-permute-start | bytes 786440 | tf_op jit(solution)/shard_map/while/body/eval_jaxpr/ppermute | solution.py:21
  194.7 6.1 %collective-permute-start.2 = (f32[128,4,128]{2,1,0:T(4,128)S(1)}, f32[128,4,128]{2,1,0:T(4,128)S(1)}, u32[]{:S(2)}, u32[]{:S(2)}) collective-permute-start(f32[128,4,128]{2,1,0:T(4,128)S(1)} %get-tuple-element.350), channel_id=1, source_target_pairs={{0,1},{1,2},{2,3},{3,4},{4,5},{5,6},{6,7},{7,8},{8,9},{9,10},{10,1... | collective-permute-start | bytes 786440 | tf_op jit(solution)/shard_map/while/body/eval_jaxpr/ppermute | solution.py:21
  212.5 6.0 %eval_jaxpr.21 = (f32[128,8,128]{2,1,0:T(8,128)}, f32[128,4,128]{2,1,0:T(4,128)}, f32[128,4,128]{2,1,0:T(4,128)}) custom-call(s32[1]{0:T(128)} %bitcast.68.moment_ref, f32[128,8,128]{2,1,0:T(8,128)} %get-tuple-element.392.cur_ref.rest_0_, f32[128,8,128]{2,1,0:T(8,128)} %copy-done.3, ...), custom_call_target="tpu_custom_call", output_to_operand_aliasing={{0}: (2, {})} | custom-call | flops 7864320 | bytes 3145728 | tf_op jit(solution)/shard_map/while/body/eval_jaxpr/pallas_call | solution.py:103
  225.1 5.7 %collective-permute-start = (f32[128,4,128]{2,1,0:T(4,128)}, f32[128,4,128]{2,1,0:T(4,128)S(1)}, u32[]{:S(2)}, u32[]{:S(2)}) collective-permute-start(f32[128,4,128]{2,1,0:T(4,128)} %get-tuple-element.381), channel_id=1, source_target_pairs={{0,1},{1,2},{2,3},{3,4},{4,5},{5,6},{6,7},{7,8},{8,9},{9,10},{10,1... | collective-permute-start | bytes 786440 | tf_op jit(solution)/shard_map/while/body/eval_jaxpr/ppermute | solution.py:21
  243.8 6.1 %collective-permute-start.2 = (f32[128,4,128]{2,1,0:T(4,128)S(1)}, f32[128,4,128]{2,1,0:T(4,128)S(1)}, u32[]{:S(2)}, u32[]{:S(2)}) collective-permute-start(f32[128,4,128]{2,1,0:T(4,128)S(1)} %get-tuple-element.350), channel_id=1, source_target_pairs={{0,1},{1,2},{2,3},{3,4},{4,5},{5,6},{6,7},{7,8},{8,9},{9,10},{10,1... | collective-permute-start | bytes 786440 | tf_op jit(solution)/shard_map/while/body/eval_jaxpr/ppermute | solution.py:21
  261.7 6.0 %eval_jaxpr.21 = (f32[128,8,128]{2,1,0:T(8,128)}, f32[128,4,128]{2,1,0:T(4,128)}, f32[128,4,128]{2,1,0:T(4,128)}) custom-call(s32[1]{0:T(128)} %bitcast.68.moment_ref, f32[128,8,128]{2,1,0:T(8,128)} %get-tuple-element.392.cur_ref.rest_0_, f32[128,8,128]{2,1,0:T(8,128)} %copy-done.3, ...), custom_call_target="tpu_custom_call", output_to_operand_aliasing={{0}: (2, {})} | custom-call | flops 7864320 | bytes 3145728 | tf_op jit(solution)/shard_map/while/body/eval_jaxpr/pallas_call | solution.py:103
  274.2 5.7 %collective-permute-start = (f32[128,4,128]{2,1,0:T(4,128)}, f32[128,4,128]{2,1,0:T(4,128)S(1)}, u32[]{:S(2)}, u32[]{:S(2)}) collective-permute-start(f32[128,4,128]{2,1,0:T(4,128)} %get-tuple-element.381), channel_id=1, source_target_pairs={{0,1},{1,2},{2,3},{3,4},{4,5},{5,6},{6,7},{7,8},{8,9},{9,10},{10,1... | collective-permute-start | bytes 786440 | tf_op jit(solution)/shard_map/while/body/eval_jaxpr/ppermute | solution.py:21
  292.9 6.1 %collective-permute-start.2 = (f32[128,4,128]{2,1,0:T(4,128)S(1)}, f32[128,4,128]{2,1,0:T(4,128)S(1)}, u32[]{:S(2)}, u32[]{:S(2)}) collective-permute-start(f32[128,4,128]{2,1,0:T(4,128)S(1)} %get-tuple-element.350), channel_id=1, source_target_pairs={{0,1},{1,2},{2,3},{3,4},{4,5},{5,6},{6,7},{7,8},{8,9},{9,10},{10,1... | collective-permute-start | bytes 786440 | tf_op jit(solution)/shard_map/while/body/eval_jaxpr/ppermute | solution.py:21
  310.8 6.0 %eval_jaxpr.21 = (f32[128,8,128]{2,1,0:T(8,128)}, f32[128,4,128]{2,1,0:T(4,128)}, f32[128,4,128]{2,1,0:T(4,128)}) custom-call(s32[1]{0:T(128)} %bitcast.68.moment_ref, f32[128,8,128]{2,1,0:T(8,128)} %get-tuple-element.392.cur_ref.rest_0_, f32[128,8,128]{2,1,0:T(8,128)} %copy-done.3, ...), custom_call_target="tpu_custom_call", output_to_operand_aliasing={{0}: (2, {})} | custom-call | flops 7864320 | bytes 3145728 | tf_op jit(solution)/shard_map/while/body/eval_jaxpr/pallas_call | solution.py:103
  323.3 5.7 %collective-permute-start = (f32[128,4,128]{2,1,0:T(4,128)}, f32[128,4,128]{2,1,0:T(4,128)S(1)}, u32[]{:S(2)}, u32[]{:S(2)}) collective-permute-start(f32[128,4,128]{2,1,0:T(4,128)} %get-tuple-element.381), channel_id=1, source_target_pairs={{0,1},{1,2},{2,3},{3,4},{4,5},{5,6},{6,7},{7,8},{8,9},{9,10},{10,1... | collective-permute-start | bytes 786440 | tf_op jit(solution)/shard_map/while/body/eval_jaxpr/ppermute | solution.py:21
  342.0 6.1 %collective-permute-start.2 = (f32[128,4,128]{2,1,0:T(4,128)S(1)}, f32[128,4,128]{2,1,0:T(4,128)S(1)}, u32[]{:S(2)}, u32[]{:S(2)}) collective-permute-start(f32[128,4,128]{2,1,0:T(4,128)S(1)} %get-tuple-element.350), channel_id=1, source_target_pairs={{0,1},{1,2},{2,3},{3,4},{4,5},{5,6},{6,7},{7,8},{8,9},{9,10},{10,1... | collective-permute-start | bytes 786440 | tf_op jit(solution)/shard_map/while/body/eval_jaxpr/ppermute | solution.py:21
  359.9 6.0 %eval_jaxpr.21 = (f32[128,8,128]{2,1,0:T(8,128)}, f32[128,4,128]{2,1,0:T(4,128)}, f32[128,4,128]{2,1,0:T(4,128)}) custom-call(s32[1]{0:T(128)} %bitcast.68.moment_ref, f32[128,8,128]{2,1,0:T(8,128)} %get-tuple-element.392.cur_ref.rest_0_, f32[128,8,128]{2,1,0:T(8,128)} %copy-done.3, ...), custom_call_target="tpu_custom_call", output_to_operand_aliasing={{0}: (2, {})} | custom-call | flops 7864320 | bytes 3145728 | tf_op jit(solution)/shard_map/while/body/eval_jaxpr/pallas_call | solution.py:103
  372.4 5.7 %collective-permute-start = (f32[128,4,128]{2,1,0:T(4,128)}, f32[128,4,128]{2,1,0:T(4,128)S(1)}, u32[]{:S(2)}, u32[]{:S(2)}) collective-permute-start(f32[128,4,128]{2,1,0:T(4,128)} %get-tuple-element.381), channel_id=1, source_target_pairs={{0,1},{1,2},{2,3},{3,4},{4,5},{5,6},{6,7},{7,8},{8,9},{9,10},{10,1... | collective-permute-start | bytes 786440 | tf_op jit(solution)/shard_map/while/body/eval_jaxpr/ppermute | solution.py:21
  391.1 6.1 %collective-permute-start.2 = (f32[128,4,128]{2,1,0:T(4,128)S(1)}, f32[128,4,128]{2,1,0:T(4,128)S(1)}, u32[]{:S(2)}, u32[]{:S(2)}) collective-permute-start(f32[128,4,128]{2,1,0:T(4,128)S(1)} %get-tuple-element.350), channel_id=1, source_target_pairs={{0,1},{1,2},{2,3},{3,4},{4,5},{5,6},{6,7},{7,8},{8,9},{9,10},{10,1... | collective-permute-start | bytes 786440 | tf_op jit(solution)/shard_map/while/body/eval_jaxpr/ppermute | solution.py:21
  409.0 6.0 %eval_jaxpr.21 = (f32[128,8,128]{2,1,0:T(8,128)}, f32[128,4,128]{2,1,0:T(4,128)}, f32[128,4,128]{2,1,0:T(4,128)}) custom-call(s32[1]{0:T(128)} %bitcast.68.moment_ref, f32[128,8,128]{2,1,0:T(8,128)} %get-tuple-element.392.cur_ref.rest_0_, f32[128,8,128]{2,1,0:T(8,128)} %copy-done.3, ...), custom_call_target="tpu_custom_call", output_to_operand_aliasing={{0}: (2, {})} | custom-call | flops 7864320 | bytes 3145728 | tf_op jit(solution)/shard_map/while/body/eval_jaxpr/pallas_call | solution.py:103
  421.5 5.7 %collective-permute-start = (f32[128,4,128]{2,1,0:T(4,128)}, f32[128,4,128]{2,1,0:T(4,128)S(1)}, u32[]{:S(2)}, u32[]{:S(2)}) collective-permute-start(f32[128,4,128]{2,1,0:T(4,128)} %get-tuple-element.381), channel_id=1, source_target_pairs={{0,1},{1,2},{2,3},{3,4},{4,5},{5,6},{6,7},{7,8},{8,9},{9,10},{10,1... | collective-permute-start | bytes 786440 | tf_op jit(solution)/shard_map/while/body/eval_jaxpr/ppermute | solution.py:21
  440.2 6.1 %collective-permute-start.2 = (f32[128,4,128]{2,1,0:T(4,128)S(1)}, f32[128,4,128]{2,1,0:T(4,128)S(1)}, u32[]{:S(2)}, u32[]{:S(2)}) collective-permute-start(f32[128,4,128]{2,1,0:T(4,128)S(1)} %get-tuple-element.350), channel_id=1, source_target_pairs={{0,1},{1,2},{2,3},{3,4},{4,5},{5,6},{6,7},{7,8},{8,9},{9,10},{10,1... | collective-permute-start | bytes 786440 | tf_op jit(solution)/shard_map/while/body/eval_jaxpr/ppermute | solution.py:21
  458.1 6.0 %eval_jaxpr.21 = (f32[128,8,128]{2,1,0:T(8,128)}, f32[128,4,128]{2,1,0:T(4,128)}, f32[128,4,128]{2,1,0:T(4,128)}) custom-call(s32[1]{0:T(128)} %bitcast.68.moment_ref, f32[128,8,128]{2,1,0:T(8,128)} %get-tuple-element.392.cur_ref.rest_0_, f32[128,8,128]{2,1,0:T(8,128)} %copy-done.3, ...), custom_call_target="tpu_custom_call", output_to_operand_aliasing={{0}: (2, {})} | custom-call | flops 7864320 | bytes 3145728 | tf_op jit(solution)/shard_map/while/body/eval_jaxpr/pallas_call | solution.py:103
  470.6 5.7 %collective-permute-start = (f32[128,4,128]{2,1,0:T(4,128)}, f32[128,4,128]{2,1,0:T(4,128)S(1)}, u32[]{:S(2)}, u32[]{:S(2)}) collective-permute-start(f32[128,4,128]{2,1,0:T(4,128)} %get-tuple-element.381), channel_id=1, source_target_pairs={{0,1},{1,2},{2,3},{3,4},{4,5},{5,6},{6,7},{7,8},{8,9},{9,10},{10,1... | collective-permute-start | bytes 786440 | tf_op jit(solution)/shard_map/while/body/eval_jaxpr/ppermute | solution.py:21
  489.3 6.1 %collective-permute-start.2 = (f32[128,4,128]{2,1,0:T(4,128)S(1)}, f32[128,4,128]{2,1,0:T(4,128)S(1)}, u32[]{:S(2)}, u32[]{:S(2)}) collective-permute-start(f32[128,4,128]{2,1,0:T(4,128)S(1)} %get-tuple-element.350), channel_id=1, source_target_pairs={{0,1},{1,2},{2,3},{3,4},{4,5},{5,6},{6,7},{7,8},{8,9},{9,10},{10,1... | collective-permute-start | bytes 786440 | tf_op jit(solution)/shard_map/while/body/eval_jaxpr/ppermute | solution.py:21
  507.2 6.0 %eval_jaxpr.21 = (f32[128,8,128]{2,1,0:T(8,128)}, f32[128,4,128]{2,1,0:T(4,128)}, f32[128,4,128]{2,1,0:T(4,128)}) custom-call(s32[1]{0:T(128)} %bitcast.68.moment_ref, f32[128,8,128]{2,1,0:T(8,128)} %get-tuple-element.392.cur_ref.rest_0_, f32[128,8,128]{2,1,0:T(8,128)} %copy-done.3, ...), custom_call_target="tpu_custom_call", output_to_operand_aliasing={{0}: (2, {})} | custom-call | flops 7864320 | bytes 3145728 | tf_op jit(solution)/shard_map/while/body/eval_jaxpr/pallas_call | solution.py:103
  521.7 12.8 %all-to-all-start.1 = ((f32[128,1,8,128]{3,2,1,0:T(8,128)}), f32[128,1,8,128]{3,2,1,0:T(8,128)S(1)}, u32[]{:S(2)}, u32[]{:S(2)}) async-start(f32[128,1,8,128]{3,2,1,0:T(8,128)} %multiply_bitcast_fusion), calls=%async_computation.1 | async-start | bytes 1048576 | tf_op jit(solution)/shard_map/all_to_all | solution.py:192
  537.6 11.3 %all-to-all-done.1 = f32[128,1,8,128]{3,2,1,0:T(8,128)S(1)} async-done(((f32[128,1,8,128]{3,2,1,0:T(8,128)}), f32[128,1,8,128]{3,2,1,0:T(8,128)S(1)}, u32[]{:S(2)}, u32[]{:S(2)}) %all-to-all-start.1) | async-done | bytes 524320 | tf_op jit(solution)/shard_map/all_to_all | solution.py:192
  (510 shorter events, 344.2 us)
Async XLA Ops:
  3.6 31.7 %all-to-all-start = ((f32[8,16,8,128]{3,2,0,1:T(8,128)}), f32[8,16,8,128]{3,2,0,1:T(8,128)S(1)}, u32[]{:S(2)}, u32[]{:S(2)}) async-start(f32[8,16,8,128]{3,2,0,1:T(8,128)} %select_bitcast_fusion), calls=%async_computation | async-start | bytes 1048576 | tf_op jit(solution)/shard_map/all_to_all | solution.py:144
  39.8 17.1 %collective-permute-start.4 = (f32[128,4,128]{2,1,0:T(4,128)S(1)}, f32[128,4,128]{2,1,0:T(4,128)S(1)}, u32[]{:S(2)}, u32[]{:S(2)}) collective-permute-start(f32[128,4,128]{2,1,0:T(4,128)S(1)} %get-tuple-element.385), channel_id=1, source_target_pairs={{0,1},{1,2},{2,3},{3,4},{4,5},{5,6},{6,7},{7,8},{8,9},{9,10},{10,1... | collective-permute-start | bytes 786440 | tf_op jit(solution)/shard_map/while/body/eval_jaxpr/ppermute | solution.py:21
  51.0 16.1 %collective-permute-start.2 = (f32[128,4,128]{2,1,0:T(4,128)S(1)}, f32[128,4,128]{2,1,0:T(4,128)S(1)}, u32[]{:S(2)}, u32[]{:S(2)}) collective-permute-start(f32[128,4,128]{2,1,0:T(4,128)S(1)} %get-tuple-element.350), channel_id=1, source_target_pairs={{0,1},{1,2},{2,3},{3,4},{4,5},{5,6},{6,7},{7,8},{8,9},{9,10},{10,1... | collective-permute-start | bytes 786440 | tf_op jit(solution)/shard_map/while/body/eval_jaxpr/ppermute | solution.py:21
  85.2 18.6 %collective-permute-start.4 = (f32[128,4,128]{2,1,0:T(4,128)S(1)}, f32[128,4,128]{2,1,0:T(4,128)S(1)}, u32[]{:S(2)}, u32[]{:S(2)}) collective-permute-start(f32[128,4,128]{2,1,0:T(4,128)S(1)} %get-tuple-element.385), channel_id=1, source_target_pairs={{0,1},{1,2},{2,3},{3,4},{4,5},{5,6},{6,7},{7,8},{8,9},{9,10},{10,1... | collective-permute-start | bytes 786440 | tf_op jit(solution)/shard_map/while/body/eval_jaxpr/ppermute | solution.py:21
  89.5 14.3 %collective-permute-start.5 = (f32[128,4,128]{2,1,0:T(4,128)}, f32[128,4,128]{2,1,0:T(4,128)S(1)}, u32[]{:S(2)}, u32[]{:S(2)}) collective-permute-start(f32[128,4,128]{2,1,0:T(4,128)} %get-tuple-element.384), channel_id=1, source_target_pairs={{1,0},{2,1},{3,2},{4,3},{5,4},{6,5},{7,6},{8,7},{9,8},{10,9},{11,1... | collective-permute-start | bytes 786440 | tf_op jit(solution)/shard_map/while/body/eval_jaxpr/ppermute | solution.py:22
  96.5 17.8 %collective-permute-start.2 = (f32[128,4,128]{2,1,0:T(4,128)S(1)}, f32[128,4,128]{2,1,0:T(4,128)S(1)}, u32[]{:S(2)}, u32[]{:S(2)}) collective-permute-start(f32[128,4,128]{2,1,0:T(4,128)S(1)} %get-tuple-element.350), channel_id=1, source_target_pairs={{0,1},{1,2},{2,3},{3,4},{4,5},{5,6},{6,7},{7,8},{8,9},{9,10},{10,1... | collective-permute-start | bytes 786440 | tf_op jit(solution)/shard_map/while/body/eval_jaxpr/ppermute | solution.py:21
  126.9 13.0 %collective-permute-start = (f32[128,4,128]{2,1,0:T(4,128)}, f32[128,4,128]{2,1,0:T(4,128)S(1)}, u32[]{:S(2)}, u32[]{:S(2)}) collective-permute-start(f32[128,4,128]{2,1,0:T(4,128)} %get-tuple-element.381), channel_id=1, source_target_pairs={{0,1},{1,2},{2,3},{3,4},{4,5},{5,6},{6,7},{7,8},{8,9},{9,10},{10,1... | collective-permute-start | bytes 786440 | tf_op jit(solution)/shard_map/while/body/eval_jaxpr/ppermute | solution.py:21
  133.9 19.0 %collective-permute-start.4 = (f32[128,4,128]{2,1,0:T(4,128)S(1)}, f32[128,4,128]{2,1,0:T(4,128)S(1)}, u32[]{:S(2)}, u32[]{:S(2)}) collective-permute-start(f32[128,4,128]{2,1,0:T(4,128)S(1)} %get-tuple-element.385), channel_id=1, source_target_pairs={{0,1},{1,2},{2,3},{3,4},{4,5},{5,6},{6,7},{7,8},{8,9},{9,10},{10,1... | collective-permute-start | bytes 786440 | tf_op jit(solution)/shard_map/while/body/eval_jaxpr/ppermute | solution.py:21
  138.5 14.4 %collective-permute-start.5 = (f32[128,4,128]{2,1,0:T(4,128)}, f32[128,4,128]{2,1,0:T(4,128)S(1)}, u32[]{:S(2)}, u32[]{:S(2)}) collective-permute-start(f32[128,4,128]{2,1,0:T(4,128)} %get-tuple-element.384), channel_id=1, source_target_pairs={{1,0},{2,1},{3,2},{4,3},{5,4},{6,5},{7,6},{8,7},{9,8},{10,9},{11,1... | collective-permute-start | bytes 786440 | tf_op jit(solution)/shard_map/while/body/eval_jaxpr/ppermute | solution.py:22
  145.6 17.9 %collective-permute-start.2 = (f32[128,4,128]{2,1,0:T(4,128)S(1)}, f32[128,4,128]{2,1,0:T(4,128)S(1)}, u32[]{:S(2)}, u32[]{:S(2)}) collective-permute-start(f32[128,4,128]{2,1,0:T(4,128)S(1)} %get-tuple-element.350), channel_id=1, source_target_pairs={{0,1},{1,2},{2,3},{3,4},{4,5},{5,6},{6,7},{7,8},{8,9},{9,10},{10,1... | collective-permute-start | bytes 786440 | tf_op jit(solution)/shard_map/while/body/eval_jaxpr/ppermute | solution.py:21
  183.0 19.0 %collective-permute-start.4 = (f32[128,4,128]{2,1,0:T(4,128)S(1)}, f32[128,4,128]{2,1,0:T(4,128)S(1)}, u32[]{:S(2)}, u32[]{:S(2)}) collective-permute-start(f32[128,4,128]{2,1,0:T(4,128)S(1)} %get-tuple-element.385), channel_id=1, source_target_pairs={{0,1},{1,2},{2,3},{3,4},{4,5},{5,6},{6,7},{7,8},{8,9},{9,10},{10,1... | collective-permute-start | bytes 786440 | tf_op jit(solution)/shard_map/while/body/eval_jaxpr/ppermute | solution.py:21
  187.6 14.4 %collective-permute-start.5 = (f32[128,4,128]{2,1,0:T(4,128)}, f32[128,4,128]{2,1,0:T(4,128)S(1)}, u32[]{:S(2)}, u32[]{:S(2)}) collective-permute-start(f32[128,4,128]{2,1,0:T(4,128)} %get-tuple-element.384), channel_id=1, source_target_pairs={{1,0},{2,1},{3,2},{4,3},{5,4},{6,5},{7,6},{8,7},{9,8},{10,9},{11,1... | collective-permute-start | bytes 786440 | tf_op jit(solution)/shard_map/while/body/eval_jaxpr/ppermute | solution.py:22
  194.7 17.9 %collective-permute-start.2 = (f32[128,4,128]{2,1,0:T(4,128)S(1)}, f32[128,4,128]{2,1,0:T(4,128)S(1)}, u32[]{:S(2)}, u32[]{:S(2)}) collective-permute-start(f32[128,4,128]{2,1,0:T(4,128)S(1)} %get-tuple-element.350), channel_id=1, source_target_pairs={{0,1},{1,2},{2,3},{3,4},{4,5},{5,6},{6,7},{7,8},{8,9},{9,10},{10,1... | collective-permute-start | bytes 786440 | tf_op jit(solution)/shard_map/while/body/eval_jaxpr/ppermute | solution.py:21
  232.1 19.0 %collective-permute-start.4 = (f32[128,4,128]{2,1,0:T(4,128)S(1)}, f32[128,4,128]{2,1,0:T(4,128)S(1)}, u32[]{:S(2)}, u32[]{:S(2)}) collective-permute-start(f32[128,4,128]{2,1,0:T(4,128)S(1)} %get-tuple-element.385), channel_id=1, source_target_pairs={{0,1},{1,2},{2,3},{3,4},{4,5},{5,6},{6,7},{7,8},{8,9},{9,10},{10,1... | collective-permute-start | bytes 786440 | tf_op jit(solution)/shard_map/while/body/eval_jaxpr/ppermute | solution.py:21
  236.7 14.4 %collective-permute-start.5 = (f32[128,4,128]{2,1,0:T(4,128)}, f32[128,4,128]{2,1,0:T(4,128)S(1)}, u32[]{:S(2)}, u32[]{:S(2)}) collective-permute-start(f32[128,4,128]{2,1,0:T(4,128)} %get-tuple-element.384), channel_id=1, source_target_pairs={{1,0},{2,1},{3,2},{4,3},{5,4},{6,5},{7,6},{8,7},{9,8},{10,9},{11,1... | collective-permute-start | bytes 786440 | tf_op jit(solution)/shard_map/while/body/eval_jaxpr/ppermute | solution.py:22
  243.8 17.9 %collective-permute-start.2 = (f32[128,4,128]{2,1,0:T(4,128)S(1)}, f32[128,4,128]{2,1,0:T(4,128)S(1)}, u32[]{:S(2)}, u32[]{:S(2)}) collective-permute-start(f32[128,4,128]{2,1,0:T(4,128)S(1)} %get-tuple-element.350), channel_id=1, source_target_pairs={{0,1},{1,2},{2,3},{3,4},{4,5},{5,6},{6,7},{7,8},{8,9},{9,10},{10,1... | collective-permute-start | bytes 786440 | tf_op jit(solution)/shard_map/while/body/eval_jaxpr/ppermute | solution.py:21
  281.2 19.0 %collective-permute-start.4 = (f32[128,4,128]{2,1,0:T(4,128)S(1)}, f32[128,4,128]{2,1,0:T(4,128)S(1)}, u32[]{:S(2)}, u32[]{:S(2)}) collective-permute-start(f32[128,4,128]{2,1,0:T(4,128)S(1)} %get-tuple-element.385), channel_id=1, source_target_pairs={{0,1},{1,2},{2,3},{3,4},{4,5},{5,6},{6,7},{7,8},{8,9},{9,10},{10,1... | collective-permute-start | bytes 786440 | tf_op jit(solution)/shard_map/while/body/eval_jaxpr/ppermute | solution.py:21
  285.8 14.4 %collective-permute-start.5 = (f32[128,4,128]{2,1,0:T(4,128)}, f32[128,4,128]{2,1,0:T(4,128)S(1)}, u32[]{:S(2)}, u32[]{:S(2)}) collective-permute-start(f32[128,4,128]{2,1,0:T(4,128)} %get-tuple-element.384), channel_id=1, source_target_pairs={{1,0},{2,1},{3,2},{4,3},{5,4},{6,5},{7,6},{8,7},{9,8},{10,9},{11,1... | collective-permute-start | bytes 786440 | tf_op jit(solution)/shard_map/while/body/eval_jaxpr/ppermute | solution.py:22
  292.9 17.9 %collective-permute-start.2 = (f32[128,4,128]{2,1,0:T(4,128)S(1)}, f32[128,4,128]{2,1,0:T(4,128)S(1)}, u32[]{:S(2)}, u32[]{:S(2)}) collective-permute-start(f32[128,4,128]{2,1,0:T(4,128)S(1)} %get-tuple-element.350), channel_id=1, source_target_pairs={{0,1},{1,2},{2,3},{3,4},{4,5},{5,6},{6,7},{7,8},{8,9},{9,10},{10,1... | collective-permute-start | bytes 786440 | tf_op jit(solution)/shard_map/while/body/eval_jaxpr/ppermute | solution.py:21
  330.3 19.0 %collective-permute-start.4 = (f32[128,4,128]{2,1,0:T(4,128)S(1)}, f32[128,4,128]{2,1,0:T(4,128)S(1)}, u32[]{:S(2)}, u32[]{:S(2)}) collective-permute-start(f32[128,4,128]{2,1,0:T(4,128)S(1)} %get-tuple-element.385), channel_id=1, source_target_pairs={{0,1},{1,2},{2,3},{3,4},{4,5},{5,6},{6,7},{7,8},{8,9},{9,10},{10,1... | collective-permute-start | bytes 786440 | tf_op jit(solution)/shard_map/while/body/eval_jaxpr/ppermute | solution.py:21
  334.9 14.4 %collective-permute-start.5 = (f32[128,4,128]{2,1,0:T(4,128)}, f32[128,4,128]{2,1,0:T(4,128)S(1)}, u32[]{:S(2)}, u32[]{:S(2)}) collective-permute-start(f32[128,4,128]{2,1,0:T(4,128)} %get-tuple-element.384), channel_id=1, source_target_pairs={{1,0},{2,1},{3,2},{4,3},{5,4},{6,5},{7,6},{8,7},{9,8},{10,9},{11,1... | collective-permute-start | bytes 786440 | tf_op jit(solution)/shard_map/while/body/eval_jaxpr/ppermute | solution.py:22
  342.0 17.9 %collective-permute-start.2 = (f32[128,4,128]{2,1,0:T(4,128)S(1)}, f32[128,4,128]{2,1,0:T(4,128)S(1)}, u32[]{:S(2)}, u32[]{:S(2)}) collective-permute-start(f32[128,4,128]{2,1,0:T(4,128)S(1)} %get-tuple-element.350), channel_id=1, source_target_pairs={{0,1},{1,2},{2,3},{3,4},{4,5},{5,6},{6,7},{7,8},{8,9},{9,10},{10,1... | collective-permute-start | bytes 786440 | tf_op jit(solution)/shard_map/while/body/eval_jaxpr/ppermute | solution.py:21
  379.4 19.0 %collective-permute-start.4 = (f32[128,4,128]{2,1,0:T(4,128)S(1)}, f32[128,4,128]{2,1,0:T(4,128)S(1)}, u32[]{:S(2)}, u32[]{:S(2)}) collective-permute-start(f32[128,4,128]{2,1,0:T(4,128)S(1)} %get-tuple-element.385), channel_id=1, source_target_pairs={{0,1},{1,2},{2,3},{3,4},{4,5},{5,6},{6,7},{7,8},{8,9},{9,10},{10,1... | collective-permute-start | bytes 786440 | tf_op jit(solution)/shard_map/while/body/eval_jaxpr/ppermute | solution.py:21
  384.1 14.4 %collective-permute-start.5 = (f32[128,4,128]{2,1,0:T(4,128)}, f32[128,4,128]{2,1,0:T(4,128)S(1)}, u32[]{:S(2)}, u32[]{:S(2)}) collective-permute-start(f32[128,4,128]{2,1,0:T(4,128)} %get-tuple-element.384), channel_id=1, source_target_pairs={{1,0},{2,1},{3,2},{4,3},{5,4},{6,5},{7,6},{8,7},{9,8},{10,9},{11,1... | collective-permute-start | bytes 786440 | tf_op jit(solution)/shard_map/while/body/eval_jaxpr/ppermute | solution.py:22
  391.1 17.9 %collective-permute-start.2 = (f32[128,4,128]{2,1,0:T(4,128)S(1)}, f32[128,4,128]{2,1,0:T(4,128)S(1)}, u32[]{:S(2)}, u32[]{:S(2)}) collective-permute-start(f32[128,4,128]{2,1,0:T(4,128)S(1)} %get-tuple-element.350), channel_id=1, source_target_pairs={{0,1},{1,2},{2,3},{3,4},{4,5},{5,6},{6,7},{7,8},{8,9},{9,10},{10,1... | collective-permute-start | bytes 786440 | tf_op jit(solution)/shard_map/while/body/eval_jaxpr/ppermute | solution.py:21
  428.5 19.0 %collective-permute-start.4 = (f32[128,4,128]{2,1,0:T(4,128)S(1)}, f32[128,4,128]{2,1,0:T(4,128)S(1)}, u32[]{:S(2)}, u32[]{:S(2)}) collective-permute-start(f32[128,4,128]{2,1,0:T(4,128)S(1)} %get-tuple-element.385), channel_id=1, source_target_pairs={{0,1},{1,2},{2,3},{3,4},{4,5},{5,6},{6,7},{7,8},{8,9},{9,10},{10,1... | collective-permute-start | bytes 786440 | tf_op jit(solution)/shard_map/while/body/eval_jaxpr/ppermute | solution.py:21
  433.2 14.4 %collective-permute-start.5 = (f32[128,4,128]{2,1,0:T(4,128)}, f32[128,4,128]{2,1,0:T(4,128)S(1)}, u32[]{:S(2)}, u32[]{:S(2)}) collective-permute-start(f32[128,4,128]{2,1,0:T(4,128)} %get-tuple-element.384), channel_id=1, source_target_pairs={{1,0},{2,1},{3,2},{4,3},{5,4},{6,5},{7,6},{8,7},{9,8},{10,9},{11,1... | collective-permute-start | bytes 786440 | tf_op jit(solution)/shard_map/while/body/eval_jaxpr/ppermute | solution.py:22
  440.2 17.9 %collective-permute-start.2 = (f32[128,4,128]{2,1,0:T(4,128)S(1)}, f32[128,4,128]{2,1,0:T(4,128)S(1)}, u32[]{:S(2)}, u32[]{:S(2)}) collective-permute-start(f32[128,4,128]{2,1,0:T(4,128)S(1)} %get-tuple-element.350), channel_id=1, source_target_pairs={{0,1},{1,2},{2,3},{3,4},{4,5},{5,6},{6,7},{7,8},{8,9},{9,10},{10,1... | collective-permute-start | bytes 786440 | tf_op jit(solution)/shard_map/while/body/eval_jaxpr/ppermute | solution.py:21
  477.7 19.0 %collective-permute-start.4 = (f32[128,4,128]{2,1,0:T(4,128)S(1)}, f32[128,4,128]{2,1,0:T(4,128)S(1)}, u32[]{:S(2)}, u32[]{:S(2)}) collective-permute-start(f32[128,4,128]{2,1,0:T(4,128)S(1)} %get-tuple-element.385), channel_id=1, source_target_pairs={{0,1},{1,2},{2,3},{3,4},{4,5},{5,6},{6,7},{7,8},{8,9},{9,10},{10,1... | collective-permute-start | bytes 786440 | tf_op jit(solution)/shard_map/while/body/eval_jaxpr/ppermute | solution.py:21
  482.3 14.4 %collective-permute-start.5 = (f32[128,4,128]{2,1,0:T(4,128)}, f32[128,4,128]{2,1,0:T(4,128)S(1)}, u32[]{:S(2)}, u32[]{:S(2)}) collective-permute-start(f32[128,4,128]{2,1,0:T(4,128)} %get-tuple-element.384), channel_id=1, source_target_pairs={{1,0},{2,1},{3,2},{4,3},{5,4},{6,5},{7,6},{8,7},{9,8},{10,9},{11,1... | collective-permute-start | bytes 786440 | tf_op jit(solution)/shard_map/while/body/eval_jaxpr/ppermute | solution.py:22
  489.3 17.9 %collective-permute-start.2 = (f32[128,4,128]{2,1,0:T(4,128)S(1)}, f32[128,4,128]{2,1,0:T(4,128)S(1)}, u32[]{:S(2)}, u32[]{:S(2)}) collective-permute-start(f32[128,4,128]{2,1,0:T(4,128)S(1)} %get-tuple-element.350), channel_id=1, source_target_pairs={{0,1},{1,2},{2,3},{3,4},{4,5},{5,6},{6,7},{7,8},{8,9},{9,10},{10,1... | collective-permute-start | bytes 786440 | tf_op jit(solution)/shard_map/while/body/eval_jaxpr/ppermute | solution.py:21
  521.7 27.2 %all-to-all-start.1 = ((f32[128,1,8,128]{3,2,1,0:T(8,128)}), f32[128,1,8,128]{3,2,1,0:T(8,128)S(1)}, u32[]{:S(2)}, u32[]{:S(2)}) async-start(f32[128,1,8,128]{3,2,1,0:T(8,128)} %multiply_bitcast_fusion), calls=%async_computation.1 | async-start | bytes 1048576 | tf_op jit(solution)/shard_map/all_to_all | solution.py:192
  (201 other events, 1805.3 us)

commit v11 on v10

--- a/solution.py
+++ b/solution.py
@@ -11,7 +11,7 @@
 stencil_weights = (8.0 / 5.0, -1.0 / 5.0, 8.0 / 315.0, -1.0 / 560.0)
 center_weight = 3.0 * (-205.0 / 72.0)
 HALO = 4
-ROWS = 4
+ROWS = 16
 XOFF = 8
 
 

time: 554 us -> 487 us (0.88)
  Pallas kernels: 219 us -> 151 us
    pallas_call x40, Pallas kernels: 219 us -> 151 us  [wave_call(): pl.pallas_call(functools.partial(wave_kernel, with_image), out_shape=tupl...]
  transfers between devices with their start and end apart: 82 -> 82, of which waited for: 1 -> 1; matrix products, arithmetic and copies ran while one was open for 5% -> 6% of each run, Pallas kernels for 30% -> 23%
where the time goes in v11:
time: 487 us; the launch traced here: 483 us
  starting transfers between devices  272 us (56%)
  Pallas kernels  151 us (31%)
  local copies, waits for them, and re-layouts  23.2 us (5%)
  matrix products  11.7 us (2%)
  waiting for transfers between devices  11.6 us (2%)
  other arithmetic  10.1 us (2%)
    ppermute x40, starting transfers between devices, trade_halos(): low = lax.ppermute(tail, axis, [(i, (i + 1) % count) for i in range(ends)])  200 us
    pallas_call x40, Pallas kernels, wave_call(): pl.pallas_call(functools.partial(wave_kernel, with_image), out_shape=tupl...  151 us
    ppermute x40, starting transfers between devices, trade_halos(): high = lax.ppermute(head, axis, [((i + 1) % count, i) for i in range(ends)])  51.7 us
    all_to_all x1, starting transfers between devices, shards(): lax.all_to_all(outgoing, 'dom', split_axis=0, concat_axis=1, tiled=True)  12.2 us
    all_to_all x1, waiting for transfers between devices, shards(): lax.all_to_all(outgoing, 'dom', split_axis=0, concat_axis=1, tiled=True)  11.3 us
    dot_general x2, matrix products, spread_points(): jnp.einsum('ny,nsc->syc', rows_y, weighted, precision=lax.Precision.HIGHEST)  11 us
    while x280, local copies, waits for them, and re-layouts  10.3 us
  transfers between devices with their start and end apart: 82, of which 1 were waited for; matrix products, arithmetic and copies ran while one was open for 6% of the time, Pallas kernels for 23%

profile of v11, /device:TPU:0, one launch (start us, length us, event | category | flops | bytes accessed | tf_op | source)
XLA Modules:
  0.0 483.3 jit_solution(6713642032220769556)
XLA Ops:
  3.6 7.4 %all-to-all-start = ((f32[8,16,8,128]{3,2,0,1:T(8,128)}), f32[8,16,8,128]{3,2,0,1:T(8,128)S(1)}, u32[]{:S(2)}, u32[]{:S(2)}) async-start(f32[8,16,8,128]{3,2,0,1:T(8,128)} %select_bitcast_fusion), calls=%async_computation | async-start | bytes 1048576 | tf_op jit(solution)/shard_map/all_to_all | solution.py:144
  12.2 10.5 %fusion = f32[20,32,128]{2,1,0:T(8,128)S(1)} fusion(f32[8192,20]{0,1:T(8,128)S(1)} %bitcast.85, f32[8192,32]{0,1:T(8,128)S(1)} %fusion.8, s32[8192]{0:T(1024)S(1)} %bitcast.83), kind=kOutput, calls=%fused_computation.1 | convolution fusion | flops 8059355136 | bytes 2064384 | tf_op jit(solution)/shard_map/ny,nsc->syc/dot_general | solution.py:131
  36.2 416.7 %while.29 = (s32[]{:T(128)}, f32[128,8,128]{2,1,0:T(8,128)}, f32[128,8,128]{2,1,0:T(8,128)S(1)}, f32[128,4,128]{2,1,0:T(4,128)}, f32[128,4,128]{2,1,0:T(4,128)},...) while((s32[]{:T(128)}, f32[128,8,128]{2,1,0:T(8,128)}, ...), condition=%wide.region_1.2_spmd, body=%wide.region_0.1_spmd.sunk | while | flops 31457284 | bytes 67109736 | solution.py:181
  49.3 4.6 collective-permute-start.2
  72.9 5.6 %collective-permute-start = (f32[128,4,128]{2,1,0:T(4,128)}, f32[128,4,128]{2,1,0:T(4,128)S(1)}, u32[]{:S(2)}, u32[]{:S(2)}) collective-permute-start(f32[128,4,128]{2,1,0:T(4,128)} %get-tuple-element.381), channel_id=1, source_target_pairs={{0,1},{1,2},{2,3},{3,4},{4,5},{5,6},{6,7},{7,8},{8,9},{9,10},{10,1... | collective-permute-start | bytes 786440 | tf_op jit(solution)/shard_map/while/body/eval_jaxpr/ppermute | solution.py:21
  88.2 7.5 %collective-permute-start.2 = (f32[128,4,128]{2,1,0:T(4,128)S(1)}, f32[128,4,128]{2,1,0:T(4,128)S(1)}, u32[]{:S(2)}, u32[]{:S(2)}) collective-permute-start(f32[128,4,128]{2,1,0:T(4,128)S(1)} %get-tuple-element.350), channel_id=1, source_target_pairs={{0,1},{1,2},{2,3},{3,4},{4,5},{5,6},{6,7},{7,8},{8,9},{9,10},{10,1... | collective-permute-start | bytes 786440 | tf_op jit(solution)/shard_map/while/body/eval_jaxpr/ppermute | solution.py:21
  114.6 6.1 %collective-permute-start = (f32[128,4,128]{2,1,0:T(4,128)}, f32[128,4,128]{2,1,0:T(4,128)S(1)}, u32[]{:S(2)}, u32[]{:S(2)}) collective-permute-start(f32[128,4,128]{2,1,0:T(4,128)} %get-tuple-element.381), channel_id=1, source_target_pairs={{0,1},{1,2},{2,3},{3,4},{4,5},{5,6},{6,7},{7,8},{8,9},{9,10},{10,1... | collective-permute-start | bytes 786440 | tf_op jit(solution)/shard_map/while/body/eval_jaxpr/ppermute | solution.py:21
  130.4 7.6 %collective-permute-start.2 = (f32[128,4,128]{2,1,0:T(4,128)S(1)}, f32[128,4,128]{2,1,0:T(4,128)S(1)}, u32[]{:S(2)}, u32[]{:S(2)}) collective-permute-start(f32[128,4,128]{2,1,0:T(4,128)S(1)} %get-tuple-element.350), channel_id=1, source_target_pairs={{0,1},{1,2},{2,3},{3,4},{4,5},{5,6},{6,7},{7,8},{8,9},{9,10},{10,1... | collective-permute-start | bytes 786440 | tf_op jit(solution)/shard_map/while/body/eval_jaxpr/ppermute | solution.py:21
  147.8 4.3 eval_jaxpr.21
  156.9 6.1 %collective-permute-start = (f32[128,4,128]{2,1,0:T(4,128)}, f32[128,4,128]{2,1,0:T(4,128)S(1)}, u32[]{:S(2)}, u32[]{:S(2)}) collective-permute-start(f32[128,4,128]{2,1,0:T(4,128)} %get-tuple-element.381), channel_id=1, source_target_pairs={{0,1},{1,2},{2,3},{3,4},{4,5},{5,6},{6,7},{7,8},{8,9},{9,10},{10,1... | collective-permute-start | bytes 786440 | tf_op jit(solution)/shard_map/while/body/eval_jaxpr/ppermute | solution.py:21
  172.7 7.6 %collective-permute-start.2 = (f32[128,4,128]{2,1,0:T(4,128)S(1)}, f32[128,4,128]{2,1,0:T(4,128)S(1)}, u32[]{:S(2)}, u32[]{:S(2)}) collective-permute-start(f32[128,4,128]{2,1,0:T(4,128)S(1)} %get-tuple-element.350), channel_id=1, source_target_pairs={{0,1},{1,2},{2,3},{3,4},{4,5},{5,6},{6,7},{7,8},{8,9},{9,10},{10,1... | collective-permute-start | bytes 786440 | tf_op jit(solution)/shard_map/while/body/eval_jaxpr/ppermute | solution.py:21
  190.1 4.3 eval_jaxpr.21
  199.2 6.1 %collective-permute-start = (f32[128,4,128]{2,1,0:T(4,128)}, f32[128,4,128]{2,1,0:T(4,128)S(1)}, u32[]{:S(2)}, u32[]{:S(2)}) collective-permute-start(f32[128,4,128]{2,1,0:T(4,128)} %get-tuple-element.381), channel_id=1, source_target_pairs={{0,1},{1,2},{2,3},{3,4},{4,5},{5,6},{6,7},{7,8},{8,9},{9,10},{10,1... | collective-permute-start | bytes 786440 | tf_op jit(solution)/shard_map/while/body/eval_jaxpr/ppermute | solution.py:21
  215.0 7.6 %collective-permute-start.2 = (f32[128,4,128]{2,1,0:T(4,128)S(1)}, f32[128,4,128]{2,1,0:T(4,128)S(1)}, u32[]{:S(2)}, u32[]{:S(2)}) collective-permute-start(f32[128,4,128]{2,1,0:T(4,128)S(1)} %get-tuple-element.350), channel_id=1, source_target_pairs={{0,1},{1,2},{2,3},{3,4},{4,5},{5,6},{6,7},{7,8},{8,9},{9,10},{10,1... | collective-permute-start | bytes 786440 | tf_op jit(solution)/shard_map/while/body/eval_jaxpr/ppermute | solution.py:21
  232.4 4.3 eval_jaxpr.21
  241.5 6.1 %collective-permute-start = (f32[128,4,128]{2,1,0:T(4,128)}, f32[128,4,128]{2,1,0:T(4,128)S(1)}, u32[]{:S(2)}, u32[]{:S(2)}) collective-permute-start(f32[128,4,128]{2,1,0:T(4,128)} %get-tuple-element.381), channel_id=1, source_target_pairs={{0,1},{1,2},{2,3},{3,4},{4,5},{5,6},{6,7},{7,8},{8,9},{9,10},{10,1... | collective-permute-start | bytes 786440 | tf_op jit(solution)/shard_map/while/body/eval_jaxpr/ppermute | solution.py:21
  257.2 7.6 %collective-permute-start.2 = (f32[128,4,128]{2,1,0:T(4,128)S(1)}, f32[128,4,128]{2,1,0:T(4,128)S(1)}, u32[]{:S(2)}, u32[]{:S(2)}) collective-permute-start(f32[128,4,128]{2,1,0:T(4,128)S(1)} %get-tuple-element.350), channel_id=1, source_target_pairs={{0,1},{1,2},{2,3},{3,4},{4,5},{5,6},{6,7},{7,8},{8,9},{9,10},{10,1... | collective-permute-start | bytes 786440 | tf_op jit(solution)/shard_map/while/body/eval_jaxpr/ppermute | solution.py:21
  274.6 4.3 eval_jaxpr.21
  283.8 6.1 %collective-permute-start = (f32[128,4,128]{2,1,0:T(4,128)}, f32[128,4,128]{2,1,0:T(4,128)S(1)}, u32[]{:S(2)}, u32[]{:S(2)}) collective-permute-start(f32[128,4,128]{2,1,0:T(4,128)} %get-tuple-element.381), channel_id=1, source_target_pairs={{0,1},{1,2},{2,3},{3,4},{4,5},{5,6},{6,7},{7,8},{8,9},{9,10},{10,1... | collective-permute-start | bytes 786440 | tf_op jit(solution)/shard_map/while/body/eval_jaxpr/ppermute | solution.py:21
  299.5 7.6 %collective-permute-start.2 = (f32[128,4,128]{2,1,0:T(4,128)S(1)}, f32[128,4,128]{2,1,0:T(4,128)S(1)}, u32[]{:S(2)}, u32[]{:S(2)}) collective-permute-start(f32[128,4,128]{2,1,0:T(4,128)S(1)} %get-tuple-element.350), channel_id=1, source_target_pairs={{0,1},{1,2},{2,3},{3,4},{4,5},{5,6},{6,7},{7,8},{8,9},{9,10},{10,1... | collective-permute-start | bytes 786440 | tf_op jit(solution)/shard_map/while/body/eval_jaxpr/ppermute | solution.py:21
  316.9 4.3 eval_jaxpr.21
  326.1 6.1 %collective-permute-start = (f32[128,4,128]{2,1,0:T(4,128)}, f32[128,4,128]{2,1,0:T(4,128)S(1)}, u32[]{:S(2)}, u32[]{:S(2)}) collective-permute-start(f32[128,4,128]{2,1,0:T(4,128)} %get-tuple-element.381), channel_id=1, source_target_pairs={{0,1},{1,2},{2,3},{3,4},{4,5},{5,6},{6,7},{7,8},{8,9},{9,10},{10,1... | collective-permute-start | bytes 786440 | tf_op jit(solution)/shard_map/while/body/eval_jaxpr/ppermute | solution.py:21
  341.8 7.6 %collective-permute-start.2 = (f32[128,4,128]{2,1,0:T(4,128)S(1)}, f32[128,4,128]{2,1,0:T(4,128)S(1)}, u32[]{:S(2)}, u32[]{:S(2)}) collective-permute-start(f32[128,4,128]{2,1,0:T(4,128)S(1)} %get-tuple-element.350), channel_id=1, source_target_pairs={{0,1},{1,2},{2,3},{3,4},{4,5},{5,6},{6,7},{7,8},{8,9},{9,10},{10,1... | collective-permute-start | bytes 786440 | tf_op jit(solution)/shard_map/while/body/eval_jaxpr/ppermute | solution.py:21
  359.2 4.3 eval_jaxpr.21
  368.4 6.1 %collective-permute-start = (f32[128,4,128]{2,1,0:T(4,128)}, f32[128,4,128]{2,1,0:T(4,128)S(1)}, u32[]{:S(2)}, u32[]{:S(2)}) collective-permute-start(f32[128,4,128]{2,1,0:T(4,128)} %get-tuple-element.381), channel_id=1, source_target_pairs={{0,1},{1,2},{2,3},{3,4},{4,5},{5,6},{6,7},{7,8},{8,9},{9,10},{10,1... | collective-permute-start | bytes 786440 | tf_op jit(solution)/shard_map/while/body/eval_jaxpr/ppermute | solution.py:21
  384.1 7.6 %collective-permute-start.2 = (f32[128,4,128]{2,1,0:T(4,128)S(1)}, f32[128,4,128]{2,1,0:T(4,128)S(1)}, u32[]{:S(2)}, u32[]{:S(2)}) collective-permute-start(f32[128,4,128]{2,1,0:T(4,128)S(1)} %get-tuple-element.350), channel_id=1, source_target_pairs={{0,1},{1,2},{2,3},{3,4},{4,5},{5,6},{6,7},{7,8},{8,9},{9,10},{10,1... | collective-permute-start | bytes 786440 | tf_op jit(solution)/shard_map/while/body/eval_jaxpr/ppermute | solution.py:21
  401.5 4.3 eval_jaxpr.21
  410.6 6.1 %collective-permute-start = (f32[128,4,128]{2,1,0:T(4,128)}, f32[128,4,128]{2,1,0:T(4,128)S(1)}, u32[]{:S(2)}, u32[]{:S(2)}) collective-permute-start(f32[128,4,128]{2,1,0:T(4,128)} %get-tuple-element.381), channel_id=1, source_target_pairs={{0,1},{1,2},{2,3},{3,4},{4,5},{5,6},{6,7},{7,8},{8,9},{9,10},{10,1... | collective-permute-start | bytes 786440 | tf_op jit(solution)/shard_map/while/body/eval_jaxpr/ppermute | solution.py:21
  426.4 7.6 %collective-permute-start.2 = (f32[128,4,128]{2,1,0:T(4,128)S(1)}, f32[128,4,128]{2,1,0:T(4,128)S(1)}, u32[]{:S(2)}, u32[]{:S(2)}) collective-permute-start(f32[128,4,128]{2,1,0:T(4,128)S(1)} %get-tuple-element.350), channel_id=1, source_target_pairs={{0,1},{1,2},{2,3},{3,4},{4,5},{5,6},{6,7},{7,8},{8,9},{9,10},{10,1... | collective-permute-start | bytes 786440 | tf_op jit(solution)/shard_map/while/body/eval_jaxpr/ppermute | solution.py:21
  443.8 4.3 eval_jaxpr.21
  454.9 12.2 %all-to-all-start.1 = ((f32[128,1,8,128]{3,2,1,0:T(8,128)}), f32[128,1,8,128]{3,2,1,0:T(8,128)S(1)}, u32[]{:S(2)}, u32[]{:S(2)}) async-start(f32[128,1,8,128]{3,2,1,0:T(8,128)} %multiply_bitcast_fusion), calls=%async_computation.1 | async-start | bytes 1048576 | tf_op jit(solution)/shard_map/all_to_all | solution.py:192
  470.3 11.3 %all-to-all-done.1 = f32[128,1,8,128]{3,2,1,0:T(8,128)S(1)} async-done(((f32[128,1,8,128]{3,2,1,0:T(8,128)}), f32[128,1,8,128]{3,2,1,0:T(8,128)S(1)}, u32[]{:S(2)}, u32[]{:S(2)}) %all-to-all-start.1) | async-done | bytes 524320 | tf_op jit(solution)/shard_map/all_to_all | solution.py:192
  (510 shorter events, 276.1 us)
Async XLA Ops:
  3.6 31.7 %all-to-all-start = ((f32[8,16,8,128]{3,2,0,1:T(8,128)}), f32[8,16,8,128]{3,2,0,1:T(8,128)S(1)}, u32[]{:S(2)}, u32[]{:S(2)}) async-start(f32[8,16,8,128]{3,2,0,1:T(8,128)} %select_bitcast_fusion), calls=%async_computation | async-start | bytes 1048576 | tf_op jit(solution)/shard_map/all_to_all | solution.py:144
  39.8 15.4 %collective-permute-start.4 = (f32[128,4,128]{2,1,0:T(4,128)S(1)}, f32[128,4,128]{2,1,0:T(4,128)S(1)}, u32[]{:S(2)}, u32[]{:S(2)}) collective-permute-start(f32[128,4,128]{2,1,0:T(4,128)S(1)} %get-tuple-element.385), channel_id=1, source_target_pairs={{0,1},{1,2},{2,3},{3,4},{4,5},{5,6},{6,7},{7,8},{8,9},{9,10},{10,1... | collective-permute-start | bytes 786440 | tf_op jit(solution)/shard_map/while/body/eval_jaxpr/ppermute | solution.py:21
  49.3 14.4 %collective-permute-start.2 = (f32[128,4,128]{2,1,0:T(4,128)S(1)}, f32[128,4,128]{2,1,0:T(4,128)S(1)}, u32[]{:S(2)}, u32[]{:S(2)}) collective-permute-start(f32[128,4,128]{2,1,0:T(4,128)S(1)} %get-tuple-element.350), channel_id=1, source_target_pairs={{0,1},{1,2},{2,3},{3,4},{4,5},{5,6},{6,7},{7,8},{8,9},{9,10},{10,1... | collective-permute-start | bytes 786440 | tf_op jit(solution)/shard_map/while/body/eval_jaxpr/ppermute | solution.py:21
  79.8 17.2 %collective-permute-start.4 = (f32[128,4,128]{2,1,0:T(4,128)S(1)}, f32[128,4,128]{2,1,0:T(4,128)S(1)}, u32[]{:S(2)}, u32[]{:S(2)}) collective-permute-start(f32[128,4,128]{2,1,0:T(4,128)S(1)} %get-tuple-element.385), channel_id=1, source_target_pairs={{0,1},{1,2},{2,3},{3,4},{4,5},{5,6},{6,7},{7,8},{8,9},{9,10},{10,1... | collective-permute-start | bytes 786440 | tf_op jit(solution)/shard_map/while/body/eval_jaxpr/ppermute | solution.py:21
  82.9 14.2 %collective-permute-start.5 = (f32[128,4,128]{2,1,0:T(4,128)}, f32[128,4,128]{2,1,0:T(4,128)S(1)}, u32[]{:S(2)}, u32[]{:S(2)}) collective-permute-start(f32[128,4,128]{2,1,0:T(4,128)} %get-tuple-element.384), channel_id=1, source_target_pairs={{1,0},{2,1},{3,2},{4,3},{5,4},{6,5},{7,6},{8,7},{9,8},{10,9},{11,1... | collective-permute-start | bytes 786440 | tf_op jit(solution)/shard_map/while/body/eval_jaxpr/ppermute | solution.py:22
  88.2 17.3 %collective-permute-start.2 = (f32[128,4,128]{2,1,0:T(4,128)S(1)}, f32[128,4,128]{2,1,0:T(4,128)S(1)}, u32[]{:S(2)}, u32[]{:S(2)}) collective-permute-start(f32[128,4,128]{2,1,0:T(4,128)S(1)} %get-tuple-element.350), channel_id=1, source_target_pairs={{0,1},{1,2},{2,3},{3,4},{4,5},{5,6},{6,7},{7,8},{8,9},{9,10},{10,1... | collective-permute-start | bytes 786440 | tf_op jit(solution)/shard_map/while/body/eval_jaxpr/ppermute | solution.py:21
  114.6 11.8 %collective-permute-start = (f32[128,4,128]{2,1,0:T(4,128)}, f32[128,4,128]{2,1,0:T(4,128)S(1)}, u32[]{:S(2)}, u32[]{:S(2)}) collective-permute-start(f32[128,4,128]{2,1,0:T(4,128)} %get-tuple-element.381), channel_id=1, source_target_pairs={{0,1},{1,2},{2,3},{3,4},{4,5},{5,6},{6,7},{7,8},{8,9},{9,10},{10,1... | collective-permute-start | bytes 786440 | tf_op jit(solution)/shard_map/while/body/eval_jaxpr/ppermute | solution.py:21
  122.0 17.3 %collective-permute-start.4 = (f32[128,4,128]{2,1,0:T(4,128)S(1)}, f32[128,4,128]{2,1,0:T(4,128)S(1)}, u32[]{:S(2)}, u32[]{:S(2)}) collective-permute-start(f32[128,4,128]{2,1,0:T(4,128)S(1)} %get-tuple-element.385), channel_id=1, source_target_pairs={{0,1},{1,2},{2,3},{3,4},{4,5},{5,6},{6,7},{7,8},{8,9},{9,10},{10,1... | collective-permute-start | bytes 786440 | tf_op jit(solution)/shard_map/while/body/eval_jaxpr/ppermute | solution.py:21
  125.0 14.3 %collective-permute-start.5 = (f32[128,4,128]{2,1,0:T(4,128)}, f32[128,4,128]{2,1,0:T(4,128)S(1)}, u32[]{:S(2)}, u32[]{:S(2)}) collective-permute-start(f32[128,4,128]{2,1,0:T(4,128)} %get-tuple-element.384), channel_id=1, source_target_pairs={{1,0},{2,1},{3,2},{4,3},{5,4},{6,5},{7,6},{8,7},{9,8},{10,9},{11,1... | collective-permute-start | bytes 786440 | tf_op jit(solution)/shard_map/while/body/eval_jaxpr/ppermute | solution.py:22
  130.4 17.4 %collective-permute-start.2 = (f32[128,4,128]{2,1,0:T(4,128)S(1)}, f32[128,4,128]{2,1,0:T(4,128)S(1)}, u32[]{:S(2)}, u32[]{:S(2)}) collective-permute-start(f32[128,4,128]{2,1,0:T(4,128)S(1)} %get-tuple-element.350), channel_id=1, source_target_pairs={{0,1},{1,2},{2,3},{3,4},{4,5},{5,6},{6,7},{7,8},{8,9},{9,10},{10,1... | collective-permute-start | bytes 786440 | tf_op jit(solution)/shard_map/while/body/eval_jaxpr/ppermute | solution.py:21
  164.3 17.3 %collective-permute-start.4 = (f32[128,4,128]{2,1,0:T(4,128)S(1)}, f32[128,4,128]{2,1,0:T(4,128)S(1)}, u32[]{:S(2)}, u32[]{:S(2)}) collective-permute-start(f32[128,4,128]{2,1,0:T(4,128)S(1)} %get-tuple-element.385), channel_id=1, source_target_pairs={{0,1},{1,2},{2,3},{3,4},{4,5},{5,6},{6,7},{7,8},{8,9},{9,10},{10,1... | collective-permute-start | bytes 786440 | tf_op jit(solution)/shard_map/while/body/eval_jaxpr/ppermute | solution.py:21
  167.3 14.3 %collective-permute-start.5 = (f32[128,4,128]{2,1,0:T(4,128)}, f32[128,4,128]{2,1,0:T(4,128)S(1)}, u32[]{:S(2)}, u32[]{:S(2)}) collective-permute-start(f32[128,4,128]{2,1,0:T(4,128)} %get-tuple-element.384), channel_id=1, source_target_pairs={{1,0},{2,1},{3,2},{4,3},{5,4},{6,5},{7,6},{8,7},{9,8},{10,9},{11,1... | collective-permute-start | bytes 786440 | tf_op jit(solution)/shard_map/while/body/eval_jaxpr/ppermute | solution.py:22
  172.7 17.4 %collective-permute-start.2 = (f32[128,4,128]{2,1,0:T(4,128)S(1)}, f32[128,4,128]{2,1,0:T(4,128)S(1)}, u32[]{:S(2)}, u32[]{:S(2)}) collective-permute-start(f32[128,4,128]{2,1,0:T(4,128)S(1)} %get-tuple-element.350), channel_id=1, source_target_pairs={{0,1},{1,2},{2,3},{3,4},{4,5},{5,6},{6,7},{7,8},{8,9},{9,10},{10,1... | collective-permute-start | bytes 786440 | tf_op jit(solution)/shard_map/while/body/eval_jaxpr/ppermute | solution.py:21
  206.6 17.3 %collective-permute-start.4 = (f32[128,4,128]{2,1,0:T(4,128)S(1)}, f32[128,4,128]{2,1,0:T(4,128)S(1)}, u32[]{:S(2)}, u32[]{:S(2)}) collective-permute-start(f32[128,4,128]{2,1,0:T(4,128)S(1)} %get-tuple-element.385), channel_id=1, source_target_pairs={{0,1},{1,2},{2,3},{3,4},{4,5},{5,6},{6,7},{7,8},{8,9},{9,10},{10,1... | collective-permute-start | bytes 786440 | tf_op jit(solution)/shard_map/while/body/eval_jaxpr/ppermute | solution.py:21
  209.6 14.3 %collective-permute-start.5 = (f32[128,4,128]{2,1,0:T(4,128)}, f32[128,4,128]{2,1,0:T(4,128)S(1)}, u32[]{:S(2)}, u32[]{:S(2)}) collective-permute-start(f32[128,4,128]{2,1,0:T(4,128)} %get-tuple-element.384), channel_id=1, source_target_pairs={{1,0},{2,1},{3,2},{4,3},{5,4},{6,5},{7,6},{8,7},{9,8},{10,9},{11,1... | collective-permute-start | bytes 786440 | tf_op jit(solution)/shard_map/while/body/eval_jaxpr/ppermute | solution.py:22
  215.0 17.4 %collective-permute-start.2 = (f32[128,4,128]{2,1,0:T(4,128)S(1)}, f32[128,4,128]{2,1,0:T(4,128)S(1)}, u32[]{:S(2)}, u32[]{:S(2)}) collective-permute-start(f32[128,4,128]{2,1,0:T(4,128)S(1)} %get-tuple-element.350), channel_id=1, source_target_pairs={{0,1},{1,2},{2,3},{3,4},{4,5},{5,6},{6,7},{7,8},{8,9},{9,10},{10,1... | collective-permute-start | bytes 786440 | tf_op jit(solution)/shard_map/while/body/eval_jaxpr/ppermute | solution.py:21
  248.9 17.3 %collective-permute-start.4 = (f32[128,4,128]{2,1,0:T(4,128)S(1)}, f32[128,4,128]{2,1,0:T(4,128)S(1)}, u32[]{:S(2)}, u32[]{:S(2)}) collective-permute-start(f32[128,4,128]{2,1,0:T(4,128)S(1)} %get-tuple-element.385), channel_id=1, source_target_pairs={{0,1},{1,2},{2,3},{3,4},{4,5},{5,6},{6,7},{7,8},{8,9},{9,10},{10,1... | collective-permute-start | bytes 786440 | tf_op jit(solution)/shard_map/while/body/eval_jaxpr/ppermute | solution.py:21
  251.9 14.3 %collective-permute-start.5 = (f32[128,4,128]{2,1,0:T(4,128)}, f32[128,4,128]{2,1,0:T(4,128)S(1)}, u32[]{:S(2)}, u32[]{:S(2)}) collective-permute-start(f32[128,4,128]{2,1,0:T(4,128)} %get-tuple-element.384), channel_id=1, source_target_pairs={{1,0},{2,1},{3,2},{4,3},{5,4},{6,5},{7,6},{8,7},{9,8},{10,9},{11,1... | collective-permute-start | bytes 786440 | tf_op jit(solution)/shard_map/while/body/eval_jaxpr/ppermute | solution.py:22
  257.2 17.4 %collective-permute-start.2 = (f32[128,4,128]{2,1,0:T(4,128)S(1)}, f32[128,4,128]{2,1,0:T(4,128)S(1)}, u32[]{:S(2)}, u32[]{:S(2)}) collective-permute-start(f32[128,4,128]{2,1,0:T(4,128)S(1)} %get-tuple-element.350), channel_id=1, source_target_pairs={{0,1},{1,2},{2,3},{3,4},{4,5},{5,6},{6,7},{7,8},{8,9},{9,10},{10,1... | collective-permute-start | bytes 786440 | tf_op jit(solution)/shard_map/while/body/eval_jaxpr/ppermute | solution.py:21
  291.1 17.3 %collective-permute-start.4 = (f32[128,4,128]{2,1,0:T(4,128)S(1)}, f32[128,4,128]{2,1,0:T(4,128)S(1)}, u32[]{:S(2)}, u32[]{:S(2)}) collective-permute-start(f32[128,4,128]{2,1,0:T(4,128)S(1)} %get-tuple-element.385), channel_id=1, source_target_pairs={{0,1},{1,2},{2,3},{3,4},{4,5},{5,6},{6,7},{7,8},{8,9},{9,10},{10,1... | collective-permute-start | bytes 786440 | tf_op jit(solution)/shard_map/while/body/eval_jaxpr/ppermute | solution.py:21
  294.2 14.3 %collective-permute-start.5 = (f32[128,4,128]{2,1,0:T(4,128)}, f32[128,4,128]{2,1,0:T(4,128)S(1)}, u32[]{:S(2)}, u32[]{:S(2)}) collective-permute-start(f32[128,4,128]{2,1,0:T(4,128)} %get-tuple-element.384), channel_id=1, source_target_pairs={{1,0},{2,1},{3,2},{4,3},{5,4},{6,5},{7,6},{8,7},{9,8},{10,9},{11,1... | collective-permute-start | bytes 786440 | tf_op jit(solution)/shard_map/while/body/eval_jaxpr/ppermute | solution.py:22
  299.5 17.4 %collective-permute-start.2 = (f32[128,4,128]{2,1,0:T(4,128)S(1)}, f32[128,4,128]{2,1,0:T(4,128)S(1)}, u32[]{:S(2)}, u32[]{:S(2)}) collective-permute-start(f32[128,4,128]{2,1,0:T(4,128)S(1)} %get-tuple-element.350), channel_id=1, source_target_pairs={{0,1},{1,2},{2,3},{3,4},{4,5},{5,6},{6,7},{7,8},{8,9},{9,10},{10,1... | collective-permute-start | bytes 786440 | tf_op jit(solution)/shard_map/while/body/eval_jaxpr/ppermute | solution.py:21
  333.4 17.3 %collective-permute-start.4 = (f32[128,4,128]{2,1,0:T(4,128)S(1)}, f32[128,4,128]{2,1,0:T(4,128)S(1)}, u32[]{:S(2)}, u32[]{:S(2)}) collective-permute-start(f32[128,4,128]{2,1,0:T(4,128)S(1)} %get-tuple-element.385), channel_id=1, source_target_pairs={{0,1},{1,2},{2,3},{3,4},{4,5},{5,6},{6,7},{7,8},{8,9},{9,10},{10,1... | collective-permute-start | bytes 786440 | tf_op jit(solution)/shard_map/while/body/eval_jaxpr/ppermute | solution.py:21
  336.5 14.3 %collective-permute-start.5 = (f32[128,4,128]{2,1,0:T(4,128)}, f32[128,4,128]{2,1,0:T(4,128)S(1)}, u32[]{:S(2)}, u32[]{:S(2)}) collective-permute-start(f32[128,4,128]{2,1,0:T(4,128)} %get-tuple-element.384), channel_id=1, source_target_pairs={{1,0},{2,1},{3,2},{4,3},{5,4},{6,5},{7,6},{8,7},{9,8},{10,9},{11,1... | collective-permute-start | bytes 786440 | tf_op jit(solution)/shard_map/while/body/eval_jaxpr/ppermute | solution.py:22
  341.8 17.4 %collective-permute-start.2 = (f32[128,4,128]{2,1,0:T(4,128)S(1)}, f32[128,4,128]{2,1,0:T(4,128)S(1)}, u32[]{:S(2)}, u32[]{:S(2)}) collective-permute-start(f32[128,4,128]{2,1,0:T(4,128)S(1)} %get-tuple-element.350), channel_id=1, source_target_pairs={{0,1},{1,2},{2,3},{3,4},{4,5},{5,6},{6,7},{7,8},{8,9},{9,10},{10,1... | collective-permute-start | bytes 786440 | tf_op jit(solution)/shard_map/while/body/eval_jaxpr/ppermute | solution.py:21
  375.7 17.3 %collective-permute-start.4 = (f32[128,4,128]{2,1,0:T(4,128)S(1)}, f32[128,4,128]{2,1,0:T(4,128)S(1)}, u32[]{:S(2)}, u32[]{:S(2)}) collective-permute-start(f32[128,4,128]{2,1,0:T(4,128)S(1)} %get-tuple-element.385), channel_id=1, source_target_pairs={{0,1},{1,2},{2,3},{3,4},{4,5},{5,6},{6,7},{7,8},{8,9},{9,10},{10,1... | collective-permute-start | bytes 786440 | tf_op jit(solution)/shard_map/while/body/eval_jaxpr/ppermute | solution.py:21
  378.8 14.3 %collective-permute-start.5 = (f32[128,4,128]{2,1,0:T(4,128)}, f32[128,4,128]{2,1,0:T(4,128)S(1)}, u32[]{:S(2)}, u32[]{:S(2)}) collective-permute-start(f32[128,4,128]{2,1,0:T(4,128)} %get-tuple-element.384), channel_id=1, source_target_pairs={{1,0},{2,1},{3,2},{4,3},{5,4},{6,5},{7,6},{8,7},{9,8},{10,9},{11,1... | collective-permute-start | bytes 786440 | tf_op jit(solution)/shard_map/while/body/eval_jaxpr/ppermute | solution.py:22
  384.1 17.4 %collective-permute-start.2 = (f32[128,4,128]{2,1,0:T(4,128)S(1)}, f32[128,4,128]{2,1,0:T(4,128)S(1)}, u32[]{:S(2)}, u32[]{:S(2)}) collective-permute-start(f32[128,4,128]{2,1,0:T(4,128)S(1)} %get-tuple-element.350), channel_id=1, source_target_pairs={{0,1},{1,2},{2,3},{3,4},{4,5},{5,6},{6,7},{7,8},{8,9},{9,10},{10,1... | collective-permute-start | bytes 786440 | tf_op jit(solution)/shard_map/while/body/eval_jaxpr/ppermute | solution.py:21
  418.0 17.3 %collective-permute-start.4 = (f32[128,4,128]{2,1,0:T(4,128)S(1)}, f32[128,4,128]{2,1,0:T(4,128)S(1)}, u32[]{:S(2)}, u32[]{:S(2)}) collective-permute-start(f32[128,4,128]{2,1,0:T(4,128)S(1)} %get-tuple-element.385), channel_id=1, source_target_pairs={{0,1},{1,2},{2,3},{3,4},{4,5},{5,6},{6,7},{7,8},{8,9},{9,10},{10,1... | collective-permute-start | bytes 786440 | tf_op jit(solution)/shard_map/while/body/eval_jaxpr/ppermute | solution.py:21
  421.1 14.3 %collective-permute-start.5 = (f32[128,4,128]{2,1,0:T(4,128)}, f32[128,4,128]{2,1,0:T(4,128)S(1)}, u32[]{:S(2)}, u32[]{:S(2)}) collective-permute-start(f32[128,4,128]{2,1,0:T(4,128)} %get-tuple-element.384), channel_id=1, source_target_pairs={{1,0},{2,1},{3,2},{4,3},{5,4},{6,5},{7,6},{8,7},{9,8},{10,9},{11,1... | collective-permute-start | bytes 786440 | tf_op jit(solution)/shard_map/while/body/eval_jaxpr/ppermute | solution.py:22
  426.4 17.4 %collective-permute-start.2 = (f32[128,4,128]{2,1,0:T(4,128)S(1)}, f32[128,4,128]{2,1,0:T(4,128)S(1)}, u32[]{:S(2)}, u32[]{:S(2)}) collective-permute-start(f32[128,4,128]{2,1,0:T(4,128)S(1)} %get-tuple-element.350), channel_id=1, source_target_pairs={{0,1},{1,2},{2,3},{3,4},{4,5},{5,6},{6,7},{7,8},{8,9},{9,10},{10,1... | collective-permute-start | bytes 786440 | tf_op jit(solution)/shard_map/while/body/eval_jaxpr/ppermute | solution.py:21
  454.9 26.7 %all-to-all-start.1 = ((f32[128,1,8,128]{3,2,1,0:T(8,128)}), f32[128,1,8,128]{3,2,1,0:T(8,128)S(1)}, u32[]{:S(2)}, u32[]{:S(2)}) async-start(f32[128,1,8,128]{3,2,1,0:T(8,128)} %multiply_bitcast_fusion), calls=%async_computation.1 | async-start | bytes 1048576 | tf_op jit(solution)/shard_map/all_to_all | solution.py:192
  (201 other events, 1607.6 us)

commit v12 on v11

--- a/solution.py
+++ b/solution.py
@@ -11,7 +11,7 @@
 stencil_weights = (8.0 / 5.0, -1.0 / 5.0, 8.0 / 315.0, -1.0 / 560.0)
 center_weight = 3.0 * (-205.0 / 72.0)
 HALO = 4
-ROWS = 16
+ROWS = 32
 XOFF = 8
 
 

time: 487 us -> 481 us (0.988)
  Pallas kernels: 151 us -> 146 us
    pallas_call x40, Pallas kernels: 151 us -> 146 us  [wave_call(): pl.pallas_call(functools.partial(wave_kernel, with_image), out_shape=tupl...]
where the time goes in v12:
time: 481 us; the launch traced here: 478 us
  starting transfers between devices  272 us (57%)
  Pallas kernels  146 us (30%)
  local copies, waits for them, and re-layouts  23.2 us (5%)
  matrix products  11.7 us (2%)
  waiting for transfers between devices  11.6 us (2%)
  other arithmetic  10.1 us (2%)
    ppermute x40, starting transfers between devices, trade_halos(): low = lax.ppermute(tail, axis, [(i, (i + 1) % count) for i in range(ends)])  201 us
    pallas_call x40, Pallas kernels, wave_call(): pl.pallas_call(functools.partial(wave_kernel, with_image), out_shape=tupl...  146 us
    ppermute x40, starting transfers between devices, trade_halos(): high = lax.ppermute(head, axis, [((i + 1) % count, i) for i in range(ends)])  51.7 us
    all_to_all x1, starting transfers between devices, shards(): lax.all_to_all(outgoing, 'dom', split_axis=0, concat_axis=1, tiled=True)  12.2 us
    all_to_all x1, waiting for transfers between devices, shards(): lax.all_to_all(outgoing, 'dom', split_axis=0, concat_axis=1, tiled=True)  11.3 us
    dot_general x2, matrix products, spread_points(): jnp.einsum('ny,nsc->syc', rows_y, weighted, precision=lax.Precision.HIGHEST)  11 us
    while x280, local copies, waits for them, and re-layouts  10.3 us
  transfers between devices with their start and end apart: 82, of which 1 were waited for; matrix products, arithmetic and copies ran while one was open for 6% of the time, Pallas kernels for 23%

profile of v12, /device:TPU:0, one launch (start us, length us, event | category | flops | bytes accessed | tf_op | source)
XLA Modules:
  0.0 477.9 jit_solution(2700447519629610859)
XLA Ops:
  3.6 7.4 %all-to-all-start = ((f32[8,16,8,128]{3,2,0,1:T(8,128)}), f32[8,16,8,128]{3,2,0,1:T(8,128)S(1)}, u32[]{:S(2)}, u32[]{:S(2)}) async-start(f32[8,16,8,128]{3,2,0,1:T(8,128)} %select_bitcast_fusion), calls=%async_computation | async-start | bytes 1048576 | tf_op jit(solution)/shard_map/all_to_all | solution.py:144
  12.2 10.5 %fusion = f32[20,32,128]{2,1,0:T(8,128)S(1)} fusion(f32[8192,20]{0,1:T(8,128)S(1)} %bitcast.85, f32[8192,32]{0,1:T(8,128)S(1)} %fusion.8, s32[8192]{0:T(1024)S(1)} %bitcast.83), kind=kOutput, calls=%fused_computation.1 | convolution fusion | flops 8059355136 | bytes 2064384 | tf_op jit(solution)/shard_map/ny,nsc->syc/dot_general | solution.py:131
  36.2 411.4 %while.29 = (s32[]{:T(128)}, f32[128,8,128]{2,1,0:T(8,128)}, f32[128,8,128]{2,1,0:T(8,128)S(1)}, f32[128,4,128]{2,1,0:T(4,128)}, f32[128,4,128]{2,1,0:T(4,128)},...) while((s32[]{:T(128)}, f32[128,8,128]{2,1,0:T(8,128)}, ...), condition=%wide.region_1.2_spmd, body=%wide.region_0.1_spmd.sunk | while | flops 31457284 | bytes 67109736 | solution.py:181
  39.8 4.2 collective-permute-start.4
  49.2 4.6 collective-permute-start.2
  63.4 4.2 eval_jaxpr.21
  72.3 5.8 %collective-permute-start = (f32[128,4,128]{2,1,0:T(4,128)}, f32[128,4,128]{2,1,0:T(4,128)S(1)}, u32[]{:S(2)}, u32[]{:S(2)}) collective-permute-start(f32[128,4,128]{2,1,0:T(4,128)} %get-tuple-element.381), channel_id=1, source_target_pairs={{0,1},{1,2},{2,3},{3,4},{4,5},{5,6},{6,7},{7,8},{8,9},{9,10},{10,1... | collective-permute-start | bytes 786440 | tf_op jit(solution)/shard_map/while/body/eval_jaxpr/ppermute | solution.py:21
  87.6 7.5 %collective-permute-start.2 = (f32[128,4,128]{2,1,0:T(4,128)S(1)}, f32[128,4,128]{2,1,0:T(4,128)S(1)}, u32[]{:S(2)}, u32[]{:S(2)}) collective-permute-start(f32[128,4,128]{2,1,0:T(4,128)S(1)} %get-tuple-element.350), channel_id=1, source_target_pairs={{0,1},{1,2},{2,3},{3,4},{4,5},{5,6},{6,7},{7,8},{8,9},{9,10},{10,1... | collective-permute-start | bytes 786440 | tf_op jit(solution)/shard_map/while/body/eval_jaxpr/ppermute | solution.py:21
  104.8 4.2 eval_jaxpr.21
  113.7 6.1 %collective-permute-start = (f32[128,4,128]{2,1,0:T(4,128)}, f32[128,4,128]{2,1,0:T(4,128)S(1)}, u32[]{:S(2)}, u32[]{:S(2)}) collective-permute-start(f32[128,4,128]{2,1,0:T(4,128)} %get-tuple-element.381), channel_id=1, source_target_pairs={{0,1},{1,2},{2,3},{3,4},{4,5},{5,6},{6,7},{7,8},{8,9},{9,10},{10,1... | collective-permute-start | bytes 786440 | tf_op jit(solution)/shard_map/while/body/eval_jaxpr/ppermute | solution.py:21
  129.3 7.6 %collective-permute-start.2 = (f32[128,4,128]{2,1,0:T(4,128)S(1)}, f32[128,4,128]{2,1,0:T(4,128)S(1)}, u32[]{:S(2)}, u32[]{:S(2)}) collective-permute-start(f32[128,4,128]{2,1,0:T(4,128)S(1)} %get-tuple-element.350), channel_id=1, source_target_pairs={{0,1},{1,2},{2,3},{3,4},{4,5},{5,6},{6,7},{7,8},{8,9},{9,10},{10,1... | collective-permute-start | bytes 786440 | tf_op jit(solution)/shard_map/while/body/eval_jaxpr/ppermute | solution.py:21
  155.4 6.1 %collective-permute-start = (f32[128,4,128]{2,1,0:T(4,128)}, f32[128,4,128]{2,1,0:T(4,128)S(1)}, u32[]{:S(2)}, u32[]{:S(2)}) collective-permute-start(f32[128,4,128]{2,1,0:T(4,128)} %get-tuple-element.381), channel_id=1, source_target_pairs={{0,1},{1,2},{2,3},{3,4},{4,5},{5,6},{6,7},{7,8},{8,9},{9,10},{10,1... | collective-permute-start | bytes 786440 | tf_op jit(solution)/shard_map/while/body/eval_jaxpr/ppermute | solution.py:21
  171.0 7.6 %collective-permute-start.2 = (f32[128,4,128]{2,1,0:T(4,128)S(1)}, f32[128,4,128]{2,1,0:T(4,128)S(1)}, u32[]{:S(2)}, u32[]{:S(2)}) collective-permute-start(f32[128,4,128]{2,1,0:T(4,128)S(1)} %get-tuple-element.350), channel_id=1, source_target_pairs={{0,1},{1,2},{2,3},{3,4},{4,5},{5,6},{6,7},{7,8},{8,9},{9,10},{10,1... | collective-permute-start | bytes 786440 | tf_op jit(solution)/shard_map/while/body/eval_jaxpr/ppermute | solution.py:21
  188.3 4.2 eval_jaxpr.21
  197.2 6.1 %collective-permute-start = (f32[128,4,128]{2,1,0:T(4,128)}, f32[128,4,128]{2,1,0:T(4,128)S(1)}, u32[]{:S(2)}, u32[]{:S(2)}) collective-permute-start(f32[128,4,128]{2,1,0:T(4,128)} %get-tuple-element.381), channel_id=1, source_target_pairs={{0,1},{1,2},{2,3},{3,4},{4,5},{5,6},{6,7},{7,8},{8,9},{9,10},{10,1... | collective-permute-start | bytes 786440 | tf_op jit(solution)/shard_map/while/body/eval_jaxpr/ppermute | solution.py:21
  212.8 7.6 %collective-permute-start.2 = (f32[128,4,128]{2,1,0:T(4,128)S(1)}, f32[128,4,128]{2,1,0:T(4,128)S(1)}, u32[]{:S(2)}, u32[]{:S(2)}) collective-permute-start(f32[128,4,128]{2,1,0:T(4,128)S(1)} %get-tuple-element.350), channel_id=1, source_target_pairs={{0,1},{1,2},{2,3},{3,4},{4,5},{5,6},{6,7},{7,8},{8,9},{9,10},{10,1... | collective-permute-start | bytes 786440 | tf_op jit(solution)/shard_map/while/body/eval_jaxpr/ppermute | solution.py:21
  230.0 4.2 eval_jaxpr.21
  238.9 6.1 %collective-permute-start = (f32[128,4,128]{2,1,0:T(4,128)}, f32[128,4,128]{2,1,0:T(4,128)S(1)}, u32[]{:S(2)}, u32[]{:S(2)}) collective-permute-start(f32[128,4,128]{2,1,0:T(4,128)} %get-tuple-element.381), channel_id=1, source_target_pairs={{0,1},{1,2},{2,3},{3,4},{4,5},{5,6},{6,7},{7,8},{8,9},{9,10},{10,1... | collective-permute-start | bytes 786440 | tf_op jit(solution)/shard_map/while/body/eval_jaxpr/ppermute | solution.py:21
  254.5 7.6 %collective-permute-start.2 = (f32[128,4,128]{2,1,0:T(4,128)S(1)}, f32[128,4,128]{2,1,0:T(4,128)S(1)}, u32[]{:S(2)}, u32[]{:S(2)}) collective-permute-start(f32[128,4,128]{2,1,0:T(4,128)S(1)} %get-tuple-element.350), channel_id=1, source_target_pairs={{0,1},{1,2},{2,3},{3,4},{4,5},{5,6},{6,7},{7,8},{8,9},{9,10},{10,1... | collective-permute-start | bytes 786440 | tf_op jit(solution)/shard_map/while/body/eval_jaxpr/ppermute | solution.py:21
  280.6 6.1 %collective-permute-start = (f32[128,4,128]{2,1,0:T(4,128)}, f32[128,4,128]{2,1,0:T(4,128)S(1)}, u32[]{:S(2)}, u32[]{:S(2)}) collective-permute-start(f32[128,4,128]{2,1,0:T(4,128)} %get-tuple-element.381), channel_id=1, source_target_pairs={{0,1},{1,2},{2,3},{3,4},{4,5},{5,6},{6,7},{7,8},{8,9},{9,10},{10,1... | collective-permute-start | bytes 786440 | tf_op jit(solution)/shard_map/while/body/eval_jaxpr/ppermute | solution.py:21
  296.2 7.6 %collective-permute-start.2 = (f32[128,4,128]{2,1,0:T(4,128)S(1)}, f32[128,4,128]{2,1,0:T(4,128)S(1)}, u32[]{:S(2)}, u32[]{:S(2)}) collective-permute-start(f32[128,4,128]{2,1,0:T(4,128)S(1)} %get-tuple-element.350), channel_id=1, source_target_pairs={{0,1},{1,2},{2,3},{3,4},{4,5},{5,6},{6,7},{7,8},{8,9},{9,10},{10,1... | collective-permute-start | bytes 786440 | tf_op jit(solution)/shard_map/while/body/eval_jaxpr/ppermute | solution.py:21
  313.5 4.2 eval_jaxpr.21
  322.4 6.1 %collective-permute-start = (f32[128,4,128]{2,1,0:T(4,128)}, f32[128,4,128]{2,1,0:T(4,128)S(1)}, u32[]{:S(2)}, u32[]{:S(2)}) collective-permute-start(f32[128,4,128]{2,1,0:T(4,128)} %get-tuple-element.381), channel_id=1, source_target_pairs={{0,1},{1,2},{2,3},{3,4},{4,5},{5,6},{6,7},{7,8},{8,9},{9,10},{10,1... | collective-permute-start | bytes 786440 | tf_op jit(solution)/shard_map/while/body/eval_jaxpr/ppermute | solution.py:21
  338.0 7.6 %collective-permute-start.2 = (f32[128,4,128]{2,1,0:T(4,128)S(1)}, f32[128,4,128]{2,1,0:T(4,128)S(1)}, u32[]{:S(2)}, u32[]{:S(2)}) collective-permute-start(f32[128,4,128]{2,1,0:T(4,128)S(1)} %get-tuple-element.350), channel_id=1, source_target_pairs={{0,1},{1,2},{2,3},{3,4},{4,5},{5,6},{6,7},{7,8},{8,9},{9,10},{10,1... | collective-permute-start | bytes 786440 | tf_op jit(solution)/shard_map/while/body/eval_jaxpr/ppermute | solution.py:21
  364.1 6.1 %collective-permute-start = (f32[128,4,128]{2,1,0:T(4,128)}, f32[128,4,128]{2,1,0:T(4,128)S(1)}, u32[]{:S(2)}, u32[]{:S(2)}) collective-permute-start(f32[128,4,128]{2,1,0:T(4,128)} %get-tuple-element.381), channel_id=1, source_target_pairs={{0,1},{1,2},{2,3},{3,4},{4,5},{5,6},{6,7},{7,8},{8,9},{9,10},{10,1... | collective-permute-start | bytes 786440 | tf_op jit(solution)/shard_map/while/body/eval_jaxpr/ppermute | solution.py:21
  379.7 7.6 %collective-permute-start.2 = (f32[128,4,128]{2,1,0:T(4,128)S(1)}, f32[128,4,128]{2,1,0:T(4,128)S(1)}, u32[]{:S(2)}, u32[]{:S(2)}) collective-permute-start(f32[128,4,128]{2,1,0:T(4,128)S(1)} %get-tuple-element.350), channel_id=1, source_target_pairs={{0,1},{1,2},{2,3},{3,4},{4,5},{5,6},{6,7},{7,8},{8,9},{9,10},{10,1... | collective-permute-start | bytes 786440 | tf_op jit(solution)/shard_map/while/body/eval_jaxpr/ppermute | solution.py:21
  397.0 4.2 eval_jaxpr.21
  405.9 6.1 %collective-permute-start = (f32[128,4,128]{2,1,0:T(4,128)}, f32[128,4,128]{2,1,0:T(4,128)S(1)}, u32[]{:S(2)}, u32[]{:S(2)}) collective-permute-start(f32[128,4,128]{2,1,0:T(4,128)} %get-tuple-element.381), channel_id=1, source_target_pairs={{0,1},{1,2},{2,3},{3,4},{4,5},{5,6},{6,7},{7,8},{8,9},{9,10},{10,1... | collective-permute-start | bytes 786440 | tf_op jit(solution)/shard_map/while/body/eval_jaxpr/ppermute | solution.py:21
  421.5 7.6 %collective-permute-start.2 = (f32[128,4,128]{2,1,0:T(4,128)S(1)}, f32[128,4,128]{2,1,0:T(4,128)S(1)}, u32[]{:S(2)}, u32[]{:S(2)}) collective-permute-start(f32[128,4,128]{2,1,0:T(4,128)S(1)} %get-tuple-element.350), channel_id=1, source_target_pairs={{0,1},{1,2},{2,3},{3,4},{4,5},{5,6},{6,7},{7,8},{8,9},{9,10},{10,1... | collective-permute-start | bytes 786440 | tf_op jit(solution)/shard_map/while/body/eval_jaxpr/ppermute | solution.py:21
  438.7 4.2 eval_jaxpr.21
  449.6 12.2 %all-to-all-start.1 = ((f32[128,1,8,128]{3,2,1,0:T(8,128)}), f32[128,1,8,128]{3,2,1,0:T(8,128)S(1)}, u32[]{:S(2)}, u32[]{:S(2)}) async-start(f32[128,1,8,128]{3,2,1,0:T(8,128)} %multiply_bitcast_fusion), calls=%async_computation.1 | async-start | bytes 1048576 | tf_op jit(solution)/shard_map/all_to_all | solution.py:192
  464.9 11.3 %all-to-all-done.1 = f32[128,1,8,128]{3,2,1,0:T(8,128)S(1)} async-done(((f32[128,1,8,128]{3,2,1,0:T(8,128)}), f32[128,1,8,128]{3,2,1,0:T(8,128)S(1)}, u32[]{:S(2)}, u32[]{:S(2)}) %all-to-all-start.1) | async-done | bytes 524320 | tf_op jit(solution)/shard_map/all_to_all | solution.py:192
  (510 shorter events, 271.9 us)
Async XLA Ops:
  3.6 31.7 %all-to-all-start = ((f32[8,16,8,128]{3,2,0,1:T(8,128)}), f32[8,16,8,128]{3,2,0,1:T(8,128)S(1)}, u32[]{:S(2)}, u32[]{:S(2)}) async-start(f32[8,16,8,128]{3,2,0,1:T(8,128)} %select_bitcast_fusion), calls=%async_computation | async-start | bytes 1048576 | tf_op jit(solution)/shard_map/all_to_all | solution.py:144
  39.8 15.3 %collective-permute-start.4 = (f32[128,4,128]{2,1,0:T(4,128)S(1)}, f32[128,4,128]{2,1,0:T(4,128)S(1)}, u32[]{:S(2)}, u32[]{:S(2)}) collective-permute-start(f32[128,4,128]{2,1,0:T(4,128)S(1)} %get-tuple-element.385), channel_id=1, source_target_pairs={{0,1},{1,2},{2,3},{3,4},{4,5},{5,6},{6,7},{7,8},{8,9},{9,10},{10,1... | collective-permute-start | bytes 786440 | tf_op jit(solution)/shard_map/while/body/eval_jaxpr/ppermute | solution.py:21
  49.2 14.2 %collective-permute-start.2 = (f32[128,4,128]{2,1,0:T(4,128)S(1)}, f32[128,4,128]{2,1,0:T(4,128)S(1)}, u32[]{:S(2)}, u32[]{:S(2)}) collective-permute-start(f32[128,4,128]{2,1,0:T(4,128)S(1)} %get-tuple-element.350), channel_id=1, source_target_pairs={{0,1},{1,2},{2,3},{3,4},{4,5},{5,6},{6,7},{7,8},{8,9},{9,10},{10,1... | collective-permute-start | bytes 786440 | tf_op jit(solution)/shard_map/while/body/eval_jaxpr/ppermute | solution.py:21
  79.4 17.1 %collective-permute-start.4 = (f32[128,4,128]{2,1,0:T(4,128)S(1)}, f32[128,4,128]{2,1,0:T(4,128)S(1)}, u32[]{:S(2)}, u32[]{:S(2)}) collective-permute-start(f32[128,4,128]{2,1,0:T(4,128)S(1)} %get-tuple-element.385), channel_id=1, source_target_pairs={{0,1},{1,2},{2,3},{3,4},{4,5},{5,6},{6,7},{7,8},{8,9},{9,10},{10,1... | collective-permute-start | bytes 786440 | tf_op jit(solution)/shard_map/while/body/eval_jaxpr/ppermute | solution.py:21
  82.5 14.0 %collective-permute-start.5 = (f32[128,4,128]{2,1,0:T(4,128)}, f32[128,4,128]{2,1,0:T(4,128)S(1)}, u32[]{:S(2)}, u32[]{:S(2)}) collective-permute-start(f32[128,4,128]{2,1,0:T(4,128)} %get-tuple-element.384), channel_id=1, source_target_pairs={{1,0},{2,1},{3,2},{4,3},{5,4},{6,5},{7,6},{8,7},{9,8},{10,9},{11,1... | collective-permute-start | bytes 786440 | tf_op jit(solution)/shard_map/while/body/eval_jaxpr/ppermute | solution.py:22
  87.6 17.2 %collective-permute-start.2 = (f32[128,4,128]{2,1,0:T(4,128)S(1)}, f32[128,4,128]{2,1,0:T(4,128)S(1)}, u32[]{:S(2)}, u32[]{:S(2)}) collective-permute-start(f32[128,4,128]{2,1,0:T(4,128)S(1)} %get-tuple-element.350), channel_id=1, source_target_pairs={{0,1},{1,2},{2,3},{3,4},{4,5},{5,6},{6,7},{7,8},{8,9},{9,10},{10,1... | collective-permute-start | bytes 786440 | tf_op jit(solution)/shard_map/while/body/eval_jaxpr/ppermute | solution.py:21
  121.1 17.2 %collective-permute-start.4 = (f32[128,4,128]{2,1,0:T(4,128)S(1)}, f32[128,4,128]{2,1,0:T(4,128)S(1)}, u32[]{:S(2)}, u32[]{:S(2)}) collective-permute-start(f32[128,4,128]{2,1,0:T(4,128)S(1)} %get-tuple-element.385), channel_id=1, source_target_pairs={{0,1},{1,2},{2,3},{3,4},{4,5},{5,6},{6,7},{7,8},{8,9},{9,10},{10,1... | collective-permute-start | bytes 786440 | tf_op jit(solution)/shard_map/while/body/eval_jaxpr/ppermute | solution.py:21
  124.1 14.1 %collective-permute-start.5 = (f32[128,4,128]{2,1,0:T(4,128)}, f32[128,4,128]{2,1,0:T(4,128)S(1)}, u32[]{:S(2)}, u32[]{:S(2)}) collective-permute-start(f32[128,4,128]{2,1,0:T(4,128)} %get-tuple-element.384), channel_id=1, source_target_pairs={{1,0},{2,1},{3,2},{4,3},{5,4},{6,5},{7,6},{8,7},{9,8},{10,9},{11,1... | collective-permute-start | bytes 786440 | tf_op jit(solution)/shard_map/while/body/eval_jaxpr/ppermute | solution.py:22
  129.3 17.3 %collective-permute-start.2 = (f32[128,4,128]{2,1,0:T(4,128)S(1)}, f32[128,4,128]{2,1,0:T(4,128)S(1)}, u32[]{:S(2)}, u32[]{:S(2)}) collective-permute-start(f32[128,4,128]{2,1,0:T(4,128)S(1)} %get-tuple-element.350), channel_id=1, source_target_pairs={{0,1},{1,2},{2,3},{3,4},{4,5},{5,6},{6,7},{7,8},{8,9},{9,10},{10,1... | collective-permute-start | bytes 786440 | tf_op jit(solution)/shard_map/while/body/eval_jaxpr/ppermute | solution.py:21
  162.8 17.2 %collective-permute-start.4 = (f32[128,4,128]{2,1,0:T(4,128)S(1)}, f32[128,4,128]{2,1,0:T(4,128)S(1)}, u32[]{:S(2)}, u32[]{:S(2)}) collective-permute-start(f32[128,4,128]{2,1,0:T(4,128)S(1)} %get-tuple-element.385), channel_id=1, source_target_pairs={{0,1},{1,2},{2,3},{3,4},{4,5},{5,6},{6,7},{7,8},{8,9},{9,10},{10,1... | collective-permute-start | bytes 786440 | tf_op jit(solution)/shard_map/while/body/eval_jaxpr/ppermute | solution.py:21
  165.8 14.1 %collective-permute-start.5 = (f32[128,4,128]{2,1,0:T(4,128)}, f32[128,4,128]{2,1,0:T(4,128)S(1)}, u32[]{:S(2)}, u32[]{:S(2)}) collective-permute-start(f32[128,4,128]{2,1,0:T(4,128)} %get-tuple-element.384), channel_id=1, source_target_pairs={{1,0},{2,1},{3,2},{4,3},{5,4},{6,5},{7,6},{8,7},{9,8},{10,9},{11,1... | collective-permute-start | bytes 786440 | tf_op jit(solution)/shard_map/while/body/eval_jaxpr/ppermute | solution.py:22
  171.0 17.3 %collective-permute-start.2 = (f32[128,4,128]{2,1,0:T(4,128)S(1)}, f32[128,4,128]{2,1,0:T(4,128)S(1)}, u32[]{:S(2)}, u32[]{:S(2)}) collective-permute-start(f32[128,4,128]{2,1,0:T(4,128)S(1)} %get-tuple-element.350), channel_id=1, source_target_pairs={{0,1},{1,2},{2,3},{3,4},{4,5},{5,6},{6,7},{7,8},{8,9},{9,10},{10,1... | collective-permute-start | bytes 786440 | tf_op jit(solution)/shard_map/while/body/eval_jaxpr/ppermute | solution.py:21
  197.2 11.8 %collective-permute-start = (f32[128,4,128]{2,1,0:T(4,128)}, f32[128,4,128]{2,1,0:T(4,128)S(1)}, u32[]{:S(2)}, u32[]{:S(2)}) collective-permute-start(f32[128,4,128]{2,1,0:T(4,128)} %get-tuple-element.381), channel_id=1, source_target_pairs={{0,1},{1,2},{2,3},{3,4},{4,5},{5,6},{6,7},{7,8},{8,9},{9,10},{10,1... | collective-permute-start | bytes 786440 | tf_op jit(solution)/shard_map/while/body/eval_jaxpr/ppermute | solution.py:21
  204.5 17.2 %collective-permute-start.4 = (f32[128,4,128]{2,1,0:T(4,128)S(1)}, f32[128,4,128]{2,1,0:T(4,128)S(1)}, u32[]{:S(2)}, u32[]{:S(2)}) collective-permute-start(f32[128,4,128]{2,1,0:T(4,128)S(1)} %get-tuple-element.385), channel_id=1, source_target_pairs={{0,1},{1,2},{2,3},{3,4},{4,5},{5,6},{6,7},{7,8},{8,9},{9,10},{10,1... | collective-permute-start | bytes 786440 | tf_op jit(solution)/shard_map/while/body/eval_jaxpr/ppermute | solution.py:21
  207.6 14.1 %collective-permute-start.5 = (f32[128,4,128]{2,1,0:T(4,128)}, f32[128,4,128]{2,1,0:T(4,128)S(1)}, u32[]{:S(2)}, u32[]{:S(2)}) collective-permute-start(f32[128,4,128]{2,1,0:T(4,128)} %get-tuple-element.384), channel_id=1, source_target_pairs={{1,0},{2,1},{3,2},{4,3},{5,4},{6,5},{7,6},{8,7},{9,8},{10,9},{11,1... | collective-permute-start | bytes 786440 | tf_op jit(solution)/shard_map/while/body/eval_jaxpr/ppermute | solution.py:22
  212.8 17.3 %collective-permute-start.2 = (f32[128,4,128]{2,1,0:T(4,128)S(1)}, f32[128,4,128]{2,1,0:T(4,128)S(1)}, u32[]{:S(2)}, u32[]{:S(2)}) collective-permute-start(f32[128,4,128]{2,1,0:T(4,128)S(1)} %get-tuple-element.350), channel_id=1, source_target_pairs={{0,1},{1,2},{2,3},{3,4},{4,5},{5,6},{6,7},{7,8},{8,9},{9,10},{10,1... | collective-permute-start | bytes 786440 | tf_op jit(solution)/shard_map/while/body/eval_jaxpr/ppermute | solution.py:21
  246.3 17.2 %collective-permute-start.4 = (f32[128,4,128]{2,1,0:T(4,128)S(1)}, f32[128,4,128]{2,1,0:T(4,128)S(1)}, u32[]{:S(2)}, u32[]{:S(2)}) collective-permute-start(f32[128,4,128]{2,1,0:T(4,128)S(1)} %get-tuple-element.385), channel_id=1, source_target_pairs={{0,1},{1,2},{2,3},{3,4},{4,5},{5,6},{6,7},{7,8},{8,9},{9,10},{10,1... | collective-permute-start | bytes 786440 | tf_op jit(solution)/shard_map/while/body/eval_jaxpr/ppermute | solution.py:21
  249.3 14.1 %collective-permute-start.5 = (f32[128,4,128]{2,1,0:T(4,128)}, f32[128,4,128]{2,1,0:T(4,128)S(1)}, u32[]{:S(2)}, u32[]{:S(2)}) collective-permute-start(f32[128,4,128]{2,1,0:T(4,128)} %get-tuple-element.384), channel_id=1, source_target_pairs={{1,0},{2,1},{3,2},{4,3},{5,4},{6,5},{7,6},{8,7},{9,8},{10,9},{11,1... | collective-permute-start | bytes 786440 | tf_op jit(solution)/shard_map/while/body/eval_jaxpr/ppermute | solution.py:22
  254.5 17.3 %collective-permute-start.2 = (f32[128,4,128]{2,1,0:T(4,128)S(1)}, f32[128,4,128]{2,1,0:T(4,128)S(1)}, u32[]{:S(2)}, u32[]{:S(2)}) collective-permute-start(f32[128,4,128]{2,1,0:T(4,128)S(1)} %get-tuple-element.350), channel_id=1, source_target_pairs={{0,1},{1,2},{2,3},{3,4},{4,5},{5,6},{6,7},{7,8},{8,9},{9,10},{10,1... | collective-permute-start | bytes 786440 | tf_op jit(solution)/shard_map/while/body/eval_jaxpr/ppermute | solution.py:21
  288.0 17.2 %collective-permute-start.4 = (f32[128,4,128]{2,1,0:T(4,128)S(1)}, f32[128,4,128]{2,1,0:T(4,128)S(1)}, u32[]{:S(2)}, u32[]{:S(2)}) collective-permute-start(f32[128,4,128]{2,1,0:T(4,128)S(1)} %get-tuple-element.385), channel_id=1, source_target_pairs={{0,1},{1,2},{2,3},{3,4},{4,5},{5,6},{6,7},{7,8},{8,9},{9,10},{10,1... | collective-permute-start | bytes 786440 | tf_op jit(solution)/shard_map/while/body/eval_jaxpr/ppermute | solution.py:21
  291.1 14.1 %collective-permute-start.5 = (f32[128,4,128]{2,1,0:T(4,128)}, f32[128,4,128]{2,1,0:T(4,128)S(1)}, u32[]{:S(2)}, u32[]{:S(2)}) collective-permute-start(f32[128,4,128]{2,1,0:T(4,128)} %get-tuple-element.384), channel_id=1, source_target_pairs={{1,0},{2,1},{3,2},{4,3},{5,4},{6,5},{7,6},{8,7},{9,8},{10,9},{11,1... | collective-permute-start | bytes 786440 | tf_op jit(solution)/shard_map/while/body/eval_jaxpr/ppermute | solution.py:22
  296.2 17.3 %collective-permute-start.2 = (f32[128,4,128]{2,1,0:T(4,128)S(1)}, f32[128,4,128]{2,1,0:T(4,128)S(1)}, u32[]{:S(2)}, u32[]{:S(2)}) collective-permute-start(f32[128,4,128]{2,1,0:T(4,128)S(1)} %get-tuple-element.350), channel_id=1, source_target_pairs={{0,1},{1,2},{2,3},{3,4},{4,5},{5,6},{6,7},{7,8},{8,9},{9,10},{10,1... | collective-permute-start | bytes 786440 | tf_op jit(solution)/shard_map/while/body/eval_jaxpr/ppermute | solution.py:21
  329.8 17.2 %collective-permute-start.4 = (f32[128,4,128]{2,1,0:T(4,128)S(1)}, f32[128,4,128]{2,1,0:T(4,128)S(1)}, u32[]{:S(2)}, u32[]{:S(2)}) collective-permute-start(f32[128,4,128]{2,1,0:T(4,128)S(1)} %get-tuple-element.385), channel_id=1, source_target_pairs={{0,1},{1,2},{2,3},{3,4},{4,5},{5,6},{6,7},{7,8},{8,9},{9,10},{10,1... | collective-permute-start | bytes 786440 | tf_op jit(solution)/shard_map/while/body/eval_jaxpr/ppermute | solution.py:21
  332.8 14.1 %collective-permute-start.5 = (f32[128,4,128]{2,1,0:T(4,128)}, f32[128,4,128]{2,1,0:T(4,128)S(1)}, u32[]{:S(2)}, u32[]{:S(2)}) collective-permute-start(f32[128,4,128]{2,1,0:T(4,128)} %get-tuple-element.384), channel_id=1, source_target_pairs={{1,0},{2,1},{3,2},{4,3},{5,4},{6,5},{7,6},{8,7},{9,8},{10,9},{11,1... | collective-permute-start | bytes 786440 | tf_op jit(solution)/shard_map/while/body/eval_jaxpr/ppermute | solution.py:22
  338.0 17.3 %collective-permute-start.2 = (f32[128,4,128]{2,1,0:T(4,128)S(1)}, f32[128,4,128]{2,1,0:T(4,128)S(1)}, u32[]{:S(2)}, u32[]{:S(2)}) collective-permute-start(f32[128,4,128]{2,1,0:T(4,128)S(1)} %get-tuple-element.350), channel_id=1, source_target_pairs={{0,1},{1,2},{2,3},{3,4},{4,5},{5,6},{6,7},{7,8},{8,9},{9,10},{10,1... | collective-permute-start | bytes 786440 | tf_op jit(solution)/shard_map/while/body/eval_jaxpr/ppermute | solution.py:21
  371.5 17.2 %collective-permute-start.4 = (f32[128,4,128]{2,1,0:T(4,128)S(1)}, f32[128,4,128]{2,1,0:T(4,128)S(1)}, u32[]{:S(2)}, u32[]{:S(2)}) collective-permute-start(f32[128,4,128]{2,1,0:T(4,128)S(1)} %get-tuple-element.385), channel_id=1, source_target_pairs={{0,1},{1,2},{2,3},{3,4},{4,5},{5,6},{6,7},{7,8},{8,9},{9,10},{10,1... | collective-permute-start | bytes 786440 | tf_op jit(solution)/shard_map/while/body/eval_jaxpr/ppermute | solution.py:21
  374.5 14.1 %collective-permute-start.5 = (f32[128,4,128]{2,1,0:T(4,128)}, f32[128,4,128]{2,1,0:T(4,128)S(1)}, u32[]{:S(2)}, u32[]{:S(2)}) collective-permute-start(f32[128,4,128]{2,1,0:T(4,128)} %get-tuple-element.384), channel_id=1, source_target_pairs={{1,0},{2,1},{3,2},{4,3},{5,4},{6,5},{7,6},{8,7},{9,8},{10,9},{11,1... | collective-permute-start | bytes 786440 | tf_op jit(solution)/shard_map/while/body/eval_jaxpr/ppermute | solution.py:22
  379.7 17.3 %collective-permute-start.2 = (f32[128,4,128]{2,1,0:T(4,128)S(1)}, f32[128,4,128]{2,1,0:T(4,128)S(1)}, u32[]{:S(2)}, u32[]{:S(2)}) collective-permute-start(f32[128,4,128]{2,1,0:T(4,128)S(1)} %get-tuple-element.350), channel_id=1, source_target_pairs={{0,1},{1,2},{2,3},{3,4},{4,5},{5,6},{6,7},{7,8},{8,9},{9,10},{10,1... | collective-permute-start | bytes 786440 | tf_op jit(solution)/shard_map/while/body/eval_jaxpr/ppermute | solution.py:21
  413.2 17.2 %collective-permute-start.4 = (f32[128,4,128]{2,1,0:T(4,128)S(1)}, f32[128,4,128]{2,1,0:T(4,128)S(1)}, u32[]{:S(2)}, u32[]{:S(2)}) collective-permute-start(f32[128,4,128]{2,1,0:T(4,128)S(1)} %get-tuple-element.385), channel_id=1, source_target_pairs={{0,1},{1,2},{2,3},{3,4},{4,5},{5,6},{6,7},{7,8},{8,9},{9,10},{10,1... | collective-permute-start | bytes 786440 | tf_op jit(solution)/shard_map/while/body/eval_jaxpr/ppermute | solution.py:21
  416.3 14.1 %collective-permute-start.5 = (f32[128,4,128]{2,1,0:T(4,128)}, f32[128,4,128]{2,1,0:T(4,128)S(1)}, u32[]{:S(2)}, u32[]{:S(2)}) collective-permute-start(f32[128,4,128]{2,1,0:T(4,128)} %get-tuple-element.384), channel_id=1, source_target_pairs={{1,0},{2,1},{3,2},{4,3},{5,4},{6,5},{7,6},{8,7},{9,8},{10,9},{11,1... | collective-permute-start | bytes 786440 | tf_op jit(solution)/shard_map/while/body/eval_jaxpr/ppermute | solution.py:22
  421.5 17.3 %collective-permute-start.2 = (f32[128,4,128]{2,1,0:T(4,128)S(1)}, f32[128,4,128]{2,1,0:T(4,128)S(1)}, u32[]{:S(2)}, u32[]{:S(2)}) collective-permute-start(f32[128,4,128]{2,1,0:T(4,128)S(1)} %get-tuple-element.350), channel_id=1, source_target_pairs={{0,1},{1,2},{2,3},{3,4},{4,5},{5,6},{6,7},{7,8},{8,9},{9,10},{10,1... | collective-permute-start | bytes 786440 | tf_op jit(solution)/shard_map/while/body/eval_jaxpr/ppermute | solution.py:21
  449.6 26.7 %all-to-all-start.1 = ((f32[128,1,8,128]{3,2,1,0:T(8,128)}), f32[128,1,8,128]{3,2,1,0:T(8,128)S(1)}, u32[]{:S(2)}, u32[]{:S(2)}) async-start(f32[128,1,8,128]{3,2,1,0:T(8,128)} %multiply_bitcast_fusion), calls=%async_computation.1 | async-start | bytes 1048576 | tf_op jit(solution)/shard_map/all_to_all | solution.py:192
  (201 other events, 1587.8 us)

commit v13 on v12

--- a/solution.py
+++ b/solution.py
@@ -11,7 +11,7 @@
 stencil_weights = (8.0 / 5.0, -1.0 / 5.0, 8.0 / 315.0, -1.0 / 560.0)
 center_weight = 3.0 * (-205.0 / 72.0)
 HALO = 4
-ROWS = 32
+ROWS = 64
 XOFF = 8
 
 

time: 481 us -> 477 us (level)
  Pallas kernels: 146 us -> 141 us
  transfers between devices with their start and end apart: 82 -> 82, of which waited for: 1 -> 1; matrix products, arithmetic and copies ran while one was open for 6% -> 6% of each run, Pallas kernels for 23% -> 22%
where the time goes in v13:
time: 477 us; the launch traced here: 473 us
  starting transfers between devices  272 us (57%)
  Pallas kernels  141 us (30%)
  local copies, waits for them, and re-layouts  23.2 us (5%)
  matrix products  11.7 us (2%)
  waiting for transfers between devices  11.6 us (2%)
  other arithmetic  10.1 us (2%)
    ppermute x40, starting transfers between devices, trade_halos(): low = lax.ppermute(tail, axis, [(i, (i + 1) % count) for i in range(ends)])  201 us
    pallas_call x40, Pallas kernels, wave_call(): pl.pallas_call(functools.partial(wave_kernel, with_image), out_shape=tupl...  141 us
    ppermute x40, starting transfers between devices, trade_halos(): high = lax.ppermute(head, axis, [((i + 1) % count, i) for i in range(ends)])  51.7 us
    all_to_all x1, starting transfers between devices, shards(): lax.all_to_all(outgoing, 'dom', split_axis=0, concat_axis=1, tiled=True)  12.2 us
    all_to_all x1, waiting for transfers between devices, shards(): lax.all_to_all(outgoing, 'dom', split_axis=0, concat_axis=1, tiled=True)  11.3 us
    dot_general x2, matrix products, spread_points(): jnp.einsum('ny,nsc->syc', rows_y, weighted, precision=lax.Precision.HIGHEST)  11 us
    while x280, local copies, waits for them, and re-layouts  10.3 us
  transfers between devices with their start and end apart: 82, of which 1 were waited for; matrix products, arithmetic and copies ran while one was open for 6% of the time, Pallas kernels for 22%

profile of v13, /device:TPU:0, one launch (start us, length us, event | category | flops | bytes accessed | tf_op | source)
XLA Modules:
  0.0 473.4 jit_solution(9528348189548965986)
XLA Ops:
  3.6 7.4 %all-to-all-start = ((f32[8,16,8,128]{3,2,0,1:T(8,128)}), f32[8,16,8,128]{3,2,0,1:T(8,128)S(1)}, u32[]{:S(2)}, u32[]{:S(2)}) async-start(f32[8,16,8,128]{3,2,0,1:T(8,128)} %select_bitcast_fusion), calls=%async_computation | async-start | bytes 1048576 | tf_op jit(solution)/shard_map/all_to_all | solution.py:144
  12.2 10.5 %fusion = f32[20,32,128]{2,1,0:T(8,128)S(1)} fusion(f32[8192,20]{0,1:T(8,128)S(1)} %bitcast.85, f32[8192,32]{0,1:T(8,128)S(1)} %fusion.8, s32[8192]{0:T(1024)S(1)} %bitcast.83), kind=kOutput, calls=%fused_computation.1 | convolution fusion | flops 8059355136 | bytes 2064384 | tf_op jit(solution)/shard_map/ny,nsc->syc/dot_general | solution.py:131
  36.2 406.8 %while.29 = (s32[]{:T(128)}, f32[128,8,128]{2,1,0:T(8,128)}, f32[128,8,128]{2,1,0:T(8,128)S(1)}, f32[128,4,128]{2,1,0:T(4,128)}, f32[128,4,128]{2,1,0:T(4,128)},...) while((s32[]{:T(128)}, f32[128,8,128]{2,1,0:T(8,128)}, ...), condition=%wide.region_1.2_spmd, body=%wide.region_0.1_spmd.sunk | while | flops 31457284 | bytes 67109736 | solution.py:181
  39.8 4.2 collective-permute-start.4
  49.1 4.6 collective-permute-start.2
  63.2 4.0 eval_jaxpr.21
  71.8 5.9 %collective-permute-start = (f32[128,4,128]{2,1,0:T(4,128)}, f32[128,4,128]{2,1,0:T(4,128)S(1)}, u32[]{:S(2)}, u32[]{:S(2)}) collective-permute-start(f32[128,4,128]{2,1,0:T(4,128)} %get-tuple-element.381), channel_id=1, source_target_pairs={{0,1},{1,2},{2,3},{3,4},{4,5},{5,6},{6,7},{7,8},{8,9},{9,10},{10,1... | collective-permute-start | bytes 786440 | tf_op jit(solution)/shard_map/while/body/eval_jaxpr/ppermute | solution.py:21
  87.2 7.5 %collective-permute-start.2 = (f32[128,4,128]{2,1,0:T(4,128)S(1)}, f32[128,4,128]{2,1,0:T(4,128)S(1)}, u32[]{:S(2)}, u32[]{:S(2)}) collective-permute-start(f32[128,4,128]{2,1,0:T(4,128)S(1)} %get-tuple-element.350), channel_id=1, source_target_pairs={{0,1},{1,2},{2,3},{3,4},{4,5},{5,6},{6,7},{7,8},{8,9},{9,10},{10,1... | collective-permute-start | bytes 786440 | tf_op jit(solution)/shard_map/while/body/eval_jaxpr/ppermute | solution.py:21
  104.2 4.0 eval_jaxpr.21
  112.9 6.1 %collective-permute-start = (f32[128,4,128]{2,1,0:T(4,128)}, f32[128,4,128]{2,1,0:T(4,128)S(1)}, u32[]{:S(2)}, u32[]{:S(2)}) collective-permute-start(f32[128,4,128]{2,1,0:T(4,128)} %get-tuple-element.381), channel_id=1, source_target_pairs={{0,1},{1,2},{2,3},{3,4},{4,5},{5,6},{6,7},{7,8},{8,9},{9,10},{10,1... | collective-permute-start | bytes 786440 | tf_op jit(solution)/shard_map/while/body/eval_jaxpr/ppermute | solution.py:21
  128.3 7.6 %collective-permute-start.2 = (f32[128,4,128]{2,1,0:T(4,128)S(1)}, f32[128,4,128]{2,1,0:T(4,128)S(1)}, u32[]{:S(2)}, u32[]{:S(2)}) collective-permute-start(f32[128,4,128]{2,1,0:T(4,128)S(1)} %get-tuple-element.350), channel_id=1, source_target_pairs={{0,1},{1,2},{2,3},{3,4},{4,5},{5,6},{6,7},{7,8},{8,9},{9,10},{10,1... | collective-permute-start | bytes 786440 | tf_op jit(solution)/shard_map/while/body/eval_jaxpr/ppermute | solution.py:21
  145.5 4.0 eval_jaxpr.21
  154.1 6.1 %collective-permute-start = (f32[128,4,128]{2,1,0:T(4,128)}, f32[128,4,128]{2,1,0:T(4,128)S(1)}, u32[]{:S(2)}, u32[]{:S(2)}) collective-permute-start(f32[128,4,128]{2,1,0:T(4,128)} %get-tuple-element.381), channel_id=1, source_target_pairs={{0,1},{1,2},{2,3},{3,4},{4,5},{5,6},{6,7},{7,8},{8,9},{9,10},{10,1... | collective-permute-start | bytes 786440 | tf_op jit(solution)/shard_map/while/body/eval_jaxpr/ppermute | solution.py:21
  169.6 7.6 %collective-permute-start.2 = (f32[128,4,128]{2,1,0:T(4,128)S(1)}, f32[128,4,128]{2,1,0:T(4,128)S(1)}, u32[]{:S(2)}, u32[]{:S(2)}) collective-permute-start(f32[128,4,128]{2,1,0:T(4,128)S(1)} %get-tuple-element.350), channel_id=1, source_target_pairs={{0,1},{1,2},{2,3},{3,4},{4,5},{5,6},{6,7},{7,8},{8,9},{9,10},{10,1... | collective-permute-start | bytes 786440 | tf_op jit(solution)/shard_map/while/body/eval_jaxpr/ppermute | solution.py:21
  186.8 4.0 eval_jaxpr.21
  195.4 6.1 %collective-permute-start = (f32[128,4,128]{2,1,0:T(4,128)}, f32[128,4,128]{2,1,0:T(4,128)S(1)}, u32[]{:S(2)}, u32[]{:S(2)}) collective-permute-start(f32[128,4,128]{2,1,0:T(4,128)} %get-tuple-element.381), channel_id=1, source_target_pairs={{0,1},{1,2},{2,3},{3,4},{4,5},{5,6},{6,7},{7,8},{8,9},{9,10},{10,1... | collective-permute-start | bytes 786440 | tf_op jit(solution)/shard_map/while/body/eval_jaxpr/ppermute | solution.py:21
  210.9 7.6 %collective-permute-start.2 = (f32[128,4,128]{2,1,0:T(4,128)S(1)}, f32[128,4,128]{2,1,0:T(4,128)S(1)}, u32[]{:S(2)}, u32[]{:S(2)}) collective-permute-start(f32[128,4,128]{2,1,0:T(4,128)S(1)} %get-tuple-element.350), channel_id=1, source_target_pairs={{0,1},{1,2},{2,3},{3,4},{4,5},{5,6},{6,7},{7,8},{8,9},{9,10},{10,1... | collective-permute-start | bytes 786440 | tf_op jit(solution)/shard_map/while/body/eval_jaxpr/ppermute | solution.py:21
  228.1 4.0 eval_jaxpr.21
  236.7 6.1 %collective-permute-start = (f32[128,4,128]{2,1,0:T(4,128)}, f32[128,4,128]{2,1,0:T(4,128)S(1)}, u32[]{:S(2)}, u32[]{:S(2)}) collective-permute-start(f32[128,4,128]{2,1,0:T(4,128)} %get-tuple-element.381), channel_id=1, source_target_pairs={{0,1},{1,2},{2,3},{3,4},{4,5},{5,6},{6,7},{7,8},{8,9},{9,10},{10,1... | collective-permute-start | bytes 786440 | tf_op jit(solution)/shard_map/while/body/eval_jaxpr/ppermute | solution.py:21
  252.2 7.6 %collective-permute-start.2 = (f32[128,4,128]{2,1,0:T(4,128)S(1)}, f32[128,4,128]{2,1,0:T(4,128)S(1)}, u32[]{:S(2)}, u32[]{:S(2)}) collective-permute-start(f32[128,4,128]{2,1,0:T(4,128)S(1)} %get-tuple-element.350), channel_id=1, source_target_pairs={{0,1},{1,2},{2,3},{3,4},{4,5},{5,6},{6,7},{7,8},{8,9},{9,10},{10,1... | collective-permute-start | bytes 786440 | tf_op jit(solution)/shard_map/while/body/eval_jaxpr/ppermute | solution.py:21
  278.0 6.1 %collective-permute-start = (f32[128,4,128]{2,1,0:T(4,128)}, f32[128,4,128]{2,1,0:T(4,128)S(1)}, u32[]{:S(2)}, u32[]{:S(2)}) collective-permute-start(f32[128,4,128]{2,1,0:T(4,128)} %get-tuple-element.381), channel_id=1, source_target_pairs={{0,1},{1,2},{2,3},{3,4},{4,5},{5,6},{6,7},{7,8},{8,9},{9,10},{10,1... | collective-permute-start | bytes 786440 | tf_op jit(solution)/shard_map/while/body/eval_jaxpr/ppermute | solution.py:21
  293.4 7.6 %collective-permute-start.2 = (f32[128,4,128]{2,1,0:T(4,128)S(1)}, f32[128,4,128]{2,1,0:T(4,128)S(1)}, u32[]{:S(2)}, u32[]{:S(2)}) collective-permute-start(f32[128,4,128]{2,1,0:T(4,128)S(1)} %get-tuple-element.350), channel_id=1, source_target_pairs={{0,1},{1,2},{2,3},{3,4},{4,5},{5,6},{6,7},{7,8},{8,9},{9,10},{10,1... | collective-permute-start | bytes 786440 | tf_op jit(solution)/shard_map/while/body/eval_jaxpr/ppermute | solution.py:21
  310.6 4.0 eval_jaxpr.21
  319.2 6.1 %collective-permute-start = (f32[128,4,128]{2,1,0:T(4,128)}, f32[128,4,128]{2,1,0:T(4,128)S(1)}, u32[]{:S(2)}, u32[]{:S(2)}) collective-permute-start(f32[128,4,128]{2,1,0:T(4,128)} %get-tuple-element.381), channel_id=1, source_target_pairs={{0,1},{1,2},{2,3},{3,4},{4,5},{5,6},{6,7},{7,8},{8,9},{9,10},{10,1... | collective-permute-start | bytes 786440 | tf_op jit(solution)/shard_map/while/body/eval_jaxpr/ppermute | solution.py:21
  334.7 7.6 %collective-permute-start.2 = (f32[128,4,128]{2,1,0:T(4,128)S(1)}, f32[128,4,128]{2,1,0:T(4,128)S(1)}, u32[]{:S(2)}, u32[]{:S(2)}) collective-permute-start(f32[128,4,128]{2,1,0:T(4,128)S(1)} %get-tuple-element.350), channel_id=1, source_target_pairs={{0,1},{1,2},{2,3},{3,4},{4,5},{5,6},{6,7},{7,8},{8,9},{9,10},{10,1... | collective-permute-start | bytes 786440 | tf_op jit(solution)/shard_map/while/body/eval_jaxpr/ppermute | solution.py:21
  360.5 6.1 %collective-permute-start = (f32[128,4,128]{2,1,0:T(4,128)}, f32[128,4,128]{2,1,0:T(4,128)S(1)}, u32[]{:S(2)}, u32[]{:S(2)}) collective-permute-start(f32[128,4,128]{2,1,0:T(4,128)} %get-tuple-element.381), channel_id=1, source_target_pairs={{0,1},{1,2},{2,3},{3,4},{4,5},{5,6},{6,7},{7,8},{8,9},{9,10},{10,1... | collective-permute-start | bytes 786440 | tf_op jit(solution)/shard_map/while/body/eval_jaxpr/ppermute | solution.py:21
  376.0 7.6 %collective-permute-start.2 = (f32[128,4,128]{2,1,0:T(4,128)S(1)}, f32[128,4,128]{2,1,0:T(4,128)S(1)}, u32[]{:S(2)}, u32[]{:S(2)}) collective-permute-start(f32[128,4,128]{2,1,0:T(4,128)S(1)} %get-tuple-element.350), channel_id=1, source_target_pairs={{0,1},{1,2},{2,3},{3,4},{4,5},{5,6},{6,7},{7,8},{8,9},{9,10},{10,1... | collective-permute-start | bytes 786440 | tf_op jit(solution)/shard_map/while/body/eval_jaxpr/ppermute | solution.py:21
  401.8 6.1 %collective-permute-start = (f32[128,4,128]{2,1,0:T(4,128)}, f32[128,4,128]{2,1,0:T(4,128)S(1)}, u32[]{:S(2)}, u32[]{:S(2)}) collective-permute-start(f32[128,4,128]{2,1,0:T(4,128)} %get-tuple-element.381), channel_id=1, source_target_pairs={{0,1},{1,2},{2,3},{3,4},{4,5},{5,6},{6,7},{7,8},{8,9},{9,10},{10,1... | collective-permute-start | bytes 786440 | tf_op jit(solution)/shard_map/while/body/eval_jaxpr/ppermute | solution.py:21
  417.2 7.6 %collective-permute-start.2 = (f32[128,4,128]{2,1,0:T(4,128)S(1)}, f32[128,4,128]{2,1,0:T(4,128)S(1)}, u32[]{:S(2)}, u32[]{:S(2)}) collective-permute-start(f32[128,4,128]{2,1,0:T(4,128)S(1)} %get-tuple-element.350), channel_id=1, source_target_pairs={{0,1},{1,2},{2,3},{3,4},{4,5},{5,6},{6,7},{7,8},{8,9},{9,10},{10,1... | collective-permute-start | bytes 786440 | tf_op jit(solution)/shard_map/while/body/eval_jaxpr/ppermute | solution.py:21
  434.4 4.0 eval_jaxpr.21
  445.0 12.2 %all-to-all-start.1 = ((f32[128,1,8,128]{3,2,1,0:T(8,128)}), f32[128,1,8,128]{3,2,1,0:T(8,128)S(1)}, u32[]{:S(2)}, u32[]{:S(2)}) async-start(f32[128,1,8,128]{3,2,1,0:T(8,128)} %multiply_bitcast_fusion), calls=%async_computation.1 | async-start | bytes 1048576 | tf_op jit(solution)/shard_map/all_to_all | solution.py:192
  460.4 11.3 %all-to-all-done.1 = f32[128,1,8,128]{3,2,1,0:T(8,128)S(1)} async-done(((f32[128,1,8,128]{3,2,1,0:T(8,128)}), f32[128,1,8,128]{3,2,1,0:T(8,128)S(1)}, u32[]{:S(2)}, u32[]{:S(2)}) %all-to-all-start.1) | async-done | bytes 524320 | tf_op jit(solution)/shard_map/all_to_all | solution.py:192
  (510 shorter events, 268.0 us)
Async XLA Ops:
  3.6 31.7 %all-to-all-start = ((f32[8,16,8,128]{3,2,0,1:T(8,128)}), f32[8,16,8,128]{3,2,0,1:T(8,128)S(1)}, u32[]{:S(2)}, u32[]{:S(2)}) async-start(f32[8,16,8,128]{3,2,0,1:T(8,128)} %select_bitcast_fusion), calls=%async_computation | async-start | bytes 1048576 | tf_op jit(solution)/shard_map/all_to_all | solution.py:144
  39.8 15.2 %collective-permute-start.4 = (f32[128,4,128]{2,1,0:T(4,128)S(1)}, f32[128,4,128]{2,1,0:T(4,128)S(1)}, u32[]{:S(2)}, u32[]{:S(2)}) collective-permute-start(f32[128,4,128]{2,1,0:T(4,128)S(1)} %get-tuple-element.385), channel_id=1, source_target_pairs={{0,1},{1,2},{2,3},{3,4},{4,5},{5,6},{6,7},{7,8},{8,9},{9,10},{10,1... | collective-permute-start | bytes 786440 | tf_op jit(solution)/shard_map/while/body/eval_jaxpr/ppermute | solution.py:21
  49.1 14.1 %collective-permute-start.2 = (f32[128,4,128]{2,1,0:T(4,128)S(1)}, f32[128,4,128]{2,1,0:T(4,128)S(1)}, u32[]{:S(2)}, u32[]{:S(2)}) collective-permute-start(f32[128,4,128]{2,1,0:T(4,128)S(1)} %get-tuple-element.350), channel_id=1, source_target_pairs={{0,1},{1,2},{2,3},{3,4},{4,5},{5,6},{6,7},{7,8},{8,9},{9,10},{10,1... | collective-permute-start | bytes 786440 | tf_op jit(solution)/shard_map/while/body/eval_jaxpr/ppermute | solution.py:21
  79.1 17.0 %collective-permute-start.4 = (f32[128,4,128]{2,1,0:T(4,128)S(1)}, f32[128,4,128]{2,1,0:T(4,128)S(1)}, u32[]{:S(2)}, u32[]{:S(2)}) collective-permute-start(f32[128,4,128]{2,1,0:T(4,128)S(1)} %get-tuple-element.385), channel_id=1, source_target_pairs={{0,1},{1,2},{2,3},{3,4},{4,5},{5,6},{6,7},{7,8},{8,9},{9,10},{10,1... | collective-permute-start | bytes 786440 | tf_op jit(solution)/shard_map/while/body/eval_jaxpr/ppermute | solution.py:21
  82.1 13.9 %collective-permute-start.5 = (f32[128,4,128]{2,1,0:T(4,128)}, f32[128,4,128]{2,1,0:T(4,128)S(1)}, u32[]{:S(2)}, u32[]{:S(2)}) collective-permute-start(f32[128,4,128]{2,1,0:T(4,128)} %get-tuple-element.384), channel_id=1, source_target_pairs={{1,0},{2,1},{3,2},{4,3},{5,4},{6,5},{7,6},{8,7},{9,8},{10,9},{11,1... | collective-permute-start | bytes 786440 | tf_op jit(solution)/shard_map/while/body/eval_jaxpr/ppermute | solution.py:22
  87.2 17.1 %collective-permute-start.2 = (f32[128,4,128]{2,1,0:T(4,128)S(1)}, f32[128,4,128]{2,1,0:T(4,128)S(1)}, u32[]{:S(2)}, u32[]{:S(2)}) collective-permute-start(f32[128,4,128]{2,1,0:T(4,128)S(1)} %get-tuple-element.350), channel_id=1, source_target_pairs={{0,1},{1,2},{2,3},{3,4},{4,5},{5,6},{6,7},{7,8},{8,9},{9,10},{10,1... | collective-permute-start | bytes 786440 | tf_op jit(solution)/shard_map/while/body/eval_jaxpr/ppermute | solution.py:21
  112.9 11.8 %collective-permute-start = (f32[128,4,128]{2,1,0:T(4,128)}, f32[128,4,128]{2,1,0:T(4,128)S(1)}, u32[]{:S(2)}, u32[]{:S(2)}) collective-permute-start(f32[128,4,128]{2,1,0:T(4,128)} %get-tuple-element.381), channel_id=1, source_target_pairs={{0,1},{1,2},{2,3},{3,4},{4,5},{5,6},{6,7},{7,8},{8,9},{9,10},{10,1... | collective-permute-start | bytes 786440 | tf_op jit(solution)/shard_map/while/body/eval_jaxpr/ppermute | solution.py:21
  120.2 17.1 %collective-permute-start.4 = (f32[128,4,128]{2,1,0:T(4,128)S(1)}, f32[128,4,128]{2,1,0:T(4,128)S(1)}, u32[]{:S(2)}, u32[]{:S(2)}) collective-permute-start(f32[128,4,128]{2,1,0:T(4,128)S(1)} %get-tuple-element.385), channel_id=1, source_target_pairs={{0,1},{1,2},{2,3},{3,4},{4,5},{5,6},{6,7},{7,8},{8,9},{9,10},{10,1... | collective-permute-start | bytes 786440 | tf_op jit(solution)/shard_map/while/body/eval_jaxpr/ppermute | solution.py:21
  123.3 14.0 %collective-permute-start.5 = (f32[128,4,128]{2,1,0:T(4,128)}, f32[128,4,128]{2,1,0:T(4,128)S(1)}, u32[]{:S(2)}, u32[]{:S(2)}) collective-permute-start(f32[128,4,128]{2,1,0:T(4,128)} %get-tuple-element.384), channel_id=1, source_target_pairs={{1,0},{2,1},{3,2},{4,3},{5,4},{6,5},{7,6},{8,7},{9,8},{10,9},{11,1... | collective-permute-start | bytes 786440 | tf_op jit(solution)/shard_map/while/body/eval_jaxpr/ppermute | solution.py:22
  128.3 17.2 %collective-permute-start.2 = (f32[128,4,128]{2,1,0:T(4,128)S(1)}, f32[128,4,128]{2,1,0:T(4,128)S(1)}, u32[]{:S(2)}, u32[]{:S(2)}) collective-permute-start(f32[128,4,128]{2,1,0:T(4,128)S(1)} %get-tuple-element.350), channel_id=1, source_target_pairs={{0,1},{1,2},{2,3},{3,4},{4,5},{5,6},{6,7},{7,8},{8,9},{9,10},{10,1... | collective-permute-start | bytes 786440 | tf_op jit(solution)/shard_map/while/body/eval_jaxpr/ppermute | solution.py:21
  161.5 17.1 %collective-permute-start.4 = (f32[128,4,128]{2,1,0:T(4,128)S(1)}, f32[128,4,128]{2,1,0:T(4,128)S(1)}, u32[]{:S(2)}, u32[]{:S(2)}) collective-permute-start(f32[128,4,128]{2,1,0:T(4,128)S(1)} %get-tuple-element.385), channel_id=1, source_target_pairs={{0,1},{1,2},{2,3},{3,4},{4,5},{5,6},{6,7},{7,8},{8,9},{9,10},{10,1... | collective-permute-start | bytes 786440 | tf_op jit(solution)/shard_map/while/body/eval_jaxpr/ppermute | solution.py:21
  164.6 14.0 %collective-permute-start.5 = (f32[128,4,128]{2,1,0:T(4,128)}, f32[128,4,128]{2,1,0:T(4,128)S(1)}, u32[]{:S(2)}, u32[]{:S(2)}) collective-permute-start(f32[128,4,128]{2,1,0:T(4,128)} %get-tuple-element.384), channel_id=1, source_target_pairs={{1,0},{2,1},{3,2},{4,3},{5,4},{6,5},{7,6},{8,7},{9,8},{10,9},{11,1... | collective-permute-start | bytes 786440 | tf_op jit(solution)/shard_map/while/body/eval_jaxpr/ppermute | solution.py:22
  169.6 17.2 %collective-permute-start.2 = (f32[128,4,128]{2,1,0:T(4,128)S(1)}, f32[128,4,128]{2,1,0:T(4,128)S(1)}, u32[]{:S(2)}, u32[]{:S(2)}) collective-permute-start(f32[128,4,128]{2,1,0:T(4,128)S(1)} %get-tuple-element.350), channel_id=1, source_target_pairs={{0,1},{1,2},{2,3},{3,4},{4,5},{5,6},{6,7},{7,8},{8,9},{9,10},{10,1... | collective-permute-start | bytes 786440 | tf_op jit(solution)/shard_map/while/body/eval_jaxpr/ppermute | solution.py:21
  202.8 17.1 %collective-permute-start.4 = (f32[128,4,128]{2,1,0:T(4,128)S(1)}, f32[128,4,128]{2,1,0:T(4,128)S(1)}, u32[]{:S(2)}, u32[]{:S(2)}) collective-permute-start(f32[128,4,128]{2,1,0:T(4,128)S(1)} %get-tuple-element.385), channel_id=1, source_target_pairs={{0,1},{1,2},{2,3},{3,4},{4,5},{5,6},{6,7},{7,8},{8,9},{9,10},{10,1... | collective-permute-start | bytes 786440 | tf_op jit(solution)/shard_map/while/body/eval_jaxpr/ppermute | solution.py:21
  205.8 14.0 %collective-permute-start.5 = (f32[128,4,128]{2,1,0:T(4,128)}, f32[128,4,128]{2,1,0:T(4,128)S(1)}, u32[]{:S(2)}, u32[]{:S(2)}) collective-permute-start(f32[128,4,128]{2,1,0:T(4,128)} %get-tuple-element.384), channel_id=1, source_target_pairs={{1,0},{2,1},{3,2},{4,3},{5,4},{6,5},{7,6},{8,7},{9,8},{10,9},{11,1... | collective-permute-start | bytes 786440 | tf_op jit(solution)/shard_map/while/body/eval_jaxpr/ppermute | solution.py:22
  210.9 17.2 %collective-permute-start.2 = (f32[128,4,128]{2,1,0:T(4,128)S(1)}, f32[128,4,128]{2,1,0:T(4,128)S(1)}, u32[]{:S(2)}, u32[]{:S(2)}) collective-permute-start(f32[128,4,128]{2,1,0:T(4,128)S(1)} %get-tuple-element.350), channel_id=1, source_target_pairs={{0,1},{1,2},{2,3},{3,4},{4,5},{5,6},{6,7},{7,8},{8,9},{9,10},{10,1... | collective-permute-start | bytes 786440 | tf_op jit(solution)/shard_map/while/body/eval_jaxpr/ppermute | solution.py:21
  244.1 17.1 %collective-permute-start.4 = (f32[128,4,128]{2,1,0:T(4,128)S(1)}, f32[128,4,128]{2,1,0:T(4,128)S(1)}, u32[]{:S(2)}, u32[]{:S(2)}) collective-permute-start(f32[128,4,128]{2,1,0:T(4,128)S(1)} %get-tuple-element.385), channel_id=1, source_target_pairs={{0,1},{1,2},{2,3},{3,4},{4,5},{5,6},{6,7},{7,8},{8,9},{9,10},{10,1... | collective-permute-start | bytes 786440 | tf_op jit(solution)/shard_map/while/body/eval_jaxpr/ppermute | solution.py:21
  247.1 14.0 %collective-permute-start.5 = (f32[128,4,128]{2,1,0:T(4,128)}, f32[128,4,128]{2,1,0:T(4,128)S(1)}, u32[]{:S(2)}, u32[]{:S(2)}) collective-permute-start(f32[128,4,128]{2,1,0:T(4,128)} %get-tuple-element.384), channel_id=1, source_target_pairs={{1,0},{2,1},{3,2},{4,3},{5,4},{6,5},{7,6},{8,7},{9,8},{10,9},{11,1... | collective-permute-start | bytes 786440 | tf_op jit(solution)/shard_map/while/body/eval_jaxpr/ppermute | solution.py:22
  252.2 17.2 %collective-permute-start.2 = (f32[128,4,128]{2,1,0:T(4,128)S(1)}, f32[128,4,128]{2,1,0:T(4,128)S(1)}, u32[]{:S(2)}, u32[]{:S(2)}) collective-permute-start(f32[128,4,128]{2,1,0:T(4,128)S(1)} %get-tuple-element.350), channel_id=1, source_target_pairs={{0,1},{1,2},{2,3},{3,4},{4,5},{5,6},{6,7},{7,8},{8,9},{9,10},{10,1... | collective-permute-start | bytes 786440 | tf_op jit(solution)/shard_map/while/body/eval_jaxpr/ppermute | solution.py:21
  285.3 17.1 %collective-permute-start.4 = (f32[128,4,128]{2,1,0:T(4,128)S(1)}, f32[128,4,128]{2,1,0:T(4,128)S(1)}, u32[]{:S(2)}, u32[]{:S(2)}) collective-permute-start(f32[128,4,128]{2,1,0:T(4,128)S(1)} %get-tuple-element.385), channel_id=1, source_target_pairs={{0,1},{1,2},{2,3},{3,4},{4,5},{5,6},{6,7},{7,8},{8,9},{9,10},{10,1... | collective-permute-start | bytes 786440 | tf_op jit(solution)/shard_map/while/body/eval_jaxpr/ppermute | solution.py:21
  288.4 14.0 %collective-permute-start.5 = (f32[128,4,128]{2,1,0:T(4,128)}, f32[128,4,128]{2,1,0:T(4,128)S(1)}, u32[]{:S(2)}, u32[]{:S(2)}) collective-permute-start(f32[128,4,128]{2,1,0:T(4,128)} %get-tuple-element.384), channel_id=1, source_target_pairs={{1,0},{2,1},{3,2},{4,3},{5,4},{6,5},{7,6},{8,7},{9,8},{10,9},{11,1... | collective-permute-start | bytes 786440 | tf_op jit(solution)/shard_map/while/body/eval_jaxpr/ppermute | solution.py:22
  293.4 17.2 %collective-permute-start.2 = (f32[128,4,128]{2,1,0:T(4,128)S(1)}, f32[128,4,128]{2,1,0:T(4,128)S(1)}, u32[]{:S(2)}, u32[]{:S(2)}) collective-permute-start(f32[128,4,128]{2,1,0:T(4,128)S(1)} %get-tuple-element.350), channel_id=1, source_target_pairs={{0,1},{1,2},{2,3},{3,4},{4,5},{5,6},{6,7},{7,8},{8,9},{9,10},{10,1... | collective-permute-start | bytes 786440 | tf_op jit(solution)/shard_map/while/body/eval_jaxpr/ppermute | solution.py:21
  326.6 17.1 %collective-permute-start.4 = (f32[128,4,128]{2,1,0:T(4,128)S(1)}, f32[128,4,128]{2,1,0:T(4,128)S(1)}, u32[]{:S(2)}, u32[]{:S(2)}) collective-permute-start(f32[128,4,128]{2,1,0:T(4,128)S(1)} %get-tuple-element.385), channel_id=1, source_target_pairs={{0,1},{1,2},{2,3},{3,4},{4,5},{5,6},{6,7},{7,8},{8,9},{9,10},{10,1... | collective-permute-start | bytes 786440 | tf_op jit(solution)/shard_map/while/body/eval_jaxpr/ppermute | solution.py:21
  329.6 14.0 %collective-permute-start.5 = (f32[128,4,128]{2,1,0:T(4,128)}, f32[128,4,128]{2,1,0:T(4,128)S(1)}, u32[]{:S(2)}, u32[]{:S(2)}) collective-permute-start(f32[128,4,128]{2,1,0:T(4,128)} %get-tuple-element.384), channel_id=1, source_target_pairs={{1,0},{2,1},{3,2},{4,3},{5,4},{6,5},{7,6},{8,7},{9,8},{10,9},{11,1... | collective-permute-start | bytes 786440 | tf_op jit(solution)/shard_map/while/body/eval_jaxpr/ppermute | solution.py:22
  334.7 17.2 %collective-permute-start.2 = (f32[128,4,128]{2,1,0:T(4,128)S(1)}, f32[128,4,128]{2,1,0:T(4,128)S(1)}, u32[]{:S(2)}, u32[]{:S(2)}) collective-permute-start(f32[128,4,128]{2,1,0:T(4,128)S(1)} %get-tuple-element.350), channel_id=1, source_target_pairs={{0,1},{1,2},{2,3},{3,4},{4,5},{5,6},{6,7},{7,8},{8,9},{9,10},{10,1... | collective-permute-start | bytes 786440 | tf_op jit(solution)/shard_map/while/body/eval_jaxpr/ppermute | solution.py:21
  367.9 17.1 %collective-permute-start.4 = (f32[128,4,128]{2,1,0:T(4,128)S(1)}, f32[128,4,128]{2,1,0:T(4,128)S(1)}, u32[]{:S(2)}, u32[]{:S(2)}) collective-permute-start(f32[128,4,128]{2,1,0:T(4,128)S(1)} %get-tuple-element.385), channel_id=1, source_target_pairs={{0,1},{1,2},{2,3},{3,4},{4,5},{5,6},{6,7},{7,8},{8,9},{9,10},{10,1... | collective-permute-start | bytes 786440 | tf_op jit(solution)/shard_map/while/body/eval_jaxpr/ppermute | solution.py:21
  370.9 14.0 %collective-permute-start.5 = (f32[128,4,128]{2,1,0:T(4,128)}, f32[128,4,128]{2,1,0:T(4,128)S(1)}, u32[]{:S(2)}, u32[]{:S(2)}) collective-permute-start(f32[128,4,128]{2,1,0:T(4,128)} %get-tuple-element.384), channel_id=1, source_target_pairs={{1,0},{2,1},{3,2},{4,3},{5,4},{6,5},{7,6},{8,7},{9,8},{10,9},{11,1... | collective-permute-start | bytes 786440 | tf_op jit(solution)/shard_map/while/body/eval_jaxpr/ppermute | solution.py:22
  376.0 17.2 %collective-permute-start.2 = (f32[128,4,128]{2,1,0:T(4,128)S(1)}, f32[128,4,128]{2,1,0:T(4,128)S(1)}, u32[]{:S(2)}, u32[]{:S(2)}) collective-permute-start(f32[128,4,128]{2,1,0:T(4,128)S(1)} %get-tuple-element.350), channel_id=1, source_target_pairs={{0,1},{1,2},{2,3},{3,4},{4,5},{5,6},{6,7},{7,8},{8,9},{9,10},{10,1... | collective-permute-start | bytes 786440 | tf_op jit(solution)/shard_map/while/body/eval_jaxpr/ppermute | solution.py:21
  409.1 17.1 %collective-permute-start.4 = (f32[128,4,128]{2,1,0:T(4,128)S(1)}, f32[128,4,128]{2,1,0:T(4,128)S(1)}, u32[]{:S(2)}, u32[]{:S(2)}) collective-permute-start(f32[128,4,128]{2,1,0:T(4,128)S(1)} %get-tuple-element.385), channel_id=1, source_target_pairs={{0,1},{1,2},{2,3},{3,4},{4,5},{5,6},{6,7},{7,8},{8,9},{9,10},{10,1... | collective-permute-start | bytes 786440 | tf_op jit(solution)/shard_map/while/body/eval_jaxpr/ppermute | solution.py:21
  412.2 14.0 %collective-permute-start.5 = (f32[128,4,128]{2,1,0:T(4,128)}, f32[128,4,128]{2,1,0:T(4,128)S(1)}, u32[]{:S(2)}, u32[]{:S(2)}) collective-permute-start(f32[128,4,128]{2,1,0:T(4,128)} %get-tuple-element.384), channel_id=1, source_target_pairs={{1,0},{2,1},{3,2},{4,3},{5,4},{6,5},{7,6},{8,7},{9,8},{10,9},{11,1... | collective-permute-start | bytes 786440 | tf_op jit(solution)/shard_map/while/body/eval_jaxpr/ppermute | solution.py:22
  417.2 17.2 %collective-permute-start.2 = (f32[128,4,128]{2,1,0:T(4,128)S(1)}, f32[128,4,128]{2,1,0:T(4,128)S(1)}, u32[]{:S(2)}, u32[]{:S(2)}) collective-permute-start(f32[128,4,128]{2,1,0:T(4,128)S(1)} %get-tuple-element.350), channel_id=1, source_target_pairs={{0,1},{1,2},{2,3},{3,4},{4,5},{5,6},{6,7},{7,8},{8,9},{9,10},{10,1... | collective-permute-start | bytes 786440 | tf_op jit(solution)/shard_map/while/body/eval_jaxpr/ppermute | solution.py:21
  445.0 26.7 %all-to-all-start.1 = ((f32[128,1,8,128]{3,2,1,0:T(8,128)}), f32[128,1,8,128]{3,2,1,0:T(8,128)S(1)}, u32[]{:S(2)}, u32[]{:S(2)}) async-start(f32[128,1,8,128]{3,2,1,0:T(8,128)} %multiply_bitcast_fusion), calls=%async_computation.1 | async-start | bytes 1048576 | tf_op jit(solution)/shard_map/all_to_all | solution.py:192
  (201 other events, 1572.4 us)

commit v14 on v13

--- a/solution.py
+++ b/solution.py
@@ -11,7 +11,7 @@
 stencil_weights = (8.0 / 5.0, -1.0 / 5.0, 8.0 / 315.0, -1.0 / 560.0)
 center_weight = 3.0 * (-205.0 / 72.0)
 HALO = 4
-ROWS = 64
+ROWS = 128
 XOFF = 8
 
 

time: 477 us -> 474 us (level)
  Pallas kernels: 141 us -> 136 us
    pallas_call x40, Pallas kernels: 141 us -> 136 us  [wave_call(): pl.pallas_call(functools.partial(wave_kernel, with_image), out_shape=tupl...]
  transfers between devices with their start and end apart: 82 -> 82, of which waited for: 1 -> 1; matrix products, arithmetic and copies ran while one was open for 6% -> 6% of each run, Pallas kernels for 22% -> 21%
where the time goes in v14:
time: 474 us; the launch traced here: 470 us
  starting transfers between devices  274 us (58%)
  Pallas kernels  136 us (29%)
  local copies, waits for them, and re-layouts  23.2 us (5%)
  matrix products  11.7 us (2%)
  waiting for transfers between devices  11.6 us (2%)
  other arithmetic  10.1 us (2%)
    ppermute x40, starting transfers between devices, trade_halos(): low = lax.ppermute(tail, axis, [(i, (i + 1) % count) for i in range(ends)])  202 us
    pallas_call x40, Pallas kernels, wave_call(): pl.pallas_call(functools.partial(wave_kernel, with_image), out_shape=tupl...  136 us
    ppermute x40, starting transfers between devices, trade_halos(): high = lax.ppermute(head, axis, [((i + 1) % count, i) for i in range(ends)])  51.7 us
    all_to_all x1, starting transfers between devices, shards(): lax.all_to_all(outgoing, 'dom', split_axis=0, concat_axis=1, tiled=True)  12.4 us
    all_to_all x1, waiting for transfers between devices, shards(): lax.all_to_all(outgoing, 'dom', split_axis=0, concat_axis=1, tiled=True)  11.3 us
    dot_general x2, matrix products, spread_points(): jnp.einsum('ny,nsc->syc', rows_y, weighted, precision=lax.Precision.HIGHEST)  11 us
    while x280, local copies, waits for them, and re-layouts  10.3 us
  transfers between devices with their start and end apart: 82, of which 1 were waited for; matrix products, arithmetic and copies ran while one was open for 6% of the time, Pallas kernels for 21%

profile of v14, /device:TPU:0, one launch (start us, length us, event | category | flops | bytes accessed | tf_op | source)
XLA Modules:
  0.0 470.2 jit_solution(14692149078948709897)
XLA Ops:
  3.6 7.4 %all-to-all-start = ((f32[8,16,8,128]{3,2,0,1:T(8,128)}), f32[8,16,8,128]{3,2,0,1:T(8,128)S(1)}, u32[]{:S(2)}, u32[]{:S(2)}) async-start(f32[8,16,8,128]{3,2,0,1:T(8,128)} %select_bitcast_fusion), calls=%async_computation | async-start | bytes 1048576 | tf_op jit(solution)/shard_map/all_to_all | solution.py:144
  12.2 10.5 %fusion = f32[20,32,128]{2,1,0:T(8,128)S(1)} fusion(f32[8192,20]{0,1:T(8,128)S(1)} %bitcast.85, f32[8192,32]{0,1:T(8,128)S(1)} %fusion.8, s32[8192]{0:T(1024)S(1)} %bitcast.83), kind=kOutput, calls=%fused_computation.1 | convolution fusion | flops 8059355136 | bytes 2064384 | tf_op jit(solution)/shard_map/ny,nsc->syc/dot_general | solution.py:131
  36.2 403.5 %while.29 = (s32[]{:T(128)}, f32[128,8,128]{2,1,0:T(8,128)}, f32[128,8,128]{2,1,0:T(8,128)S(1)}, f32[128,4,128]{2,1,0:T(4,128)}, f32[128,4,128]{2,1,0:T(4,128)},...) while((s32[]{:T(128)}, f32[128,8,128]{2,1,0:T(8,128)}, ...), condition=%wide.region_1.2_spmd, body=%wide.region_0.1_spmd.sunk | while | flops 31457284 | bytes 67109736 | solution.py:181
  39.8 4.2 collective-permute-start.4
  48.8 4.6 collective-permute-start.2
  57.7 3.9 collective-permute-start.6
  71.4 6.1 %collective-permute-start = (f32[128,4,128]{2,1,0:T(4,128)}, f32[128,4,128]{2,1,0:T(4,128)S(1)}, u32[]{:S(2)}, u32[]{:S(2)}) collective-permute-start(f32[128,4,128]{2,1,0:T(4,128)} %get-tuple-element.381), channel_id=1, source_target_pairs={{0,1},{1,2},{2,3},{3,4},{4,5},{5,6},{6,7},{7,8},{8,9},{9,10},{10,1... | collective-permute-start | bytes 786440 | tf_op jit(solution)/shard_map/while/body/eval_jaxpr/ppermute | solution.py:21
  86.7 7.5 %collective-permute-start.2 = (f32[128,4,128]{2,1,0:T(4,128)S(1)}, f32[128,4,128]{2,1,0:T(4,128)S(1)}, u32[]{:S(2)}, u32[]{:S(2)}) collective-permute-start(f32[128,4,128]{2,1,0:T(4,128)S(1)} %get-tuple-element.350), channel_id=1, source_target_pairs={{0,1},{1,2},{2,3},{3,4},{4,5},{5,6},{6,7},{7,8},{8,9},{9,10},{10,1... | collective-permute-start | bytes 786440 | tf_op jit(solution)/shard_map/while/body/eval_jaxpr/ppermute | solution.py:21
  98.4 3.9 collective-permute-start.6
  112.1 6.2 %collective-permute-start = (f32[128,4,128]{2,1,0:T(4,128)}, f32[128,4,128]{2,1,0:T(4,128)S(1)}, u32[]{:S(2)}, u32[]{:S(2)}) collective-permute-start(f32[128,4,128]{2,1,0:T(4,128)} %get-tuple-element.381), channel_id=1, source_target_pairs={{0,1},{1,2},{2,3},{3,4},{4,5},{5,6},{6,7},{7,8},{8,9},{9,10},{10,1... | collective-permute-start | bytes 786440 | tf_op jit(solution)/shard_map/while/body/eval_jaxpr/ppermute | solution.py:21
  127.5 7.6 %collective-permute-start.2 = (f32[128,4,128]{2,1,0:T(4,128)S(1)}, f32[128,4,128]{2,1,0:T(4,128)S(1)}, u32[]{:S(2)}, u32[]{:S(2)}) collective-permute-start(f32[128,4,128]{2,1,0:T(4,128)S(1)} %get-tuple-element.350), channel_id=1, source_target_pairs={{0,1},{1,2},{2,3},{3,4},{4,5},{5,6},{6,7},{7,8},{8,9},{9,10},{10,1... | collective-permute-start | bytes 786440 | tf_op jit(solution)/shard_map/while/body/eval_jaxpr/ppermute | solution.py:21
  139.4 3.9 collective-permute-start.6
  153.1 6.2 %collective-permute-start = (f32[128,4,128]{2,1,0:T(4,128)}, f32[128,4,128]{2,1,0:T(4,128)S(1)}, u32[]{:S(2)}, u32[]{:S(2)}) collective-permute-start(f32[128,4,128]{2,1,0:T(4,128)} %get-tuple-element.381), channel_id=1, source_target_pairs={{0,1},{1,2},{2,3},{3,4},{4,5},{5,6},{6,7},{7,8},{8,9},{9,10},{10,1... | collective-permute-start | bytes 786440 | tf_op jit(solution)/shard_map/while/body/eval_jaxpr/ppermute | solution.py:21
  168.5 7.6 %collective-permute-start.2 = (f32[128,4,128]{2,1,0:T(4,128)S(1)}, f32[128,4,128]{2,1,0:T(4,128)S(1)}, u32[]{:S(2)}, u32[]{:S(2)}) collective-permute-start(f32[128,4,128]{2,1,0:T(4,128)S(1)} %get-tuple-element.350), channel_id=1, source_target_pairs={{0,1},{1,2},{2,3},{3,4},{4,5},{5,6},{6,7},{7,8},{8,9},{9,10},{10,1... | collective-permute-start | bytes 786440 | tf_op jit(solution)/shard_map/while/body/eval_jaxpr/ppermute | solution.py:21
  180.3 3.9 collective-permute-start.6
  194.0 6.2 %collective-permute-start = (f32[128,4,128]{2,1,0:T(4,128)}, f32[128,4,128]{2,1,0:T(4,128)S(1)}, u32[]{:S(2)}, u32[]{:S(2)}) collective-permute-start(f32[128,4,128]{2,1,0:T(4,128)} %get-tuple-element.381), channel_id=1, source_target_pairs={{0,1},{1,2},{2,3},{3,4},{4,5},{5,6},{6,7},{7,8},{8,9},{9,10},{10,1... | collective-permute-start | bytes 786440 | tf_op jit(solution)/shard_map/while/body/eval_jaxpr/ppermute | solution.py:21
  209.4 7.6 %collective-permute-start.2 = (f32[128,4,128]{2,1,0:T(4,128)S(1)}, f32[128,4,128]{2,1,0:T(4,128)S(1)}, u32[]{:S(2)}, u32[]{:S(2)}) collective-permute-start(f32[128,4,128]{2,1,0:T(4,128)S(1)} %get-tuple-element.350), channel_id=1, source_target_pairs={{0,1},{1,2},{2,3},{3,4},{4,5},{5,6},{6,7},{7,8},{8,9},{9,10},{10,1... | collective-permute-start | bytes 786440 | tf_op jit(solution)/shard_map/while/body/eval_jaxpr/ppermute | solution.py:21
  221.3 3.9 collective-permute-start.6
  235.0 6.2 %collective-permute-start = (f32[128,4,128]{2,1,0:T(4,128)}, f32[128,4,128]{2,1,0:T(4,128)S(1)}, u32[]{:S(2)}, u32[]{:S(2)}) collective-permute-start(f32[128,4,128]{2,1,0:T(4,128)} %get-tuple-element.381), channel_id=1, source_target_pairs={{0,1},{1,2},{2,3},{3,4},{4,5},{5,6},{6,7},{7,8},{8,9},{9,10},{10,1... | collective-permute-start | bytes 786440 | tf_op jit(solution)/shard_map/while/body/eval_jaxpr/ppermute | solution.py:21
  250.3 7.6 %collective-permute-start.2 = (f32[128,4,128]{2,1,0:T(4,128)S(1)}, f32[128,4,128]{2,1,0:T(4,128)S(1)}, u32[]{:S(2)}, u32[]{:S(2)}) collective-permute-start(f32[128,4,128]{2,1,0:T(4,128)S(1)} %get-tuple-element.350), channel_id=1, source_target_pairs={{0,1},{1,2},{2,3},{3,4},{4,5},{5,6},{6,7},{7,8},{8,9},{9,10},{10,1... | collective-permute-start | bytes 786440 | tf_op jit(solution)/shard_map/while/body/eval_jaxpr/ppermute | solution.py:21
  262.2 3.9 collective-permute-start.6
  275.9 6.2 %collective-permute-start = (f32[128,4,128]{2,1,0:T(4,128)}, f32[128,4,128]{2,1,0:T(4,128)S(1)}, u32[]{:S(2)}, u32[]{:S(2)}) collective-permute-start(f32[128,4,128]{2,1,0:T(4,128)} %get-tuple-element.381), channel_id=1, source_target_pairs={{0,1},{1,2},{2,3},{3,4},{4,5},{5,6},{6,7},{7,8},{8,9},{9,10},{10,1... | collective-permute-start | bytes 786440 | tf_op jit(solution)/shard_map/while/body/eval_jaxpr/ppermute | solution.py:21
  291.3 7.6 %collective-permute-start.2 = (f32[128,4,128]{2,1,0:T(4,128)S(1)}, f32[128,4,128]{2,1,0:T(4,128)S(1)}, u32[]{:S(2)}, u32[]{:S(2)}) collective-permute-start(f32[128,4,128]{2,1,0:T(4,128)S(1)} %get-tuple-element.350), channel_id=1, source_target_pairs={{0,1},{1,2},{2,3},{3,4},{4,5},{5,6},{6,7},{7,8},{8,9},{9,10},{10,1... | collective-permute-start | bytes 786440 | tf_op jit(solution)/shard_map/while/body/eval_jaxpr/ppermute | solution.py:21
  303.2 3.9 collective-permute-start.6
  316.9 6.2 %collective-permute-start = (f32[128,4,128]{2,1,0:T(4,128)}, f32[128,4,128]{2,1,0:T(4,128)S(1)}, u32[]{:S(2)}, u32[]{:S(2)}) collective-permute-start(f32[128,4,128]{2,1,0:T(4,128)} %get-tuple-element.381), channel_id=1, source_target_pairs={{0,1},{1,2},{2,3},{3,4},{4,5},{5,6},{6,7},{7,8},{8,9},{9,10},{10,1... | collective-permute-start | bytes 786440 | tf_op jit(solution)/shard_map/while/body/eval_jaxpr/ppermute | solution.py:21
  332.2 7.6 %collective-permute-start.2 = (f32[128,4,128]{2,1,0:T(4,128)S(1)}, f32[128,4,128]{2,1,0:T(4,128)S(1)}, u32[]{:S(2)}, u32[]{:S(2)}) collective-permute-start(f32[128,4,128]{2,1,0:T(4,128)S(1)} %get-tuple-element.350), channel_id=1, source_target_pairs={{0,1},{1,2},{2,3},{3,4},{4,5},{5,6},{6,7},{7,8},{8,9},{9,10},{10,1... | collective-permute-start | bytes 786440 | tf_op jit(solution)/shard_map/while/body/eval_jaxpr/ppermute | solution.py:21
  357.8 6.2 %collective-permute-start = (f32[128,4,128]{2,1,0:T(4,128)}, f32[128,4,128]{2,1,0:T(4,128)S(1)}, u32[]{:S(2)}, u32[]{:S(2)}) collective-permute-start(f32[128,4,128]{2,1,0:T(4,128)} %get-tuple-element.381), channel_id=1, source_target_pairs={{0,1},{1,2},{2,3},{3,4},{4,5},{5,6},{6,7},{7,8},{8,9},{9,10},{10,1... | collective-permute-start | bytes 786440 | tf_op jit(solution)/shard_map/while/body/eval_jaxpr/ppermute | solution.py:21
  373.2 7.6 %collective-permute-start.2 = (f32[128,4,128]{2,1,0:T(4,128)S(1)}, f32[128,4,128]{2,1,0:T(4,128)S(1)}, u32[]{:S(2)}, u32[]{:S(2)}) collective-permute-start(f32[128,4,128]{2,1,0:T(4,128)S(1)} %get-tuple-element.350), channel_id=1, source_target_pairs={{0,1},{1,2},{2,3},{3,4},{4,5},{5,6},{6,7},{7,8},{8,9},{9,10},{10,1... | collective-permute-start | bytes 786440 | tf_op jit(solution)/shard_map/while/body/eval_jaxpr/ppermute | solution.py:21
  398.8 6.2 %collective-permute-start = (f32[128,4,128]{2,1,0:T(4,128)}, f32[128,4,128]{2,1,0:T(4,128)S(1)}, u32[]{:S(2)}, u32[]{:S(2)}) collective-permute-start(f32[128,4,128]{2,1,0:T(4,128)} %get-tuple-element.381), channel_id=1, source_target_pairs={{0,1},{1,2},{2,3},{3,4},{4,5},{5,6},{6,7},{7,8},{8,9},{9,10},{10,1... | collective-permute-start | bytes 786440 | tf_op jit(solution)/shard_map/while/body/eval_jaxpr/ppermute | solution.py:21
  414.1 7.6 %collective-permute-start.2 = (f32[128,4,128]{2,1,0:T(4,128)S(1)}, f32[128,4,128]{2,1,0:T(4,128)S(1)}, u32[]{:S(2)}, u32[]{:S(2)}) collective-permute-start(f32[128,4,128]{2,1,0:T(4,128)S(1)} %get-tuple-element.350), channel_id=1, source_target_pairs={{0,1},{1,2},{2,3},{3,4},{4,5},{5,6},{6,7},{7,8},{8,9},{9,10},{10,1... | collective-permute-start | bytes 786440 | tf_op jit(solution)/shard_map/while/body/eval_jaxpr/ppermute | solution.py:21
  441.7 12.4 %all-to-all-start.1 = ((f32[128,1,8,128]{3,2,1,0:T(8,128)}), f32[128,1,8,128]{3,2,1,0:T(8,128)S(1)}, u32[]{:S(2)}, u32[]{:S(2)}) async-start(f32[128,1,8,128]{3,2,1,0:T(8,128)} %multiply_bitcast_fusion), calls=%async_computation.1 | async-start | bytes 1048576 | tf_op jit(solution)/shard_map/all_to_all | solution.py:192
  457.2 11.3 %all-to-all-done.1 = f32[128,1,8,128]{3,2,1,0:T(8,128)S(1)} async-done(((f32[128,1,8,128]{3,2,1,0:T(8,128)}), f32[128,1,8,128]{3,2,1,0:T(8,128)S(1)}, u32[]{:S(2)}, u32[]{:S(2)}) %all-to-all-start.1) | async-done | bytes 524320 | tf_op jit(solution)/shard_map/all_to_all | solution.py:192
  (510 shorter events, 264.1 us)
Async XLA Ops:
  3.6 31.7 %all-to-all-start = ((f32[8,16,8,128]{3,2,0,1:T(8,128)}), f32[8,16,8,128]{3,2,0,1:T(8,128)S(1)}, u32[]{:S(2)}, u32[]{:S(2)}) async-start(f32[8,16,8,128]{3,2,0,1:T(8,128)} %select_bitcast_fusion), calls=%async_computation | async-start | bytes 1048576 | tf_op jit(solution)/shard_map/all_to_all | solution.py:144
  39.8 14.9 %collective-permute-start.4 = (f32[128,4,128]{2,1,0:T(4,128)S(1)}, f32[128,4,128]{2,1,0:T(4,128)S(1)}, u32[]{:S(2)}, u32[]{:S(2)}) collective-permute-start(f32[128,4,128]{2,1,0:T(4,128)S(1)} %get-tuple-element.385), channel_id=1, source_target_pairs={{0,1},{1,2},{2,3},{3,4},{4,5},{5,6},{6,7},{7,8},{8,9},{9,10},{10,1... | collective-permute-start | bytes 786440 | tf_op jit(solution)/shard_map/while/body/eval_jaxpr/ppermute | solution.py:21
  48.8 14.1 %collective-permute-start.2 = (f32[128,4,128]{2,1,0:T(4,128)S(1)}, f32[128,4,128]{2,1,0:T(4,128)S(1)}, u32[]{:S(2)}, u32[]{:S(2)}) collective-permute-start(f32[128,4,128]{2,1,0:T(4,128)S(1)} %get-tuple-element.350), channel_id=1, source_target_pairs={{0,1},{1,2},{2,3},{3,4},{4,5},{5,6},{6,7},{7,8},{8,9},{9,10},{10,1... | collective-permute-start | bytes 786440 | tf_op jit(solution)/shard_map/while/body/eval_jaxpr/ppermute | solution.py:21
  78.8 16.7 %collective-permute-start.4 = (f32[128,4,128]{2,1,0:T(4,128)S(1)}, f32[128,4,128]{2,1,0:T(4,128)S(1)}, u32[]{:S(2)}, u32[]{:S(2)}) collective-permute-start(f32[128,4,128]{2,1,0:T(4,128)S(1)} %get-tuple-element.385), channel_id=1, source_target_pairs={{0,1},{1,2},{2,3},{3,4},{4,5},{5,6},{6,7},{7,8},{8,9},{9,10},{10,1... | collective-permute-start | bytes 786440 | tf_op jit(solution)/shard_map/while/body/eval_jaxpr/ppermute | solution.py:21
  81.9 13.7 %collective-permute-start.5 = (f32[128,4,128]{2,1,0:T(4,128)}, f32[128,4,128]{2,1,0:T(4,128)S(1)}, u32[]{:S(2)}, u32[]{:S(2)}) collective-permute-start(f32[128,4,128]{2,1,0:T(4,128)} %get-tuple-element.384), channel_id=1, source_target_pairs={{1,0},{2,1},{3,2},{4,3},{5,4},{6,5},{7,6},{8,7},{9,8},{10,9},{11,1... | collective-permute-start | bytes 786440 | tf_op jit(solution)/shard_map/while/body/eval_jaxpr/ppermute | solution.py:22
  86.7 17.1 %collective-permute-start.2 = (f32[128,4,128]{2,1,0:T(4,128)S(1)}, f32[128,4,128]{2,1,0:T(4,128)S(1)}, u32[]{:S(2)}, u32[]{:S(2)}) collective-permute-start(f32[128,4,128]{2,1,0:T(4,128)S(1)} %get-tuple-element.350), channel_id=1, source_target_pairs={{0,1},{1,2},{2,3},{3,4},{4,5},{5,6},{6,7},{7,8},{8,9},{9,10},{10,1... | collective-permute-start | bytes 786440 | tf_op jit(solution)/shard_map/while/body/eval_jaxpr/ppermute | solution.py:21
  112.1 11.9 %collective-permute-start = (f32[128,4,128]{2,1,0:T(4,128)}, f32[128,4,128]{2,1,0:T(4,128)S(1)}, u32[]{:S(2)}, u32[]{:S(2)}) collective-permute-start(f32[128,4,128]{2,1,0:T(4,128)} %get-tuple-element.381), channel_id=1, source_target_pairs={{0,1},{1,2},{2,3},{3,4},{4,5},{5,6},{6,7},{7,8},{8,9},{9,10},{10,1... | collective-permute-start | bytes 786440 | tf_op jit(solution)/shard_map/while/body/eval_jaxpr/ppermute | solution.py:21
  119.7 16.8 %collective-permute-start.4 = (f32[128,4,128]{2,1,0:T(4,128)S(1)}, f32[128,4,128]{2,1,0:T(4,128)S(1)}, u32[]{:S(2)}, u32[]{:S(2)}) collective-permute-start(f32[128,4,128]{2,1,0:T(4,128)S(1)} %get-tuple-element.385), channel_id=1, source_target_pairs={{0,1},{1,2},{2,3},{3,4},{4,5},{5,6},{6,7},{7,8},{8,9},{9,10},{10,1... | collective-permute-start | bytes 786440 | tf_op jit(solution)/shard_map/while/body/eval_jaxpr/ppermute | solution.py:21
  122.7 13.8 %collective-permute-start.5 = (f32[128,4,128]{2,1,0:T(4,128)}, f32[128,4,128]{2,1,0:T(4,128)S(1)}, u32[]{:S(2)}, u32[]{:S(2)}) collective-permute-start(f32[128,4,128]{2,1,0:T(4,128)} %get-tuple-element.384), channel_id=1, source_target_pairs={{1,0},{2,1},{3,2},{4,3},{5,4},{6,5},{7,6},{8,7},{9,8},{10,9},{11,1... | collective-permute-start | bytes 786440 | tf_op jit(solution)/shard_map/while/body/eval_jaxpr/ppermute | solution.py:22
  127.5 17.2 %collective-permute-start.2 = (f32[128,4,128]{2,1,0:T(4,128)S(1)}, f32[128,4,128]{2,1,0:T(4,128)S(1)}, u32[]{:S(2)}, u32[]{:S(2)}) collective-permute-start(f32[128,4,128]{2,1,0:T(4,128)S(1)} %get-tuple-element.350), channel_id=1, source_target_pairs={{0,1},{1,2},{2,3},{3,4},{4,5},{5,6},{6,7},{7,8},{8,9},{9,10},{10,1... | collective-permute-start | bytes 786440 | tf_op jit(solution)/shard_map/while/body/eval_jaxpr/ppermute | solution.py:21
  160.6 16.8 %collective-permute-start.4 = (f32[128,4,128]{2,1,0:T(4,128)S(1)}, f32[128,4,128]{2,1,0:T(4,128)S(1)}, u32[]{:S(2)}, u32[]{:S(2)}) collective-permute-start(f32[128,4,128]{2,1,0:T(4,128)S(1)} %get-tuple-element.385), channel_id=1, source_target_pairs={{0,1},{1,2},{2,3},{3,4},{4,5},{5,6},{6,7},{7,8},{8,9},{9,10},{10,1... | collective-permute-start | bytes 786440 | tf_op jit(solution)/shard_map/while/body/eval_jaxpr/ppermute | solution.py:21
  163.7 13.8 %collective-permute-start.5 = (f32[128,4,128]{2,1,0:T(4,128)}, f32[128,4,128]{2,1,0:T(4,128)S(1)}, u32[]{:S(2)}, u32[]{:S(2)}) collective-permute-start(f32[128,4,128]{2,1,0:T(4,128)} %get-tuple-element.384), channel_id=1, source_target_pairs={{1,0},{2,1},{3,2},{4,3},{5,4},{6,5},{7,6},{8,7},{9,8},{10,9},{11,1... | collective-permute-start | bytes 786440 | tf_op jit(solution)/shard_map/while/body/eval_jaxpr/ppermute | solution.py:22
  168.5 17.2 %collective-permute-start.2 = (f32[128,4,128]{2,1,0:T(4,128)S(1)}, f32[128,4,128]{2,1,0:T(4,128)S(1)}, u32[]{:S(2)}, u32[]{:S(2)}) collective-permute-start(f32[128,4,128]{2,1,0:T(4,128)S(1)} %get-tuple-element.350), channel_id=1, source_target_pairs={{0,1},{1,2},{2,3},{3,4},{4,5},{5,6},{6,7},{7,8},{8,9},{9,10},{10,1... | collective-permute-start | bytes 786440 | tf_op jit(solution)/shard_map/while/body/eval_jaxpr/ppermute | solution.py:21
  201.6 16.8 %collective-permute-start.4 = (f32[128,4,128]{2,1,0:T(4,128)S(1)}, f32[128,4,128]{2,1,0:T(4,128)S(1)}, u32[]{:S(2)}, u32[]{:S(2)}) collective-permute-start(f32[128,4,128]{2,1,0:T(4,128)S(1)} %get-tuple-element.385), channel_id=1, source_target_pairs={{0,1},{1,2},{2,3},{3,4},{4,5},{5,6},{6,7},{7,8},{8,9},{9,10},{10,1... | collective-permute-start | bytes 786440 | tf_op jit(solution)/shard_map/while/body/eval_jaxpr/ppermute | solution.py:21
  204.6 13.8 %collective-permute-start.5 = (f32[128,4,128]{2,1,0:T(4,128)}, f32[128,4,128]{2,1,0:T(4,128)S(1)}, u32[]{:S(2)}, u32[]{:S(2)}) collective-permute-start(f32[128,4,128]{2,1,0:T(4,128)} %get-tuple-element.384), channel_id=1, source_target_pairs={{1,0},{2,1},{3,2},{4,3},{5,4},{6,5},{7,6},{8,7},{9,8},{10,9},{11,1... | collective-permute-start | bytes 786440 | tf_op jit(solution)/shard_map/while/body/eval_jaxpr/ppermute | solution.py:22
  209.4 17.2 %collective-permute-start.2 = (f32[128,4,128]{2,1,0:T(4,128)S(1)}, f32[128,4,128]{2,1,0:T(4,128)S(1)}, u32[]{:S(2)}, u32[]{:S(2)}) collective-permute-start(f32[128,4,128]{2,1,0:T(4,128)S(1)} %get-tuple-element.350), channel_id=1, source_target_pairs={{0,1},{1,2},{2,3},{3,4},{4,5},{5,6},{6,7},{7,8},{8,9},{9,10},{10,1... | collective-permute-start | bytes 786440 | tf_op jit(solution)/shard_map/while/body/eval_jaxpr/ppermute | solution.py:21
  242.5 16.8 %collective-permute-start.4 = (f32[128,4,128]{2,1,0:T(4,128)S(1)}, f32[128,4,128]{2,1,0:T(4,128)S(1)}, u32[]{:S(2)}, u32[]{:S(2)}) collective-permute-start(f32[128,4,128]{2,1,0:T(4,128)S(1)} %get-tuple-element.385), channel_id=1, source_target_pairs={{0,1},{1,2},{2,3},{3,4},{4,5},{5,6},{6,7},{7,8},{8,9},{9,10},{10,1... | collective-permute-start | bytes 786440 | tf_op jit(solution)/shard_map/while/body/eval_jaxpr/ppermute | solution.py:21
  245.6 13.8 %collective-permute-start.5 = (f32[128,4,128]{2,1,0:T(4,128)}, f32[128,4,128]{2,1,0:T(4,128)S(1)}, u32[]{:S(2)}, u32[]{:S(2)}) collective-permute-start(f32[128,4,128]{2,1,0:T(4,128)} %get-tuple-element.384), channel_id=1, source_target_pairs={{1,0},{2,1},{3,2},{4,3},{5,4},{6,5},{7,6},{8,7},{9,8},{10,9},{11,1... | collective-permute-start | bytes 786440 | tf_op jit(solution)/shard_map/while/body/eval_jaxpr/ppermute | solution.py:22
  250.3 17.2 %collective-permute-start.2 = (f32[128,4,128]{2,1,0:T(4,128)S(1)}, f32[128,4,128]{2,1,0:T(4,128)S(1)}, u32[]{:S(2)}, u32[]{:S(2)}) collective-permute-start(f32[128,4,128]{2,1,0:T(4,128)S(1)} %get-tuple-element.350), channel_id=1, source_target_pairs={{0,1},{1,2},{2,3},{3,4},{4,5},{5,6},{6,7},{7,8},{8,9},{9,10},{10,1... | collective-permute-start | bytes 786440 | tf_op jit(solution)/shard_map/while/body/eval_jaxpr/ppermute | solution.py:21
  283.4 16.8 %collective-permute-start.4 = (f32[128,4,128]{2,1,0:T(4,128)S(1)}, f32[128,4,128]{2,1,0:T(4,128)S(1)}, u32[]{:S(2)}, u32[]{:S(2)}) collective-permute-start(f32[128,4,128]{2,1,0:T(4,128)S(1)} %get-tuple-element.385), channel_id=1, source_target_pairs={{0,1},{1,2},{2,3},{3,4},{4,5},{5,6},{6,7},{7,8},{8,9},{9,10},{10,1... | collective-permute-start | bytes 786440 | tf_op jit(solution)/shard_map/while/body/eval_jaxpr/ppermute | solution.py:21
  286.5 13.8 %collective-permute-start.5 = (f32[128,4,128]{2,1,0:T(4,128)}, f32[128,4,128]{2,1,0:T(4,128)S(1)}, u32[]{:S(2)}, u32[]{:S(2)}) collective-permute-start(f32[128,4,128]{2,1,0:T(4,128)} %get-tuple-element.384), channel_id=1, source_target_pairs={{1,0},{2,1},{3,2},{4,3},{5,4},{6,5},{7,6},{8,7},{9,8},{10,9},{11,1... | collective-permute-start | bytes 786440 | tf_op jit(solution)/shard_map/while/body/eval_jaxpr/ppermute | solution.py:22
  291.3 17.2 %collective-permute-start.2 = (f32[128,4,128]{2,1,0:T(4,128)S(1)}, f32[128,4,128]{2,1,0:T(4,128)S(1)}, u32[]{:S(2)}, u32[]{:S(2)}) collective-permute-start(f32[128,4,128]{2,1,0:T(4,128)S(1)} %get-tuple-element.350), channel_id=1, source_target_pairs={{0,1},{1,2},{2,3},{3,4},{4,5},{5,6},{6,7},{7,8},{8,9},{9,10},{10,1... | collective-permute-start | bytes 786440 | tf_op jit(solution)/shard_map/while/body/eval_jaxpr/ppermute | solution.py:21
  324.4 16.8 %collective-permute-start.4 = (f32[128,4,128]{2,1,0:T(4,128)S(1)}, f32[128,4,128]{2,1,0:T(4,128)S(1)}, u32[]{:S(2)}, u32[]{:S(2)}) collective-permute-start(f32[128,4,128]{2,1,0:T(4,128)S(1)} %get-tuple-element.385), channel_id=1, source_target_pairs={{0,1},{1,2},{2,3},{3,4},{4,5},{5,6},{6,7},{7,8},{8,9},{9,10},{10,1... | collective-permute-start | bytes 786440 | tf_op jit(solution)/shard_map/while/body/eval_jaxpr/ppermute | solution.py:21
  327.4 13.8 %collective-permute-start.5 = (f32[128,4,128]{2,1,0:T(4,128)}, f32[128,4,128]{2,1,0:T(4,128)S(1)}, u32[]{:S(2)}, u32[]{:S(2)}) collective-permute-start(f32[128,4,128]{2,1,0:T(4,128)} %get-tuple-element.384), channel_id=1, source_target_pairs={{1,0},{2,1},{3,2},{4,3},{5,4},{6,5},{7,6},{8,7},{9,8},{10,9},{11,1... | collective-permute-start | bytes 786440 | tf_op jit(solution)/shard_map/while/body/eval_jaxpr/ppermute | solution.py:22
  332.2 17.2 %collective-permute-start.2 = (f32[128,4,128]{2,1,0:T(4,128)S(1)}, f32[128,4,128]{2,1,0:T(4,128)S(1)}, u32[]{:S(2)}, u32[]{:S(2)}) collective-permute-start(f32[128,4,128]{2,1,0:T(4,128)S(1)} %get-tuple-element.350), channel_id=1, source_target_pairs={{0,1},{1,2},{2,3},{3,4},{4,5},{5,6},{6,7},{7,8},{8,9},{9,10},{10,1... | collective-permute-start | bytes 786440 | tf_op jit(solution)/shard_map/while/body/eval_jaxpr/ppermute | solution.py:21
  365.3 16.8 %collective-permute-start.4 = (f32[128,4,128]{2,1,0:T(4,128)S(1)}, f32[128,4,128]{2,1,0:T(4,128)S(1)}, u32[]{:S(2)}, u32[]{:S(2)}) collective-permute-start(f32[128,4,128]{2,1,0:T(4,128)S(1)} %get-tuple-element.385), channel_id=1, source_target_pairs={{0,1},{1,2},{2,3},{3,4},{4,5},{5,6},{6,7},{7,8},{8,9},{9,10},{10,1... | collective-permute-start | bytes 786440 | tf_op jit(solution)/shard_map/while/body/eval_jaxpr/ppermute | solution.py:21
  368.4 13.8 %collective-permute-start.5 = (f32[128,4,128]{2,1,0:T(4,128)}, f32[128,4,128]{2,1,0:T(4,128)S(1)}, u32[]{:S(2)}, u32[]{:S(2)}) collective-permute-start(f32[128,4,128]{2,1,0:T(4,128)} %get-tuple-element.384), channel_id=1, source_target_pairs={{1,0},{2,1},{3,2},{4,3},{5,4},{6,5},{7,6},{8,7},{9,8},{10,9},{11,1... | collective-permute-start | bytes 786440 | tf_op jit(solution)/shard_map/while/body/eval_jaxpr/ppermute | solution.py:22
  373.2 17.2 %collective-permute-start.2 = (f32[128,4,128]{2,1,0:T(4,128)S(1)}, f32[128,4,128]{2,1,0:T(4,128)S(1)}, u32[]{:S(2)}, u32[]{:S(2)}) collective-permute-start(f32[128,4,128]{2,1,0:T(4,128)S(1)} %get-tuple-element.350), channel_id=1, source_target_pairs={{0,1},{1,2},{2,3},{3,4},{4,5},{5,6},{6,7},{7,8},{8,9},{9,10},{10,1... | collective-permute-start | bytes 786440 | tf_op jit(solution)/shard_map/while/body/eval_jaxpr/ppermute | solution.py:21
  406.3 16.8 %collective-permute-start.4 = (f32[128,4,128]{2,1,0:T(4,128)S(1)}, f32[128,4,128]{2,1,0:T(4,128)S(1)}, u32[]{:S(2)}, u32[]{:S(2)}) collective-permute-start(f32[128,4,128]{2,1,0:T(4,128)S(1)} %get-tuple-element.385), channel_id=1, source_target_pairs={{0,1},{1,2},{2,3},{3,4},{4,5},{5,6},{6,7},{7,8},{8,9},{9,10},{10,1... | collective-permute-start | bytes 786440 | tf_op jit(solution)/shard_map/while/body/eval_jaxpr/ppermute | solution.py:21
  409.3 13.8 %collective-permute-start.5 = (f32[128,4,128]{2,1,0:T(4,128)}, f32[128,4,128]{2,1,0:T(4,128)S(1)}, u32[]{:S(2)}, u32[]{:S(2)}) collective-permute-start(f32[128,4,128]{2,1,0:T(4,128)} %get-tuple-element.384), channel_id=1, source_target_pairs={{1,0},{2,1},{3,2},{4,3},{5,4},{6,5},{7,6},{8,7},{9,8},{10,9},{11,1... | collective-permute-start | bytes 786440 | tf_op jit(solution)/shard_map/while/body/eval_jaxpr/ppermute | solution.py:22
  414.1 17.2 %collective-permute-start.2 = (f32[128,4,128]{2,1,0:T(4,128)S(1)}, f32[128,4,128]{2,1,0:T(4,128)S(1)}, u32[]{:S(2)}, u32[]{:S(2)}) collective-permute-start(f32[128,4,128]{2,1,0:T(4,128)S(1)} %get-tuple-element.350), channel_id=1, source_target_pairs={{0,1},{1,2},{2,3},{3,4},{4,5},{5,6},{6,7},{7,8},{8,9},{9,10},{10,1... | collective-permute-start | bytes 786440 | tf_op jit(solution)/shard_map/while/body/eval_jaxpr/ppermute | solution.py:21
  441.7 26.9 %all-to-all-start.1 = ((f32[128,1,8,128]{3,2,1,0:T(8,128)}), f32[128,1,8,128]{3,2,1,0:T(8,128)S(1)}, u32[]{:S(2)}, u32[]{:S(2)}) async-start(f32[128,1,8,128]{3,2,1,0:T(8,128)} %multiply_bitcast_fusion), calls=%async_computation.1 | async-start | bytes 1048576 | tf_op jit(solution)/shard_map/all_to_all | solution.py:192
  (201 other events, 1548.7 us)

commit v15 on v14

--- a/solution.py
+++ b/solution.py
@@ -127,8 +127,16 @@
 
 def spread_points(tables, amounts):
     rows_y, places = tables
-    weighted = places[:, None, :] * jnp.transpose(amounts)[:, :, None]
-    return jnp.einsum("ny,nsc->syc", rows_y, weighted, precision=lax.Precision.HIGHEST)
+    rows_y = rows_y.astype(jnp.bfloat16)
+    rest = jnp.transpose(amounts)
+    total = None
+    for _ in range(3):
+        piece = rest.astype(jnp.bfloat16)
+        rest = rest - piece.astype(jnp.float32)
+        weighted = places.astype(jnp.bfloat16)[:, None, :] * piece[:, :, None]
+        term = jnp.einsum("ny,nsc->syc", rows_y, weighted, preferred_element_type=jnp.float32)
+        total = term if total is None else total + term
+    return total
 
 
 def shards(older_fields, fields_now, velocity, aperture, source_pos, wavelet, receiver_pos, traces):

time: 474 us -> 473 us (level)
    dot_general x2 -> x6, matrix products: 11 us -> 9.97 us  [spread_points(): jnp.einsum('ny,nsc->syc', rows_y, weighted, preferred_element_type=jnp.fl...]
where the time goes in v15:
time: 473 us; the launch traced here: 469 us
  starting transfers between devices  274 us (58%)
  Pallas kernels  136 us (29%)
  local copies, waits for them, and re-layouts  23.2 us (5%)
  waiting for transfers between devices  11.6 us (2%)
  matrix products  10.6 us (2%)
  other arithmetic  10.3 us (2%)
    ppermute x40, starting transfers between devices, trade_halos(): low = lax.ppermute(tail, axis, [(i, (i + 1) % count) for i in range(ends)])  202 us
    pallas_call x40, Pallas kernels, wave_call(): pl.pallas_call(functools.partial(wave_kernel, with_image), out_shape=tupl...  136 us
    ppermute x40, starting transfers between devices, trade_halos(): high = lax.ppermute(head, axis, [((i + 1) % count, i) for i in range(ends)])  51.7 us
    all_to_all x1, starting transfers between devices, shards(): lax.all_to_all(outgoing, 'dom', split_axis=0, concat_axis=1, tiled=True)  12.4 us
    all_to_all x1, waiting for transfers between devices, shards(): lax.all_to_all(outgoing, 'dom', split_axis=0, concat_axis=1, tiled=True)  11.3 us
    while x280, local copies, waits for them, and re-layouts  10.3 us
    dot_general x6, matrix products, spread_points(): jnp.einsum('ny,nsc->syc', rows_y, weighted, preferred_element_type=jnp.fl...  9.97 us
  transfers between devices with their start and end apart: 82, of which 1 were waited for; matrix products, arithmetic and copies ran while one was open for 6% of the time, Pallas kernels for 21%

profile of v15, /device:TPU:0, one launch (start us, length us, event | category | flops | bytes accessed | tf_op | source)
XLA Modules:
  0.0 469.3 jit_solution(15006008718123125746)
XLA Ops:
  3.7 7.4 %all-to-all-start = ((f32[8,16,8,128]{3,2,0,1:T(8,128)}), f32[8,16,8,128]{3,2,0,1:T(8,128)S(1)}, u32[]{:S(2)}, u32[]{:S(2)}) async-start(f32[8,16,8,128]{3,2,0,1:T(8,128)} %select_bitcast_fusion), calls=%async_computation | async-start | bytes 1048576 | tf_op jit(solution)/shard_map/all_to_all | solution.py:152
  35.4 403.4 %while.29 = (s32[]{:T(128)}, f32[128,8,128]{2,1,0:T(8,128)}, f32[128,8,128]{2,1,0:T(8,128)S(1)}, f32[128,4,128]{2,1,0:T(4,128)}, f32[128,4,128]{2,1,0:T(4,128)},...) while((s32[]{:T(128)}, f32[128,8,128]{2,1,0:T(8,128)}, ...), condition=%wide.region_1.2_spmd, body=%wide.region_0.1_spmd.sunk | while | flops 31457284 | bytes 67109736 | solution.py:189
  39.1 4.2 collective-permute-start.4
  48.0 4.6 collective-permute-start.2
  56.9 3.9 collective-permute-start.6
  70.6 6.1 %collective-permute-start = (f32[128,4,128]{2,1,0:T(4,128)}, f32[128,4,128]{2,1,0:T(4,128)S(1)}, u32[]{:S(2)}, u32[]{:S(2)}) collective-permute-start(f32[128,4,128]{2,1,0:T(4,128)} %get-tuple-element.385), channel_id=1, source_target_pairs={{0,1},{1,2},{2,3},{3,4},{4,5},{5,6},{6,7},{7,8},{8,9},{9,10},{10,1... | collective-permute-start | bytes 786440 | tf_op jit(solution)/shard_map/while/body/eval_jaxpr/ppermute | solution.py:21
  85.9 7.5 %collective-permute-start.2 = (f32[128,4,128]{2,1,0:T(4,128)S(1)}, f32[128,4,128]{2,1,0:T(4,128)S(1)}, u32[]{:S(2)}, u32[]{:S(2)}) collective-permute-start(f32[128,4,128]{2,1,0:T(4,128)S(1)} %get-tuple-element.354), channel_id=1, source_target_pairs={{0,1},{1,2},{2,3},{3,4},{4,5},{5,6},{6,7},{7,8},{8,9},{9,10},{10,1... | collective-permute-start | bytes 786440 | tf_op jit(solution)/shard_map/while/body/eval_jaxpr/ppermute | solution.py:21
  97.6 3.9 collective-permute-start.6
  111.3 6.2 %collective-permute-start = (f32[128,4,128]{2,1,0:T(4,128)}, f32[128,4,128]{2,1,0:T(4,128)S(1)}, u32[]{:S(2)}, u32[]{:S(2)}) collective-permute-start(f32[128,4,128]{2,1,0:T(4,128)} %get-tuple-element.385), channel_id=1, source_target_pairs={{0,1},{1,2},{2,3},{3,4},{4,5},{5,6},{6,7},{7,8},{8,9},{9,10},{10,1... | collective-permute-start | bytes 786440 | tf_op jit(solution)/shard_map/while/body/eval_jaxpr/ppermute | solution.py:21
  126.7 7.6 %collective-permute-start.2 = (f32[128,4,128]{2,1,0:T(4,128)S(1)}, f32[128,4,128]{2,1,0:T(4,128)S(1)}, u32[]{:S(2)}, u32[]{:S(2)}) collective-permute-start(f32[128,4,128]{2,1,0:T(4,128)S(1)} %get-tuple-element.354), channel_id=1, source_target_pairs={{0,1},{1,2},{2,3},{3,4},{4,5},{5,6},{6,7},{7,8},{8,9},{9,10},{10,1... | collective-permute-start | bytes 786440 | tf_op jit(solution)/shard_map/while/body/eval_jaxpr/ppermute | solution.py:21
  138.6 3.9 collective-permute-start.6
  152.3 6.2 %collective-permute-start = (f32[128,4,128]{2,1,0:T(4,128)}, f32[128,4,128]{2,1,0:T(4,128)S(1)}, u32[]{:S(2)}, u32[]{:S(2)}) collective-permute-start(f32[128,4,128]{2,1,0:T(4,128)} %get-tuple-element.385), channel_id=1, source_target_pairs={{0,1},{1,2},{2,3},{3,4},{4,5},{5,6},{6,7},{7,8},{8,9},{9,10},{10,1... | collective-permute-start | bytes 786440 | tf_op jit(solution)/shard_map/while/body/eval_jaxpr/ppermute | solution.py:21
  167.6 7.6 %collective-permute-start.2 = (f32[128,4,128]{2,1,0:T(4,128)S(1)}, f32[128,4,128]{2,1,0:T(4,128)S(1)}, u32[]{:S(2)}, u32[]{:S(2)}) collective-permute-start(f32[128,4,128]{2,1,0:T(4,128)S(1)} %get-tuple-element.354), channel_id=1, source_target_pairs={{0,1},{1,2},{2,3},{3,4},{4,5},{5,6},{6,7},{7,8},{8,9},{9,10},{10,1... | collective-permute-start | bytes 786440 | tf_op jit(solution)/shard_map/while/body/eval_jaxpr/ppermute | solution.py:21
  179.5 3.9 collective-permute-start.6
  193.2 6.2 %collective-permute-start = (f32[128,4,128]{2,1,0:T(4,128)}, f32[128,4,128]{2,1,0:T(4,128)S(1)}, u32[]{:S(2)}, u32[]{:S(2)}) collective-permute-start(f32[128,4,128]{2,1,0:T(4,128)} %get-tuple-element.385), channel_id=1, source_target_pairs={{0,1},{1,2},{2,3},{3,4},{4,5},{5,6},{6,7},{7,8},{8,9},{9,10},{10,1... | collective-permute-start | bytes 786440 | tf_op jit(solution)/shard_map/while/body/eval_jaxpr/ppermute | solution.py:21
  208.6 7.6 %collective-permute-start.2 = (f32[128,4,128]{2,1,0:T(4,128)S(1)}, f32[128,4,128]{2,1,0:T(4,128)S(1)}, u32[]{:S(2)}, u32[]{:S(2)}) collective-permute-start(f32[128,4,128]{2,1,0:T(4,128)S(1)} %get-tuple-element.354), channel_id=1, source_target_pairs={{0,1},{1,2},{2,3},{3,4},{4,5},{5,6},{6,7},{7,8},{8,9},{9,10},{10,1... | collective-permute-start | bytes 786440 | tf_op jit(solution)/shard_map/while/body/eval_jaxpr/ppermute | solution.py:21
  220.5 3.9 collective-permute-start.6
  234.2 6.2 %collective-permute-start = (f32[128,4,128]{2,1,0:T(4,128)}, f32[128,4,128]{2,1,0:T(4,128)S(1)}, u32[]{:S(2)}, u32[]{:S(2)}) collective-permute-start(f32[128,4,128]{2,1,0:T(4,128)} %get-tuple-element.385), channel_id=1, source_target_pairs={{0,1},{1,2},{2,3},{3,4},{4,5},{5,6},{6,7},{7,8},{8,9},{9,10},{10,1... | collective-permute-start | bytes 786440 | tf_op jit(solution)/shard_map/while/body/eval_jaxpr/ppermute | solution.py:21
  249.5 7.6 %collective-permute-start.2 = (f32[128,4,128]{2,1,0:T(4,128)S(1)}, f32[128,4,128]{2,1,0:T(4,128)S(1)}, u32[]{:S(2)}, u32[]{:S(2)}) collective-permute-start(f32[128,4,128]{2,1,0:T(4,128)S(1)} %get-tuple-element.354), channel_id=1, source_target_pairs={{0,1},{1,2},{2,3},{3,4},{4,5},{5,6},{6,7},{7,8},{8,9},{9,10},{10,1... | collective-permute-start | bytes 786440 | tf_op jit(solution)/shard_map/while/body/eval_jaxpr/ppermute | solution.py:21
  261.4 3.9 collective-permute-start.6
  275.1 6.2 %collective-permute-start = (f32[128,4,128]{2,1,0:T(4,128)}, f32[128,4,128]{2,1,0:T(4,128)S(1)}, u32[]{:S(2)}, u32[]{:S(2)}) collective-permute-start(f32[128,4,128]{2,1,0:T(4,128)} %get-tuple-element.385), channel_id=1, source_target_pairs={{0,1},{1,2},{2,3},{3,4},{4,5},{5,6},{6,7},{7,8},{8,9},{9,10},{10,1... | collective-permute-start | bytes 786440 | tf_op jit(solution)/shard_map/while/body/eval_jaxpr/ppermute | solution.py:21
  290.5 7.6 %collective-permute-start.2 = (f32[128,4,128]{2,1,0:T(4,128)S(1)}, f32[128,4,128]{2,1,0:T(4,128)S(1)}, u32[]{:S(2)}, u32[]{:S(2)}) collective-permute-start(f32[128,4,128]{2,1,0:T(4,128)S(1)} %get-tuple-element.354), channel_id=1, source_target_pairs={{0,1},{1,2},{2,3},{3,4},{4,5},{5,6},{6,7},{7,8},{8,9},{9,10},{10,1... | collective-permute-start | bytes 786440 | tf_op jit(solution)/shard_map/while/body/eval_jaxpr/ppermute | solution.py:21
  302.3 3.9 collective-permute-start.6
  316.0 6.2 %collective-permute-start = (f32[128,4,128]{2,1,0:T(4,128)}, f32[128,4,128]{2,1,0:T(4,128)S(1)}, u32[]{:S(2)}, u32[]{:S(2)}) collective-permute-start(f32[128,4,128]{2,1,0:T(4,128)} %get-tuple-element.385), channel_id=1, source_target_pairs={{0,1},{1,2},{2,3},{3,4},{4,5},{5,6},{6,7},{7,8},{8,9},{9,10},{10,1... | collective-permute-start | bytes 786440 | tf_op jit(solution)/shard_map/while/body/eval_jaxpr/ppermute | solution.py:21
  331.4 7.6 %collective-permute-start.2 = (f32[128,4,128]{2,1,0:T(4,128)S(1)}, f32[128,4,128]{2,1,0:T(4,128)S(1)}, u32[]{:S(2)}, u32[]{:S(2)}) collective-permute-start(f32[128,4,128]{2,1,0:T(4,128)S(1)} %get-tuple-element.354), channel_id=1, source_target_pairs={{0,1},{1,2},{2,3},{3,4},{4,5},{5,6},{6,7},{7,8},{8,9},{9,10},{10,1... | collective-permute-start | bytes 786440 | tf_op jit(solution)/shard_map/while/body/eval_jaxpr/ppermute | solution.py:21
  343.3 3.9 collective-permute-start.6
  357.0 6.2 %collective-permute-start = (f32[128,4,128]{2,1,0:T(4,128)}, f32[128,4,128]{2,1,0:T(4,128)S(1)}, u32[]{:S(2)}, u32[]{:S(2)}) collective-permute-start(f32[128,4,128]{2,1,0:T(4,128)} %get-tuple-element.385), channel_id=1, source_target_pairs={{0,1},{1,2},{2,3},{3,4},{4,5},{5,6},{6,7},{7,8},{8,9},{9,10},{10,1... | collective-permute-start | bytes 786440 | tf_op jit(solution)/shard_map/while/body/eval_jaxpr/ppermute | solution.py:21
  372.3 7.6 %collective-permute-start.2 = (f32[128,4,128]{2,1,0:T(4,128)S(1)}, f32[128,4,128]{2,1,0:T(4,128)S(1)}, u32[]{:S(2)}, u32[]{:S(2)}) collective-permute-start(f32[128,4,128]{2,1,0:T(4,128)S(1)} %get-tuple-element.354), channel_id=1, source_target_pairs={{0,1},{1,2},{2,3},{3,4},{4,5},{5,6},{6,7},{7,8},{8,9},{9,10},{10,1... | collective-permute-start | bytes 786440 | tf_op jit(solution)/shard_map/while/body/eval_jaxpr/ppermute | solution.py:21
  397.9 6.2 %collective-permute-start = (f32[128,4,128]{2,1,0:T(4,128)}, f32[128,4,128]{2,1,0:T(4,128)S(1)}, u32[]{:S(2)}, u32[]{:S(2)}) collective-permute-start(f32[128,4,128]{2,1,0:T(4,128)} %get-tuple-element.385), channel_id=1, source_target_pairs={{0,1},{1,2},{2,3},{3,4},{4,5},{5,6},{6,7},{7,8},{8,9},{9,10},{10,1... | collective-permute-start | bytes 786440 | tf_op jit(solution)/shard_map/while/body/eval_jaxpr/ppermute | solution.py:21
  413.3 7.6 %collective-permute-start.2 = (f32[128,4,128]{2,1,0:T(4,128)S(1)}, f32[128,4,128]{2,1,0:T(4,128)S(1)}, u32[]{:S(2)}, u32[]{:S(2)}) collective-permute-start(f32[128,4,128]{2,1,0:T(4,128)S(1)} %get-tuple-element.354), channel_id=1, source_target_pairs={{0,1},{1,2},{2,3},{3,4},{4,5},{5,6},{6,7},{7,8},{8,9},{9,10},{10,1... | collective-permute-start | bytes 786440 | tf_op jit(solution)/shard_map/while/body/eval_jaxpr/ppermute | solution.py:21
  440.8 12.4 %all-to-all-start.1 = ((f32[128,1,8,128]{3,2,1,0:T(8,128)}), f32[128,1,8,128]{3,2,1,0:T(8,128)S(1)}, u32[]{:S(2)}, u32[]{:S(2)}) async-start(f32[128,1,8,128]{3,2,1,0:T(8,128)} %multiply_bitcast_fusion), calls=%async_computation.1 | async-start | bytes 1048576 | tf_op jit(solution)/shard_map/all_to_all | solution.py:200
  456.3 11.3 %all-to-all-done.1 = f32[128,1,8,128]{3,2,1,0:T(8,128)S(1)} async-done(((f32[128,1,8,128]{3,2,1,0:T(8,128)}), f32[128,1,8,128]{3,2,1,0:T(8,128)S(1)}, u32[]{:S(2)}, u32[]{:S(2)}) %all-to-all-start.1) | async-done | bytes 524320 | tf_op jit(solution)/shard_map/all_to_all | solution.py:200
  (520 shorter events, 269.8 us)
Async XLA Ops:
  3.7 30.9 %all-to-all-start = ((f32[8,16,8,128]{3,2,0,1:T(8,128)}), f32[8,16,8,128]{3,2,0,1:T(8,128)S(1)}, u32[]{:S(2)}, u32[]{:S(2)}) async-start(f32[8,16,8,128]{3,2,0,1:T(8,128)} %select_bitcast_fusion), calls=%async_computation | async-start | bytes 1048576 | tf_op jit(solution)/shard_map/all_to_all | solution.py:152
  39.1 14.9 %collective-permute-start.4 = (f32[128,4,128]{2,1,0:T(4,128)S(1)}, f32[128,4,128]{2,1,0:T(4,128)S(1)}, u32[]{:S(2)}, u32[]{:S(2)}) collective-permute-start(f32[128,4,128]{2,1,0:T(4,128)S(1)} %get-tuple-element.389), channel_id=1, source_target_pairs={{0,1},{1,2},{2,3},{3,4},{4,5},{5,6},{6,7},{7,8},{8,9},{9,10},{10,1... | collective-permute-start | bytes 786440 | tf_op jit(solution)/shard_map/while/body/eval_jaxpr/ppermute | solution.py:21
  48.0 14.1 %collective-permute-start.2 = (f32[128,4,128]{2,1,0:T(4,128)S(1)}, f32[128,4,128]{2,1,0:T(4,128)S(1)}, u32[]{:S(2)}, u32[]{:S(2)}) collective-permute-start(f32[128,4,128]{2,1,0:T(4,128)S(1)} %get-tuple-element.354), channel_id=1, source_target_pairs={{0,1},{1,2},{2,3},{3,4},{4,5},{5,6},{6,7},{7,8},{8,9},{9,10},{10,1... | collective-permute-start | bytes 786440 | tf_op jit(solution)/shard_map/while/body/eval_jaxpr/ppermute | solution.py:21
  78.0 16.7 %collective-permute-start.4 = (f32[128,4,128]{2,1,0:T(4,128)S(1)}, f32[128,4,128]{2,1,0:T(4,128)S(1)}, u32[]{:S(2)}, u32[]{:S(2)}) collective-permute-start(f32[128,4,128]{2,1,0:T(4,128)S(1)} %get-tuple-element.389), channel_id=1, source_target_pairs={{0,1},{1,2},{2,3},{3,4},{4,5},{5,6},{6,7},{7,8},{8,9},{9,10},{10,1... | collective-permute-start | bytes 786440 | tf_op jit(solution)/shard_map/while/body/eval_jaxpr/ppermute | solution.py:21
  81.1 13.7 %collective-permute-start.5 = (f32[128,4,128]{2,1,0:T(4,128)}, f32[128,4,128]{2,1,0:T(4,128)S(1)}, u32[]{:S(2)}, u32[]{:S(2)}) collective-permute-start(f32[128,4,128]{2,1,0:T(4,128)} %get-tuple-element.388), channel_id=1, source_target_pairs={{1,0},{2,1},{3,2},{4,3},{5,4},{6,5},{7,6},{8,7},{9,8},{10,9},{11,1... | collective-permute-start | bytes 786440 | tf_op jit(solution)/shard_map/while/body/eval_jaxpr/ppermute | solution.py:22
  85.9 17.1 %collective-permute-start.2 = (f32[128,4,128]{2,1,0:T(4,128)S(1)}, f32[128,4,128]{2,1,0:T(4,128)S(1)}, u32[]{:S(2)}, u32[]{:S(2)}) collective-permute-start(f32[128,4,128]{2,1,0:T(4,128)S(1)} %get-tuple-element.354), channel_id=1, source_target_pairs={{0,1},{1,2},{2,3},{3,4},{4,5},{5,6},{6,7},{7,8},{8,9},{9,10},{10,1... | collective-permute-start | bytes 786440 | tf_op jit(solution)/shard_map/while/body/eval_jaxpr/ppermute | solution.py:21
  118.9 16.8 %collective-permute-start.4 = (f32[128,4,128]{2,1,0:T(4,128)S(1)}, f32[128,4,128]{2,1,0:T(4,128)S(1)}, u32[]{:S(2)}, u32[]{:S(2)}) collective-permute-start(f32[128,4,128]{2,1,0:T(4,128)S(1)} %get-tuple-element.389), channel_id=1, source_target_pairs={{0,1},{1,2},{2,3},{3,4},{4,5},{5,6},{6,7},{7,8},{8,9},{9,10},{10,1... | collective-permute-start | bytes 786440 | tf_op jit(solution)/shard_map/while/body/eval_jaxpr/ppermute | solution.py:21
  121.9 13.8 %collective-permute-start.5 = (f32[128,4,128]{2,1,0:T(4,128)}, f32[128,4,128]{2,1,0:T(4,128)S(1)}, u32[]{:S(2)}, u32[]{:S(2)}) collective-permute-start(f32[128,4,128]{2,1,0:T(4,128)} %get-tuple-element.388), channel_id=1, source_target_pairs={{1,0},{2,1},{3,2},{4,3},{5,4},{6,5},{7,6},{8,7},{9,8},{10,9},{11,1... | collective-permute-start | bytes 786440 | tf_op jit(solution)/shard_map/while/body/eval_jaxpr/ppermute | solution.py:22
  126.7 17.2 %collective-permute-start.2 = (f32[128,4,128]{2,1,0:T(4,128)S(1)}, f32[128,4,128]{2,1,0:T(4,128)S(1)}, u32[]{:S(2)}, u32[]{:S(2)}) collective-permute-start(f32[128,4,128]{2,1,0:T(4,128)S(1)} %get-tuple-element.354), channel_id=1, source_target_pairs={{0,1},{1,2},{2,3},{3,4},{4,5},{5,6},{6,7},{7,8},{8,9},{9,10},{10,1... | collective-permute-start | bytes 786440 | tf_op jit(solution)/shard_map/while/body/eval_jaxpr/ppermute | solution.py:21
  159.8 16.8 %collective-permute-start.4 = (f32[128,4,128]{2,1,0:T(4,128)S(1)}, f32[128,4,128]{2,1,0:T(4,128)S(1)}, u32[]{:S(2)}, u32[]{:S(2)}) collective-permute-start(f32[128,4,128]{2,1,0:T(4,128)S(1)} %get-tuple-element.389), channel_id=1, source_target_pairs={{0,1},{1,2},{2,3},{3,4},{4,5},{5,6},{6,7},{7,8},{8,9},{9,10},{10,1... | collective-permute-start | bytes 786440 | tf_op jit(solution)/shard_map/while/body/eval_jaxpr/ppermute | solution.py:21
  162.9 13.8 %collective-permute-start.5 = (f32[128,4,128]{2,1,0:T(4,128)}, f32[128,4,128]{2,1,0:T(4,128)S(1)}, u32[]{:S(2)}, u32[]{:S(2)}) collective-permute-start(f32[128,4,128]{2,1,0:T(4,128)} %get-tuple-element.388), channel_id=1, source_target_pairs={{1,0},{2,1},{3,2},{4,3},{5,4},{6,5},{7,6},{8,7},{9,8},{10,9},{11,1... | collective-permute-start | bytes 786440 | tf_op jit(solution)/shard_map/while/body/eval_jaxpr/ppermute | solution.py:22
  167.6 17.2 %collective-permute-start.2 = (f32[128,4,128]{2,1,0:T(4,128)S(1)}, f32[128,4,128]{2,1,0:T(4,128)S(1)}, u32[]{:S(2)}, u32[]{:S(2)}) collective-permute-start(f32[128,4,128]{2,1,0:T(4,128)S(1)} %get-tuple-element.354), channel_id=1, source_target_pairs={{0,1},{1,2},{2,3},{3,4},{4,5},{5,6},{6,7},{7,8},{8,9},{9,10},{10,1... | collective-permute-start | bytes 786440 | tf_op jit(solution)/shard_map/while/body/eval_jaxpr/ppermute | solution.py:21
  193.2 11.9 %collective-permute-start = (f32[128,4,128]{2,1,0:T(4,128)}, f32[128,4,128]{2,1,0:T(4,128)S(1)}, u32[]{:S(2)}, u32[]{:S(2)}) collective-permute-start(f32[128,4,128]{2,1,0:T(4,128)} %get-tuple-element.385), channel_id=1, source_target_pairs={{0,1},{1,2},{2,3},{3,4},{4,5},{5,6},{6,7},{7,8},{8,9},{9,10},{10,1... | collective-permute-start | bytes 786440 | tf_op jit(solution)/shard_map/while/body/eval_jaxpr/ppermute | solution.py:21
  200.7 16.8 %collective-permute-start.4 = (f32[128,4,128]{2,1,0:T(4,128)S(1)}, f32[128,4,128]{2,1,0:T(4,128)S(1)}, u32[]{:S(2)}, u32[]{:S(2)}) collective-permute-start(f32[128,4,128]{2,1,0:T(4,128)S(1)} %get-tuple-element.389), channel_id=1, source_target_pairs={{0,1},{1,2},{2,3},{3,4},{4,5},{5,6},{6,7},{7,8},{8,9},{9,10},{10,1... | collective-permute-start | bytes 786440 | tf_op jit(solution)/shard_map/while/body/eval_jaxpr/ppermute | solution.py:21
  203.8 13.8 %collective-permute-start.5 = (f32[128,4,128]{2,1,0:T(4,128)}, f32[128,4,128]{2,1,0:T(4,128)S(1)}, u32[]{:S(2)}, u32[]{:S(2)}) collective-permute-start(f32[128,4,128]{2,1,0:T(4,128)} %get-tuple-element.388), channel_id=1, source_target_pairs={{1,0},{2,1},{3,2},{4,3},{5,4},{6,5},{7,6},{8,7},{9,8},{10,9},{11,1... | collective-permute-start | bytes 786440 | tf_op jit(solution)/shard_map/while/body/eval_jaxpr/ppermute | solution.py:22
  208.6 17.2 %collective-permute-start.2 = (f32[128,4,128]{2,1,0:T(4,128)S(1)}, f32[128,4,128]{2,1,0:T(4,128)S(1)}, u32[]{:S(2)}, u32[]{:S(2)}) collective-permute-start(f32[128,4,128]{2,1,0:T(4,128)S(1)} %get-tuple-element.354), channel_id=1, source_target_pairs={{0,1},{1,2},{2,3},{3,4},{4,5},{5,6},{6,7},{7,8},{8,9},{9,10},{10,1... | collective-permute-start | bytes 786440 | tf_op jit(solution)/shard_map/while/body/eval_jaxpr/ppermute | solution.py:21
  241.7 16.8 %collective-permute-start.4 = (f32[128,4,128]{2,1,0:T(4,128)S(1)}, f32[128,4,128]{2,1,0:T(4,128)S(1)}, u32[]{:S(2)}, u32[]{:S(2)}) collective-permute-start(f32[128,4,128]{2,1,0:T(4,128)S(1)} %get-tuple-element.389), channel_id=1, source_target_pairs={{0,1},{1,2},{2,3},{3,4},{4,5},{5,6},{6,7},{7,8},{8,9},{9,10},{10,1... | collective-permute-start | bytes 786440 | tf_op jit(solution)/shard_map/while/body/eval_jaxpr/ppermute | solution.py:21
  244.7 13.8 %collective-permute-start.5 = (f32[128,4,128]{2,1,0:T(4,128)}, f32[128,4,128]{2,1,0:T(4,128)S(1)}, u32[]{:S(2)}, u32[]{:S(2)}) collective-permute-start(f32[128,4,128]{2,1,0:T(4,128)} %get-tuple-element.388), channel_id=1, source_target_pairs={{1,0},{2,1},{3,2},{4,3},{5,4},{6,5},{7,6},{8,7},{9,8},{10,9},{11,1... | collective-permute-start | bytes 786440 | tf_op jit(solution)/shard_map/while/body/eval_jaxpr/ppermute | solution.py:22
  249.5 17.2 %collective-permute-start.2 = (f32[128,4,128]{2,1,0:T(4,128)S(1)}, f32[128,4,128]{2,1,0:T(4,128)S(1)}, u32[]{:S(2)}, u32[]{:S(2)}) collective-permute-start(f32[128,4,128]{2,1,0:T(4,128)S(1)} %get-tuple-element.354), channel_id=1, source_target_pairs={{0,1},{1,2},{2,3},{3,4},{4,5},{5,6},{6,7},{7,8},{8,9},{9,10},{10,1... | collective-permute-start | bytes 786440 | tf_op jit(solution)/shard_map/while/body/eval_jaxpr/ppermute | solution.py:21
  282.6 16.8 %collective-permute-start.4 = (f32[128,4,128]{2,1,0:T(4,128)S(1)}, f32[128,4,128]{2,1,0:T(4,128)S(1)}, u32[]{:S(2)}, u32[]{:S(2)}) collective-permute-start(f32[128,4,128]{2,1,0:T(4,128)S(1)} %get-tuple-element.389), channel_id=1, source_target_pairs={{0,1},{1,2},{2,3},{3,4},{4,5},{5,6},{6,7},{7,8},{8,9},{9,10},{10,1... | collective-permute-start | bytes 786440 | tf_op jit(solution)/shard_map/while/body/eval_jaxpr/ppermute | solution.py:21
  285.7 13.8 %collective-permute-start.5 = (f32[128,4,128]{2,1,0:T(4,128)}, f32[128,4,128]{2,1,0:T(4,128)S(1)}, u32[]{:S(2)}, u32[]{:S(2)}) collective-permute-start(f32[128,4,128]{2,1,0:T(4,128)} %get-tuple-element.388), channel_id=1, source_target_pairs={{1,0},{2,1},{3,2},{4,3},{5,4},{6,5},{7,6},{8,7},{9,8},{10,9},{11,1... | collective-permute-start | bytes 786440 | tf_op jit(solution)/shard_map/while/body/eval_jaxpr/ppermute | solution.py:22
  290.5 17.2 %collective-permute-start.2 = (f32[128,4,128]{2,1,0:T(4,128)S(1)}, f32[128,4,128]{2,1,0:T(4,128)S(1)}, u32[]{:S(2)}, u32[]{:S(2)}) collective-permute-start(f32[128,4,128]{2,1,0:T(4,128)S(1)} %get-tuple-element.354), channel_id=1, source_target_pairs={{0,1},{1,2},{2,3},{3,4},{4,5},{5,6},{6,7},{7,8},{8,9},{9,10},{10,1... | collective-permute-start | bytes 786440 | tf_op jit(solution)/shard_map/while/body/eval_jaxpr/ppermute | solution.py:21
  323.5 16.8 %collective-permute-start.4 = (f32[128,4,128]{2,1,0:T(4,128)S(1)}, f32[128,4,128]{2,1,0:T(4,128)S(1)}, u32[]{:S(2)}, u32[]{:S(2)}) collective-permute-start(f32[128,4,128]{2,1,0:T(4,128)S(1)} %get-tuple-element.389), channel_id=1, source_target_pairs={{0,1},{1,2},{2,3},{3,4},{4,5},{5,6},{6,7},{7,8},{8,9},{9,10},{10,1... | collective-permute-start | bytes 786440 | tf_op jit(solution)/shard_map/while/body/eval_jaxpr/ppermute | solution.py:21
  326.6 13.8 %collective-permute-start.5 = (f32[128,4,128]{2,1,0:T(4,128)}, f32[128,4,128]{2,1,0:T(4,128)S(1)}, u32[]{:S(2)}, u32[]{:S(2)}) collective-permute-start(f32[128,4,128]{2,1,0:T(4,128)} %get-tuple-element.388), channel_id=1, source_target_pairs={{1,0},{2,1},{3,2},{4,3},{5,4},{6,5},{7,6},{8,7},{9,8},{10,9},{11,1... | collective-permute-start | bytes 786440 | tf_op jit(solution)/shard_map/while/body/eval_jaxpr/ppermute | solution.py:22
  331.4 17.2 %collective-permute-start.2 = (f32[128,4,128]{2,1,0:T(4,128)S(1)}, f32[128,4,128]{2,1,0:T(4,128)S(1)}, u32[]{:S(2)}, u32[]{:S(2)}) collective-permute-start(f32[128,4,128]{2,1,0:T(4,128)S(1)} %get-tuple-element.354), channel_id=1, source_target_pairs={{0,1},{1,2},{2,3},{3,4},{4,5},{5,6},{6,7},{7,8},{8,9},{9,10},{10,1... | collective-permute-start | bytes 786440 | tf_op jit(solution)/shard_map/while/body/eval_jaxpr/ppermute | solution.py:21
  364.5 16.8 %collective-permute-start.4 = (f32[128,4,128]{2,1,0:T(4,128)S(1)}, f32[128,4,128]{2,1,0:T(4,128)S(1)}, u32[]{:S(2)}, u32[]{:S(2)}) collective-permute-start(f32[128,4,128]{2,1,0:T(4,128)S(1)} %get-tuple-element.389), channel_id=1, source_target_pairs={{0,1},{1,2},{2,3},{3,4},{4,5},{5,6},{6,7},{7,8},{8,9},{9,10},{10,1... | collective-permute-start | bytes 786440 | tf_op jit(solution)/shard_map/while/body/eval_jaxpr/ppermute | solution.py:21
  367.5 13.8 %collective-permute-start.5 = (f32[128,4,128]{2,1,0:T(4,128)}, f32[128,4,128]{2,1,0:T(4,128)S(1)}, u32[]{:S(2)}, u32[]{:S(2)}) collective-permute-start(f32[128,4,128]{2,1,0:T(4,128)} %get-tuple-element.388), channel_id=1, source_target_pairs={{1,0},{2,1},{3,2},{4,3},{5,4},{6,5},{7,6},{8,7},{9,8},{10,9},{11,1... | collective-permute-start | bytes 786440 | tf_op jit(solution)/shard_map/while/body/eval_jaxpr/ppermute | solution.py:22
  372.3 17.2 %collective-permute-start.2 = (f32[128,4,128]{2,1,0:T(4,128)S(1)}, f32[128,4,128]{2,1,0:T(4,128)S(1)}, u32[]{:S(2)}, u32[]{:S(2)}) collective-permute-start(f32[128,4,128]{2,1,0:T(4,128)S(1)} %get-tuple-element.354), channel_id=1, source_target_pairs={{0,1},{1,2},{2,3},{3,4},{4,5},{5,6},{6,7},{7,8},{8,9},{9,10},{10,1... | collective-permute-start | bytes 786440 | tf_op jit(solution)/shard_map/while/body/eval_jaxpr/ppermute | solution.py:21
  405.4 16.8 %collective-permute-start.4 = (f32[128,4,128]{2,1,0:T(4,128)S(1)}, f32[128,4,128]{2,1,0:T(4,128)S(1)}, u32[]{:S(2)}, u32[]{:S(2)}) collective-permute-start(f32[128,4,128]{2,1,0:T(4,128)S(1)} %get-tuple-element.389), channel_id=1, source_target_pairs={{0,1},{1,2},{2,3},{3,4},{4,5},{5,6},{6,7},{7,8},{8,9},{9,10},{10,1... | collective-permute-start | bytes 786440 | tf_op jit(solution)/shard_map/while/body/eval_jaxpr/ppermute | solution.py:21
  408.5 13.8 %collective-permute-start.5 = (f32[128,4,128]{2,1,0:T(4,128)}, f32[128,4,128]{2,1,0:T(4,128)S(1)}, u32[]{:S(2)}, u32[]{:S(2)}) collective-permute-start(f32[128,4,128]{2,1,0:T(4,128)} %get-tuple-element.388), channel_id=1, source_target_pairs={{1,0},{2,1},{3,2},{4,3},{5,4},{6,5},{7,6},{8,7},{9,8},{10,9},{11,1... | collective-permute-start | bytes 786440 | tf_op jit(solution)/shard_map/while/body/eval_jaxpr/ppermute | solution.py:22
  413.3 17.2 %collective-permute-start.2 = (f32[128,4,128]{2,1,0:T(4,128)S(1)}, f32[128,4,128]{2,1,0:T(4,128)S(1)}, u32[]{:S(2)}, u32[]{:S(2)}) collective-permute-start(f32[128,4,128]{2,1,0:T(4,128)S(1)} %get-tuple-element.354), channel_id=1, source_target_pairs={{0,1},{1,2},{2,3},{3,4},{4,5},{5,6},{6,7},{7,8},{8,9},{9,10},{10,1... | collective-permute-start | bytes 786440 | tf_op jit(solution)/shard_map/while/body/eval_jaxpr/ppermute | solution.py:21
  440.8 26.8 %all-to-all-start.1 = ((f32[128,1,8,128]{3,2,1,0:T(8,128)}), f32[128,1,8,128]{3,2,1,0:T(8,128)S(1)}, u32[]{:S(2)}, u32[]{:S(2)}) async-start(f32[128,1,8,128]{3,2,1,0:T(8,128)} %multiply_bitcast_fusion), calls=%async_computation.1 | async-start | bytes 1048576 | tf_op jit(solution)/shard_map/all_to_all | solution.py:200
  (201 other events, 1546.0 us)

commit v16 on v14

--- a/solution.py
+++ b/solution.py
@@ -12,6 +12,7 @@
 center_weight = 3.0 * (-205.0 / 72.0)
 HALO = 4
 ROWS = 128
+TRIP = 4
 XOFF = 8
 
 
@@ -168,7 +169,9 @@
         return (cur0, new0, head0, tail0), (cur1, new1, head1, tail1), image_acc
 
     def pair(index, state):
-        return advance(2 * index + 1, advance(2 * index, state))
+        for offset in range(TRIP):
+            state = advance(TRIP * index + offset, state)
+        return state
 
     def edges(field):
         return (field[:, :HALO], field[:, cells_x - HALO :])
@@ -178,9 +181,9 @@
         (older_fields[1], fields_now[1]) + edges(fields_now[1]),
         image_zero,
     )
-    state = lax.fori_loop(0, steps_total // 2, pair, start)
-    if steps_total % 2:
-        state = advance(steps_total - 1, state)
+    state = lax.fori_loop(0, steps_total // TRIP, pair, start)
+    for moment in range(steps_total - steps_total % TRIP, steps_total):
+        state = advance(moment, state)
     (prev0, cur0, _, _), (prev1, cur1, _, _), image_acc = state
     previous = jnp.stack([prev0, prev1])
     current = jnp.stack([cur0, cur1])

time: 474 us -> 467 us (0.985)
  local copies, waits for them, and re-layouts: 23.2 us -> 18 us
    while x280 -> x200, local copies, waits for them, and re-layouts: 10.3 us -> 4.48 us
  transfers between devices with their start and end apart: 82 -> 82, of which waited for: 1 -> 6; matrix products, arithmetic and copies ran while one was open for 6% -> 6% of each run, Pallas kernels for 21% -> 25%
where the time goes in v16:
time: 467 us; the launch traced here: 463 us
  starting transfers between devices  271 us (58%)
  Pallas kernels  136 us (29%)
  local copies, waits for them, and re-layouts  18 us (4%)
  waiting for transfers between devices  13.6 us (3%)
  matrix products  11.7 us (3%)
  other arithmetic  10.1 us (2%)
    ppermute x40, starting transfers between devices, trade_halos(): low = lax.ppermute(tail, axis, [(i, (i + 1) % count) for i in range(ends)])  198 us
    pallas_call x40, Pallas kernels, wave_call(): pl.pallas_call(functools.partial(wave_kernel, with_image), out_shape=tupl...  136 us
    ppermute x40, starting transfers between devices, trade_halos(): high = lax.ppermute(head, axis, [((i + 1) % count, i) for i in range(ends)])  51.7 us
    all_to_all x1, starting transfers between devices, shards(): lax.all_to_all(outgoing, 'dom', split_axis=0, concat_axis=1, tiled=True)  13.7 us
    all_to_all x1, waiting for transfers between devices, shards(): lax.all_to_all(outgoing, 'dom', split_axis=0, concat_axis=1, tiled=True)  11.3 us
    dot_general x2, matrix products, spread_points(): jnp.einsum('ny,nsc->syc', rows_y, weighted, precision=lax.Precision.HIGHEST)  11 us
  transfers between devices with their start and end apart: 82, of which 6 were waited for; matrix products, arithmetic and copies ran while one was open for 6% of the time, Pallas kernels for 25%

profile of v16, /device:TPU:0, one launch (start us, length us, event | category | flops | bytes accessed | tf_op | source)
XLA Modules:
  0.0 463.3 jit_solution(1120291753714507824)
XLA Ops:
  3.6 7.4 %all-to-all-start = ((f32[8,16,8,128]{3,2,0,1:T(8,128)}), f32[8,16,8,128]{3,2,0,1:T(8,128)S(1)}, u32[]{:S(2)}, u32[]{:S(2)}) async-start(f32[8,16,8,128]{3,2,0,1:T(8,128)} %select_bitcast_fusion), calls=%async_computation | async-start | bytes 1048576 | tf_op jit(solution)/shard_map/all_to_all | solution.py:145
  12.2 10.5 %fusion = f32[20,32,128]{2,1,0:T(8,128)S(1)} fusion(f32[8192,20]{0,1:T(8,128)S(1)} %bitcast.90, f32[8192,32]{0,1:T(8,128)S(1)} %fusion.8, s32[8192]{0:T(1024)S(1)} %bitcast.88), kind=kOutput, calls=%fused_computation.1 | convolution fusion | flops 8059355136 | bytes 2064384 | tf_op jit(solution)/shard_map/ny,nsc->syc/dot_general | solution.py:132
  36.8 394.7 %while.29 = (s32[]{:T(128)}, f32[128,8,128]{2,1,0:T(8,128)}, f32[128,8,128]{2,1,0:T(8,128)S(1)}, f32[128,4,128]{2,1,0:T(4,128)}, f32[128,4,128]{2,1,0:T(4,128)},...) while((s32[]{:T(128)}, f32[128,8,128]{2,1,0:T(8,128)}, ...), condition=%wide.region_1.2_spmd, body=%wide.region_0.1_spmd.sunk | while | flops 62914564 | bytes 117441936 | solution.py:184
  49.4 4.6 collective-permute-start.2
  67.1 4.3 collective-permute-start.4
  76.2 4.3 collective-permute-start.12
  85.4 5.1 %collective-permute-start.6 = (f32[128,4,128]{2,1,0:T(4,128)S(1)}, f32[128,4,128]{2,1,0:T(4,128)S(1)}, u32[]{:S(2)}, u32[]{:S(2)}) collective-permute-start(f32[128,4,128]{2,1,0:T(4,128)S(1)} %get-tuple-element.384), channel_id=1, source_target_pairs={{0,1},{1,2},{2,3},{3,4},{4,5},{5,6},{6,7},{7,8},{8,9},{9,10},{10,1... | collective-permute-start | bytes 786440 | tf_op jit(solution)/shard_map/while/body/eval_jaxpr/ppermute | solution.py:22
  94.7 5.2 %collective-permute-start.14 = (f32[128,4,128]{2,1,0:T(4,128)S(1)}, f32[128,4,128]{2,1,0:T(4,128)S(1)}, u32[]{:S(2)}, u32[]{:S(2)}) collective-permute-start(f32[128,4,128]{2,1,0:T(4,128)S(1)} %get-tuple-element.398), channel_id=1, source_target_pairs={{0,1},{1,2},{2,3},{3,4},{4,5},{5,6},{6,7},{7,8},{8,9},{9,10},{10,1... | collective-permute-start | bytes 786440 | tf_op jit(solution)/shard_map/while/body/eval_jaxpr/ppermute | solution.py:22
  109.9 7.6 %collective-permute-start = (f32[128,4,128]{2,1,0:T(4,128)}, f32[128,4,128]{2,1,0:T(4,128)S(1)}, u32[]{:S(2)}, u32[]{:S(2)}) collective-permute-start(f32[128,4,128]{2,1,0:T(4,128)} %get-tuple-element.425), channel_id=1, source_target_pairs={{0,1},{1,2},{2,3},{3,4},{4,5},{5,6},{6,7},{7,8},{8,9},{9,10},{10,1... | collective-permute-start | bytes 786440 | tf_op jit(solution)/shard_map/while/body/eval_jaxpr/ppermute | solution.py:22
  126.6 7.7 %collective-permute-start.2 = (f32[128,4,128]{2,1,0:T(4,128)S(1)}, f32[128,4,128]{2,1,0:T(4,128)S(1)}, u32[]{:S(2)}, u32[]{:S(2)}) collective-permute-start(f32[128,4,128]{2,1,0:T(4,128)S(1)} %get-tuple-element.378), channel_id=1, source_target_pairs={{0,1},{1,2},{2,3},{3,4},{4,5},{5,6},{6,7},{7,8},{8,9},{9,10},{10,1... | collective-permute-start | bytes 786440 | tf_op jit(solution)/shard_map/while/body/eval_jaxpr/ppermute | solution.py:22
  147.3 4.3 collective-permute-start.4
  156.5 4.3 collective-permute-start.12
  165.8 5.2 %collective-permute-start.6 = (f32[128,4,128]{2,1,0:T(4,128)S(1)}, f32[128,4,128]{2,1,0:T(4,128)S(1)}, u32[]{:S(2)}, u32[]{:S(2)}) collective-permute-start(f32[128,4,128]{2,1,0:T(4,128)S(1)} %get-tuple-element.384), channel_id=1, source_target_pairs={{0,1},{1,2},{2,3},{3,4},{4,5},{5,6},{6,7},{7,8},{8,9},{9,10},{10,1... | collective-permute-start | bytes 786440 | tf_op jit(solution)/shard_map/while/body/eval_jaxpr/ppermute | solution.py:22
  175.1 5.2 %collective-permute-start.14 = (f32[128,4,128]{2,1,0:T(4,128)S(1)}, f32[128,4,128]{2,1,0:T(4,128)S(1)}, u32[]{:S(2)}, u32[]{:S(2)}) collective-permute-start(f32[128,4,128]{2,1,0:T(4,128)S(1)} %get-tuple-element.398), channel_id=1, source_target_pairs={{0,1},{1,2},{2,3},{3,4},{4,5},{5,6},{6,7},{7,8},{8,9},{9,10},{10,1... | collective-permute-start | bytes 786440 | tf_op jit(solution)/shard_map/while/body/eval_jaxpr/ppermute | solution.py:22
  190.3 7.6 %collective-permute-start = (f32[128,4,128]{2,1,0:T(4,128)}, f32[128,4,128]{2,1,0:T(4,128)S(1)}, u32[]{:S(2)}, u32[]{:S(2)}) collective-permute-start(f32[128,4,128]{2,1,0:T(4,128)} %get-tuple-element.425), channel_id=1, source_target_pairs={{0,1},{1,2},{2,3},{3,4},{4,5},{5,6},{6,7},{7,8},{8,9},{9,10},{10,1... | collective-permute-start | bytes 786440 | tf_op jit(solution)/shard_map/while/body/eval_jaxpr/ppermute | solution.py:22
  207.0 7.7 %collective-permute-start.2 = (f32[128,4,128]{2,1,0:T(4,128)S(1)}, f32[128,4,128]{2,1,0:T(4,128)S(1)}, u32[]{:S(2)}, u32[]{:S(2)}) collective-permute-start(f32[128,4,128]{2,1,0:T(4,128)S(1)} %get-tuple-element.378), channel_id=1, source_target_pairs={{0,1},{1,2},{2,3},{3,4},{4,5},{5,6},{6,7},{7,8},{8,9},{9,10},{10,1... | collective-permute-start | bytes 786440 | tf_op jit(solution)/shard_map/while/body/eval_jaxpr/ppermute | solution.py:22
  227.7 4.3 collective-permute-start.4
  236.9 4.3 collective-permute-start.12
  246.2 5.2 %collective-permute-start.6 = (f32[128,4,128]{2,1,0:T(4,128)S(1)}, f32[128,4,128]{2,1,0:T(4,128)S(1)}, u32[]{:S(2)}, u32[]{:S(2)}) collective-permute-start(f32[128,4,128]{2,1,0:T(4,128)S(1)} %get-tuple-element.384), channel_id=1, source_target_pairs={{0,1},{1,2},{2,3},{3,4},{4,5},{5,6},{6,7},{7,8},{8,9},{9,10},{10,1... | collective-permute-start | bytes 786440 | tf_op jit(solution)/shard_map/while/body/eval_jaxpr/ppermute | solution.py:22
  255.5 5.2 %collective-permute-start.14 = (f32[128,4,128]{2,1,0:T(4,128)S(1)}, f32[128,4,128]{2,1,0:T(4,128)S(1)}, u32[]{:S(2)}, u32[]{:S(2)}) collective-permute-start(f32[128,4,128]{2,1,0:T(4,128)S(1)} %get-tuple-element.398), channel_id=1, source_target_pairs={{0,1},{1,2},{2,3},{3,4},{4,5},{5,6},{6,7},{7,8},{8,9},{9,10},{10,1... | collective-permute-start | bytes 786440 | tf_op jit(solution)/shard_map/while/body/eval_jaxpr/ppermute | solution.py:22
  270.7 7.6 %collective-permute-start = (f32[128,4,128]{2,1,0:T(4,128)}, f32[128,4,128]{2,1,0:T(4,128)S(1)}, u32[]{:S(2)}, u32[]{:S(2)}) collective-permute-start(f32[128,4,128]{2,1,0:T(4,128)} %get-tuple-element.425), channel_id=1, source_target_pairs={{0,1},{1,2},{2,3},{3,4},{4,5},{5,6},{6,7},{7,8},{8,9},{9,10},{10,1... | collective-permute-start | bytes 786440 | tf_op jit(solution)/shard_map/while/body/eval_jaxpr/ppermute | solution.py:22
  287.4 7.7 %collective-permute-start.2 = (f32[128,4,128]{2,1,0:T(4,128)S(1)}, f32[128,4,128]{2,1,0:T(4,128)S(1)}, u32[]{:S(2)}, u32[]{:S(2)}) collective-permute-start(f32[128,4,128]{2,1,0:T(4,128)S(1)} %get-tuple-element.378), channel_id=1, source_target_pairs={{0,1},{1,2},{2,3},{3,4},{4,5},{5,6},{6,7},{7,8},{8,9},{9,10},{10,1... | collective-permute-start | bytes 786440 | tf_op jit(solution)/shard_map/while/body/eval_jaxpr/ppermute | solution.py:22
  317.3 4.3 collective-permute-start.12
  326.6 5.2 %collective-permute-start.6 = (f32[128,4,128]{2,1,0:T(4,128)S(1)}, f32[128,4,128]{2,1,0:T(4,128)S(1)}, u32[]{:S(2)}, u32[]{:S(2)}) collective-permute-start(f32[128,4,128]{2,1,0:T(4,128)S(1)} %get-tuple-element.384), channel_id=1, source_target_pairs={{0,1},{1,2},{2,3},{3,4},{4,5},{5,6},{6,7},{7,8},{8,9},{9,10},{10,1... | collective-permute-start | bytes 786440 | tf_op jit(solution)/shard_map/while/body/eval_jaxpr/ppermute | solution.py:22
  335.9 5.2 %collective-permute-start.14 = (f32[128,4,128]{2,1,0:T(4,128)S(1)}, f32[128,4,128]{2,1,0:T(4,128)S(1)}, u32[]{:S(2)}, u32[]{:S(2)}) collective-permute-start(f32[128,4,128]{2,1,0:T(4,128)S(1)} %get-tuple-element.398), channel_id=1, source_target_pairs={{0,1},{1,2},{2,3},{3,4},{4,5},{5,6},{6,7},{7,8},{8,9},{9,10},{10,1... | collective-permute-start | bytes 786440 | tf_op jit(solution)/shard_map/while/body/eval_jaxpr/ppermute | solution.py:22
  351.1 7.6 %collective-permute-start = (f32[128,4,128]{2,1,0:T(4,128)}, f32[128,4,128]{2,1,0:T(4,128)S(1)}, u32[]{:S(2)}, u32[]{:S(2)}) collective-permute-start(f32[128,4,128]{2,1,0:T(4,128)} %get-tuple-element.425), channel_id=1, source_target_pairs={{0,1},{1,2},{2,3},{3,4},{4,5},{5,6},{6,7},{7,8},{8,9},{9,10},{10,1... | collective-permute-start | bytes 786440 | tf_op jit(solution)/shard_map/while/body/eval_jaxpr/ppermute | solution.py:22
  367.8 7.7 %collective-permute-start.2 = (f32[128,4,128]{2,1,0:T(4,128)S(1)}, f32[128,4,128]{2,1,0:T(4,128)S(1)}, u32[]{:S(2)}, u32[]{:S(2)}) collective-permute-start(f32[128,4,128]{2,1,0:T(4,128)S(1)} %get-tuple-element.378), channel_id=1, source_target_pairs={{0,1},{1,2},{2,3},{3,4},{4,5},{5,6},{6,7},{7,8},{8,9},{9,10},{10,1... | collective-permute-start | bytes 786440 | tf_op jit(solution)/shard_map/while/body/eval_jaxpr/ppermute | solution.py:22
  397.7 4.3 collective-permute-start.12
  406.9 5.2 %collective-permute-start.6 = (f32[128,4,128]{2,1,0:T(4,128)S(1)}, f32[128,4,128]{2,1,0:T(4,128)S(1)}, u32[]{:S(2)}, u32[]{:S(2)}) collective-permute-start(f32[128,4,128]{2,1,0:T(4,128)S(1)} %get-tuple-element.384), channel_id=1, source_target_pairs={{0,1},{1,2},{2,3},{3,4},{4,5},{5,6},{6,7},{7,8},{8,9},{9,10},{10,1... | collective-permute-start | bytes 786440 | tf_op jit(solution)/shard_map/while/body/eval_jaxpr/ppermute | solution.py:22
  416.2 5.2 %collective-permute-start.14 = (f32[128,4,128]{2,1,0:T(4,128)S(1)}, f32[128,4,128]{2,1,0:T(4,128)S(1)}, u32[]{:S(2)}, u32[]{:S(2)}) collective-permute-start(f32[128,4,128]{2,1,0:T(4,128)S(1)} %get-tuple-element.398), channel_id=1, source_target_pairs={{0,1},{1,2},{2,3},{3,4},{4,5},{5,6},{6,7},{7,8},{8,9},{9,10},{10,1... | collective-permute-start | bytes 786440 | tf_op jit(solution)/shard_map/while/body/eval_jaxpr/ppermute | solution.py:22
  433.5 13.7 %all-to-all-start.1 = ((f32[128,1,8,128]{3,2,1,0:T(8,128)}), f32[128,1,8,128]{3,2,1,0:T(8,128)S(1)}, u32[]{:S(2)}, u32[]{:S(2)}) async-start(f32[128,1,8,128]{3,2,1,0:T(8,128)} %multiply_bitcast_fusion), calls=%async_computation.1 | async-start | bytes 1048576 | tf_op jit(solution)/shard_map/all_to_all | solution.py:195
  450.3 11.3 %all-to-all-done.1 = f32[128,1,8,128]{3,2,1,0:T(8,128)S(1)} async-done(((f32[128,1,8,128]{3,2,1,0:T(8,128)}), f32[128,1,8,128]{3,2,1,0:T(8,128)S(1)}, u32[]{:S(2)}, u32[]{:S(2)}) %all-to-all-start.1) | async-done | bytes 524320 | tf_op jit(solution)/shard_map/all_to_all | solution.py:195
  (430 shorter events, 265.5 us)
Async XLA Ops:
  3.6 32.3 %all-to-all-start = ((f32[8,16,8,128]{3,2,0,1:T(8,128)}), f32[8,16,8,128]{3,2,0,1:T(8,128)S(1)}, u32[]{:S(2)}, u32[]{:S(2)}) async-start(f32[8,16,8,128]{3,2,0,1:T(8,128)} %select_bitcast_fusion), calls=%async_computation | async-start | bytes 1048576 | tf_op jit(solution)/shard_map/all_to_all | solution.py:145
  40.4 14.9 %collective-permute-start.8 = (f32[128,4,128]{2,1,0:T(4,128)S(1)}, f32[128,4,128]{2,1,0:T(4,128)S(1)}, u32[]{:S(2)}, u32[]{:S(2)}) collective-permute-start(f32[128,4,128]{2,1,0:T(4,128)S(1)} %get-tuple-element.429), channel_id=1, source_target_pairs={{0,1},{1,2},{2,3},{3,4},{4,5},{5,6},{6,7},{7,8},{8,9},{9,10},{10,1... | collective-permute-start | bytes 786440 | tf_op jit(solution)/shard_map/while/body/eval_jaxpr/ppermute | solution.py:22
  49.4 14.1 %collective-permute-start.2 = (f32[128,4,128]{2,1,0:T(4,128)S(1)}, f32[128,4,128]{2,1,0:T(4,128)S(1)}, u32[]{:S(2)}, u32[]{:S(2)}) collective-permute-start(f32[128,4,128]{2,1,0:T(4,128)S(1)} %get-tuple-element.378), channel_id=1, source_target_pairs={{0,1},{1,2},{2,3},{3,4},{4,5},{5,6},{6,7},{7,8},{8,9},{9,10},{10,1... | collective-permute-start | bytes 786440 | tf_op jit(solution)/shard_map/while/body/eval_jaxpr/ppermute | solution.py:22
  58.2 14.5 %collective-permute-start.10 = (f32[128,4,128]{2,1,0:T(4,128)S(1)}, f32[128,4,128]{2,1,0:T(4,128)S(1)}, u32[]{:S(2)}, u32[]{:S(2)}) collective-permute-start(f32[128,4,128]{2,1,0:T(4,128)S(1)} %get-tuple-element.390), channel_id=1, source_target_pairs={{0,1},{1,2},{2,3},{3,4},{4,5},{5,6},{6,7},{7,8},{8,9},{9,10},{10,1... | collective-permute-start | bytes 786440 | tf_op jit(solution)/shard_map/while/body/eval_jaxpr/ppermute | solution.py:22
  67.1 14.8 %collective-permute-start.4 = (f32[128,4,128]{2,1,0:T(4,128)S(1)}, f32[128,4,128]{2,1,0:T(4,128)S(1)}, u32[]{:S(2)}, u32[]{:S(2)}) collective-permute-start(f32[128,4,128]{2,1,0:T(4,128)S(1)} %get-tuple-element.381), channel_id=1, source_target_pairs={{0,1},{1,2},{2,3},{3,4},{4,5},{5,6},{6,7},{7,8},{8,9},{9,10},{10,1... | collective-permute-start | bytes 786440 | tf_op jit(solution)/shard_map/while/body/eval_jaxpr/ppermute | solution.py:22
  76.2 15.6 %collective-permute-start.12 = (f32[128,4,128]{2,1,0:T(4,128)S(1)}, f32[128,4,128]{2,1,0:T(4,128)S(1)}, u32[]{:S(2)}, u32[]{:S(2)}) collective-permute-start(f32[128,4,128]{2,1,0:T(4,128)S(1)} %get-tuple-element.394), channel_id=1, source_target_pairs={{0,1},{1,2},{2,3},{3,4},{4,5},{5,6},{6,7},{7,8},{8,9},{9,10},{10,1... | collective-permute-start | bytes 786440 | tf_op jit(solution)/shard_map/while/body/eval_jaxpr/ppermute | solution.py:22
  85.4 15.7 %collective-permute-start.6 = (f32[128,4,128]{2,1,0:T(4,128)S(1)}, f32[128,4,128]{2,1,0:T(4,128)S(1)}, u32[]{:S(2)}, u32[]{:S(2)}) collective-permute-start(f32[128,4,128]{2,1,0:T(4,128)S(1)} %get-tuple-element.384), channel_id=1, source_target_pairs={{0,1},{1,2},{2,3},{3,4},{4,5},{5,6},{6,7},{7,8},{8,9},{9,10},{10,1... | collective-permute-start | bytes 786440 | tf_op jit(solution)/shard_map/while/body/eval_jaxpr/ppermute | solution.py:22
  118.8 16.8 %collective-permute-start.8 = (f32[128,4,128]{2,1,0:T(4,128)S(1)}, f32[128,4,128]{2,1,0:T(4,128)S(1)}, u32[]{:S(2)}, u32[]{:S(2)}) collective-permute-start(f32[128,4,128]{2,1,0:T(4,128)S(1)} %get-tuple-element.429), channel_id=1, source_target_pairs={{0,1},{1,2},{2,3},{3,4},{4,5},{5,6},{6,7},{7,8},{8,9},{9,10},{10,1... | collective-permute-start | bytes 786440 | tf_op jit(solution)/shard_map/while/body/eval_jaxpr/ppermute | solution.py:22
  126.6 17.1 %collective-permute-start.2 = (f32[128,4,128]{2,1,0:T(4,128)S(1)}, f32[128,4,128]{2,1,0:T(4,128)S(1)}, u32[]{:S(2)}, u32[]{:S(2)}) collective-permute-start(f32[128,4,128]{2,1,0:T(4,128)S(1)} %get-tuple-element.378), channel_id=1, source_target_pairs={{0,1},{1,2},{2,3},{3,4},{4,5},{5,6},{6,7},{7,8},{8,9},{9,10},{10,1... | collective-permute-start | bytes 786440 | tf_op jit(solution)/shard_map/while/body/eval_jaxpr/ppermute | solution.py:22
  138.4 14.5 %collective-permute-start.10 = (f32[128,4,128]{2,1,0:T(4,128)S(1)}, f32[128,4,128]{2,1,0:T(4,128)S(1)}, u32[]{:S(2)}, u32[]{:S(2)}) collective-permute-start(f32[128,4,128]{2,1,0:T(4,128)S(1)} %get-tuple-element.390), channel_id=1, source_target_pairs={{0,1},{1,2},{2,3},{3,4},{4,5},{5,6},{6,7},{7,8},{8,9},{9,10},{10,1... | collective-permute-start | bytes 786440 | tf_op jit(solution)/shard_map/while/body/eval_jaxpr/ppermute | solution.py:22
  147.3 14.9 %collective-permute-start.4 = (f32[128,4,128]{2,1,0:T(4,128)S(1)}, f32[128,4,128]{2,1,0:T(4,128)S(1)}, u32[]{:S(2)}, u32[]{:S(2)}) collective-permute-start(f32[128,4,128]{2,1,0:T(4,128)S(1)} %get-tuple-element.381), channel_id=1, source_target_pairs={{0,1},{1,2},{2,3},{3,4},{4,5},{5,6},{6,7},{7,8},{8,9},{9,10},{10,1... | collective-permute-start | bytes 786440 | tf_op jit(solution)/shard_map/while/body/eval_jaxpr/ppermute | solution.py:22
  156.5 15.8 %collective-permute-start.12 = (f32[128,4,128]{2,1,0:T(4,128)S(1)}, f32[128,4,128]{2,1,0:T(4,128)S(1)}, u32[]{:S(2)}, u32[]{:S(2)}) collective-permute-start(f32[128,4,128]{2,1,0:T(4,128)S(1)} %get-tuple-element.394), channel_id=1, source_target_pairs={{0,1},{1,2},{2,3},{3,4},{4,5},{5,6},{6,7},{7,8},{8,9},{9,10},{10,1... | collective-permute-start | bytes 786440 | tf_op jit(solution)/shard_map/while/body/eval_jaxpr/ppermute | solution.py:22
  165.8 15.8 %collective-permute-start.6 = (f32[128,4,128]{2,1,0:T(4,128)S(1)}, f32[128,4,128]{2,1,0:T(4,128)S(1)}, u32[]{:S(2)}, u32[]{:S(2)}) collective-permute-start(f32[128,4,128]{2,1,0:T(4,128)S(1)} %get-tuple-element.384), channel_id=1, source_target_pairs={{0,1},{1,2},{2,3},{3,4},{4,5},{5,6},{6,7},{7,8},{8,9},{9,10},{10,1... | collective-permute-start | bytes 786440 | tf_op jit(solution)/shard_map/while/body/eval_jaxpr/ppermute | solution.py:22
  199.2 16.8 %collective-permute-start.8 = (f32[128,4,128]{2,1,0:T(4,128)S(1)}, f32[128,4,128]{2,1,0:T(4,128)S(1)}, u32[]{:S(2)}, u32[]{:S(2)}) collective-permute-start(f32[128,4,128]{2,1,0:T(4,128)S(1)} %get-tuple-element.429), channel_id=1, source_target_pairs={{0,1},{1,2},{2,3},{3,4},{4,5},{5,6},{6,7},{7,8},{8,9},{9,10},{10,1... | collective-permute-start | bytes 786440 | tf_op jit(solution)/shard_map/while/body/eval_jaxpr/ppermute | solution.py:22
  207.0 17.1 %collective-permute-start.2 = (f32[128,4,128]{2,1,0:T(4,128)S(1)}, f32[128,4,128]{2,1,0:T(4,128)S(1)}, u32[]{:S(2)}, u32[]{:S(2)}) collective-permute-start(f32[128,4,128]{2,1,0:T(4,128)S(1)} %get-tuple-element.378), channel_id=1, source_target_pairs={{0,1},{1,2},{2,3},{3,4},{4,5},{5,6},{6,7},{7,8},{8,9},{9,10},{10,1... | collective-permute-start | bytes 786440 | tf_op jit(solution)/shard_map/while/body/eval_jaxpr/ppermute | solution.py:22
  218.8 14.5 %collective-permute-start.10 = (f32[128,4,128]{2,1,0:T(4,128)S(1)}, f32[128,4,128]{2,1,0:T(4,128)S(1)}, u32[]{:S(2)}, u32[]{:S(2)}) collective-permute-start(f32[128,4,128]{2,1,0:T(4,128)S(1)} %get-tuple-element.390), channel_id=1, source_target_pairs={{0,1},{1,2},{2,3},{3,4},{4,5},{5,6},{6,7},{7,8},{8,9},{9,10},{10,1... | collective-permute-start | bytes 786440 | tf_op jit(solution)/shard_map/while/body/eval_jaxpr/ppermute | solution.py:22
  227.7 14.9 %collective-permute-start.4 = (f32[128,4,128]{2,1,0:T(4,128)S(1)}, f32[128,4,128]{2,1,0:T(4,128)S(1)}, u32[]{:S(2)}, u32[]{:S(2)}) collective-permute-start(f32[128,4,128]{2,1,0:T(4,128)S(1)} %get-tuple-element.381), channel_id=1, source_target_pairs={{0,1},{1,2},{2,3},{3,4},{4,5},{5,6},{6,7},{7,8},{8,9},{9,10},{10,1... | collective-permute-start | bytes 786440 | tf_op jit(solution)/shard_map/while/body/eval_jaxpr/ppermute | solution.py:22
  236.9 15.8 %collective-permute-start.12 = (f32[128,4,128]{2,1,0:T(4,128)S(1)}, f32[128,4,128]{2,1,0:T(4,128)S(1)}, u32[]{:S(2)}, u32[]{:S(2)}) collective-permute-start(f32[128,4,128]{2,1,0:T(4,128)S(1)} %get-tuple-element.394), channel_id=1, source_target_pairs={{0,1},{1,2},{2,3},{3,4},{4,5},{5,6},{6,7},{7,8},{8,9},{9,10},{10,1... | collective-permute-start | bytes 786440 | tf_op jit(solution)/shard_map/while/body/eval_jaxpr/ppermute | solution.py:22
  246.2 15.8 %collective-permute-start.6 = (f32[128,4,128]{2,1,0:T(4,128)S(1)}, f32[128,4,128]{2,1,0:T(4,128)S(1)}, u32[]{:S(2)}, u32[]{:S(2)}) collective-permute-start(f32[128,4,128]{2,1,0:T(4,128)S(1)} %get-tuple-element.384), channel_id=1, source_target_pairs={{0,1},{1,2},{2,3},{3,4},{4,5},{5,6},{6,7},{7,8},{8,9},{9,10},{10,1... | collective-permute-start | bytes 786440 | tf_op jit(solution)/shard_map/while/body/eval_jaxpr/ppermute | solution.py:22
  279.6 16.8 %collective-permute-start.8 = (f32[128,4,128]{2,1,0:T(4,128)S(1)}, f32[128,4,128]{2,1,0:T(4,128)S(1)}, u32[]{:S(2)}, u32[]{:S(2)}) collective-permute-start(f32[128,4,128]{2,1,0:T(4,128)S(1)} %get-tuple-element.429), channel_id=1, source_target_pairs={{0,1},{1,2},{2,3},{3,4},{4,5},{5,6},{6,7},{7,8},{8,9},{9,10},{10,1... | collective-permute-start | bytes 786440 | tf_op jit(solution)/shard_map/while/body/eval_jaxpr/ppermute | solution.py:22
  287.4 17.1 %collective-permute-start.2 = (f32[128,4,128]{2,1,0:T(4,128)S(1)}, f32[128,4,128]{2,1,0:T(4,128)S(1)}, u32[]{:S(2)}, u32[]{:S(2)}) collective-permute-start(f32[128,4,128]{2,1,0:T(4,128)S(1)} %get-tuple-element.378), channel_id=1, source_target_pairs={{0,1},{1,2},{2,3},{3,4},{4,5},{5,6},{6,7},{7,8},{8,9},{9,10},{10,1... | collective-permute-start | bytes 786440 | tf_op jit(solution)/shard_map/while/body/eval_jaxpr/ppermute | solution.py:22
  299.2 14.5 %collective-permute-start.10 = (f32[128,4,128]{2,1,0:T(4,128)S(1)}, f32[128,4,128]{2,1,0:T(4,128)S(1)}, u32[]{:S(2)}, u32[]{:S(2)}) collective-permute-start(f32[128,4,128]{2,1,0:T(4,128)S(1)} %get-tuple-element.390), channel_id=1, source_target_pairs={{0,1},{1,2},{2,3},{3,4},{4,5},{5,6},{6,7},{7,8},{8,9},{9,10},{10,1... | collective-permute-start | bytes 786440 | tf_op jit(solution)/shard_map/while/body/eval_jaxpr/ppermute | solution.py:22
  308.1 14.9 %collective-permute-start.4 = (f32[128,4,128]{2,1,0:T(4,128)S(1)}, f32[128,4,128]{2,1,0:T(4,128)S(1)}, u32[]{:S(2)}, u32[]{:S(2)}) collective-permute-start(f32[128,4,128]{2,1,0:T(4,128)S(1)} %get-tuple-element.381), channel_id=1, source_target_pairs={{0,1},{1,2},{2,3},{3,4},{4,5},{5,6},{6,7},{7,8},{8,9},{9,10},{10,1... | collective-permute-start | bytes 786440 | tf_op jit(solution)/shard_map/while/body/eval_jaxpr/ppermute | solution.py:22
  317.3 15.8 %collective-permute-start.12 = (f32[128,4,128]{2,1,0:T(4,128)S(1)}, f32[128,4,128]{2,1,0:T(4,128)S(1)}, u32[]{:S(2)}, u32[]{:S(2)}) collective-permute-start(f32[128,4,128]{2,1,0:T(4,128)S(1)} %get-tuple-element.394), channel_id=1, source_target_pairs={{0,1},{1,2},{2,3},{3,4},{4,5},{5,6},{6,7},{7,8},{8,9},{9,10},{10,1... | collective-permute-start | bytes 786440 | tf_op jit(solution)/shard_map/while/body/eval_jaxpr/ppermute | solution.py:22
  326.6 15.8 %collective-permute-start.6 = (f32[128,4,128]{2,1,0:T(4,128)S(1)}, f32[128,4,128]{2,1,0:T(4,128)S(1)}, u32[]{:S(2)}, u32[]{:S(2)}) collective-permute-start(f32[128,4,128]{2,1,0:T(4,128)S(1)} %get-tuple-element.384), channel_id=1, source_target_pairs={{0,1},{1,2},{2,3},{3,4},{4,5},{5,6},{6,7},{7,8},{8,9},{9,10},{10,1... | collective-permute-start | bytes 786440 | tf_op jit(solution)/shard_map/while/body/eval_jaxpr/ppermute | solution.py:22
  360.0 16.8 %collective-permute-start.8 = (f32[128,4,128]{2,1,0:T(4,128)S(1)}, f32[128,4,128]{2,1,0:T(4,128)S(1)}, u32[]{:S(2)}, u32[]{:S(2)}) collective-permute-start(f32[128,4,128]{2,1,0:T(4,128)S(1)} %get-tuple-element.429), channel_id=1, source_target_pairs={{0,1},{1,2},{2,3},{3,4},{4,5},{5,6},{6,7},{7,8},{8,9},{9,10},{10,1... | collective-permute-start | bytes 786440 | tf_op jit(solution)/shard_map/while/body/eval_jaxpr/ppermute | solution.py:22
  367.8 17.1 %collective-permute-start.2 = (f32[128,4,128]{2,1,0:T(4,128)S(1)}, f32[128,4,128]{2,1,0:T(4,128)S(1)}, u32[]{:S(2)}, u32[]{:S(2)}) collective-permute-start(f32[128,4,128]{2,1,0:T(4,128)S(1)} %get-tuple-element.378), channel_id=1, source_target_pairs={{0,1},{1,2},{2,3},{3,4},{4,5},{5,6},{6,7},{7,8},{8,9},{9,10},{10,1... | collective-permute-start | bytes 786440 | tf_op jit(solution)/shard_map/while/body/eval_jaxpr/ppermute | solution.py:22
  379.6 14.5 %collective-permute-start.10 = (f32[128,4,128]{2,1,0:T(4,128)S(1)}, f32[128,4,128]{2,1,0:T(4,128)S(1)}, u32[]{:S(2)}, u32[]{:S(2)}) collective-permute-start(f32[128,4,128]{2,1,0:T(4,128)S(1)} %get-tuple-element.390), channel_id=1, source_target_pairs={{0,1},{1,2},{2,3},{3,4},{4,5},{5,6},{6,7},{7,8},{8,9},{9,10},{10,1... | collective-permute-start | bytes 786440 | tf_op jit(solution)/shard_map/while/body/eval_jaxpr/ppermute | solution.py:22
  388.5 14.9 %collective-permute-start.4 = (f32[128,4,128]{2,1,0:T(4,128)S(1)}, f32[128,4,128]{2,1,0:T(4,128)S(1)}, u32[]{:S(2)}, u32[]{:S(2)}) collective-permute-start(f32[128,4,128]{2,1,0:T(4,128)S(1)} %get-tuple-element.381), channel_id=1, source_target_pairs={{0,1},{1,2},{2,3},{3,4},{4,5},{5,6},{6,7},{7,8},{8,9},{9,10},{10,1... | collective-permute-start | bytes 786440 | tf_op jit(solution)/shard_map/while/body/eval_jaxpr/ppermute | solution.py:22
  397.7 15.8 %collective-permute-start.12 = (f32[128,4,128]{2,1,0:T(4,128)S(1)}, f32[128,4,128]{2,1,0:T(4,128)S(1)}, u32[]{:S(2)}, u32[]{:S(2)}) collective-permute-start(f32[128,4,128]{2,1,0:T(4,128)S(1)} %get-tuple-element.394), channel_id=1, source_target_pairs={{0,1},{1,2},{2,3},{3,4},{4,5},{5,6},{6,7},{7,8},{8,9},{9,10},{10,1... | collective-permute-start | bytes 786440 | tf_op jit(solution)/shard_map/while/body/eval_jaxpr/ppermute | solution.py:22
  406.9 15.8 %collective-permute-start.6 = (f32[128,4,128]{2,1,0:T(4,128)S(1)}, f32[128,4,128]{2,1,0:T(4,128)S(1)}, u32[]{:S(2)}, u32[]{:S(2)}) collective-permute-start(f32[128,4,128]{2,1,0:T(4,128)S(1)} %get-tuple-element.384), channel_id=1, source_target_pairs={{0,1},{1,2},{2,3},{3,4},{4,5},{5,6},{6,7},{7,8},{8,9},{9,10},{10,1... | collective-permute-start | bytes 786440 | tf_op jit(solution)/shard_map/while/body/eval_jaxpr/ppermute | solution.py:22
  433.5 28.2 %all-to-all-start.1 = ((f32[128,1,8,128]{3,2,1,0:T(8,128)}), f32[128,1,8,128]{3,2,1,0:T(8,128)S(1)}, u32[]{:S(2)}, u32[]{:S(2)}) async-start(f32[128,1,8,128]{3,2,1,0:T(8,128)} %multiply_bitcast_fusion), calls=%async_computation.1 | async-start | bytes 1048576 | tf_op jit(solution)/shard_map/all_to_all | solution.py:195
  (161 other events, 1412.1 us)

commit v17 on v16

--- a/solution.py
+++ b/solution.py
@@ -11,9 +11,7 @@
 stencil_weights = (8.0 / 5.0, -1.0 / 5.0, 8.0 / 315.0, -1.0 / 560.0)
 center_weight = 3.0 * (-205.0 / 72.0)
 HALO = 4
-ROWS = 128
 TRIP = 4
-XOFF = 8
 
 
 def trade_halos(head, tail, axis):
@@ -30,19 +28,15 @@
     else:
         out_ref, head_ref, tail_ref, ey_ref, hx_ref = rest
     block_y, block_x, depth_z = cur_ref.shape
-    zeros_y = jnp.zeros((HALO, block_x, depth_z), jnp.float32)
-    ey_ref[0:HALO] = zeros_y
-    ey_ref[HALO + block_y : 2 * HALO + block_y] = zeros_y
-    ey_ref[HALO : HALO + block_y] = cur_ref[...]
     hx_ref[0, :, block_x - HALO : block_x, :] = xlo_ref[...]
     hx_ref[1, :, 0:HALO, :] = xhi_ref[...]
-    rows = ROWS
+    rows = block_y
     lane = lax.broadcasted_iota(jnp.int32, (rows, block_x, depth_z), 2)
     sub = lax.broadcasted_iota(jnp.int32, (rows, block_x, depth_z), 1)
 
     def chunk(index, carry):
         y = pl.multiple_of(index * rows, rows)
-        ctr = ey_ref[pl.ds(HALO + y, rows)]
+        ctr = cur_ref[...]
         left = hx_ref[0, pl.ds(y, rows)]
         right = hx_ref[1, pl.ds(y, rows)]
         acc = center_weight * ctr
@@ -50,7 +44,8 @@
             ahead = pltpu.roll(jnp.where(sub >= m, ctr, right), block_x - m, 1)
             behind = pltpu.roll(jnp.where(sub < block_x - m, ctr, left), m, 1)
             b = ahead + behind
-            b = b + ey_ref[pl.ds(HALO + y + m, rows)] + ey_ref[pl.ds(HALO + y - m, rows)]
+            zeros_m = jnp.zeros((m, block_x, depth_z), jnp.float32)
+            b = b + jnp.concatenate([ctr[m:], zeros_m], 0) + jnp.concatenate([zeros_m, ctr[:-m]], 0)
             up = jnp.where(lane < depth_z - m, pltpu.roll(ctr, depth_z - m, 2), 0.0)
             down = jnp.where(lane >= m, pltpu.roll(ctr, m, 2), 0.0)
             b = b + up + down

time: 467 us -> 467 us (level)
  no operation moved by 1% of the time
where the time goes in v17:
time: 467 us; the launch traced here: 463 us
  starting transfers between devices  271 us (58%)
  Pallas kernels  136 us (29%)
  local copies, waits for them, and re-layouts  18 us (4%)
  waiting for transfers between devices  13.6 us (3%)
  matrix products  11.7 us (3%)
  other arithmetic  10.1 us (2%)
    ppermute x40, starting transfers between devices, trade_halos(): low = lax.ppermute(tail, axis, [(i, (i + 1) % count) for i in range(ends)])  198 us
    pallas_call x40, Pallas kernels, wave_call(): pl.pallas_call(functools.partial(wave_kernel, with_image), out_shape=tupl...  136 us
    ppermute x40, starting transfers between devices, trade_halos(): high = lax.ppermute(head, axis, [((i + 1) % count, i) for i in range(ends)])  51.7 us
    all_to_all x1, starting transfers between devices, shards(): lax.all_to_all(outgoing, 'dom', split_axis=0, concat_axis=1, tiled=True)  13.7 us
    all_to_all x1, waiting for transfers between devices, shards(): lax.all_to_all(outgoing, 'dom', split_axis=0, concat_axis=1, tiled=True)  11.3 us
    dot_general x2, matrix products, spread_points(): jnp.einsum('ny,nsc->syc', rows_y, weighted, precision=lax.Precision.HIGHEST)  11 us
  transfers between devices with their start and end apart: 82, of which 6 were waited for; matrix products, arithmetic and copies ran while one was open for 6% of the time, Pallas kernels for 25%

profile of v17, /device:TPU:0, one launch (start us, length us, event | category | flops | bytes accessed | tf_op | source)
XLA Modules:
  0.0 463.3 jit_solution(6544104556673579655)
XLA Ops:
  3.6 7.4 %all-to-all-start = ((f32[8,16,8,128]{3,2,0,1:T(8,128)}), f32[8,16,8,128]{3,2,0,1:T(8,128)S(1)}, u32[]{:S(2)}, u32[]{:S(2)}) async-start(f32[8,16,8,128]{3,2,0,1:T(8,128)} %select_bitcast_fusion), calls=%async_computation | async-start | bytes 1048576 | tf_op jit(solution)/shard_map/all_to_all | solution.py:140
  12.2 10.5 %fusion = f32[20,32,128]{2,1,0:T(8,128)S(1)} fusion(f32[8192,20]{0,1:T(8,128)S(1)} %bitcast.90, f32[8192,32]{0,1:T(8,128)S(1)} %fusion.8, s32[8192]{0:T(1024)S(1)} %bitcast.88), kind=kOutput, calls=%fused_computation.1 | convolution fusion | flops 8059355136 | bytes 2064384 | tf_op jit(solution)/shard_map/ny,nsc->syc/dot_general | solution.py:127
  36.8 394.7 %while.29 = (s32[]{:T(128)}, f32[128,8,128]{2,1,0:T(8,128)}, f32[128,8,128]{2,1,0:T(8,128)S(1)}, f32[128,4,128]{2,1,0:T(4,128)}, f32[128,4,128]{2,1,0:T(4,128)},...) while((s32[]{:T(128)}, f32[128,8,128]{2,1,0:T(8,128)}, ...), condition=%wide.region_1.2_spmd, body=%wide.region_0.1_spmd.sunk | while | flops 62914564 | bytes 117441936 | solution.py:179
  49.4 4.6 collective-permute-start.2
  67.1 4.3 collective-permute-start.4
  76.2 4.3 collective-permute-start.12
  85.4 5.1 %collective-permute-start.6 = (f32[128,4,128]{2,1,0:T(4,128)S(1)}, f32[128,4,128]{2,1,0:T(4,128)S(1)}, u32[]{:S(2)}, u32[]{:S(2)}) collective-permute-start(f32[128,4,128]{2,1,0:T(4,128)S(1)} %get-tuple-element.384), channel_id=1, source_target_pairs={{0,1},{1,2},{2,3},{3,4},{4,5},{5,6},{6,7},{7,8},{8,9},{9,10},{10,1... | collective-permute-start | bytes 786440 | tf_op jit(solution)/shard_map/while/body/eval_jaxpr/ppermute | solution.py:20
  94.7 5.2 %collective-permute-start.14 = (f32[128,4,128]{2,1,0:T(4,128)S(1)}, f32[128,4,128]{2,1,0:T(4,128)S(1)}, u32[]{:S(2)}, u32[]{:S(2)}) collective-permute-start(f32[128,4,128]{2,1,0:T(4,128)S(1)} %get-tuple-element.398), channel_id=1, source_target_pairs={{0,1},{1,2},{2,3},{3,4},{4,5},{5,6},{6,7},{7,8},{8,9},{9,10},{10,1... | collective-permute-start | bytes 786440 | tf_op jit(solution)/shard_map/while/body/eval_jaxpr/ppermute | solution.py:20
  109.9 7.6 %collective-permute-start = (f32[128,4,128]{2,1,0:T(4,128)}, f32[128,4,128]{2,1,0:T(4,128)S(1)}, u32[]{:S(2)}, u32[]{:S(2)}) collective-permute-start(f32[128,4,128]{2,1,0:T(4,128)} %get-tuple-element.425), channel_id=1, source_target_pairs={{0,1},{1,2},{2,3},{3,4},{4,5},{5,6},{6,7},{7,8},{8,9},{9,10},{10,1... | collective-permute-start | bytes 786440 | tf_op jit(solution)/shard_map/while/body/eval_jaxpr/ppermute | solution.py:20
  126.6 7.7 %collective-permute-start.2 = (f32[128,4,128]{2,1,0:T(4,128)S(1)}, f32[128,4,128]{2,1,0:T(4,128)S(1)}, u32[]{:S(2)}, u32[]{:S(2)}) collective-permute-start(f32[128,4,128]{2,1,0:T(4,128)S(1)} %get-tuple-element.378), channel_id=1, source_target_pairs={{0,1},{1,2},{2,3},{3,4},{4,5},{5,6},{6,7},{7,8},{8,9},{9,10},{10,1... | collective-permute-start | bytes 786440 | tf_op jit(solution)/shard_map/while/body/eval_jaxpr/ppermute | solution.py:20
  147.3 4.3 collective-permute-start.4
  156.5 4.3 collective-permute-start.12
  165.8 5.2 %collective-permute-start.6 = (f32[128,4,128]{2,1,0:T(4,128)S(1)}, f32[128,4,128]{2,1,0:T(4,128)S(1)}, u32[]{:S(2)}, u32[]{:S(2)}) collective-permute-start(f32[128,4,128]{2,1,0:T(4,128)S(1)} %get-tuple-element.384), channel_id=1, source_target_pairs={{0,1},{1,2},{2,3},{3,4},{4,5},{5,6},{6,7},{7,8},{8,9},{9,10},{10,1... | collective-permute-start | bytes 786440 | tf_op jit(solution)/shard_map/while/body/eval_jaxpr/ppermute | solution.py:20
  175.1 5.2 %collective-permute-start.14 = (f32[128,4,128]{2,1,0:T(4,128)S(1)}, f32[128,4,128]{2,1,0:T(4,128)S(1)}, u32[]{:S(2)}, u32[]{:S(2)}) collective-permute-start(f32[128,4,128]{2,1,0:T(4,128)S(1)} %get-tuple-element.398), channel_id=1, source_target_pairs={{0,1},{1,2},{2,3},{3,4},{4,5},{5,6},{6,7},{7,8},{8,9},{9,10},{10,1... | collective-permute-start | bytes 786440 | tf_op jit(solution)/shard_map/while/body/eval_jaxpr/ppermute | solution.py:20
  190.3 7.6 %collective-permute-start = (f32[128,4,128]{2,1,0:T(4,128)}, f32[128,4,128]{2,1,0:T(4,128)S(1)}, u32[]{:S(2)}, u32[]{:S(2)}) collective-permute-start(f32[128,4,128]{2,1,0:T(4,128)} %get-tuple-element.425), channel_id=1, source_target_pairs={{0,1},{1,2},{2,3},{3,4},{4,5},{5,6},{6,7},{7,8},{8,9},{9,10},{10,1... | collective-permute-start | bytes 786440 | tf_op jit(solution)/shard_map/while/body/eval_jaxpr/ppermute | solution.py:20
  207.0 7.7 %collective-permute-start.2 = (f32[128,4,128]{2,1,0:T(4,128)S(1)}, f32[128,4,128]{2,1,0:T(4,128)S(1)}, u32[]{:S(2)}, u32[]{:S(2)}) collective-permute-start(f32[128,4,128]{2,1,0:T(4,128)S(1)} %get-tuple-element.378), channel_id=1, source_target_pairs={{0,1},{1,2},{2,3},{3,4},{4,5},{5,6},{6,7},{7,8},{8,9},{9,10},{10,1... | collective-permute-start | bytes 786440 | tf_op jit(solution)/shard_map/while/body/eval_jaxpr/ppermute | solution.py:20
  227.7 4.3 collective-permute-start.4
  236.9 4.3 collective-permute-start.12
  246.2 5.2 %collective-permute-start.6 = (f32[128,4,128]{2,1,0:T(4,128)S(1)}, f32[128,4,128]{2,1,0:T(4,128)S(1)}, u32[]{:S(2)}, u32[]{:S(2)}) collective-permute-start(f32[128,4,128]{2,1,0:T(4,128)S(1)} %get-tuple-element.384), channel_id=1, source_target_pairs={{0,1},{1,2},{2,3},{3,4},{4,5},{5,6},{6,7},{7,8},{8,9},{9,10},{10,1... | collective-permute-start | bytes 786440 | tf_op jit(solution)/shard_map/while/body/eval_jaxpr/ppermute | solution.py:20
  255.5 5.2 %collective-permute-start.14 = (f32[128,4,128]{2,1,0:T(4,128)S(1)}, f32[128,4,128]{2,1,0:T(4,128)S(1)}, u32[]{:S(2)}, u32[]{:S(2)}) collective-permute-start(f32[128,4,128]{2,1,0:T(4,128)S(1)} %get-tuple-element.398), channel_id=1, source_target_pairs={{0,1},{1,2},{2,3},{3,4},{4,5},{5,6},{6,7},{7,8},{8,9},{9,10},{10,1... | collective-permute-start | bytes 786440 | tf_op jit(solution)/shard_map/while/body/eval_jaxpr/ppermute | solution.py:20
  270.7 7.6 %collective-permute-start = (f32[128,4,128]{2,1,0:T(4,128)}, f32[128,4,128]{2,1,0:T(4,128)S(1)}, u32[]{:S(2)}, u32[]{:S(2)}) collective-permute-start(f32[128,4,128]{2,1,0:T(4,128)} %get-tuple-element.425), channel_id=1, source_target_pairs={{0,1},{1,2},{2,3},{3,4},{4,5},{5,6},{6,7},{7,8},{8,9},{9,10},{10,1... | collective-permute-start | bytes 786440 | tf_op jit(solution)/shard_map/while/body/eval_jaxpr/ppermute | solution.py:20
  287.4 7.7 %collective-permute-start.2 = (f32[128,4,128]{2,1,0:T(4,128)S(1)}, f32[128,4,128]{2,1,0:T(4,128)S(1)}, u32[]{:S(2)}, u32[]{:S(2)}) collective-permute-start(f32[128,4,128]{2,1,0:T(4,128)S(1)} %get-tuple-element.378), channel_id=1, source_target_pairs={{0,1},{1,2},{2,3},{3,4},{4,5},{5,6},{6,7},{7,8},{8,9},{9,10},{10,1... | collective-permute-start | bytes 786440 | tf_op jit(solution)/shard_map/while/body/eval_jaxpr/ppermute | solution.py:20
  317.3 4.3 collective-permute-start.12
  326.6 5.2 %collective-permute-start.6 = (f32[128,4,128]{2,1,0:T(4,128)S(1)}, f32[128,4,128]{2,1,0:T(4,128)S(1)}, u32[]{:S(2)}, u32[]{:S(2)}) collective-permute-start(f32[128,4,128]{2,1,0:T(4,128)S(1)} %get-tuple-element.384), channel_id=1, source_target_pairs={{0,1},{1,2},{2,3},{3,4},{4,5},{5,6},{6,7},{7,8},{8,9},{9,10},{10,1... | collective-permute-start | bytes 786440 | tf_op jit(solution)/shard_map/while/body/eval_jaxpr/ppermute | solution.py:20
  335.9 5.2 %collective-permute-start.14 = (f32[128,4,128]{2,1,0:T(4,128)S(1)}, f32[128,4,128]{2,1,0:T(4,128)S(1)}, u32[]{:S(2)}, u32[]{:S(2)}) collective-permute-start(f32[128,4,128]{2,1,0:T(4,128)S(1)} %get-tuple-element.398), channel_id=1, source_target_pairs={{0,1},{1,2},{2,3},{3,4},{4,5},{5,6},{6,7},{7,8},{8,9},{9,10},{10,1... | collective-permute-start | bytes 786440 | tf_op jit(solution)/shard_map/while/body/eval_jaxpr/ppermute | solution.py:20
  351.1 7.6 %collective-permute-start = (f32[128,4,128]{2,1,0:T(4,128)}, f32[128,4,128]{2,1,0:T(4,128)S(1)}, u32[]{:S(2)}, u32[]{:S(2)}) collective-permute-start(f32[128,4,128]{2,1,0:T(4,128)} %get-tuple-element.425), channel_id=1, source_target_pairs={{0,1},{1,2},{2,3},{3,4},{4,5},{5,6},{6,7},{7,8},{8,9},{9,10},{10,1... | collective-permute-start | bytes 786440 | tf_op jit(solution)/shard_map/while/body/eval_jaxpr/ppermute | solution.py:20
  367.8 7.7 %collective-permute-start.2 = (f32[128,4,128]{2,1,0:T(4,128)S(1)}, f32[128,4,128]{2,1,0:T(4,128)S(1)}, u32[]{:S(2)}, u32[]{:S(2)}) collective-permute-start(f32[128,4,128]{2,1,0:T(4,128)S(1)} %get-tuple-element.378), channel_id=1, source_target_pairs={{0,1},{1,2},{2,3},{3,4},{4,5},{5,6},{6,7},{7,8},{8,9},{9,10},{10,1... | collective-permute-start | bytes 786440 | tf_op jit(solution)/shard_map/while/body/eval_jaxpr/ppermute | solution.py:20
  397.7 4.3 collective-permute-start.12
  406.9 5.2 %collective-permute-start.6 = (f32[128,4,128]{2,1,0:T(4,128)S(1)}, f32[128,4,128]{2,1,0:T(4,128)S(1)}, u32[]{:S(2)}, u32[]{:S(2)}) collective-permute-start(f32[128,4,128]{2,1,0:T(4,128)S(1)} %get-tuple-element.384), channel_id=1, source_target_pairs={{0,1},{1,2},{2,3},{3,4},{4,5},{5,6},{6,7},{7,8},{8,9},{9,10},{10,1... | collective-permute-start | bytes 786440 | tf_op jit(solution)/shard_map/while/body/eval_jaxpr/ppermute | solution.py:20
  416.2 5.2 %collective-permute-start.14 = (f32[128,4,128]{2,1,0:T(4,128)S(1)}, f32[128,4,128]{2,1,0:T(4,128)S(1)}, u32[]{:S(2)}, u32[]{:S(2)}) collective-permute-start(f32[128,4,128]{2,1,0:T(4,128)S(1)} %get-tuple-element.398), channel_id=1, source_target_pairs={{0,1},{1,2},{2,3},{3,4},{4,5},{5,6},{6,7},{7,8},{8,9},{9,10},{10,1... | collective-permute-start | bytes 786440 | tf_op jit(solution)/shard_map/while/body/eval_jaxpr/ppermute | solution.py:20
  433.5 13.7 %all-to-all-start.1 = ((f32[128,1,8,128]{3,2,1,0:T(8,128)}), f32[128,1,8,128]{3,2,1,0:T(8,128)S(1)}, u32[]{:S(2)}, u32[]{:S(2)}) async-start(f32[128,1,8,128]{3,2,1,0:T(8,128)} %multiply_bitcast_fusion), calls=%async_computation.1 | async-start | bytes 1048576 | tf_op jit(solution)/shard_map/all_to_all | solution.py:190
  450.3 11.3 %all-to-all-done.1 = f32[128,1,8,128]{3,2,1,0:T(8,128)S(1)} async-done(((f32[128,1,8,128]{3,2,1,0:T(8,128)}), f32[128,1,8,128]{3,2,1,0:T(8,128)S(1)}, u32[]{:S(2)}, u32[]{:S(2)}) %all-to-all-start.1) | async-done | bytes 524320 | tf_op jit(solution)/shard_map/all_to_all | solution.py:190
  (430 shorter events, 265.5 us)
Async XLA Ops:
  3.6 32.3 %all-to-all-start = ((f32[8,16,8,128]{3,2,0,1:T(8,128)}), f32[8,16,8,128]{3,2,0,1:T(8,128)S(1)}, u32[]{:S(2)}, u32[]{:S(2)}) async-start(f32[8,16,8,128]{3,2,0,1:T(8,128)} %select_bitcast_fusion), calls=%async_computation | async-start | bytes 1048576 | tf_op jit(solution)/shard_map/all_to_all | solution.py:140
  40.4 14.9 %collective-permute-start.8 = (f32[128,4,128]{2,1,0:T(4,128)S(1)}, f32[128,4,128]{2,1,0:T(4,128)S(1)}, u32[]{:S(2)}, u32[]{:S(2)}) collective-permute-start(f32[128,4,128]{2,1,0:T(4,128)S(1)} %get-tuple-element.429), channel_id=1, source_target_pairs={{0,1},{1,2},{2,3},{3,4},{4,5},{5,6},{6,7},{7,8},{8,9},{9,10},{10,1... | collective-permute-start | bytes 786440 | tf_op jit(solution)/shard_map/while/body/eval_jaxpr/ppermute | solution.py:20
  49.4 14.1 %collective-permute-start.2 = (f32[128,4,128]{2,1,0:T(4,128)S(1)}, f32[128,4,128]{2,1,0:T(4,128)S(1)}, u32[]{:S(2)}, u32[]{:S(2)}) collective-permute-start(f32[128,4,128]{2,1,0:T(4,128)S(1)} %get-tuple-element.378), channel_id=1, source_target_pairs={{0,1},{1,2},{2,3},{3,4},{4,5},{5,6},{6,7},{7,8},{8,9},{9,10},{10,1... | collective-permute-start | bytes 786440 | tf_op jit(solution)/shard_map/while/body/eval_jaxpr/ppermute | solution.py:20
  58.2 14.5 %collective-permute-start.10 = (f32[128,4,128]{2,1,0:T(4,128)S(1)}, f32[128,4,128]{2,1,0:T(4,128)S(1)}, u32[]{:S(2)}, u32[]{:S(2)}) collective-permute-start(f32[128,4,128]{2,1,0:T(4,128)S(1)} %get-tuple-element.390), channel_id=1, source_target_pairs={{0,1},{1,2},{2,3},{3,4},{4,5},{5,6},{6,7},{7,8},{8,9},{9,10},{10,1... | collective-permute-start | bytes 786440 | tf_op jit(solution)/shard_map/while/body/eval_jaxpr/ppermute | solution.py:20
  67.1 14.8 %collective-permute-start.4 = (f32[128,4,128]{2,1,0:T(4,128)S(1)}, f32[128,4,128]{2,1,0:T(4,128)S(1)}, u32[]{:S(2)}, u32[]{:S(2)}) collective-permute-start(f32[128,4,128]{2,1,0:T(4,128)S(1)} %get-tuple-element.381), channel_id=1, source_target_pairs={{0,1},{1,2},{2,3},{3,4},{4,5},{5,6},{6,7},{7,8},{8,9},{9,10},{10,1... | collective-permute-start | bytes 786440 | tf_op jit(solution)/shard_map/while/body/eval_jaxpr/ppermute | solution.py:20
  76.2 15.6 %collective-permute-start.12 = (f32[128,4,128]{2,1,0:T(4,128)S(1)}, f32[128,4,128]{2,1,0:T(4,128)S(1)}, u32[]{:S(2)}, u32[]{:S(2)}) collective-permute-start(f32[128,4,128]{2,1,0:T(4,128)S(1)} %get-tuple-element.394), channel_id=1, source_target_pairs={{0,1},{1,2},{2,3},{3,4},{4,5},{5,6},{6,7},{7,8},{8,9},{9,10},{10,1... | collective-permute-start | bytes 786440 | tf_op jit(solution)/shard_map/while/body/eval_jaxpr/ppermute | solution.py:20
  85.4 15.7 %collective-permute-start.6 = (f32[128,4,128]{2,1,0:T(4,128)S(1)}, f32[128,4,128]{2,1,0:T(4,128)S(1)}, u32[]{:S(2)}, u32[]{:S(2)}) collective-permute-start(f32[128,4,128]{2,1,0:T(4,128)S(1)} %get-tuple-element.384), channel_id=1, source_target_pairs={{0,1},{1,2},{2,3},{3,4},{4,5},{5,6},{6,7},{7,8},{8,9},{9,10},{10,1... | collective-permute-start | bytes 786440 | tf_op jit(solution)/shard_map/while/body/eval_jaxpr/ppermute | solution.py:20
  118.8 16.8 %collective-permute-start.8 = (f32[128,4,128]{2,1,0:T(4,128)S(1)}, f32[128,4,128]{2,1,0:T(4,128)S(1)}, u32[]{:S(2)}, u32[]{:S(2)}) collective-permute-start(f32[128,4,128]{2,1,0:T(4,128)S(1)} %get-tuple-element.429), channel_id=1, source_target_pairs={{0,1},{1,2},{2,3},{3,4},{4,5},{5,6},{6,7},{7,8},{8,9},{9,10},{10,1... | collective-permute-start | bytes 786440 | tf_op jit(solution)/shard_map/while/body/eval_jaxpr/ppermute | solution.py:20
  126.6 17.1 %collective-permute-start.2 = (f32[128,4,128]{2,1,0:T(4,128)S(1)}, f32[128,4,128]{2,1,0:T(4,128)S(1)}, u32[]{:S(2)}, u32[]{:S(2)}) collective-permute-start(f32[128,4,128]{2,1,0:T(4,128)S(1)} %get-tuple-element.378), channel_id=1, source_target_pairs={{0,1},{1,2},{2,3},{3,4},{4,5},{5,6},{6,7},{7,8},{8,9},{9,10},{10,1... | collective-permute-start | bytes 786440 | tf_op jit(solution)/shard_map/while/body/eval_jaxpr/ppermute | solution.py:20
  138.4 14.5 %collective-permute-start.10 = (f32[128,4,128]{2,1,0:T(4,128)S(1)}, f32[128,4,128]{2,1,0:T(4,128)S(1)}, u32[]{:S(2)}, u32[]{:S(2)}) collective-permute-start(f32[128,4,128]{2,1,0:T(4,128)S(1)} %get-tuple-element.390), channel_id=1, source_target_pairs={{0,1},{1,2},{2,3},{3,4},{4,5},{5,6},{6,7},{7,8},{8,9},{9,10},{10,1... | collective-permute-start | bytes 786440 | tf_op jit(solution)/shard_map/while/body/eval_jaxpr/ppermute | solution.py:20
  147.3 14.9 %collective-permute-start.4 = (f32[128,4,128]{2,1,0:T(4,128)S(1)}, f32[128,4,128]{2,1,0:T(4,128)S(1)}, u32[]{:S(2)}, u32[]{:S(2)}) collective-permute-start(f32[128,4,128]{2,1,0:T(4,128)S(1)} %get-tuple-element.381), channel_id=1, source_target_pairs={{0,1},{1,2},{2,3},{3,4},{4,5},{5,6},{6,7},{7,8},{8,9},{9,10},{10,1... | collective-permute-start | bytes 786440 | tf_op jit(solution)/shard_map/while/body/eval_jaxpr/ppermute | solution.py:20
  156.5 15.8 %collective-permute-start.12 = (f32[128,4,128]{2,1,0:T(4,128)S(1)}, f32[128,4,128]{2,1,0:T(4,128)S(1)}, u32[]{:S(2)}, u32[]{:S(2)}) collective-permute-start(f32[128,4,128]{2,1,0:T(4,128)S(1)} %get-tuple-element.394), channel_id=1, source_target_pairs={{0,1},{1,2},{2,3},{3,4},{4,5},{5,6},{6,7},{7,8},{8,9},{9,10},{10,1... | collective-permute-start | bytes 786440 | tf_op jit(solution)/shard_map/while/body/eval_jaxpr/ppermute | solution.py:20
  165.8 15.8 %collective-permute-start.6 = (f32[128,4,128]{2,1,0:T(4,128)S(1)}, f32[128,4,128]{2,1,0:T(4,128)S(1)}, u32[]{:S(2)}, u32[]{:S(2)}) collective-permute-start(f32[128,4,128]{2,1,0:T(4,128)S(1)} %get-tuple-element.384), channel_id=1, source_target_pairs={{0,1},{1,2},{2,3},{3,4},{4,5},{5,6},{6,7},{7,8},{8,9},{9,10},{10,1... | collective-permute-start | bytes 786440 | tf_op jit(solution)/shard_map/while/body/eval_jaxpr/ppermute | solution.py:20
  199.2 16.8 %collective-permute-start.8 = (f32[128,4,128]{2,1,0:T(4,128)S(1)}, f32[128,4,128]{2,1,0:T(4,128)S(1)}, u32[]{:S(2)}, u32[]{:S(2)}) collective-permute-start(f32[128,4,128]{2,1,0:T(4,128)S(1)} %get-tuple-element.429), channel_id=1, source_target_pairs={{0,1},{1,2},{2,3},{3,4},{4,5},{5,6},{6,7},{7,8},{8,9},{9,10},{10,1... | collective-permute-start | bytes 786440 | tf_op jit(solution)/shard_map/while/body/eval_jaxpr/ppermute | solution.py:20
  207.0 17.1 %collective-permute-start.2 = (f32[128,4,128]{2,1,0:T(4,128)S(1)}, f32[128,4,128]{2,1,0:T(4,128)S(1)}, u32[]{:S(2)}, u32[]{:S(2)}) collective-permute-start(f32[128,4,128]{2,1,0:T(4,128)S(1)} %get-tuple-element.378), channel_id=1, source_target_pairs={{0,1},{1,2},{2,3},{3,4},{4,5},{5,6},{6,7},{7,8},{8,9},{9,10},{10,1... | collective-permute-start | bytes 786440 | tf_op jit(solution)/shard_map/while/body/eval_jaxpr/ppermute | solution.py:20
  218.8 14.5 %collective-permute-start.10 = (f32[128,4,128]{2,1,0:T(4,128)S(1)}, f32[128,4,128]{2,1,0:T(4,128)S(1)}, u32[]{:S(2)}, u32[]{:S(2)}) collective-permute-start(f32[128,4,128]{2,1,0:T(4,128)S(1)} %get-tuple-element.390), channel_id=1, source_target_pairs={{0,1},{1,2},{2,3},{3,4},{4,5},{5,6},{6,7},{7,8},{8,9},{9,10},{10,1... | collective-permute-start | bytes 786440 | tf_op jit(solution)/shard_map/while/body/eval_jaxpr/ppermute | solution.py:20
  227.7 14.9 %collective-permute-start.4 = (f32[128,4,128]{2,1,0:T(4,128)S(1)}, f32[128,4,128]{2,1,0:T(4,128)S(1)}, u32[]{:S(2)}, u32[]{:S(2)}) collective-permute-start(f32[128,4,128]{2,1,0:T(4,128)S(1)} %get-tuple-element.381), channel_id=1, source_target_pairs={{0,1},{1,2},{2,3},{3,4},{4,5},{5,6},{6,7},{7,8},{8,9},{9,10},{10,1... | collective-permute-start | bytes 786440 | tf_op jit(solution)/shard_map/while/body/eval_jaxpr/ppermute | solution.py:20
  236.9 15.8 %collective-permute-start.12 = (f32[128,4,128]{2,1,0:T(4,128)S(1)}, f32[128,4,128]{2,1,0:T(4,128)S(1)}, u32[]{:S(2)}, u32[]{:S(2)}) collective-permute-start(f32[128,4,128]{2,1,0:T(4,128)S(1)} %get-tuple-element.394), channel_id=1, source_target_pairs={{0,1},{1,2},{2,3},{3,4},{4,5},{5,6},{6,7},{7,8},{8,9},{9,10},{10,1... | collective-permute-start | bytes 786440 | tf_op jit(solution)/shard_map/while/body/eval_jaxpr/ppermute | solution.py:20
  246.2 15.8 %collective-permute-start.6 = (f32[128,4,128]{2,1,0:T(4,128)S(1)}, f32[128,4,128]{2,1,0:T(4,128)S(1)}, u32[]{:S(2)}, u32[]{:S(2)}) collective-permute-start(f32[128,4,128]{2,1,0:T(4,128)S(1)} %get-tuple-element.384), channel_id=1, source_target_pairs={{0,1},{1,2},{2,3},{3,4},{4,5},{5,6},{6,7},{7,8},{8,9},{9,10},{10,1... | collective-permute-start | bytes 786440 | tf_op jit(solution)/shard_map/while/body/eval_jaxpr/ppermute | solution.py:20
  279.6 16.8 %collective-permute-start.8 = (f32[128,4,128]{2,1,0:T(4,128)S(1)}, f32[128,4,128]{2,1,0:T(4,128)S(1)}, u32[]{:S(2)}, u32[]{:S(2)}) collective-permute-start(f32[128,4,128]{2,1,0:T(4,128)S(1)} %get-tuple-element.429), channel_id=1, source_target_pairs={{0,1},{1,2},{2,3},{3,4},{4,5},{5,6},{6,7},{7,8},{8,9},{9,10},{10,1... | collective-permute-start | bytes 786440 | tf_op jit(solution)/shard_map/while/body/eval_jaxpr/ppermute | solution.py:20
  287.4 17.1 %collective-permute-start.2 = (f32[128,4,128]{2,1,0:T(4,128)S(1)}, f32[128,4,128]{2,1,0:T(4,128)S(1)}, u32[]{:S(2)}, u32[]{:S(2)}) collective-permute-start(f32[128,4,128]{2,1,0:T(4,128)S(1)} %get-tuple-element.378), channel_id=1, source_target_pairs={{0,1},{1,2},{2,3},{3,4},{4,5},{5,6},{6,7},{7,8},{8,9},{9,10},{10,1... | collective-permute-start | bytes 786440 | tf_op jit(solution)/shard_map/while/body/eval_jaxpr/ppermute | solution.py:20
  299.2 14.5 %collective-permute-start.10 = (f32[128,4,128]{2,1,0:T(4,128)S(1)}, f32[128,4,128]{2,1,0:T(4,128)S(1)}, u32[]{:S(2)}, u32[]{:S(2)}) collective-permute-start(f32[128,4,128]{2,1,0:T(4,128)S(1)} %get-tuple-element.390), channel_id=1, source_target_pairs={{0,1},{1,2},{2,3},{3,4},{4,5},{5,6},{6,7},{7,8},{8,9},{9,10},{10,1... | collective-permute-start | bytes 786440 | tf_op jit(solution)/shard_map/while/body/eval_jaxpr/ppermute | solution.py:20
  308.1 14.9 %collective-permute-start.4 = (f32[128,4,128]{2,1,0:T(4,128)S(1)}, f32[128,4,128]{2,1,0:T(4,128)S(1)}, u32[]{:S(2)}, u32[]{:S(2)}) collective-permute-start(f32[128,4,128]{2,1,0:T(4,128)S(1)} %get-tuple-element.381), channel_id=1, source_target_pairs={{0,1},{1,2},{2,3},{3,4},{4,5},{5,6},{6,7},{7,8},{8,9},{9,10},{10,1... | collective-permute-start | bytes 786440 | tf_op jit(solution)/shard_map/while/body/eval_jaxpr/ppermute | solution.py:20
  317.3 15.8 %collective-permute-start.12 = (f32[128,4,128]{2,1,0:T(4,128)S(1)}, f32[128,4,128]{2,1,0:T(4,128)S(1)}, u32[]{:S(2)}, u32[]{:S(2)}) collective-permute-start(f32[128,4,128]{2,1,0:T(4,128)S(1)} %get-tuple-element.394), channel_id=1, source_target_pairs={{0,1},{1,2},{2,3},{3,4},{4,5},{5,6},{6,7},{7,8},{8,9},{9,10},{10,1... | collective-permute-start | bytes 786440 | tf_op jit(solution)/shard_map/while/body/eval_jaxpr/ppermute | solution.py:20
  326.6 15.8 %collective-permute-start.6 = (f32[128,4,128]{2,1,0:T(4,128)S(1)}, f32[128,4,128]{2,1,0:T(4,128)S(1)}, u32[]{:S(2)}, u32[]{:S(2)}) collective-permute-start(f32[128,4,128]{2,1,0:T(4,128)S(1)} %get-tuple-element.384), channel_id=1, source_target_pairs={{0,1},{1,2},{2,3},{3,4},{4,5},{5,6},{6,7},{7,8},{8,9},{9,10},{10,1... | collective-permute-start | bytes 786440 | tf_op jit(solution)/shard_map/while/body/eval_jaxpr/ppermute | solution.py:20
  360.0 16.8 %collective-permute-start.8 = (f32[128,4,128]{2,1,0:T(4,128)S(1)}, f32[128,4,128]{2,1,0:T(4,128)S(1)}, u32[]{:S(2)}, u32[]{:S(2)}) collective-permute-start(f32[128,4,128]{2,1,0:T(4,128)S(1)} %get-tuple-element.429), channel_id=1, source_target_pairs={{0,1},{1,2},{2,3},{3,4},{4,5},{5,6},{6,7},{7,8},{8,9},{9,10},{10,1... | collective-permute-start | bytes 786440 | tf_op jit(solution)/shard_map/while/body/eval_jaxpr/ppermute | solution.py:20
  367.8 17.1 %collective-permute-start.2 = (f32[128,4,128]{2,1,0:T(4,128)S(1)}, f32[128,4,128]{2,1,0:T(4,128)S(1)}, u32[]{:S(2)}, u32[]{:S(2)}) collective-permute-start(f32[128,4,128]{2,1,0:T(4,128)S(1)} %get-tuple-element.378), channel_id=1, source_target_pairs={{0,1},{1,2},{2,3},{3,4},{4,5},{5,6},{6,7},{7,8},{8,9},{9,10},{10,1... | collective-permute-start | bytes 786440 | tf_op jit(solution)/shard_map/while/body/eval_jaxpr/ppermute | solution.py:20
  379.6 14.5 %collective-permute-start.10 = (f32[128,4,128]{2,1,0:T(4,128)S(1)}, f32[128,4,128]{2,1,0:T(4,128)S(1)}, u32[]{:S(2)}, u32[]{:S(2)}) collective-permute-start(f32[128,4,128]{2,1,0:T(4,128)S(1)} %get-tuple-element.390), channel_id=1, source_target_pairs={{0,1},{1,2},{2,3},{3,4},{4,5},{5,6},{6,7},{7,8},{8,9},{9,10},{10,1... | collective-permute-start | bytes 786440 | tf_op jit(solution)/shard_map/while/body/eval_jaxpr/ppermute | solution.py:20
  388.5 14.9 %collective-permute-start.4 = (f32[128,4,128]{2,1,0:T(4,128)S(1)}, f32[128,4,128]{2,1,0:T(4,128)S(1)}, u32[]{:S(2)}, u32[]{:S(2)}) collective-permute-start(f32[128,4,128]{2,1,0:T(4,128)S(1)} %get-tuple-element.381), channel_id=1, source_target_pairs={{0,1},{1,2},{2,3},{3,4},{4,5},{5,6},{6,7},{7,8},{8,9},{9,10},{10,1... | collective-permute-start | bytes 786440 | tf_op jit(solution)/shard_map/while/body/eval_jaxpr/ppermute | solution.py:20
  397.7 15.8 %collective-permute-start.12 = (f32[128,4,128]{2,1,0:T(4,128)S(1)}, f32[128,4,128]{2,1,0:T(4,128)S(1)}, u32[]{:S(2)}, u32[]{:S(2)}) collective-permute-start(f32[128,4,128]{2,1,0:T(4,128)S(1)} %get-tuple-element.394), channel_id=1, source_target_pairs={{0,1},{1,2},{2,3},{3,4},{4,5},{5,6},{6,7},{7,8},{8,9},{9,10},{10,1... | collective-permute-start | bytes 786440 | tf_op jit(solution)/shard_map/while/body/eval_jaxpr/ppermute | solution.py:20
  406.9 15.8 %collective-permute-start.6 = (f32[128,4,128]{2,1,0:T(4,128)S(1)}, f32[128,4,128]{2,1,0:T(4,128)S(1)}, u32[]{:S(2)}, u32[]{:S(2)}) collective-permute-start(f32[128,4,128]{2,1,0:T(4,128)S(1)} %get-tuple-element.384), channel_id=1, source_target_pairs={{0,1},{1,2},{2,3},{3,4},{4,5},{5,6},{6,7},{7,8},{8,9},{9,10},{10,1... | collective-permute-start | bytes 786440 | tf_op jit(solution)/shard_map/while/body/eval_jaxpr/ppermute | solution.py:20
  433.5 28.2 %all-to-all-start.1 = ((f32[128,1,8,128]{3,2,1,0:T(8,128)}), f32[128,1,8,128]{3,2,1,0:T(8,128)S(1)}, u32[]{:S(2)}, u32[]{:S(2)}) async-start(f32[128,1,8,128]{3,2,1,0:T(8,128)} %multiply_bitcast_fusion), calls=%async_computation.1 | async-start | bytes 1048576 | tf_op jit(solution)/shard_map/all_to_all | solution.py:190
  (161 other events, 1412.1 us)
